TPU v7x, 128 devices: a whole 4x4x4 slice. The times are simulated.
128 devices in a mesh: blk: 16 (over x, y_hi, core), req: 8 (over y_lo, z).
Axes of the slice: x: 4, y: 4 (y_hi: 2, y_lo: 2; y = y_hi * 2 + y_lo), z: 4, core: 2. Of those that a mesh axis runs over, the one named last changes fastest.
Arguments:
- long_q: bfloat16 [16384, 2048], P('blk', 'req'), may hold values from -6 to 6
- long_k: bfloat16 [16384, 2048], P('blk', 'req'), may hold values from -6 to 6
- long_v: bfloat16 [16384, 2048], P('blk', 'req'), may hold values from -6 to 6
- short_q: bfloat16 [8192, 2048], P('blk', 'req'), may hold values from -6 to 6
- short_k: bfloat16 [8192, 2048], P('blk', 'req'), may hold values from -6 to 6
- short_v: bfloat16 [8192, 2048], P('blk', 'req'), may hold values from -6 to 6
- short_seg: int32 [16, 512], P('blk'), may hold values from 0 to 15, never falling along the last dimension, each value on 1 to 96 neighbouring positions
- pool_kv: bfloat16 [1024, 2, 16, 2048], P('blk', None, None, 'req'), may hold values from -6 to 6
- page_table: int32 [16, 16, 4], replicated, may hold values from 0 to 1023, as said below
- w_out: bfloat16 [2048, 2048], replicated, may hold values from -0.125 to 0.125
Outputs:
- long_out: bfloat16 [16384, 2048], P(('blk', 'req'))
- short_out: bfloat16 [8192, 2048], P(('blk', 'req'))
Inputs may be any that keep to these rules, and one draw needn't show every extreme that they name: `short_seg`: along each pack the request numbers never fall, and each of the 16 requests has 1 to 96 tokens, one of them exactly 96. `page_table`: entry [b, s, j] is o * 64 + i for page i of the pool rows held by index o of blk; for every pack b and every o exactly 4 of the 64 entries of b name pages of o.
All inputs are finite; a program needn't handle non-finite values.
Results may differ from a plain program's by a relative error of at most 0.015.
Values may be sent and summed in bfloat16 or wider, within the bound.
No kernel may reach another device: no remote copies, remote signals or barrier semaphores. Data moves between devices by JAX's collectives and lax.ppermute only.
A program may use at most 128 MiB of HBM per device.

v0:
```python
import math

import jax
import jax.numpy as jnp
from jax import lax
from jax.sharding import PartitionSpec as P

HD = 128
PPS = 4


very_negative = -1e30


def fold_block(state_now, query_heads, query_pos, key_block, value_block, block_first):
    acc_sum, run_max, run_total = state_now
    heads_dev = query_heads.shape[1]
    key_heads = key_block.reshape(key_block.shape[0], heads_dev, HD)
    value_heads = value_block.reshape(value_block.shape[0], heads_dev, HD)
    scores = jnp.einsum(
        "qhd,khd->hqk", query_heads, key_heads, preferred_element_type=jnp.float32
    ) * HD ** (-0.5)
    key_pos = block_first + jnp.arange(key_block.shape[0], dtype=jnp.int32)
    allowed = (key_pos[None, :] <= query_pos[:, None])[None]
    scores = jnp.where(allowed, scores, very_negative)
    new_max = jnp.maximum(run_max, jnp.max(scores, axis=-1))
    weights = jnp.where(allowed, jnp.exp(scores - new_max[..., None]), 0.0)
    factor = jnp.exp(run_max - new_max)
    run_total = run_total * factor + jnp.sum(weights, axis=-1)
    acc_sum = acc_sum * factor[..., None] + jnp.einsum(
        "hqk,khd->hqd",
        weights.astype(jnp.bfloat16),
        value_heads,
        preferred_element_type=jnp.float32,
    )
    return (acc_sum, new_max, run_total)


def prompt_attention(queries, query_pos, long_k, long_v):
    row_count, width = queries.shape
    heads_dev = width // HD
    query_heads = queries.reshape(row_count, heads_dev, HD)
    last_pos = jnp.max(query_pos)
    init = (
        jnp.zeros((heads_dev, row_count, HD), jnp.float32),
        jnp.full((heads_dev, row_count), very_negative, jnp.float32),
        jnp.zeros((heads_dev, row_count), jnp.float32),
    )
    key_piece = lax.all_gather(long_k, "blk", axis=0, tiled=True)
    value_piece = lax.all_gather(long_v, "blk", axis=0, tiled=True)
    piece_rows = key_piece.shape[0]
    step_rows = math.gcd(piece_rows, 1024)

    def one_step(block_num, state_in):
        block_start = block_num * step_rows
        key_block = lax.dynamic_slice_in_dim(key_piece, block_start, step_rows, 0)
        value_block = lax.dynamic_slice_in_dim(value_piece, block_start, step_rows, 0)

        def compute_block(state_live):
            return fold_block(
                state_live, query_heads, query_pos, key_block, value_block, block_start
            )

        def keep_state(state_skip):
            return state_skip

        return lax.cond(block_start <= last_pos, compute_block, keep_state, state_in)

    acc_sum, run_max, run_total = lax.fori_loop(0, piece_rows // step_rows, one_step, init)
    merged = acc_sum / run_total[..., None]
    return merged.transpose(1, 0, 2).reshape(row_count, width).astype(jnp.bfloat16)


def pack_attention(
    short_q, short_k, short_v, short_seg, pool_kv, page_table, block_index, block_count
):
    pack_rows, width = short_q.shape
    heads_dev = width // HD
    pool_pages = pool_kv.shape[0]
    page_len = pool_kv.shape[2]
    page_rows = page_table.reshape(block_count, -1)
    entries = page_rows.shape[1]
    capacity = entries // block_count
    owners = page_rows // pool_pages
    places = page_rows % pool_pages
    wanted = owners == block_index
    ranks = jnp.cumsum(wanted.astype(jnp.int32), axis=1) - 1
    picked = wanted[:, :, None] & (
        ranks[:, :, None] == jnp.arange(capacity, dtype=jnp.int32)[None, None, :]
    )
    send_places = jnp.sum(jnp.where(picked, places[:, :, None], 0), axis=1)
    outgoing = pool_kv[send_places.reshape(-1)].reshape(block_count, capacity, 2, page_len, width)
    arrived = lax.all_to_all(outgoing, "blk", split_axis=0, concat_axis=0, tiled=True)
    my_owners = lax.dynamic_index_in_dim(owners, block_index, 0, keepdims=False)
    order = jnp.arange(entries, dtype=jnp.int32)
    before = (my_owners[None, :] == my_owners[:, None]) & (order[None, :] < order[:, None])
    slots = my_owners * capacity + jnp.sum(before.astype(jnp.int32), axis=1)
    fetched = arrived.reshape(block_count * capacity, 2, page_len, width)[slots]
    cache_len = entries * page_len
    key_rows = jnp.concatenate([fetched[:, 0].reshape(cache_len, width), short_k], 0)
    value_rows = jnp.concatenate([fetched[:, 1].reshape(cache_len, width), short_v], 0)
    segment = short_seg[0]
    positions = jnp.arange(pack_rows, dtype=jnp.int32)
    key_seg = jnp.concatenate([jnp.arange(cache_len, dtype=jnp.int32) // (PPS * page_len), segment])
    key_pos = jnp.concatenate([jnp.full((cache_len,), -1, jnp.int32), positions])
    allowed = ((key_seg[None, :] == segment[:, None]) & (key_pos[None, :] <= positions[:, None]))[
        None
    ]
    query_heads = short_q.reshape(pack_rows, heads_dev, HD)
    key_heads = key_rows.reshape(cache_len + pack_rows, heads_dev, HD)
    value_heads = value_rows.reshape(cache_len + pack_rows, heads_dev, HD)
    scores = jnp.einsum(
        "qhd,khd->hqk", query_heads, key_heads, preferred_element_type=jnp.float32
    ) * HD ** (-0.5)
    scores = jnp.where(allowed, scores, very_negative)
    row_max = jnp.max(scores, axis=-1)
    weights = jnp.where(allowed, jnp.exp(scores - row_max[..., None]), 0.0)
    total = jnp.sum(weights, axis=-1)
    numer = jnp.einsum(
        "hqk,khd->hqd",
        weights.astype(jnp.bfloat16),
        value_heads,
        preferred_element_type=jnp.float32,
    )
    merged = numer / total[..., None]
    return merged.transpose(1, 0, 2).reshape(pack_rows, width).astype(jnp.bfloat16)


def per_device(
    long_q, long_k, long_v, short_q, short_k, short_v, short_seg, pool_kv, page_table, w_out
):
    block_count = lax.axis_size("blk")
    block_index = lax.axis_index("blk")
    group_index = lax.axis_index("req")
    row_count, width = long_q.shape
    query_pos = block_index * row_count + jnp.arange(row_count, dtype=jnp.int32)
    long_attn = prompt_attention(long_q, query_pos, long_k, long_v)
    short_attn = pack_attention(
        short_q, short_k, short_v, short_seg, pool_kv, page_table, block_index, block_count
    )
    w_rows = lax.dynamic_slice_in_dim(w_out, group_index * width, width, 0)
    long_out = lax.psum_scatter(
        jnp.dot(long_attn, w_rows, preferred_element_type=jnp.float32).astype(jnp.bfloat16),
        "req",
        scatter_dimension=0,
        tiled=True,
    )
    short_out = lax.psum_scatter(
        jnp.dot(short_attn, w_rows, preferred_element_type=jnp.float32).astype(jnp.bfloat16),
        "req",
        scatter_dimension=0,
        tiled=True,
    )
    return (long_out, short_out)


def solution(mesh):
    placed = (
        P("blk", "req"),
        P("blk", "req"),
        P("blk", "req"),
        P("blk", "req"),
        P("blk", "req"),
        P("blk", "req"),
        P("blk", None),
        P("blk", None, None, "req"),
        P(),
        P(),
    )
    return jax.shard_map(
        per_device,
        mesh=mesh,
        in_specs=placed,
        out_specs=(P(("blk", "req"), None), P(("blk", "req"), None)),
        check_vma=False,
    )
```

profile of v0, /device:TPU:0, one launch (start us, length us, event | category | flops | bytes accessed | tf_op | source)
XLA Modules:
  0.0 403.2 jit_solution(17348322285215755611)
XLA Ops:
  8.0 0.0 copy-start
  8.0 0.0 copy-start.4
  8.0 0.0 copy-start.2
  8.0 0.0 copy-start.3
  8.0 0.0 copy-start.5
  8.1 0.0 all-gather.3.cloned.1.call-start
  8.1 2.1 copy.40
  10.2 0.0 all-gather.3.cloned.1.call-update
  10.3 0.0 all-gather.5.cloned.1.call-start
  10.3 2.1 copy.42
  12.4 0.0 all-gather.5.cloned.1.call-update
  12.4 0.8 copy.45
  13.2 0.1 copy.46
  13.3 0.2 reduce_window_sum.11
  13.6 0.1 select_reduce_fusion
  13.7 0.1 copy.50
  13.8 0.1 reshape.279
  13.9 0.0 copy-done
  13.9 1.6 gather_fusion
  15.5 7.1 %all-to-all-start = ((bf16[16,4,2,16,256]{4,3,2,1,0:T(8,128)(2,1)}), bf16[16,4,2,16,256]{4,3,2,1,0:T(8,128)(2,1)S(1)}, u32[]{:S(2)}, u32[]{:S(2)}) async-start(bf16[16,4,2,16,256]{4,3,2,1,0:T(8,128)(2,1)} %bitcast.9), calls=%async_computation.1 | async-start | bytes 2097152 | tf_op jit(solution)/shard_map/all_to_all | solution.py:93
  22.7 0.0 reduce-scatter.5.cloned.1.call-start
  22.7 0.0 copy-done.2
  22.7 0.1 copy.51
  22.9 0.8 copy.53
  23.7 0.0 copy-done.3
  23.7 0.1 copy.55
  23.9 0.2 convert_reduce_fusion
  24.1 0.0 copy-done.5
  24.1 0.0 copy-done.4
  24.1 1.9 fusion.20
  26.0 19.2 %all-to-all-done = bf16[16,4,2,16,256]{4,3,2,1,0:T(8,128)(2,1)S(1)} async-done(((bf16[16,4,2,16,256]{4,3,2,1,0:T(8,128)(2,1)}), bf16[16,4,2,16,256]{4,3,2,1,0:T(8,128)(2,1)S(1)}, u32[]{:S(2)}, u32[]{:S(2)}) %all-to-all-start) | async-done | bytes 1048608 | tf_op jit(solution)/shard_map/all_to_all | solution.py:93
  45.3 0.6 gather_fusion.1
  45.9 0.9 fusion.64
  46.7 1.2 concatenate.21
  47.9 0.1 copy.52
  48.0 0.1 concatenate.24
  48.1 0.4 copy.56
  48.6 6.6 %fusion.65 = (f32[2,512]{1,0:T(2,128)S(1)}, bf16[2,512,1536]{1,2,0:T(8,128)(2,1)}) fusion(pred[512,1536]{0,1:T(8,128)(4,1)} %fusion.20, bf16[512,2,128]{2,0,1:T(8,128)(2,1)} %copy.53, bf16[1024,2,128]{2,0,1:T(8,128)(2,1)S(1)} %copy.52, bf16[512,256]{1,0:T(8,128)(2,1)} %param.17), kind=kOutput, calls=%fused_computation.93 | convolution fusion | flops 413664768 | bytes 4984832 | tf_op jit(solution)/shard_map/sub | solution.py:117
  55.1 0.0 copy-start.1
  55.1 2.5 fusion.28
  57.7 3.6 convolution_convert_fusion.1
  61.3 0.0 reduce-scatter.5.cloned.1.call-update
  61.3 0.2 reduce-scatter.3.cloned.1.call-start
  61.6 0.6 add_reduce_fusion
  62.2 0.0 copy-done.1
  62.2 0.2 copy.41
  62.4 0.3 copy.43
  62.7 33.8 %all-gather.3.cloned.1.call-done = bf16[16384,256]{0,1:T(8,128)(2,1)} async-done(((bf16[1024,256]{0,1:T(8,128)(2,1)}), bf16[16384,256]{0,1:T(8,128)(2,1)}) %all-gather.3.cloned.1.call-update) | async-done | bytes 8388624 | tf_op jit(solution)/shard_map/all_gather | solution.py:49
  96.5 73.6 %all-gather.5.cloned.1.call-done = bf16[16384,256]{0,1:T(8,128)(2,1)} async-done(((bf16[1024,256]{0,1:T(8,128)(2,1)}), bf16[16384,256]{0,1:T(8,128)(2,1)}) %all-gather.5.cloned.1.call-update) | async-done | bytes 8388624 | tf_op jit(solution)/shard_map/all_gather | solution.py:50
  170.1 0.1 broadcast_in_dim.90
  170.2 20.7 %while.18 = (s32[]{:T(128)}, f32[2,1024,128]{2,1,0:T(8,128)S(1)}, f32[2,1024]{1,0:T(2,128)S(1)}, f32[2,1024]{1,0:T(2,128)S(1)}, s32[]{:T(128)}, /*index=5*/bf16[...) while((s32[]{:T(128)}, f32[2,1024,128]{2,1,0:T(8,128)S(1)}, ...), condition=%wide.region_6.7_spmd.clone, body=%wide.region_1.6_spmd.clone.sunk | while | flops 1102583808 | bytes 35283264 | solution.py:69
  170.9 10.0 %conditional.3 = ((f32[2,1024,128]{2,1,0:T(8,128)S(1)}, f32[2,1024]{1,0:T(2,128)S(1)}, f32[2,1024]{1,0:T(2,128)S(1)})) conditional(s32[]{:T(128)} %convert_element_type.77, (f32[2,1024,128]{2,1,0:T(8,128)S(1)}, f32[2,1024]{1,0:T(2,128)S(1)}, f32[2,1024]{1,0:T(2,128)S(1)}) %tuple.66, (s32[]{:T(128)}, s32[]{:T(128)}, bf16[16384,256]{0,1:T(8,128)(2,1)}, ...), branch_computations={%region_2.0_spmd, %region_3.5_spmd} | conditional | flops 1102583808 | bytes 35278928 | solution.py:67
  170.9 1.3 constant_dynamic-slice_fusion
  172.2 0.7 broadcast_compare_fusion
  172.8 2.0 fusion.2
  174.8 2.3 fusion.3
  177.1 3.7 fusion.8
  190.9 0.3 copy.44
  191.2 0.1 divide_convert_fusion
  191.3 4.5 %convolution_convert_fusion = bf16[1024,2048]{1,0:T(8,128)(2,1)} fusion(bf16[1024,256]{0,1:T(8,128)(2,1)S(1)} %bitcast.78, bf16[2048,2048]{1,0:T(8,128)(2,1)} %param.23, s32[]{:T(128)S(6)} %select_n.90), kind=kOutput, calls=%fused_computation.25 | convolution fusion | flops 1075838976 | bytes 5767172 | tf_op jit(solution)/shard_map/dot_general | solution.py:143
  195.8 0.0 reduce-scatter.3.cloned.1.call-update
  195.8 0.0 reduce-scatter.5.cloned.1.call-done
  195.9 199.9 %reduce-scatter.3.cloned.1.call-done = bf16[128,2048]{1,0:T(8,128)(2,1)} async-done(((bf16[1024,2048]{1,0:T(8,128)(2,1)}), bf16[128,2048]{1,0:T(8,128)(2,1)}) %reduce-scatter.3.cloned.1.call-update) | async-done | bytes 524304 | tf_op jit(solution)/shard_map/reduce_scatter | solution.py:142
  (47 shorter events, 0.4 us)
Async XLA Ops:
  8.0 5.9 %copy-start = (bf16[64,2,16,256]{3,2,1,0:T(8,128)(2,1)S(1)}, bf16[64,2,16,256]{3,2,1,0:T(8,128)(2,1)}, u32[]{:S(2)}) copy-start(bf16[64,2,16,256]{3,2,1,0:T(8,128)(2,1)} %param.21) | copy-start | bytes 3145732
  8.0 16.1 %copy-start.4 = (s32[1536]{0:T(1024)S(1)}, s32[1536]{0:T(1024)}, u32[]{:S(2)}) copy-start(s32[1536]{0:T(1024)} %constant.138.clone.1) | copy-start | bytes 18436
  8.0 14.7 %copy-start.2 = (bf16[512,256]{1,0:T(8,128)(2,1)S(1)}, bf16[512,256]{1,0:T(8,128)(2,1)}, u32[]{:S(2)}) copy-start(bf16[512,256]{1,0:T(8,128)(2,1)} %param.18) | copy-start | bytes 786436
  8.0 15.7 %copy-start.3 = (bf16[512,256]{1,0:T(8,128)(2,1)S(1)}, bf16[512,256]{1,0:T(8,128)(2,1)}, u32[]{:S(2)}) copy-start(bf16[512,256]{1,0:T(8,128)(2,1)} %param.19) | copy-start | bytes 786436
  8.0 16.1 %copy-start.5 = (s32[1,512]{1,0:T(1,128)S(1)}, s32[1,512]{1,0:T(1,128)}, u32[]{:S(2)}) copy-start(s32[1,512]{1,0:T(1,128)} %param.20) | copy-start | bytes 6148
  8.1 88.4 %all-gather.3.cloned.1.call-start = ((), (), s32[]{:S(2)}) async-start(), calls=%async_computation.3 | async-start | bytes 8912896 | tf_op jit(solution)/shard_map/all_gather | solution.py:49
  10.3 159.8 %all-gather.5.cloned.1.call-start = ((), (), s32[]{:S(2)}) async-start(), calls=%async_computation.4 | async-start | bytes 8912896 | tf_op jit(solution)/shard_map/all_gather | solution.py:50
  15.5 29.7 %all-to-all-start = ((bf16[16,4,2,16,256]{4,3,2,1,0:T(8,128)(2,1)}), bf16[16,4,2,16,256]{4,3,2,1,0:T(8,128)(2,1)S(1)}, u32[]{:S(2)}, u32[]{:S(2)}) async-start(bf16[16,4,2,16,256]{4,3,2,1,0:T(8,128)(2,1)} %bitcast.9), calls=%async_computation.1 | async-start | bytes 2097152 | tf_op jit(solution)/shard_map/all_to_all | solution.py:93
  22.7 173.2 %reduce-scatter.5.cloned.1.call-start = ((), (), s32[]{:S(2)}) async-start(), calls=%async_computation.6 | async-start | bytes 2359296 | tf_op jit(solution)/shard_map/reduce_scatter | solution.py:148
  55.1 7.1 %copy-start.1 = (bf16[1024,256]{1,0:T(8,128)(2,1)S(1)}, bf16[1024,256]{1,0:T(8,128)(2,1)}, u32[]{:S(2)}) copy-start(bf16[1024,256]{1,0:T(8,128)(2,1)} %param.14) | copy-start | bytes 1572868
  61.3 334.5 %reduce-scatter.3.cloned.1.call-start = ((), (), s32[]{:S(2)}) async-start(), calls=%async_computation.5 | async-start | bytes 4718592 | tf_op jit(solution)/shard_map/reduce_scatter | solution.py:142
Sparse Core Ops, SparseCore 0:
  11.9 84.5 all-gather.2
  98.9 71.1 all-gather.4
Sparse Core Ops, SparseCore 1:
  61.4 58.2 reduce-scatter.4
  195.9 199.8 reduce-scatter.2
where the time goes:
time: 405 us; the launch traced here: 403 us
  waiting for transfers between devices  327 us (81%)
  matrix products  22.9 us (6%)
  between operations  15.8 us (4%)
  local copies, waits for them, and re-layouts  13.5 us (3%)
  loops' own time  10.7 us (3%)
  starting transfers between devices  7.47 us (2%)
  other arithmetic  6.19 us (2%)
    reduce_scatter x1, waiting for transfers between devices, per_device(): lax.psum_scatter(jnp.dot(long_attn, w_rows, preferred_element_type=jnp.fl...  200 us
    all_gather x1, waiting for transfers between devices, prompt_attention(): value_piece = lax.all_gather(long_v, 'blk', axis=0, tiled=True)  73.6 us
    all_gather x1, waiting for transfers between devices, prompt_attention(): key_piece = lax.all_gather(long_k, 'blk', axis=0, tiled=True)  33.8 us
    all_to_all x1, waiting for transfers between devices, pack_attention(): lax.all_to_all(outgoing, 'blk', split_axis=0, concat_axis=0, tiled=True)  19.2 us
    another operation x1, loops' own time, prompt_attention(): lax.fori_loop(0, piece_rows // step_rows, one_step, init)  10.4 us
  transfers between devices with their start and end apart: 5, of which 4 were waited for; matrix products, arithmetic and copies ran while one was open for 10% of the time, Pallas kernels for 0%

commit v1 on v0

--- a/solution.py
+++ b/solution.py
@@ -131,26 +131,16 @@
 ):
     block_count = lax.axis_size("blk")
     block_index = lax.axis_index("blk")
-    group_index = lax.axis_index("req")
     row_count, width = long_q.shape
     query_pos = block_index * row_count + jnp.arange(row_count, dtype=jnp.int32)
     long_attn = prompt_attention(long_q, query_pos, long_k, long_v)
     short_attn = pack_attention(
         short_q, short_k, short_v, short_seg, pool_kv, page_table, block_index, block_count
     )
-    w_rows = lax.dynamic_slice_in_dim(w_out, group_index * width, width, 0)
-    long_out = lax.psum_scatter(
-        jnp.dot(long_attn, w_rows, preferred_element_type=jnp.float32).astype(jnp.bfloat16),
-        "req",
-        scatter_dimension=0,
-        tiled=True,
-    )
-    short_out = lax.psum_scatter(
-        jnp.dot(short_attn, w_rows, preferred_element_type=jnp.float32).astype(jnp.bfloat16),
-        "req",
-        scatter_dimension=0,
-        tiled=True,
-    )
+    long_rows = lax.all_to_all(long_attn, "req", 0, 1, tiled=True)
+    short_rows = lax.all_to_all(short_attn, "req", 0, 1, tiled=True)
+    long_out = jnp.dot(long_rows, w_out, preferred_element_type=jnp.float32).astype(jnp.bfloat16)
+    short_out = jnp.dot(short_rows, w_out, preferred_element_type=jnp.float32).astype(jnp.bfloat16)
     return (long_out, short_out)
 
 

time: 405 us -> 366 us (0.904)
  the two profiles are of different devices: /device:TPU:0 before, /device:TPU:23 now
where the time goes in v1:
time: 366 us; the launch traced here: 365 us
  waiting for transfers between devices  121 us (33%)
  matrix products  112 us (31%)
  other arithmetic  50.7 us (14%)
  local copies, waits for them, and re-layouts  35.5 us (10%)
  starting transfers between devices  19.5 us (5%)
  between operations  14.3 us (4%)
  loops' own time  12.7 us (3%)
    all_gather x1, waiting for transfers between devices, prompt_attention(): value_piece = lax.all_gather(long_v, 'blk', axis=0, tiled=True)  73 us
    dot_general x16, matrix products, fold_block(): jnp.einsum('hqk,khd->hqd', weights.astype(jnp.bfloat16), value_heads, pre...  59.4 us
    reduce_sum x16, other arithmetic, fold_block(): run_total = run_total * factor + jnp.sum(weights, axis=-1)  36.1 us
    dot_general x16, matrix products, fold_block(): jnp.einsum('qhd,khd->hqk', query_heads, key_heads, preferred_element_type...  31.7 us
    all_gather x1, waiting for transfers between devices, prompt_attention(): key_piece = lax.all_gather(long_k, 'blk', axis=0, tiled=True)  24.4 us
    dynamic_slice x16, local copies, waits for them, and re-layouts, one_step(): lax.dynamic_slice_in_dim(value_piece, block_start, step_rows, 0)  20.4 us
    all_to_all x1, waiting for transfers between devices, pack_attention(): lax.all_to_all(outgoing, 'blk', split_axis=0, concat_axis=0, tiled=True)  13.7 us
    another operation x1, loops' own time, prompt_attention(): lax.fori_loop(0, piece_rows // step_rows, one_step, init)  11.5 us
  transfers between devices with their start and end apart: 5, of which 5 were waited for; matrix products, arithmetic and copies ran while one was open for 8% of the time, Pallas kernels for 0%

profile of v1, /device:TPU:23, one launch (start us, length us, event | category | flops | bytes accessed | tf_op | source)
XLA Modules:
  0.0 365.3 jit_solution(18137479885718596948)
XLA Ops:
  7.3 2.1 copy.91
  9.5 2.0 copy.93
  14.7 7.5 %all-to-all-start.1 = ((bf16[16,4,2,16,256]{4,3,2,1,0:T(8,128)(2,1)}), bf16[16,4,2,16,256]{4,3,2,1,0:T(8,128)(2,1)S(1)}, u32[]{:S(2)}, u32[]{:S(2)}) async-start(bf16[16,4,2,16,256]{4,3,2,1,0:T(8,128)(2,1)} %bitcast.10), calls=%async_computation.1 | async-start | bytes 2097152 | tf_op jit(solution)/shard_map/all_to_all | solution.py:93
  26.6 13.7 %all-to-all-done.1 = bf16[16,4,2,16,256]{4,3,2,1,0:T(8,128)(2,1)S(1)} async-done(((bf16[16,4,2,16,256]{4,3,2,1,0:T(8,128)(2,1)}), bf16[16,4,2,16,256]{4,3,2,1,0:T(8,128)(2,1)S(1)}, u32[]{:S(2)}, u32[]{:S(2)}) %all-to-all-start.1) | async-done | bytes 1048608 | tf_op jit(solution)/shard_map/all_to_all | solution.py:93
  43.3 6.5 %fusion.62 = (f32[2,512]{1,0:T(2,128)S(1)}, bf16[2,512,1536]{1,2,0:T(8,128)(2,1)}) fusion(pred[512,1536]{0,1:T(8,128)(4,1)} %fusion.20, bf16[512,2,128]{2,0,1:T(8,128)(2,1)S(1)} %copy.105, bf16[1024,2,128]{2,0,1:T(8,128)(2,1)S(1)} %copy.104, bf16[512,256]{1,0:T(8,128)(2,1)} %param.17), kind=kOutput, calls=%fused_computation.90 | convolution fusion | flops 413664768 | bytes 4984832 | tf_op jit(solution)/shard_map/sub | solution.py:117
  49.8 3.3 fusion.28
  54.3 6.3 %all-to-all-start.2 = ((bf16[8,64,256]{2,1,0:T(8,128)(2,1)}), bf16[8,64,256]{2,1,0:T(8,128)(2,1)S(1)}, u32[]{:S(2)}, u32[]{:S(2)}) async-start(bf16[8,64,256]{2,1,0:T(8,128)(2,1)} %convert_element_type.57), calls=%async_computation.2 | async-start | bytes 524288 | tf_op jit(solution)/shard_map/all_to_all | solution.py:141
  61.8 7.9 %all-to-all-done.2 = bf16[8,64,256]{2,1,0:T(8,128)(2,1)S(1)} async-done(((bf16[8,64,256]{2,1,0:T(8,128)(2,1)}), bf16[8,64,256]{2,1,0:T(8,128)(2,1)S(1)}, u32[]{:S(2)}, u32[]{:S(2)}) %all-to-all-start.2) | async-done | bytes 262176 | tf_op jit(solution)/shard_map/all_to_all | solution.py:141
  69.8 24.4 %all-gather.3.cloned.1.call-done = bf16[16384,256]{0,1:T(8,128)(2,1)} async-done(((bf16[1024,256]{0,1:T(8,128)(2,1)}), bf16[16384,256]{0,1:T(8,128)(2,1)}) %all-gather.3.cloned.1.call-update) | async-done | bytes 8388624 | tf_op jit(solution)/shard_map/all_gather | solution.py:49
  94.1 73.0 %all-gather.5.cloned.1.call-done = bf16[16384,256]{0,1:T(8,128)(2,1)} async-done(((bf16[1024,256]{0,1:T(8,128)(2,1)}), bf16[16384,256]{0,1:T(8,128)(2,1)}) %all-gather.5.cloned.1.call-update) | async-done | bytes 8388624 | tf_op jit(solution)/shard_map/all_gather | solution.py:50
  167.3 171.3 %while.18 = (s32[]{:T(128)}, f32[2,1024,128]{2,1,0:T(8,128)S(1)}, f32[2,1024]{1,0:T(2,128)S(1)}, f32[2,1024]{1,0:T(2,128)S(1)}, s32[]{:T(128)}, /*index=5*/bf16[...) while((s32[]{:T(128)}, f32[2,1024,128]{2,1,0:T(8,128)S(1)}, ...), condition=%wide.region_6.7_spmd.clone, body=%wide.region_1.6_spmd.clone.sunk | while | flops 1102583808 | bytes 35283264 | solution.py:69
  168.0 10.0 %conditional.3 = ((f32[2,1024,128]{2,1,0:T(8,128)S(1)}, f32[2,1024]{1,0:T(2,128)S(1)}, f32[2,1024]{1,0:T(2,128)S(1)})) conditional(s32[]{:T(128)} %convert_element_type.81, (f32[2,1024,128]{2,1,0:T(8,128)S(1)}, f32[2,1024]{1,0:T(2,128)S(1)}, f32[2,1024]{1,0:T(2,128)S(1)}) %tuple.69, (s32[]{:T(128)}, s32[]{:T(128)}, bf16[16384,256]{0,1:T(8,128)(2,1)}, ...), branch_computations={%region_2.0_spmd, %region_3.5_spmd} | conditional | flops 1102583808 | bytes 35278928 | solution.py:67
  172.0 2.3 fusion.3
  174.3 3.7 %fusion.8 = f32[2,1024,128]{2,1,0:T(8,128)S(1)} fusion(bf16[1024,2,128]{0,2,1:T(8,128)(2,1)S(1)} %bitcast.86, f32[2,1024,1024]{2,1,0:T(8,128)S(1)} %get-tuple-element.359, f32[2,1024]{1,0:T(2,128)S(1)} %max.5, pred[1024,1024]{0,1:T(8,128)(4,1)S(1)} %broadcast_compare_fusion, f32[2,1024,128]{2,1,0:T(8,128)S(1)} %get-tuple-element.245, ...), kind=kOutput, calls=%fused_computation.11 | convolution fusion | flops 547880960 | bytes 12075008 | tf_op jit(solution)/shard_map/while/body/eval_jaxpr/cond/branch_1_fun/hqk,khd->hqd/dot_general | solution.py:30
  178.7 10.0 %conditional.3 = ((f32[2,1024,128]{2,1,0:T(8,128)S(1)}, f32[2,1024]{1,0:T(2,128)S(1)}, f32[2,1024]{1,0:T(2,128)S(1)})) conditional(s32[]{:T(128)} %convert_element_type.81, (f32[2,1024,128]{2,1,0:T(8,128)S(1)}, f32[2,1024]{1,0:T(2,128)S(1)}, f32[2,1024]{1,0:T(2,128)S(1)}) %tuple.69, (s32[]{:T(128)}, s32[]{:T(128)}, bf16[16384,256]{0,1:T(8,128)(2,1)}, ...), branch_computations={%region_2.0_spmd, %region_3.5_spmd} | conditional | flops 1102583808 | bytes 35278928 | solution.py:67
  180.7 2.0 fusion.2
  182.7 2.3 fusion.3
  185.0 3.7 %fusion.8 = f32[2,1024,128]{2,1,0:T(8,128)S(1)} fusion(bf16[1024,2,128]{0,2,1:T(8,128)(2,1)S(1)} %bitcast.86, f32[2,1024,1024]{2,1,0:T(8,128)S(1)} %get-tuple-element.359, f32[2,1024]{1,0:T(2,128)S(1)} %max.5, pred[1024,1024]{0,1:T(8,128)(4,1)S(1)} %broadcast_compare_fusion, f32[2,1024,128]{2,1,0:T(8,128)S(1)} %get-tuple-element.245, ...), kind=kOutput, calls=%fused_computation.11 | convolution fusion | flops 547880960 | bytes 12075008 | tf_op jit(solution)/shard_map/while/body/eval_jaxpr/cond/branch_1_fun/hqk,khd->hqd/dot_general | solution.py:30
  189.4 10.0 %conditional.3 = ((f32[2,1024,128]{2,1,0:T(8,128)S(1)}, f32[2,1024]{1,0:T(2,128)S(1)}, f32[2,1024]{1,0:T(2,128)S(1)})) conditional(s32[]{:T(128)} %convert_element_type.81, (f32[2,1024,128]{2,1,0:T(8,128)S(1)}, f32[2,1024]{1,0:T(2,128)S(1)}, f32[2,1024]{1,0:T(2,128)S(1)}) %tuple.69, (s32[]{:T(128)}, s32[]{:T(128)}, bf16[16384,256]{0,1:T(8,128)(2,1)}, ...), branch_computations={%region_2.0_spmd, %region_3.5_spmd} | conditional | flops 1102583808 | bytes 35278928 | solution.py:67
  193.4 2.3 fusion.3
  195.7 3.7 %fusion.8 = f32[2,1024,128]{2,1,0:T(8,128)S(1)} fusion(bf16[1024,2,128]{0,2,1:T(8,128)(2,1)S(1)} %bitcast.86, f32[2,1024,1024]{2,1,0:T(8,128)S(1)} %get-tuple-element.359, f32[2,1024]{1,0:T(2,128)S(1)} %max.5, pred[1024,1024]{0,1:T(8,128)(4,1)S(1)} %broadcast_compare_fusion, f32[2,1024,128]{2,1,0:T(8,128)S(1)} %get-tuple-element.245, ...), kind=kOutput, calls=%fused_computation.11 | convolution fusion | flops 547880960 | bytes 12075008 | tf_op jit(solution)/shard_map/while/body/eval_jaxpr/cond/branch_1_fun/hqk,khd->hqd/dot_general | solution.py:30
  200.1 10.0 %conditional.3 = ((f32[2,1024,128]{2,1,0:T(8,128)S(1)}, f32[2,1024]{1,0:T(2,128)S(1)}, f32[2,1024]{1,0:T(2,128)S(1)})) conditional(s32[]{:T(128)} %convert_element_type.81, (f32[2,1024,128]{2,1,0:T(8,128)S(1)}, f32[2,1024]{1,0:T(2,128)S(1)}, f32[2,1024]{1,0:T(2,128)S(1)}) %tuple.69, (s32[]{:T(128)}, s32[]{:T(128)}, bf16[16384,256]{0,1:T(8,128)(2,1)}, ...), branch_computations={%region_2.0_spmd, %region_3.5_spmd} | conditional | flops 1102583808 | bytes 35278928 | solution.py:67
  204.1 2.3 fusion.3
  206.4 3.7 %fusion.8 = f32[2,1024,128]{2,1,0:T(8,128)S(1)} fusion(bf16[1024,2,128]{0,2,1:T(8,128)(2,1)S(1)} %bitcast.86, f32[2,1024,1024]{2,1,0:T(8,128)S(1)} %get-tuple-element.359, f32[2,1024]{1,0:T(2,128)S(1)} %max.5, pred[1024,1024]{0,1:T(8,128)(4,1)S(1)} %broadcast_compare_fusion, f32[2,1024,128]{2,1,0:T(8,128)S(1)} %get-tuple-element.245, ...), kind=kOutput, calls=%fused_computation.11 | convolution fusion | flops 547880960 | bytes 12075008 | tf_op jit(solution)/shard_map/while/body/eval_jaxpr/cond/branch_1_fun/hqk,khd->hqd/dot_general | solution.py:30
  210.8 10.0 %conditional.3 = ((f32[2,1024,128]{2,1,0:T(8,128)S(1)}, f32[2,1024]{1,0:T(2,128)S(1)}, f32[2,1024]{1,0:T(2,128)S(1)})) conditional(s32[]{:T(128)} %convert_element_type.81, (f32[2,1024,128]{2,1,0:T(8,128)S(1)}, f32[2,1024]{1,0:T(2,128)S(1)}, f32[2,1024]{1,0:T(2,128)S(1)}) %tuple.69, (s32[]{:T(128)}, s32[]{:T(128)}, bf16[16384,256]{0,1:T(8,128)(2,1)}, ...), branch_computations={%region_2.0_spmd, %region_3.5_spmd} | conditional | flops 1102583808 | bytes 35278928 | solution.py:67
  214.8 2.3 fusion.3
  217.1 3.7 %fusion.8 = f32[2,1024,128]{2,1,0:T(8,128)S(1)} fusion(bf16[1024,2,128]{0,2,1:T(8,128)(2,1)S(1)} %bitcast.86, f32[2,1024,1024]{2,1,0:T(8,128)S(1)} %get-tuple-element.359, f32[2,1024]{1,0:T(2,128)S(1)} %max.5, pred[1024,1024]{0,1:T(8,128)(4,1)S(1)} %broadcast_compare_fusion, f32[2,1024,128]{2,1,0:T(8,128)S(1)} %get-tuple-element.245, ...), kind=kOutput, calls=%fused_computation.11 | convolution fusion | flops 547880960 | bytes 12075008 | tf_op jit(solution)/shard_map/while/body/eval_jaxpr/cond/branch_1_fun/hqk,khd->hqd/dot_general | solution.py:30
  221.5 10.0 %conditional.3 = ((f32[2,1024,128]{2,1,0:T(8,128)S(1)}, f32[2,1024]{1,0:T(2,128)S(1)}, f32[2,1024]{1,0:T(2,128)S(1)})) conditional(s32[]{:T(128)} %convert_element_type.81, (f32[2,1024,128]{2,1,0:T(8,128)S(1)}, f32[2,1024]{1,0:T(2,128)S(1)}, f32[2,1024]{1,0:T(2,128)S(1)}) %tuple.69, (s32[]{:T(128)}, s32[]{:T(128)}, bf16[16384,256]{0,1:T(8,128)(2,1)}, ...), branch_computations={%region_2.0_spmd, %region_3.5_spmd} | conditional | flops 1102583808 | bytes 35278928 | solution.py:67
  225.5 2.3 fusion.3
  227.8 3.7 %fusion.8 = f32[2,1024,128]{2,1,0:T(8,128)S(1)} fusion(bf16[1024,2,128]{0,2,1:T(8,128)(2,1)S(1)} %bitcast.86, f32[2,1024,1024]{2,1,0:T(8,128)S(1)} %get-tuple-element.359, f32[2,1024]{1,0:T(2,128)S(1)} %max.5, pred[1024,1024]{0,1:T(8,128)(4,1)S(1)} %broadcast_compare_fusion, f32[2,1024,128]{2,1,0:T(8,128)S(1)} %get-tuple-element.245, ...), kind=kOutput, calls=%fused_computation.11 | convolution fusion | flops 547880960 | bytes 12075008 | tf_op jit(solution)/shard_map/while/body/eval_jaxpr/cond/branch_1_fun/hqk,khd->hqd/dot_general | solution.py:30
  232.2 10.0 %conditional.3 = ((f32[2,1024,128]{2,1,0:T(8,128)S(1)}, f32[2,1024]{1,0:T(2,128)S(1)}, f32[2,1024]{1,0:T(2,128)S(1)})) conditional(s32[]{:T(128)} %convert_element_type.81, (f32[2,1024,128]{2,1,0:T(8,128)S(1)}, f32[2,1024]{1,0:T(2,128)S(1)}, f32[2,1024]{1,0:T(2,128)S(1)}) %tuple.69, (s32[]{:T(128)}, s32[]{:T(128)}, bf16[16384,256]{0,1:T(8,128)(2,1)}, ...), branch_computations={%region_2.0_spmd, %region_3.5_spmd} | conditional | flops 1102583808 | bytes 35278928 | solution.py:67
  234.2 2.0 fusion.2
  236.2 2.3 fusion.3
  238.5 3.7 %fusion.8 = f32[2,1024,128]{2,1,0:T(8,128)S(1)} fusion(bf16[1024,2,128]{0,2,1:T(8,128)(2,1)S(1)} %bitcast.86, f32[2,1024,1024]{2,1,0:T(8,128)S(1)} %get-tuple-element.359, f32[2,1024]{1,0:T(2,128)S(1)} %max.5, pred[1024,1024]{0,1:T(8,128)(4,1)S(1)} %broadcast_compare_fusion, f32[2,1024,128]{2,1,0:T(8,128)S(1)} %get-tuple-element.245, ...), kind=kOutput, calls=%fused_computation.11 | convolution fusion | flops 547880960 | bytes 12075008 | tf_op jit(solution)/shard_map/while/body/eval_jaxpr/cond/branch_1_fun/hqk,khd->hqd/dot_general | solution.py:30
  243.0 10.0 %conditional.3 = ((f32[2,1024,128]{2,1,0:T(8,128)S(1)}, f32[2,1024]{1,0:T(2,128)S(1)}, f32[2,1024]{1,0:T(2,128)S(1)})) conditional(s32[]{:T(128)} %convert_element_type.81, (f32[2,1024,128]{2,1,0:T(8,128)S(1)}, f32[2,1024]{1,0:T(2,128)S(1)}, f32[2,1024]{1,0:T(2,128)S(1)}) %tuple.69, (s32[]{:T(128)}, s32[]{:T(128)}, bf16[16384,256]{0,1:T(8,128)(2,1)}, ...), branch_computations={%region_2.0_spmd, %region_3.5_spmd} | conditional | flops 1102583808 | bytes 35278928 | solution.py:67
  246.9 2.3 fusion.3
  249.2 3.7 %fusion.8 = f32[2,1024,128]{2,1,0:T(8,128)S(1)} fusion(bf16[1024,2,128]{0,2,1:T(8,128)(2,1)S(1)} %bitcast.86, f32[2,1024,1024]{2,1,0:T(8,128)S(1)} %get-tuple-element.359, f32[2,1024]{1,0:T(2,128)S(1)} %max.5, pred[1024,1024]{0,1:T(8,128)(4,1)S(1)} %broadcast_compare_fusion, f32[2,1024,128]{2,1,0:T(8,128)S(1)} %get-tuple-element.245, ...), kind=kOutput, calls=%fused_computation.11 | convolution fusion | flops 547880960 | bytes 12075008 | tf_op jit(solution)/shard_map/while/body/eval_jaxpr/cond/branch_1_fun/hqk,khd->hqd/dot_general | solution.py:30
  253.7 10.0 %conditional.3 = ((f32[2,1024,128]{2,1,0:T(8,128)S(1)}, f32[2,1024]{1,0:T(2,128)S(1)}, f32[2,1024]{1,0:T(2,128)S(1)})) conditional(s32[]{:T(128)} %convert_element_type.81, (f32[2,1024,128]{2,1,0:T(8,128)S(1)}, f32[2,1024]{1,0:T(2,128)S(1)}, f32[2,1024]{1,0:T(2,128)S(1)}) %tuple.69, (s32[]{:T(128)}, s32[]{:T(128)}, bf16[16384,256]{0,1:T(8,128)(2,1)}, ...), branch_computations={%region_2.0_spmd, %region_3.5_spmd} | conditional | flops 1102583808 | bytes 35278928 | solution.py:67
  257.6 2.3 fusion.3
  259.9 3.7 %fusion.8 = f32[2,1024,128]{2,1,0:T(8,128)S(1)} fusion(bf16[1024,2,128]{0,2,1:T(8,128)(2,1)S(1)} %bitcast.86, f32[2,1024,1024]{2,1,0:T(8,128)S(1)} %get-tuple-element.359, f32[2,1024]{1,0:T(2,128)S(1)} %max.5, pred[1024,1024]{0,1:T(8,128)(4,1)S(1)} %broadcast_compare_fusion, f32[2,1024,128]{2,1,0:T(8,128)S(1)} %get-tuple-element.245, ...), kind=kOutput, calls=%fused_computation.11 | convolution fusion | flops 547880960 | bytes 12075008 | tf_op jit(solution)/shard_map/while/body/eval_jaxpr/cond/branch_1_fun/hqk,khd->hqd/dot_general | solution.py:30
  264.4 10.0 %conditional.3 = ((f32[2,1024,128]{2,1,0:T(8,128)S(1)}, f32[2,1024]{1,0:T(2,128)S(1)}, f32[2,1024]{1,0:T(2,128)S(1)})) conditional(s32[]{:T(128)} %convert_element_type.81, (f32[2,1024,128]{2,1,0:T(8,128)S(1)}, f32[2,1024]{1,0:T(2,128)S(1)}, f32[2,1024]{1,0:T(2,128)S(1)}) %tuple.69, (s32[]{:T(128)}, s32[]{:T(128)}, bf16[16384,256]{0,1:T(8,128)(2,1)}, ...), branch_computations={%region_2.0_spmd, %region_3.5_spmd} | conditional | flops 1102583808 | bytes 35278928 | solution.py:67
  268.4 2.3 fusion.3
  270.6 3.7 %fusion.8 = f32[2,1024,128]{2,1,0:T(8,128)S(1)} fusion(bf16[1024,2,128]{0,2,1:T(8,128)(2,1)S(1)} %bitcast.86, f32[2,1024,1024]{2,1,0:T(8,128)S(1)} %get-tuple-element.359, f32[2,1024]{1,0:T(2,128)S(1)} %max.5, pred[1024,1024]{0,1:T(8,128)(4,1)S(1)} %broadcast_compare_fusion, f32[2,1024,128]{2,1,0:T(8,128)S(1)} %get-tuple-element.245, ...), kind=kOutput, calls=%fused_computation.11 | convolution fusion | flops 547880960 | bytes 12075008 | tf_op jit(solution)/shard_map/while/body/eval_jaxpr/cond/branch_1_fun/hqk,khd->hqd/dot_general | solution.py:30
  275.1 10.0 %conditional.3 = ((f32[2,1024,128]{2,1,0:T(8,128)S(1)}, f32[2,1024]{1,0:T(2,128)S(1)}, f32[2,1024]{1,0:T(2,128)S(1)})) conditional(s32[]{:T(128)} %convert_element_type.81, (f32[2,1024,128]{2,1,0:T(8,128)S(1)}, f32[2,1024]{1,0:T(2,128)S(1)}, f32[2,1024]{1,0:T(2,128)S(1)}) %tuple.69, (s32[]{:T(128)}, s32[]{:T(128)}, bf16[16384,256]{0,1:T(8,128)(2,1)}, ...), branch_computations={%region_2.0_spmd, %region_3.5_spmd} | conditional | flops 1102583808 | bytes 35278928 | solution.py:67
  279.1 2.3 fusion.3
  281.3 3.7 %fusion.8 = f32[2,1024,128]{2,1,0:T(8,128)S(1)} fusion(bf16[1024,2,128]{0,2,1:T(8,128)(2,1)S(1)} %bitcast.86, f32[2,1024,1024]{2,1,0:T(8,128)S(1)} %get-tuple-element.359, f32[2,1024]{1,0:T(2,128)S(1)} %max.5, pred[1024,1024]{0,1:T(8,128)(4,1)S(1)} %broadcast_compare_fusion, f32[2,1024,128]{2,1,0:T(8,128)S(1)} %get-tuple-element.245, ...), kind=kOutput, calls=%fused_computation.11 | convolution fusion | flops 547880960 | bytes 12075008 | tf_op jit(solution)/shard_map/while/body/eval_jaxpr/cond/branch_1_fun/hqk,khd->hqd/dot_general | solution.py:30
  285.8 10.0 %conditional.3 = ((f32[2,1024,128]{2,1,0:T(8,128)S(1)}, f32[2,1024]{1,0:T(2,128)S(1)}, f32[2,1024]{1,0:T(2,128)S(1)})) conditional(s32[]{:T(128)} %convert_element_type.81, (f32[2,1024,128]{2,1,0:T(8,128)S(1)}, f32[2,1024]{1,0:T(2,128)S(1)}, f32[2,1024]{1,0:T(2,128)S(1)}) %tuple.69, (s32[]{:T(128)}, s32[]{:T(128)}, bf16[16384,256]{0,1:T(8,128)(2,1)}, ...), branch_computations={%region_2.0_spmd, %region_3.5_spmd} | conditional | flops 1102583808 | bytes 35278928 | solution.py:67
  289.8 2.3 fusion.3
  292.1 3.7 %fusion.8 = f32[2,1024,128]{2,1,0:T(8,128)S(1)} fusion(bf16[1024,2,128]{0,2,1:T(8,128)(2,1)S(1)} %bitcast.86, f32[2,1024,1024]{2,1,0:T(8,128)S(1)} %get-tuple-element.359, f32[2,1024]{1,0:T(2,128)S(1)} %max.5, pred[1024,1024]{0,1:T(8,128)(4,1)S(1)} %broadcast_compare_fusion, f32[2,1024,128]{2,1,0:T(8,128)S(1)} %get-tuple-element.245, ...), kind=kOutput, calls=%fused_computation.11 | convolution fusion | flops 547880960 | bytes 12075008 | tf_op jit(solution)/shard_map/while/body/eval_jaxpr/cond/branch_1_fun/hqk,khd->hqd/dot_general | solution.py:30
  296.5 10.0 %conditional.3 = ((f32[2,1024,128]{2,1,0:T(8,128)S(1)}, f32[2,1024]{1,0:T(2,128)S(1)}, f32[2,1024]{1,0:T(2,128)S(1)})) conditional(s32[]{:T(128)} %convert_element_type.81, (f32[2,1024,128]{2,1,0:T(8,128)S(1)}, f32[2,1024]{1,0:T(2,128)S(1)}, f32[2,1024]{1,0:T(2,128)S(1)}) %tuple.69, (s32[]{:T(128)}, s32[]{:T(128)}, bf16[16384,256]{0,1:T(8,128)(2,1)}, ...), branch_computations={%region_2.0_spmd, %region_3.5_spmd} | conditional | flops 1102583808 | bytes 35278928 | solution.py:67
  300.5 2.3 fusion.3
  302.8 3.7 %fusion.8 = f32[2,1024,128]{2,1,0:T(8,128)S(1)} fusion(bf16[1024,2,128]{0,2,1:T(8,128)(2,1)S(1)} %bitcast.86, f32[2,1024,1024]{2,1,0:T(8,128)S(1)} %get-tuple-element.359, f32[2,1024]{1,0:T(2,128)S(1)} %max.5, pred[1024,1024]{0,1:T(8,128)(4,1)S(1)} %broadcast_compare_fusion, f32[2,1024,128]{2,1,0:T(8,128)S(1)} %get-tuple-element.245, ...), kind=kOutput, calls=%fused_computation.11 | convolution fusion | flops 547880960 | bytes 12075008 | tf_op jit(solution)/shard_map/while/body/eval_jaxpr/cond/branch_1_fun/hqk,khd->hqd/dot_general | solution.py:30
  307.2 10.0 %conditional.3 = ((f32[2,1024,128]{2,1,0:T(8,128)S(1)}, f32[2,1024]{1,0:T(2,128)S(1)}, f32[2,1024]{1,0:T(2,128)S(1)})) conditional(s32[]{:T(128)} %convert_element_type.81, (f32[2,1024,128]{2,1,0:T(8,128)S(1)}, f32[2,1024]{1,0:T(2,128)S(1)}, f32[2,1024]{1,0:T(2,128)S(1)}) %tuple.69, (s32[]{:T(128)}, s32[]{:T(128)}, bf16[16384,256]{0,1:T(8,128)(2,1)}, ...), branch_computations={%region_2.0_spmd, %region_3.5_spmd} | conditional | flops 1102583808 | bytes 35278928 | solution.py:67
  311.2 2.3 fusion.3
  313.5 3.7 %fusion.8 = f32[2,1024,128]{2,1,0:T(8,128)S(1)} fusion(bf16[1024,2,128]{0,2,1:T(8,128)(2,1)S(1)} %bitcast.86, f32[2,1024,1024]{2,1,0:T(8,128)S(1)} %get-tuple-element.359, f32[2,1024]{1,0:T(2,128)S(1)} %max.5, pred[1024,1024]{0,1:T(8,128)(4,1)S(1)} %broadcast_compare_fusion, f32[2,1024,128]{2,1,0:T(8,128)S(1)} %get-tuple-element.245, ...), kind=kOutput, calls=%fused_computation.11 | convolution fusion | flops 547880960 | bytes 12075008 | tf_op jit(solution)/shard_map/while/body/eval_jaxpr/cond/branch_1_fun/hqk,khd->hqd/dot_general | solution.py:30
  317.9 10.0 %conditional.3 = ((f32[2,1024,128]{2,1,0:T(8,128)S(1)}, f32[2,1024]{1,0:T(2,128)S(1)}, f32[2,1024]{1,0:T(2,128)S(1)})) conditional(s32[]{:T(128)} %convert_element_type.81, (f32[2,1024,128]{2,1,0:T(8,128)S(1)}, f32[2,1024]{1,0:T(2,128)S(1)}, f32[2,1024]{1,0:T(2,128)S(1)}) %tuple.69, (s32[]{:T(128)}, s32[]{:T(128)}, bf16[16384,256]{0,1:T(8,128)(2,1)}, ...), branch_computations={%region_2.0_spmd, %region_3.5_spmd} | conditional | flops 1102583808 | bytes 35278928 | solution.py:67
  321.9 2.3 fusion.3
  324.2 3.7 %fusion.8 = f32[2,1024,128]{2,1,0:T(8,128)S(1)} fusion(bf16[1024,2,128]{0,2,1:T(8,128)(2,1)S(1)} %bitcast.86, f32[2,1024,1024]{2,1,0:T(8,128)S(1)} %get-tuple-element.359, f32[2,1024]{1,0:T(2,128)S(1)} %max.5, pred[1024,1024]{0,1:T(8,128)(4,1)S(1)} %broadcast_compare_fusion, f32[2,1024,128]{2,1,0:T(8,128)S(1)} %get-tuple-element.245, ...), kind=kOutput, calls=%fused_computation.11 | convolution fusion | flops 547880960 | bytes 12075008 | tf_op jit(solution)/shard_map/while/body/eval_jaxpr/cond/branch_1_fun/hqk,khd->hqd/dot_general | solution.py:30
  328.6 10.0 %conditional.3 = ((f32[2,1024,128]{2,1,0:T(8,128)S(1)}, f32[2,1024]{1,0:T(2,128)S(1)}, f32[2,1024]{1,0:T(2,128)S(1)})) conditional(s32[]{:T(128)} %convert_element_type.81, (f32[2,1024,128]{2,1,0:T(8,128)S(1)}, f32[2,1024]{1,0:T(2,128)S(1)}, f32[2,1024]{1,0:T(2,128)S(1)}) %tuple.69, (s32[]{:T(128)}, s32[]{:T(128)}, bf16[16384,256]{0,1:T(8,128)(2,1)}, ...), branch_computations={%region_2.0_spmd, %region_3.5_spmd} | conditional | flops 1102583808 | bytes 35278928 | solution.py:67
  332.6 2.3 fusion.3
  334.9 3.7 %fusion.8 = f32[2,1024,128]{2,1,0:T(8,128)S(1)} fusion(bf16[1024,2,128]{0,2,1:T(8,128)(2,1)S(1)} %bitcast.86, f32[2,1024,1024]{2,1,0:T(8,128)S(1)} %get-tuple-element.359, f32[2,1024]{1,0:T(2,128)S(1)} %max.5, pred[1024,1024]{0,1:T(8,128)(4,1)S(1)} %broadcast_compare_fusion, f32[2,1024,128]{2,1,0:T(8,128)S(1)} %get-tuple-element.245, ...), kind=kOutput, calls=%fused_computation.11 | convolution fusion | flops 547880960 | bytes 12075008 | tf_op jit(solution)/shard_map/while/body/eval_jaxpr/cond/branch_1_fun/hqk,khd->hqd/dot_general | solution.py:30
  340.2 5.7 %all-to-all-start = ((bf16[8,128,256]{1,2,0:T(8,128)(2,1)}), bf16[8,128,256]{1,2,0:T(8,128)(2,1)S(1)}, u32[]{:S(2)}, u32[]{:S(2)}) async-start(bf16[8,128,256]{1,2,0:T(8,128)(2,1)} %copy.96), calls=%async_computation | async-start | bytes 1048576 | tf_op jit(solution)/shard_map/all_to_all | solution.py:140
  345.8 5.7 %convolution_convert_fusion.1 = bf16[64,2048]{1,0:T(8,128)(2,1)} fusion(bf16[64,2048]{1,0:T(8,128)(2,1)S(1)} %bitcast.90, bf16[2048,2048]{1,0:T(8,128)(2,1)} %param.23), kind=kOutput, calls=%fused_computation.33 | convolution fusion | flops 537001984 | bytes 8912896 | tf_op jit(solution)/shard_map/dot_general | solution.py:143
  353.0 5.5 %convolution_convert_fusion = bf16[128,2048]{1,0:T(8,128)(2,1)} fusion(bf16[128,2048]{0,1:T(8,128)(2,1)S(1)} %bitcast.88, bf16[2048,2048]{1,0:T(8,128)(2,1)} %param.23), kind=kOutput, calls=%fused_computation.32 | convolution fusion | flops 1074003968 | bytes 9437184 | tf_op jit(solution)/shard_map/dot_general | solution.py:142
  (184 shorter events, 75.2 us)
Async XLA Ops:
  7.2 5.9 %copy-start = (bf16[64,2,16,256]{3,2,1,0:T(8,128)(2,1)S(1)}, bf16[64,2,16,256]{3,2,1,0:T(8,128)(2,1)}, u32[]{:S(2)}) copy-start(bf16[64,2,16,256]{3,2,1,0:T(8,128)(2,1)} %param.21) | copy-start | bytes 3145732
  7.2 17.5 %copy-start.4 = (s32[1536]{0:T(1024)S(1)}, s32[1536]{0:T(1024)}, u32[]{:S(2)}) copy-start(s32[1536]{0:T(1024)} %constant.131.clone.1) | copy-start | bytes 18436
  7.2 16.3 %copy-start.2 = (bf16[512,256]{1,0:T(8,128)(2,1)S(1)}, bf16[512,256]{1,0:T(8,128)(2,1)}, u32[]{:S(2)}) copy-start(bf16[512,256]{1,0:T(8,128)(2,1)} %param.19) | copy-start | bytes 786436
  7.2 17.5 %copy-start.5 = (s32[1,512]{1,0:T(1,128)S(1)}, s32[1,512]{1,0:T(1,128)}, u32[]{:S(2)}) copy-start(s32[1,512]{1,0:T(1,128)} %param.20) | copy-start | bytes 6148
  7.2 86.9 %all-gather.3.cloned.1.call-start = ((), (), s32[]{:S(2)}) async-start(), calls=%async_computation.3 | async-start | bytes 8912896 | tf_op jit(solution)/shard_map/all_gather | solution.py:49
  9.4 157.8 %all-gather.5.cloned.1.call-start = ((), (), s32[]{:S(2)}) async-start(), calls=%async_computation.4 | async-start | bytes 8912896 | tf_op jit(solution)/shard_map/all_gather | solution.py:50
  14.7 25.7 %all-to-all-start.1 = ((bf16[16,4,2,16,256]{4,3,2,1,0:T(8,128)(2,1)}), bf16[16,4,2,16,256]{4,3,2,1,0:T(8,128)(2,1)S(1)}, u32[]{:S(2)}, u32[]{:S(2)}) async-start(bf16[16,4,2,16,256]{4,3,2,1,0:T(8,128)(2,1)} %bitcast.10), calls=%async_computation.1 | async-start | bytes 2097152 | tf_op jit(solution)/shard_map/all_to_all | solution.py:93
  43.3 6.5 %copy-start.3 = (bf16[512,2,128]{2,0,1:T(8,128)(2,1)S(1)}, bf16[512,2,128]{2,0,1:T(8,128)(2,1)}, u32[]{:S(2)}) copy-start(bf16[512,2,128]{2,0,1:T(8,128)(2,1)} %copy.109) | copy-start | bytes 786436
  49.8 11.5 %copy-start.1 = (bf16[1024,256]{1,0:T(8,128)(2,1)S(1)}, bf16[1024,256]{1,0:T(8,128)(2,1)}, u32[]{:S(2)}) copy-start(bf16[1024,256]{1,0:T(8,128)(2,1)} %param.14) | copy-start | bytes 1572868
  54.3 15.4 %all-to-all-start.2 = ((bf16[8,64,256]{2,1,0:T(8,128)(2,1)}), bf16[8,64,256]{2,1,0:T(8,128)(2,1)S(1)}, u32[]{:S(2)}, u32[]{:S(2)}) async-start(bf16[8,64,256]{2,1,0:T(8,128)(2,1)} %convert_element_type.57), calls=%async_computation.2 | async-start | bytes 524288 | tf_op jit(solution)/shard_map/all_to_all | solution.py:141
  340.2 12.8 %all-to-all-start = ((bf16[8,128,256]{1,2,0:T(8,128)(2,1)}), bf16[8,128,256]{1,2,0:T(8,128)(2,1)S(1)}, u32[]{:S(2)}, u32[]{:S(2)}) async-start(bf16[8,128,256]{1,2,0:T(8,128)(2,1)} %copy.96), calls=%async_computation | async-start | bytes 1048576 | tf_op jit(solution)/shard_map/all_to_all | solution.py:140
Sparse Core Ops, SparseCore 0:
  11.1 83.0 all-gather.2
  96.6 70.5 all-gather.4

commit v2 on v1

--- a/solution.py
+++ b/solution.py
@@ -1,8 +1,11 @@
+import functools
 import math
 
 import jax
 import jax.numpy as jnp
 from jax import lax
+from jax.experimental import pallas as pl
+from jax.experimental.pallas import tpu as pltpu
 from jax.sharding import PartitionSpec as P
 
 HD = 128
@@ -12,63 +15,89 @@
 very_negative = -1e30
 
 
-def fold_block(state_now, query_heads, query_pos, key_block, value_block, block_first):
-    acc_sum, run_max, run_total = state_now
-    heads_dev = query_heads.shape[1]
-    key_heads = key_block.reshape(key_block.shape[0], heads_dev, HD)
-    value_heads = value_block.reshape(value_block.shape[0], heads_dev, HD)
-    scores = jnp.einsum(
-        "qhd,khd->hqk", query_heads, key_heads, preferred_element_type=jnp.float32
-    ) * HD ** (-0.5)
-    key_pos = block_first + jnp.arange(key_block.shape[0], dtype=jnp.int32)
-    allowed = (key_pos[None, :] <= query_pos[:, None])[None]
-    scores = jnp.where(allowed, scores, very_negative)
-    new_max = jnp.maximum(run_max, jnp.max(scores, axis=-1))
-    weights = jnp.where(allowed, jnp.exp(scores - new_max[..., None]), 0.0)
-    factor = jnp.exp(run_max - new_max)
-    run_total = run_total * factor + jnp.sum(weights, axis=-1)
-    acc_sum = acc_sum * factor[..., None] + jnp.einsum(
-        "hqk,khd->hqd",
-        weights.astype(jnp.bfloat16),
-        value_heads,
-        preferred_element_type=jnp.float32,
-    )
-    return (acc_sum, new_max, run_total)
+def flash_body(blk_ref, q_ref, k_ref, v_ref, o_ref, m_sc, l_sc, acc_sc, *, heads, tq, tk, q_rows):
+    q_tile = pl.program_id(0)
+    k_tile = pl.program_id(1)
+    first_query = blk_ref[0] * q_rows + q_tile * tq
+    last_tile = (first_query + tq - 1) // tk
+
+    @pl.when(k_tile == 0)
+    def _():
+        m_sc[...] = jnp.full(m_sc.shape, very_negative, jnp.float32)
+        l_sc[...] = jnp.zeros(l_sc.shape, jnp.float32)
+        acc_sc[...] = jnp.zeros(acc_sc.shape, jnp.float32)
+
+    def fold(masked):
+        for h in range(heads):
+            cols = slice(h * HD, (h + 1) * HD)
+            scores = lax.dot_general(
+                q_ref[:, cols], k_ref[:, cols], (((1,), (1,)), ((), ())),
+                preferred_element_type=jnp.float32,
+            ) * HD ** (-0.5)
+            if masked:
+                query_pos = first_query + lax.broadcasted_iota(jnp.int32, (tq, tk), 0)
+                key_pos = k_tile * tk + lax.broadcasted_iota(jnp.int32, (tq, tk), 1)
+                scores = jnp.where(key_pos <= query_pos, scores, very_negative)
+            run_max = m_sc[h]
+            new_max = jnp.maximum(run_max, jnp.max(scores, axis=1, keepdims=True))
+            weights = jnp.exp(scores - new_max[:, :1])
+            factor = jnp.exp(run_max - new_max)
+            l_sc[h] = l_sc[h] * factor + jnp.sum(weights, axis=1, keepdims=True)
+            m_sc[h] = new_max
+            acc_sc[h] = acc_sc[h] * factor + jnp.dot(
+                weights.astype(jnp.bfloat16), v_ref[:, cols], preferred_element_type=jnp.float32
+            )
+
+    needs_mask = (k_tile + 1) * tk - 1 > first_query
+
+    @pl.when((k_tile <= last_tile) & jnp.logical_not(needs_mask))
+    def _():
+        fold(False)
+
+    @pl.when((k_tile <= last_tile) & needs_mask)
+    def _():
+        fold(True)
+
+    @pl.when(k_tile == last_tile)
+    def _():
+        for h in range(heads):
+            o_ref[:, h * HD:(h + 1) * HD] = (acc_sc[h] / l_sc[h]).astype(o_ref.dtype)
 
 
-def prompt_attention(queries, query_pos, long_k, long_v):
+def prompt_attention(queries, block_index, long_k, long_v):
     row_count, width = queries.shape
     heads_dev = width // HD
-    query_heads = queries.reshape(row_count, heads_dev, HD)
-    last_pos = jnp.max(query_pos)
-    init = (
-        jnp.zeros((heads_dev, row_count, HD), jnp.float32),
-        jnp.full((heads_dev, row_count), very_negative, jnp.float32),
-        jnp.zeros((heads_dev, row_count), jnp.float32),
-    )
     key_piece = lax.all_gather(long_k, "blk", axis=0, tiled=True)
     value_piece = lax.all_gather(long_v, "blk", axis=0, tiled=True)
     piece_rows = key_piece.shape[0]
-    step_rows = math.gcd(piece_rows, 1024)
+    tq = min(row_count, 512)
+    tk = min(row_count, 1024)
 
-    def one_step(block_num, state_in):
-        block_start = block_num * step_rows
-        key_block = lax.dynamic_slice_in_dim(key_piece, block_start, step_rows, 0)
-        value_block = lax.dynamic_slice_in_dim(value_piece, block_start, step_rows, 0)
+    def kv_map(q_tile, k_tile, blk_ref):
+        last_tile = (blk_ref[0] * row_count + q_tile * tq + tq - 1) // tk
+        return (jnp.minimum(k_tile, last_tile), 0)
 
-        def compute_block(state_live):
-            return fold_block(
-                state_live, query_heads, query_pos, key_block, value_block, block_start
-            )
-
-        def keep_state(state_skip):
-            return state_skip
-
-        return lax.cond(block_start <= last_pos, compute_block, keep_state, state_in)
-
-    acc_sum, run_max, run_total = lax.fori_loop(0, piece_rows // step_rows, one_step, init)
-    merged = acc_sum / run_total[..., None]
-    return merged.transpose(1, 0, 2).reshape(row_count, width).astype(jnp.bfloat16)
+    body = functools.partial(flash_body, heads=heads_dev, tq=tq, tk=tk, q_rows=row_count)
+    return pl.pallas_call(
+        body,
+        out_shape=jax.ShapeDtypeStruct((row_count, width), jnp.bfloat16),
+        grid_spec=pltpu.PrefetchScalarGridSpec(
+            num_scalar_prefetch=1,
+            grid=(row_count // tq, piece_rows // tk),
+            in_specs=[
+                pl.BlockSpec((tq, width), lambda q_tile, k_tile, blk_ref: (q_tile, 0)),
+                pl.BlockSpec((tk, width), kv_map),
+                pl.BlockSpec((tk, width), kv_map),
+            ],
+            out_specs=pl.BlockSpec((tq, width), lambda q_tile, k_tile, blk_ref: (q_tile, 0)),
+            scratch_shapes=[
+                pltpu.VMEM((heads_dev, tq, HD), jnp.float32),
+                pltpu.VMEM((heads_dev, tq, HD), jnp.float32),
+                pltpu.VMEM((heads_dev, tq, HD), jnp.float32),
+            ],
+        ),
+        compiler_params=pltpu.CompilerParams(dimension_semantics=("arbitrary", "arbitrary")),
+    )(jnp.reshape(block_index, (1,)).astype(jnp.int32), queries, key_piece, value_piece)
 
 
 def pack_attention(
@@ -131,9 +160,7 @@
 ):
     block_count = lax.axis_size("blk")
     block_index = lax.axis_index("blk")
-    row_count, width = long_q.shape
-    query_pos = block_index * row_count + jnp.arange(row_count, dtype=jnp.int32)
-    long_attn = prompt_attention(long_q, query_pos, long_k, long_v)
+    long_attn = prompt_attention(long_q, block_index, long_k, long_v)
     short_attn = pack_attention(
         short_q, short_k, short_v, short_seg, pool_kv, page_table, block_index, block_count
     )

time: 366 us -> 281 us (0.77)
  matrix products: 112 us -> 20.9 us
  Pallas kernels: 0 us -> 88.4 us
  other arithmetic: 50.7 us -> 2.52 us
  local copies, waits for them, and re-layouts: 35.5 us -> 10.4 us
  blocking collectives: 0 us -> 14.8 us
  loops' own time: 12.7 us -> 0 us
  starting transfers between devices: 19.5 us -> 13.3 us
  waiting for transfers between devices: 121 us -> 115 us
    dot_general x32 -> x0, matrix products: 91 us -> none  [the longest x16 59.4 us: fold_block(): jnp.einsum('hqk,khd->hqd', weights.astype(jnp.bfloat16), value_heads, pre...]
    pallas_call x0 -> x1, Pallas kernels: none -> 88.4 us  [prompt_attention(): pl.pallas_call(body, out_shape=jax.ShapeDtypeStruct((row_count, width), j...]
    reduce_sum x16 -> x0, other arithmetic: 36.1 us -> none  [fold_block(): run_total = run_total * factor + jnp.sum(weights, axis=-1)]
    dynamic_slice x16 -> x0, local copies, waits for them, and re-layouts: 20.4 us -> none  [one_step(): lax.dynamic_slice_in_dim(value_piece, block_start, step_rows, 0)]
    all_to_all x0 -> x1, blocking collectives: none -> 14.8 us  [per_device(): short_rows = lax.all_to_all(short_attn, 'req', 0, 1, tiled=True)]
    another operation x17 -> x0, loops' own time: 12.7 us -> none  [the longest x1 11.5 us: prompt_attention(): lax.fori_loop(0, piece_rows // step_rows, one_step, init)]
    le x16 -> x0, other arithmetic: 10.4 us -> none  [fold_block(): allowed = (key_pos[None, :] <= query_pos[:, None])[None]]
    all_to_all x1 -> x0, waiting for transfers between devices: 7.95 us -> none  [per_device(): short_rows = lax.all_to_all(short_attn, 'req', 0, 1, tiled=True)]
  transfers between devices with their start and end apart: 5 -> 4, of which waited for: 5 -> 4; matrix products, arithmetic and copies ran while one was open for 8% -> 9% of each run, Pallas kernels for 0% -> 0%
where the time goes in v2:
time: 281 us; the launch traced here: 280 us
  waiting for transfers between devices  115 us (41%)
  Pallas kernels  88.4 us (31%)
  matrix products  20.9 us (7%)
  blocking collectives  14.8 us (5%)
  between operations  14.3 us (5%)
  starting transfers between devices  13.3 us (5%)
  local copies, waits for them, and re-layouts  10.4 us (4%)
    pallas_call x1, Pallas kernels, prompt_attention(): pl.pallas_call(body, out_shape=jax.ShapeDtypeStruct((row_count, width), j...  88.4 us
    all_gather x1, waiting for transfers between devices, prompt_attention(): value_piece = lax.all_gather(long_v, 'blk', axis=0, tiled=True)  73 us
    all_gather x1, waiting for transfers between devices, prompt_attention(): key_piece = lax.all_gather(long_k, 'blk', axis=0, tiled=True)  26.3 us
    all_to_all x1, blocking collectives, per_device(): short_rows = lax.all_to_all(short_attn, 'req', 0, 1, tiled=True)  14.8 us
    all_to_all x1, waiting for transfers between devices, pack_attention(): lax.all_to_all(outgoing, 'blk', split_axis=0, concat_axis=0, tiled=True)  13.4 us
    all_to_all x1, starting transfers between devices, pack_attention(): lax.all_to_all(outgoing, 'blk', split_axis=0, concat_axis=0, tiled=True)  7.51 us
    sub x1, matrix products, pack_attention(): weights = jnp.where(allowed, jnp.exp(scores - row_max[..., None]), 0.0)  6.5 us
    all_to_all x1, starting transfers between devices, per_device(): long_rows = lax.all_to_all(long_attn, 'req', 0, 1, tiled=True)  5.67 us
  transfers between devices with their start and end apart: 4, of which 4 were waited for; matrix products, arithmetic and copies ran while one was open for 9% of the time, Pallas kernels for 0%

profile of v2, /device:TPU:23, one launch (start us, length us, event | category | flops | bytes accessed | tf_op | source)
XLA Modules:
  0.0 280.0 jit_solution(2030330261579297580)
XLA Ops:
  7.2 0.0 copy-start
  7.2 0.0 copy-start.3
  7.2 0.0 copy-start.1
  7.2 0.0 copy-start.4
  7.2 0.0 all-gather.3.cloned.1.call-start
  7.3 0.7 all-gather.3.cloned.1.call-update
  7.9 0.0 all-gather.5.cloned.1.call-start
  8.0 0.7 all-gather.5.cloned.1.call-update
  8.7 0.8 copy.48
  9.5 0.1 copy.49
  9.6 0.2 reduce_window_sum.11
  9.9 0.1 select_reduce_fusion
  10.0 0.1 copy.53
  10.1 0.1 reshape.238
  10.2 0.0 copy-done
  10.2 1.6 gather_fusion
  11.8 7.5 %all-to-all-start.1 = ((bf16[16,4,2,16,256]{4,3,2,1,0:T(8,128)(2,1)}), bf16[16,4,2,16,256]{4,3,2,1,0:T(8,128)(2,1)S(1)}, u32[]{:S(2)}, u32[]{:S(2)}) async-start(bf16[16,4,2,16,256]{4,3,2,1,0:T(8,128)(2,1)} %bitcast.7), calls=%async_computation.1 | async-start | bytes 2097152 | tf_op jit(solution)/shard_map/all_to_all | solution.py:122
  19.3 1.1 copy.54
  20.4 0.2 copy.56
  20.6 0.0 copy-done.1
  20.6 0.1 copy.58
  20.8 0.8 copy.60
  21.6 0.2 convert_reduce_fusion
  21.8 0.0 copy-done.4
  21.8 0.0 copy-done.3
  21.9 1.9 fusion.6
  23.8 13.4 %all-to-all-done.1 = bf16[16,4,2,16,256]{4,3,2,1,0:T(8,128)(2,1)S(1)} async-done(((bf16[16,4,2,16,256]{4,3,2,1,0:T(8,128)(2,1)}), bf16[16,4,2,16,256]{4,3,2,1,0:T(8,128)(2,1)S(1)}, u32[]{:S(2)}, u32[]{:S(2)}) %all-to-all-start.1) | async-done | bytes 1048608 | tf_op jit(solution)/shard_map/all_to_all | solution.py:122
  37.2 0.6 gather_fusion.1
  37.8 0.9 fusion.46
  38.6 1.2 concatenate.21
  39.8 0.1 copy.55
  39.9 0.1 concatenate.24
  40.1 0.1 copy.59
  40.1 0.0 copy-start.2
  40.1 6.5 %fusion.47 = (f32[2,512]{1,0:T(2,128)S(1)}, bf16[2,512,1536]{1,2,0:T(8,128)(2,1)}) fusion(pred[512,1536]{0,1:T(8,128)(4,1)} %fusion.6, bf16[512,2,128]{2,0,1:T(8,128)(2,1)S(1)} %copy.56, bf16[1024,2,128]{2,0,1:T(8,128)(2,1)S(1)} %copy.55, bf16[512,256]{1,0:T(8,128)(2,1)} %param.13), kind=kOutput, calls=%fused_computation.68 | convolution fusion | flops 413664768 | bytes 4984832 | tf_op jit(solution)/shard_map/sub | solution.py:146
  46.7 0.0 copy-done.2
  46.7 3.3 %fusion.14 = bf16[512,2,128]{2,0,1:T(8,128)(2,1)S(1)} fusion(bf16[2,512,1536]{1,2,0:T(8,128)(2,1)} %get-tuple-element.8, bf16[512,2,128]{2,0,1:T(8,128)(2,1)S(1)} %copy-done.2, bf16[1024,2,128]{2,0,1:T(8,128)(2,1)S(1)} %copy.59, f32[512,2]{0,1:T(2,128)S(1)} %bitcast.72), kind=kOutput, calls=%fused_computation.17 | convolution fusion | flops 404488192 | bytes 4198400 | tf_op jit(solution)/shard_map/hqk,khd->hqd/dot_general | solution.py:148
  49.9 0.3 copy.62
  50.2 0.2 convert_element_type.31
  50.4 14.8 %all_to_all.40 = bf16[8,64,256]{2,1,0:T(8,128)(2,1)S(1)} all-to-all(bf16[8,64,256]{2,1,0:T(8,128)(2,1)S(1)} %convert_element_type.31), channel_id=1, replica_groups=mesh['blk'=16,'req'=8] {'req'}, dimensions={0} | all-to-all | bytes 524288 | tf_op jit(solution)/shard_map/all_to_all | solution.py:168
  65.2 26.3 %all-gather.3.cloned.1.call-done.k_ref = bf16[16384,256]{1,0:T(8,128)(2,1)} async-done(((bf16[1024,256]{1,0:T(8,128)(2,1)}), bf16[16384,256]{1,0:T(8,128)(2,1)}) %all-gather.3.cloned.1.call-update) | async-done | bytes 8388624 | tf_op jit(solution)/shard_map/all_gather | solution.py:70
  91.5 73.0 %all-gather.5.cloned.1.call-done.v_ref = bf16[16384,256]{1,0:T(8,128)(2,1)} async-done(((bf16[1024,256]{1,0:T(8,128)(2,1)}), bf16[16384,256]{1,0:T(8,128)(2,1)}) %all-gather.5.cloned.1.call-update) | async-done | bytes 8388624 | tf_op jit(solution)/shard_map/all_gather | solution.py:71
  164.5 88.4 %shard_map.113 = bf16[1024,256]{1,0:T(8,128)(2,1)} custom-call(s32[1]{0:T(128)} %bitcast.blk_ref, bf16[1024,256]{1,0:T(8,128)(2,1)} %q_ref.1, bf16[16384,256]{1,0:T(8,128)(2,1)} %all-gather.3.cloned.1.call-done.k_ref, bf16[16384,256]{1,0:T(8,128)(2,1)} %all-gather.5.cloned.1.call-done.v_ref), custom_call_target="tpu_custom_call" | custom-call | tf_op jit(solution)/shard_map/pallas_call | solution.py:81
  252.9 2.0 copy.47
  254.9 5.7 %all-to-all-start = ((bf16[8,128,256]{1,2,0:T(8,128)(2,1)}), bf16[8,128,256]{1,2,0:T(8,128)(2,1)S(1)}, u32[]{:S(2)}, u32[]{:S(2)}) async-start(bf16[8,128,256]{1,2,0:T(8,128)(2,1)} %copy.47), calls=%async_computation | async-start | bytes 1048576 | tf_op jit(solution)/shard_map/all_to_all | solution.py:167
  260.6 5.7 %convolution_convert_fusion.1 = bf16[64,2048]{1,0:T(8,128)(2,1)} fusion(bf16[64,2048]{1,0:T(8,128)(2,1)S(1)} %bitcast.64, bf16[2048,2048]{1,0:T(8,128)(2,1)} %param.19), kind=kOutput, calls=%fused_computation.14 | convolution fusion | flops 537001984 | bytes 8912896 | tf_op jit(solution)/shard_map/dot_general | solution.py:170
  266.2 1.5 all-to-all-done
  267.7 5.5 %convolution_convert_fusion = bf16[128,2048]{1,0:T(8,128)(2,1)} fusion(bf16[128,2048]{0,1:T(8,128)(2,1)S(1)} %bitcast.62, bf16[2048,2048]{1,0:T(8,128)(2,1)} %param.19), kind=kOutput, calls=%fused_computation.13 | convolution fusion | flops 1074003968 | bytes 9437184 | tf_op jit(solution)/shard_map/dot_general | solution.py:169
  (10 shorter events, 0.1 us)
Async XLA Ops:
  7.2 3.1 %copy-start = (bf16[64,2,16,256]{3,2,1,0:T(8,128)(2,1)S(1)}, bf16[64,2,16,256]{3,2,1,0:T(8,128)(2,1)}, u32[]{:S(2)}) copy-start(bf16[64,2,16,256]{3,2,1,0:T(8,128)(2,1)} %param.17) | copy-start | bytes 3145732
  7.2 14.7 %copy-start.3 = (s32[1536]{0:T(1024)S(1)}, s32[1536]{0:T(1024)}, u32[]{:S(2)}) copy-start(s32[1536]{0:T(1024)} %constant.63.clone.1) | copy-start | bytes 18436
  7.2 13.4 %copy-start.1 = (bf16[512,256]{1,0:T(8,128)(2,1)S(1)}, bf16[512,256]{1,0:T(8,128)(2,1)}, u32[]{:S(2)}) copy-start(bf16[512,256]{1,0:T(8,128)(2,1)} %param.15) | copy-start | bytes 786436
  7.2 14.6 %copy-start.4 = (s32[1,512]{1,0:T(1,128)S(1)}, s32[1,512]{1,0:T(1,128)}, u32[]{:S(2)}) copy-start(s32[1,512]{1,0:T(1,128)} %param.16) | copy-start | bytes 6148
  7.2 84.3 %all-gather.3.cloned.1.call-start = ((), (), s32[]{:S(2)}) async-start(), calls=%async_computation.3 | async-start | bytes 8912896 | tf_op jit(solution)/shard_map/all_gather | solution.py:70
  7.9 156.5 %all-gather.5.cloned.1.call-start = ((), (), s32[]{:S(2)}) async-start(), calls=%async_computation.4 | async-start | bytes 8912896 | tf_op jit(solution)/shard_map/all_gather | solution.py:71
  11.8 25.3 %all-to-all-start.1 = ((bf16[16,4,2,16,256]{4,3,2,1,0:T(8,128)(2,1)}), bf16[16,4,2,16,256]{4,3,2,1,0:T(8,128)(2,1)S(1)}, u32[]{:S(2)}, u32[]{:S(2)}) async-start(bf16[16,4,2,16,256]{4,3,2,1,0:T(8,128)(2,1)} %bitcast.7), calls=%async_computation.1 | async-start | bytes 2097152 | tf_op jit(solution)/shard_map/all_to_all | solution.py:122
  40.1 6.5 %copy-start.2 = (bf16[512,2,128]{2,0,1:T(8,128)(2,1)S(1)}, bf16[512,2,128]{2,0,1:T(8,128)(2,1)}, u32[]{:S(2)}) copy-start(bf16[512,2,128]{2,0,1:T(8,128)(2,1)} %copy.60) | copy-start | bytes 786436
  254.9 12.8 %all-to-all-start = ((bf16[8,128,256]{1,2,0:T(8,128)(2,1)}), bf16[8,128,256]{1,2,0:T(8,128)(2,1)S(1)}, u32[]{:S(2)}, u32[]{:S(2)}) async-start(bf16[8,128,256]{1,2,0:T(8,128)(2,1)} %copy.47), calls=%async_computation | async-start | bytes 1048576 | tf_op jit(solution)/shard_map/all_to_all | solution.py:167
Sparse Core Ops, SparseCore 0:
  10.4 80.9 all-gather.2
  93.9 70.5 all-gather.4

commit v3 on v2

v3 whole, which is shorter than its diff:
```python
import functools
import math

import jax
import jax.numpy as jnp
from jax import lax
from jax.experimental import pallas as pl
from jax.experimental.pallas import tpu as pltpu
from jax.sharding import PartitionSpec as P

HD = 128
PPS = 4


very_negative = -1e30


def flash_body(pos_ref, q_ref, a_ref, b_ref, o_ref, m_sc, l_sc, acc_sc, *, tq, tk, q_rows):
    q_tile = pl.program_id(0)
    k_tile = pl.program_id(1)
    first_query = pos_ref[0] * q_rows + q_tile * tq
    last_tile = (first_query + tq - 1) // tk

    @pl.when(k_tile == 0)
    def _():
        m_sc[...] = jnp.full(m_sc.shape, very_negative, jnp.float32)
        l_sc[...] = jnp.zeros(l_sc.shape, jnp.float32)
        acc_sc[...] = jnp.zeros(acc_sc.shape, jnp.float32)

    def fold(masked, k_ref, v_ref):
        scores = lax.dot_general(
            q_ref[...], k_ref[...], (((1,), (1,)), ((), ())),
            preferred_element_type=jnp.float32,
        ) * HD ** (-0.5)
        if masked:
            query_pos = first_query + lax.broadcasted_iota(jnp.int32, (tq, tk), 0)
            key_pos = k_tile * tk + lax.broadcasted_iota(jnp.int32, (tq, tk), 1)
            scores = jnp.where(key_pos <= query_pos, scores, very_negative)
        run_max = m_sc[...]
        new_max = jnp.maximum(run_max, jnp.max(scores, axis=1, keepdims=True))
        weights = jnp.exp(scores - new_max[:, :1])
        factor = jnp.exp(run_max - new_max)
        l_sc[...] = l_sc[...] * factor + jnp.sum(weights, axis=1, keepdims=True)
        m_sc[...] = new_max
        acc_sc[...] = acc_sc[...] * factor + jnp.dot(
            weights.astype(jnp.bfloat16), v_ref[...], preferred_element_type=jnp.float32
        )

    needs_mask = (k_tile + 1) * tk - 1 > first_query
    live = k_tile <= last_tile
    keys_first = pos_ref[1] == 0
    for masked in (False, True):
        mask_case = needs_mask if masked else jnp.logical_not(needs_mask)

        @pl.when(live & mask_case & keys_first)
        def _():
            fold(masked, a_ref, b_ref)

        @pl.when(live & mask_case & jnp.logical_not(keys_first))
        def _():
            fold(masked, b_ref, a_ref)

    @pl.when(k_tile == last_tile)
    def _():
        o_ref[...] = (acc_sc[...] / l_sc[...]).astype(o_ref.dtype)


def flash_head(queries, head, block_index, core, first_piece, second_piece):
    row_count = queries.shape[0]
    piece_rows = first_piece.shape[0]
    tq = min(row_count, 512)
    tk = min(row_count, 1024)

    def kv_map(q_tile, k_tile, pos_ref):
        last_tile = (pos_ref[0] * row_count + q_tile * tq + tq - 1) // tk
        return (jnp.minimum(k_tile, last_tile), 0)

    body = functools.partial(flash_body, tq=tq, tk=tk, q_rows=row_count)
    return pl.pallas_call(
        body,
        out_shape=jax.ShapeDtypeStruct((row_count, HD), jnp.bfloat16),
        grid_spec=pltpu.PrefetchScalarGridSpec(
            num_scalar_prefetch=1,
            grid=(row_count // tq, piece_rows // tk),
            in_specs=[
                pl.BlockSpec((tq, HD), lambda q_tile, k_tile, pos_ref: (q_tile, head)),
                pl.BlockSpec((tk, HD), kv_map),
                pl.BlockSpec((tk, HD), kv_map),
            ],
            out_specs=pl.BlockSpec((tq, HD), lambda q_tile, k_tile, pos_ref: (q_tile, 0)),
            scratch_shapes=[
                pltpu.VMEM((tq, HD), jnp.float32),
                pltpu.VMEM((tq, HD), jnp.float32),
                pltpu.VMEM((tq, HD), jnp.float32),
            ],
        ),
        compiler_params=pltpu.CompilerParams(dimension_semantics=("arbitrary", "arbitrary")),
    )(jnp.stack([block_index, core]).astype(jnp.int32), queries, first_piece, second_piece)


def prompt_attention(queries, block_index, core, long_k, long_v):
    heads_dev = queries.shape[1] // HD
    swap = [(0, 1), (1, 0)]
    outs = []
    for head in range(heads_dev):
        cols = slice(head * HD, (head + 1) * HD)
        key_head = long_k[:, cols]
        value_head = long_v[:, cols]
        first_core = core == 0
        partner = lax.ppermute(jnp.where(first_core, value_head, key_head), "core", swap)
        pair = jnp.where(
            first_core,
            jnp.concatenate([key_head, partner], 0),
            jnp.concatenate([partner, value_head], 0),
        )
        first_piece = lax.all_gather(pair, "chip", axis=0, tiled=True)
        second_piece = lax.ppermute(first_piece, "core", swap)
        outs.append(flash_head(queries, head, block_index, core, first_piece, second_piece))
    return jnp.concatenate(outs, 1)


def pack_attention(
    short_q, short_k, short_v, short_seg, pool_kv, page_table, block_index, block_count
):
    pack_rows, width = short_q.shape
    heads_dev = width // HD
    pool_pages = pool_kv.shape[0]
    page_len = pool_kv.shape[2]
    page_rows = page_table.reshape(block_count, -1)
    entries = page_rows.shape[1]
    capacity = entries // block_count
    owners = page_rows // pool_pages
    places = page_rows % pool_pages
    wanted = owners == block_index
    ranks = jnp.cumsum(wanted.astype(jnp.int32), axis=1) - 1
    picked = wanted[:, :, None] & (
        ranks[:, :, None] == jnp.arange(capacity, dtype=jnp.int32)[None, None, :]
    )
    send_places = jnp.sum(jnp.where(picked, places[:, :, None], 0), axis=1)
    outgoing = pool_kv[send_places.reshape(-1)].reshape(block_count, capacity, 2, page_len, width)
    arrived = lax.all_to_all(outgoing, ("chip", "core"), split_axis=0, concat_axis=0, tiled=True)
    my_owners = lax.dynamic_index_in_dim(owners, block_index, 0, keepdims=False)
    order = jnp.arange(entries, dtype=jnp.int32)
    before = (my_owners[None, :] == my_owners[:, None]) & (order[None, :] < order[:, None])
    slots = my_owners * capacity + jnp.sum(before.astype(jnp.int32), axis=1)
    fetched = arrived.reshape(block_count * capacity, 2, page_len, width)[slots]
    cache_len = entries * page_len
    key_rows = jnp.concatenate([fetched[:, 0].reshape(cache_len, width), short_k], 0)
    value_rows = jnp.concatenate([fetched[:, 1].reshape(cache_len, width), short_v], 0)
    segment = short_seg[0]
    positions = jnp.arange(pack_rows, dtype=jnp.int32)
    key_seg = jnp.concatenate([jnp.arange(cache_len, dtype=jnp.int32) // (PPS * page_len), segment])
    key_pos = jnp.concatenate([jnp.full((cache_len,), -1, jnp.int32), positions])
    allowed = ((key_seg[None, :] == segment[:, None]) & (key_pos[None, :] <= positions[:, None]))[
        None
    ]
    query_heads = short_q.reshape(pack_rows, heads_dev, HD)
    key_heads = key_rows.reshape(cache_len + pack_rows, heads_dev, HD)
    value_heads = value_rows.reshape(cache_len + pack_rows, heads_dev, HD)
    scores = jnp.einsum(
        "qhd,khd->hqk", query_heads, key_heads, preferred_element_type=jnp.float32
    ) * HD ** (-0.5)
    scores = jnp.where(allowed, scores, very_negative)
    row_max = jnp.max(scores, axis=-1)
    weights = jnp.where(allowed, jnp.exp(scores - row_max[..., None]), 0.0)
    total = jnp.sum(weights, axis=-1)
    numer = jnp.einsum(
        "hqk,khd->hqd",
        weights.astype(jnp.bfloat16),
        value_heads,
        preferred_element_type=jnp.float32,
    )
    merged = numer / total[..., None]
    return merged.transpose(1, 0, 2).reshape(pack_rows, width).astype(jnp.bfloat16)


def per_device(
    long_q, long_k, long_v, short_q, short_k, short_v, short_seg, pool_kv, page_table, w_out
):
    block_count = lax.axis_size("chip") * lax.axis_size("core")
    core = lax.axis_index("core")
    block_index = lax.axis_index("chip") * lax.axis_size("core") + core
    long_attn = prompt_attention(long_q, block_index, core, long_k, long_v)
    short_attn = pack_attention(
        short_q, short_k, short_v, short_seg, pool_kv, page_table, block_index, block_count
    )
    long_rows = lax.all_to_all(long_attn, "req", 0, 1, tiled=True)
    short_rows = lax.all_to_all(short_attn, "req", 0, 1, tiled=True)
    long_out = jnp.dot(long_rows, w_out, preferred_element_type=jnp.float32).astype(jnp.bfloat16)
    short_out = jnp.dot(short_rows, w_out, preferred_element_type=jnp.float32).astype(jnp.bfloat16)
    return (long_out, short_out)


def solution(mesh):
    chips = mesh.shape["blk"] // 2
    mesh = jax.sharding.Mesh(
        mesh.devices.reshape(chips, 2, mesh.shape["req"]), ("chip", "core", "req")
    )
    blk = ("chip", "core")
    placed = (
        P(blk, "req"),
        P(blk, "req"),
        P(blk, "req"),
        P(blk, "req"),
        P(blk, "req"),
        P(blk, "req"),
        P(blk, None),
        P(blk, None, None, "req"),
        P(),
        P(),
    )
    return jax.shard_map(
        per_device,
        mesh=mesh,
        in_specs=placed,
        out_specs=(P(blk + ("req",), None), P(blk + ("req",), None)),
        check_vma=False,
    )
```

time: 281 us -> 331 us (1.18)
  waiting for transfers between devices: 115 us -> 156 us
  blocking collectives: 14.8 us -> 0 us
  Pallas kernels: 88.4 us -> 103 us
  starting transfers between devices: 13.3 us -> 20.2 us
  other arithmetic: 2.52 us -> 7.39 us
    all_gather x2, waiting for transfers between devices: 99.2 us -> 137 us  [prompt_attention(): first_piece = lax.all_gather(pair, 'chip', axis=0, tiled=True)]
    pallas_call x1 -> x2, Pallas kernels: 88.4 us -> 103 us  [flash_head(): pl.pallas_call(body, out_shape=jax.ShapeDtypeStruct((row_count, HD), jnp....]
    all_to_all x1 -> x0, blocking collectives: 14.8 us -> none  [per_device(): short_rows = lax.all_to_all(short_attn, 'req', 0, 1, tiled=True)]
    all_to_all x1 -> x2, starting transfers between devices: 7.51 us -> 13.1 us  [the longest x1 8 us: pack_attention(): lax.all_to_all(outgoing, ('chip', 'core'), split_axis=0, concat_axis=0, t...]
    all_to_all x1 -> x2, waiting for transfers between devices: 13.4 us -> 14.2 us  [the longest x1 8.6 us: pack_attention(): lax.all_to_all(outgoing, ('chip', 'core'), split_axis=0, concat_axis=0, t...]
  transfers between devices with their start and end apart: 4 -> 9, of which waited for: 4 -> 7; matrix products, arithmetic and copies ran while one was open for 9% -> 8% of each run, Pallas kernels for 0% -> 16%
where the time goes in v3:
time: 331 us
  waiting for transfers between devices  156 us (47%)
  Pallas kernels  103 us (31%)
  matrix products  20.5 us (6%)
  starting transfers between devices  20.2 us (6%)
  between operations  14.3 us (4%)
  local copies, waits for them, and re-layouts  9.08 us (3%)
  other arithmetic  7.39 us (2%)
    all_gather x2, waiting for transfers between devices, prompt_attention(): first_piece = lax.all_gather(pair, 'chip', axis=0, tiled=True)  137 us
    pallas_call x2, Pallas kernels, flash_head(): pl.pallas_call(body, out_shape=jax.ShapeDtypeStruct((row_count, HD), jnp....  103 us
    all_to_all x1, waiting for transfers between devices, pack_attention(): lax.all_to_all(outgoing, ('chip', 'core'), split_axis=0, concat_axis=0, t...  8.6 us
    all_to_all x1, starting transfers between devices, pack_attention(): lax.all_to_all(outgoing, ('chip', 'core'), split_axis=0, concat_axis=0, t...  8 us
  transfers between devices with their start and end apart: 9, of which 7 were waited for; matrix products, arithmetic and copies ran while one was open for 8% of the time, Pallas kernels for 16%

profile of v3, /device:TPU:23, one launch (start us, length us, event | category | flops | bytes accessed | tf_op | source)
XLA Modules:
  0.0 330.7 jit_solution(17114400803145384036)
XLA Ops:
  7.2 0.0 copy-start
  7.2 0.0 copy-start.6
  7.2 0.0 all-gather.5.cloned.1.call-start
  7.2 1.4 broadcast_select_fusion.1
  8.6 0.0 copy-start.3
  8.6 0.8 collective-permute-start.2
  9.4 1.2 collective-permute-done.2
  10.5 0.9 maximum_select_fusion.1
  11.5 0.0 all-gather.5.cloned.1.call-update
  11.5 0.0 all-gather.3.cloned.1.call-start
  11.6 0.5 collective-permute-start
  12.0 1.2 collective-permute-done
  13.2 1.0 maximum_select_fusion
  14.1 0.0 all-gather.3.cloned.1.call-update
  14.2 66.1 %all-gather.5.cloned.1.call-done.a_ref = bf16[16384,128]{1,0:T(8,128)(2,1)} async-done(((bf16[2048,128]{1,0:T(8,128)(2,1)}), bf16[16384,128]{1,0:T(8,128)(2,1)}) %all-gather.5.cloned.1.call-update) | async-done | bytes 4194320 | tf_op jit(solution)/shard_map/all_gather | solution.py:116
  80.3 1.0 collective-permute-start.3
  81.3 70.8 %all-gather.3.cloned.1.call-done.a_ref = bf16[16384,128]{1,0:T(8,128)(2,1)} async-done(((bf16[2048,128]{1,0:T(8,128)(2,1)}), bf16[16384,128]{1,0:T(8,128)(2,1)}) %all-gather.3.cloned.1.call-update) | async-done | bytes 4194320 | tf_op jit(solution)/shard_map/all_gather | solution.py:116
  152.1 1.0 collective-permute-start.1
  153.1 0.0 copy-done.6
  153.2 0.1 copy.48
  153.2 0.1 copy.49
  153.3 0.2 reduce_window_sum.11
  153.6 0.1 select_reduce_fusion
  153.7 0.1 copy.53
  153.8 0.1 reshape.234
  153.9 0.0 copy-done
  153.9 1.6 gather_fusion
  155.5 8.0 %all-to-all-start.1 = ((bf16[16,4,2,16,256]{4,3,2,1,0:T(8,128)(2,1)}), bf16[16,4,2,16,256]{4,3,2,1,0:T(8,128)(2,1)S(1)}, u32[]{:S(2)}, u32[]{:S(2)}) async-start(bf16[16,4,2,16,256]{4,3,2,1,0:T(8,128)(2,1)} %bitcast.8), calls=%async_computation.1 | async-start | bytes 2097152 | tf_op jit(solution)/shard_map/all_to_all | solution.py:141
  163.5 0.0 copy-done.3
  163.5 0.1 copy.54
  163.7 0.8 copy.56
  164.5 0.0 copy-done.4
  164.5 0.1 copy.58
  164.7 0.8 copy.60
  165.5 0.2 convert_reduce_fusion
  165.7 0.0 copy-done.8
  165.8 0.0 copy-done.7
  165.8 1.9 fusion.6
  167.7 8.6 %all-to-all-done.1 = bf16[16,4,2,16,256]{4,3,2,1,0:T(8,128)(2,1)S(1)} async-done(((bf16[16,4,2,16,256]{4,3,2,1,0:T(8,128)(2,1)}), bf16[16,4,2,16,256]{4,3,2,1,0:T(8,128)(2,1)S(1)}, u32[]{:S(2)}, u32[]{:S(2)}) %all-to-all-start.1) | async-done | bytes 1048608 | tf_op jit(solution)/shard_map/all_to_all | solution.py:141
  176.3 0.6 gather_fusion.1
  176.9 0.9 fusion.46
  177.8 1.2 concatenate.41
  179.0 0.1 copy.55
  179.1 0.1 concatenate.44
  179.3 0.1 copy.59
  179.3 0.0 copy-done.2
  179.3 0.0 copy-start.5
  179.4 6.1 %fusion.47 = (f32[2,512]{1,0:T(2,128)S(1)}, bf16[2,512,1536]{1,2,0:T(8,128)(2,1)}) fusion(pred[512,1536]{0,1:T(8,128)(4,1)S(1)} %copy-done.2, bf16[512,2,128]{2,0,1:T(8,128)(2,1)} %copy.56, bf16[1024,2,128]{2,0,1:T(8,128)(2,1)S(1)} %copy.55, bf16[512,256]{1,0:T(8,128)(2,1)} %param.13), kind=kOutput, calls=%fused_computation.74 | convolution fusion | flops 413664768 | bytes 4984832 | tf_op jit(solution)/shard_map/sub | solution.py:165
  185.4 3.3 fusion.14
  188.7 0.3 copy.62
  189.0 0.9 convert_element_type.31
  189.9 5.1 %all-to-all-start.2 = ((bf16[8,64,256]{2,1,0:T(8,128)(2,1)}), bf16[8,64,256]{2,1,0:T(8,128)(2,1)S(1)}, u32[]{:S(2)}, u32[]{:S(2)}) async-start(bf16[8,64,256]{2,1,0:T(8,128)(2,1)} %convert_element_type.31), calls=%async_computation.2 | async-start | bytes 524288 | tf_op jit(solution)/shard_map/all_to_all | solution.py:188
  195.0 0.6 pad_add_fusion.1.pos_ref
  195.6 5.6 %all-to-all-done.2 = bf16[8,64,256]{2,1,0:T(8,128)(2,1)S(1)} async-done(((bf16[8,64,256]{2,1,0:T(8,128)(2,1)}), bf16[8,64,256]{2,1,0:T(8,128)(2,1)S(1)}, u32[]{:S(2)}, u32[]{:S(2)}) %all-to-all-start.2) | async-done | bytes 262176 | tf_op jit(solution)/shard_map/all_to_all | solution.py:188
  201.2 0.0 collective-permute-done.3.b_ref
  201.2 51.7 %shard_map.114 = bf16[1024,128]{1,0:T(8,128)(2,1)} custom-call(s32[2]{0:T(128)} %pad_add_fusion.1.pos_ref, bf16[1024,256]{1,0:T(8,128)(2,1)} %q_ref.3, bf16[16384,128]{1,0:T(8,128)(2,1)} %all-gather.5.cloned.1.call-done.a_ref, bf16[16384,128]{1,0:T(8,128)(2,1)} %collective-permute-done.3.b_ref), custom_call_target="tpu_custom_call" | custom-call | tf_op jit(solution)/shard_map/pallas_call | solution.py:79
  252.9 0.0 collective-permute-done.1.b_ref
  252.9 51.6 %shard_map.113 = bf16[1024,128]{1,0:T(8,128)(2,1)} custom-call(s32[2]{0:T(128)} %pad_add_fusion.1.pos_ref, bf16[1024,256]{1,0:T(8,128)(2,1)} %q_ref.3, bf16[16384,128]{1,0:T(8,128)(2,1)} %all-gather.3.cloned.1.call-done.a_ref, bf16[16384,128]{1,0:T(8,128)(2,1)} %collective-permute-done.1.b_ref), custom_call_target="tpu_custom_call" | custom-call | tf_op jit(solution)/shard_map/pallas_call | solution.py:79
  304.6 1.0 pad_maximum_fusion.1
  305.6 1.0 copy.47
  306.6 3.7 %all-to-all-start = ((bf16[8,128,256]{1,2,0:T(8,128)(2,1)}), bf16[8,128,256]{1,2,0:T(8,128)(2,1)S(1)}, u32[]{:S(2)}, u32[]{:S(2)}) async-start(bf16[8,128,256]{1,2,0:T(8,128)(2,1)} %copy.47), calls=%async_computation | async-start | bytes 1048576 | tf_op jit(solution)/shard_map/all_to_all | solution.py:187
  310.3 5.7 %convolution_convert_fusion.1 = bf16[64,2048]{1,0:T(8,128)(2,1)} fusion(bf16[64,2048]{1,0:T(8,128)(2,1)S(1)} %bitcast.65, bf16[2048,2048]{1,0:T(8,128)(2,1)} %param.19), kind=kOutput, calls=%fused_computation.14 | convolution fusion | flops 537001984 | bytes 8912896 | tf_op jit(solution)/shard_map/dot_general | solution.py:190
  315.9 2.5 all-to-all-done
  318.4 5.5 %convolution_convert_fusion = bf16[128,2048]{1,0:T(8,128)(2,1)} fusion(bf16[128,2048]{0,1:T(8,128)(2,1)S(1)} %bitcast.63, bf16[2048,2048]{1,0:T(8,128)(2,1)} %param.19), kind=kOutput, calls=%fused_computation.13 | convolution fusion | flops 1074003968 | bytes 9437184 | tf_op jit(solution)/shard_map/dot_general | solution.py:189
  (18 shorter events, 0.1 us)
Async XLA Ops:
  7.2 146.8 %copy-start = (bf16[64,2,16,256]{3,2,1,0:T(8,128)(2,1)S(1)}, bf16[64,2,16,256]{3,2,1,0:T(8,128)(2,1)}, u32[]{:S(2)}) copy-start(bf16[64,2,16,256]{3,2,1,0:T(8,128)(2,1)} %param.17) | copy-start | bytes 3145732
  7.2 146.0 %copy-start.6 = (s32[16,16,4]{1,2,0:T(4,128)S(1)}, s32[16,16,4]{1,2,0:T(4,128)}, u32[]{:S(2)}) copy-start(s32[16,16,4]{1,2,0:T(4,128)} %param.18) | copy-start | bytes 12292
  7.2 73.1 %all-gather.5.cloned.1.call-start = ((), (), s32[]{:S(2)}) async-start(), calls=%async_computation.4 | async-start | bytes 4718592 | tf_op jit(solution)/shard_map/all_gather | solution.py:116
  8.6 154.9 %copy-start.3 = (bf16[512,256]{1,0:T(8,128)(2,1)S(1)}, bf16[512,256]{1,0:T(8,128)(2,1)}, u32[]{:S(2)}) copy-start(bf16[512,256]{1,0:T(8,128)(2,1)} %param.14) | copy-start | bytes 786436
  8.6 1.9 collective-permute-start.2
  11.5 153.1 %copy-start.4 = (bf16[512,256]{1,0:T(8,128)(2,1)S(1)}, bf16[512,256]{1,0:T(8,128)(2,1)}, u32[]{:S(2)}) copy-start(bf16[512,256]{1,0:T(8,128)(2,1)} %param.15) | copy-start | bytes 786436
  11.5 140.6 %all-gather.3.cloned.1.call-start = ((), (), s32[]{:S(2)}) async-start(), calls=%async_computation.3 | async-start | bytes 4718592 | tf_op jit(solution)/shard_map/all_gather | solution.py:116
  11.6 1.6 collective-permute-start
  13.2 152.6 %copy-start.8 = (s32[1,512]{1,0:T(1,128)S(1)}, s32[1,512]{1,0:T(1,128)}, u32[]{:S(2)}) copy-start(s32[1,512]{1,0:T(1,128)} %param.16) | copy-start | bytes 6148
  13.2 152.6 %copy-start.7 = (s32[1536]{0:T(1024)S(1)}, s32[1536]{0:T(1024)}, u32[]{:S(2)}) copy-start(s32[1536]{0:T(1024)} %constant.70.clone.1) | copy-start | bytes 18436
  80.3 120.9 %collective-permute-start.3 = (bf16[16384,128]{1,0:T(8,128)(2,1)}, bf16[16384,128]{1,0:T(8,128)(2,1)}, u32[]{:S(2)}, u32[]{:S(2)}) collective-permute-start(bf16[16384,128]{1,0:T(8,128)(2,1)} %all-gather.5.cloned.1.call-done.a_ref), channel_id=1, source_target_pairs={{0,8},{8,0},{1,9},{9,1},{2,10},{10,2},{3,11},{11,3},{4,12},{12,4},... | collective-permute-start | bytes 12582920 | tf_op jit(solution)/shard_map/ppermute | solution.py:117
  152.1 100.8 %collective-permute-start.1 = (bf16[16384,128]{1,0:T(8,128)(2,1)}, bf16[16384,128]{1,0:T(8,128)(2,1)}, u32[]{:S(2)}, u32[]{:S(2)}) collective-permute-start(bf16[16384,128]{1,0:T(8,128)(2,1)} %all-gather.3.cloned.1.call-done.a_ref), channel_id=1, source_target_pairs={{0,8},{8,0},{1,9},{9,1},{2,10},{10,2},{3,11},{11,3},{4,12},{12,4},... | collective-permute-start | bytes 12582920 | tf_op jit(solution)/shard_map/ppermute | solution.py:117
  155.5 20.8 %all-to-all-start.1 = ((bf16[16,4,2,16,256]{4,3,2,1,0:T(8,128)(2,1)}), bf16[16,4,2,16,256]{4,3,2,1,0:T(8,128)(2,1)S(1)}, u32[]{:S(2)}, u32[]{:S(2)}) async-start(bf16[16,4,2,16,256]{4,3,2,1,0:T(8,128)(2,1)} %bitcast.8), calls=%async_computation.1 | async-start | bytes 2097152 | tf_op jit(solution)/shard_map/all_to_all | solution.py:141
  177.8 1.5 copy-start.2
  179.3 6.1 %copy-start.5 = (bf16[512,2,128]{2,0,1:T(8,128)(2,1)S(1)}, bf16[512,2,128]{2,0,1:T(8,128)(2,1)}, u32[]{:S(2)}) copy-start(bf16[512,2,128]{2,0,1:T(8,128)(2,1)} %copy.60) | copy-start | bytes 786436
  189.9 11.3 %all-to-all-start.2 = ((bf16[8,64,256]{2,1,0:T(8,128)(2,1)}), bf16[8,64,256]{2,1,0:T(8,128)(2,1)S(1)}, u32[]{:S(2)}, u32[]{:S(2)}) async-start(bf16[8,64,256]{2,1,0:T(8,128)(2,1)} %convert_element_type.31), calls=%async_computation.2 | async-start | bytes 524288 | tf_op jit(solution)/shard_map/all_to_all | solution.py:188
  252.9 51.7 %copy-start.1 = (bf16[1024,128]{1,0:T(8,128)(2,1)S(1)}, bf16[1024,128]{1,0:T(8,128)(2,1)}, u32[]{:S(2)}) copy-start(bf16[1024,128]{1,0:T(8,128)(2,1)} %shard_map.114) | copy-start | bytes 786436
  306.6 11.9 %all-to-all-start = ((bf16[8,128,256]{1,2,0:T(8,128)(2,1)}), bf16[8,128,256]{1,2,0:T(8,128)(2,1)S(1)}, u32[]{:S(2)}, u32[]{:S(2)}) async-start(bf16[8,128,256]{1,2,0:T(8,128)(2,1)} %copy.47), calls=%async_computation | async-start | bytes 1048576 | tf_op jit(solution)/shard_map/all_to_all | solution.py:187
Sparse Core Ops, SparseCore 0:
  11.6 68.6 all-gather.4
  82.6 69.4 all-gather.2

commit v4 on v2

--- a/solution.py
+++ b/solution.py
@@ -67,15 +67,23 @@
 def prompt_attention(queries, block_index, long_k, long_v):
     row_count, width = queries.shape
     heads_dev = width // HD
-    key_piece = lax.all_gather(long_k, "blk", axis=0, tiled=True)
-    value_piece = lax.all_gather(long_v, "blk", axis=0, tiled=True)
-    piece_rows = key_piece.shape[0]
+    block_count = lax.axis_size("blk")
+    own = jnp.concatenate([long_k, long_v], 1)
+    pieces = [own]
+    for shift in range(1, block_count):
+        pairs = [(src, src + shift) for src in range(block_count - shift)]
+        pieces.append(lax.ppermute(own, "blk", pairs))
+    stacked = jnp.stack(pieces)
+    piece_rows = block_count * row_count
     tq = min(row_count, 512)
     tk = min(row_count, 1024)
 
-    def kv_map(q_tile, k_tile, blk_ref):
-        last_tile = (blk_ref[0] * row_count + q_tile * tq + tq - 1) // tk
-        return (jnp.minimum(k_tile, last_tile), 0)
+    def kv_map(column):
+        def index(q_tile, k_tile, blk_ref):
+            last_tile = (blk_ref[0] * row_count + q_tile * tq + tq - 1) // tk
+            return (blk_ref[0] - jnp.minimum(k_tile, last_tile), 0, column)
+
+        return index
 
     body = functools.partial(flash_body, heads=heads_dev, tq=tq, tk=tk, q_rows=row_count)
     return pl.pallas_call(
@@ -86,8 +94,8 @@
             grid=(row_count // tq, piece_rows // tk),
             in_specs=[
                 pl.BlockSpec((tq, width), lambda q_tile, k_tile, blk_ref: (q_tile, 0)),
-                pl.BlockSpec((tk, width), kv_map),
-                pl.BlockSpec((tk, width), kv_map),
+                pl.BlockSpec((None, tk, width), kv_map(0)),
+                pl.BlockSpec((None, tk, width), kv_map(1)),
             ],
             out_specs=pl.BlockSpec((tq, width), lambda q_tile, k_tile, blk_ref: (q_tile, 0)),
             scratch_shapes=[
@@ -97,7 +105,7 @@
             ],
         ),
         compiler_params=pltpu.CompilerParams(dimension_semantics=("arbitrary", "arbitrary")),
-    )(jnp.reshape(block_index, (1,)).astype(jnp.int32), queries, key_piece, value_piece)
+    )(jnp.reshape(block_index, (1,)).astype(jnp.int32), queries, stacked, stacked)
 
 
 def pack_attention(

time: 281 us -> 453 us (1.61)
  waiting for transfers between devices: 115 us -> 246 us
  starting transfers between devices: 13.3 us -> 50.6 us
  local copies, waits for them, and re-layouts: 10.4 us -> 40.3 us
  blocking collectives: 14.8 us -> 0 us
  between operations: 14.3 us -> 0.92 us
    ppermute x0 -> x15, waiting for transfers between devices: none -> 161 us  [prompt_attention(): pieces.append(lax.ppermute(own, 'blk', pairs))]
    all_gather x2 -> x0, waiting for transfers between devices: 99.2 us -> none  [the longest x1 73 us: prompt_attention(): value_piece = lax.all_gather(long_v, 'blk', axis=0, tiled=True)]
    all_to_all x1, waiting for transfers between devices: 13.4 us -> 83.6 us  [pack_attention(): lax.all_to_all(outgoing, 'blk', split_axis=0, concat_axis=0, tiled=True)]
    unnamed x13 -> x21, local copies, waits for them, and re-layouts: 2.1 us -> 28.3 us
    ppermute x0 -> x15, starting transfers between devices: none -> 19.4 us  [prompt_attention(): pieces.append(lax.ppermute(own, 'blk', pairs))]
    all_to_all x1 -> x0, blocking collectives: 14.8 us -> none  [per_device(): short_rows = lax.all_to_all(short_attn, 'req', 0, 1, tiled=True)]
    all_to_all x1, starting transfers between devices: 7.51 us -> 18.5 us  [pack_attention(): lax.all_to_all(outgoing, 'blk', split_axis=0, concat_axis=0, tiled=True)]
    all_to_all x0 -> x1, starting transfers between devices: none -> 6.65 us  [per_device(): short_rows = lax.all_to_all(short_attn, 'req', 0, 1, tiled=True)]
  transfers between devices with their start and end apart: 4 -> 18, of which waited for: 4 -> 10; matrix products, arithmetic and copies ran while one was open for 9% -> 12% of each run, Pallas kernels for 0% -> 20%
where the time goes in v4:
time: 453 us; the launch traced here: 451 us
  waiting for transfers between devices  246 us (54%)
  Pallas kernels  88.5 us (20%)
  starting transfers between devices  50.6 us (11%)
  local copies, waits for them, and re-layouts  40.3 us (9%)
  matrix products  21 us (5%)
    ppermute x15, waiting for transfers between devices, prompt_attention(): pieces.append(lax.ppermute(own, 'blk', pairs))  161 us
    pallas_call x1, Pallas kernels, prompt_attention(): pl.pallas_call(body, out_shape=jax.ShapeDtypeStruct((row_count, width), j...  88.5 us
    all_to_all x1, waiting for transfers between devices, pack_attention(): lax.all_to_all(outgoing, 'blk', split_axis=0, concat_axis=0, tiled=True)  83.6 us
    unnamed x21, local copies, waits for them, and re-layouts  28.3 us
    ppermute x15, starting transfers between devices, prompt_attention(): pieces.append(lax.ppermute(own, 'blk', pairs))  19.4 us
    all_to_all x1, starting transfers between devices, pack_attention(): lax.all_to_all(outgoing, 'blk', split_axis=0, concat_axis=0, tiled=True)  18.5 us
  transfers between devices with their start and end apart: 18, of which 10 were waited for; matrix products, arithmetic and copies ran while one was open for 12% of the time, Pallas kernels for 20%

profile of v4, /device:TPU:23, one launch (start us, length us, event | category | flops | bytes accessed | tf_op | source)
XLA Modules:
  0.0 451.3 jit_solution(407500065196276999)
XLA Ops:
  0.6 2.0 constant_dynamic-update-slice_fusion.1
  2.6 1.9 constant_dynamic-update-slice_fusion
  4.6 1.3 collective-permute-start
  5.9 1.3 collective-permute-start.1
  7.2 1.3 collective-permute-start.2
  8.5 1.3 collective-permute-start.3
  9.8 1.3 collective-permute-start.4
  11.1 0.8 copy.48
  12.6 1.6 gather_fusion
  14.2 18.5 %all-to-all-start.1 = ((bf16[16,4,2,16,256]{4,3,2,1,0:T(8,128)(2,1)}), bf16[16,4,2,16,256]{4,3,2,1,0:T(8,128)(2,1)S(1)}, u32[]{:S(2)}, u32[]{:S(2)}) async-start(bf16[16,4,2,16,256]{4,3,2,1,0:T(8,128)(2,1)} %bitcast.23), calls=%async_computation.1 | async-start | bytes 2097152 | tf_op jit(solution)/shard_map/all_to_all | solution.py:130
  32.9 1.1 copy.54
  34.0 0.8 copy.56
  34.8 1.1 copy.58
  36.1 0.7 pad_add_fusion
  36.8 2.3 bitcast_dynamic-update-slice_fusion.15
  39.1 2.7 fusion.6
  41.8 83.6 %all-to-all-done.1 = bf16[16,4,2,16,256]{4,3,2,1,0:T(8,128)(2,1)S(1)} async-done(((bf16[16,4,2,16,256]{4,3,2,1,0:T(8,128)(2,1)}), bf16[16,4,2,16,256]{4,3,2,1,0:T(8,128)(2,1)S(1)}, u32[]{:S(2)}, u32[]{:S(2)}) %all-to-all-start.1) | async-done | bytes 1048608 | tf_op jit(solution)/shard_map/all_to_all | solution.py:130
  125.3 0.6 gather_fusion.1
  126.0 0.9 fusion.46
  126.8 1.2 concatenate.25
  128.1 6.6 %fusion.47 = (f32[2,512]{1,0:T(2,128)S(1)}, bf16[2,512,1536]{1,2,0:T(8,128)(2,1)}) fusion(pred[512,1536]{0,1:T(8,128)(4,1)} %fusion.6, bf16[512,2,128]{2,0,1:T(8,128)(2,1)} %copy.56, bf16[1024,2,128]{2,0,1:T(8,128)(2,1)S(1)} %copy.55, bf16[512,256]{1,0:T(8,128)(2,1)} %param.13), kind=kOutput, calls=%fused_computation.86 | convolution fusion | flops 413664768 | bytes 4984832 | tf_op jit(solution)/shard_map/sub | solution.py:154
  134.9 3.3 fusion.14
  138.2 0.3 copy.62
  138.5 0.9 convert_element_type.31
  139.3 6.7 %all-to-all-start.2 = ((bf16[8,64,256]{2,1,0:T(8,128)(2,1)}), bf16[8,64,256]{2,1,0:T(8,128)(2,1)S(1)}, u32[]{:S(2)}, u32[]{:S(2)}) async-start(bf16[8,64,256]{2,1,0:T(8,128)(2,1)} %convert_element_type.31), calls=%async_computation.2 | async-start | bytes 524288 | tf_op jit(solution)/shard_map/all_to_all | solution.py:176
  146.0 1.3 collective-permute-start.5
  147.3 2.3 bitcast_dynamic-update-slice_fusion.14
  149.6 1.3 collective-permute-start.6
  150.9 2.3 bitcast_dynamic-update-slice_fusion.13
  153.2 1.3 collective-permute-start.7
  154.4 2.3 bitcast_dynamic-update-slice_fusion.12
  156.7 1.3 collective-permute-start.8
  158.0 2.3 bitcast_dynamic-update-slice_fusion.11
  160.3 1.3 collective-permute-start.9
  161.6 2.3 bitcast_dynamic-update-slice_fusion.10
  163.9 11.6 %collective-permute-done.5 = bf16[1024,512]{1,0:T(8,128)(2,1)S(1)} collective-permute-done((bf16[1024,512]{1,0:T(8,128)(2,1)}, bf16[1024,512]{1,0:T(8,128)(2,1)S(1)}, u32[]{:S(2)}, u32[]{:S(2)}) %collective-permute-start.5) | collective-permute-done | bytes 1048608 | tf_op jit(solution)/shard_map/ppermute | solution.py:75
  175.4 1.3 collective-permute-start.10
  176.7 1.1 bitcast_dynamic-update-slice_fusion.9
  177.8 9.1 %collective-permute-done.6 = bf16[1024,512]{1,0:T(8,128)(2,1)S(1)} collective-permute-done((bf16[1024,512]{1,0:T(8,128)(2,1)}, bf16[1024,512]{1,0:T(8,128)(2,1)S(1)}, u32[]{:S(2)}, u32[]{:S(2)}) %collective-permute-start.6) | collective-permute-done | bytes 1048608 | tf_op jit(solution)/shard_map/ppermute | solution.py:75
  187.0 1.3 collective-permute-start.11
  188.2 1.1 bitcast_dynamic-update-slice_fusion.8
  189.3 27.7 %collective-permute-done.7 = bf16[1024,512]{1,0:T(8,128)(2,1)S(1)} collective-permute-done((bf16[1024,512]{1,0:T(8,128)(2,1)}, bf16[1024,512]{1,0:T(8,128)(2,1)S(1)}, u32[]{:S(2)}, u32[]{:S(2)}) %collective-permute-start.7) | collective-permute-done | bytes 1048608 | tf_op jit(solution)/shard_map/ppermute | solution.py:75
  217.0 1.3 collective-permute-start.12
  218.3 1.1 bitcast_dynamic-update-slice_fusion.7
  219.4 12.9 %collective-permute-done.8 = bf16[1024,512]{1,0:T(8,128)(2,1)S(1)} collective-permute-done((bf16[1024,512]{1,0:T(8,128)(2,1)}, bf16[1024,512]{1,0:T(8,128)(2,1)S(1)}, u32[]{:S(2)}, u32[]{:S(2)}) %collective-permute-start.8) | collective-permute-done | bytes 1048608 | tf_op jit(solution)/shard_map/ppermute | solution.py:75
  232.3 1.3 collective-permute-start.13
  233.6 1.0 bitcast_dynamic-update-slice_fusion.6
  234.6 11.5 %collective-permute-done.9 = bf16[1024,512]{1,0:T(8,128)(2,1)S(1)} collective-permute-done((bf16[1024,512]{1,0:T(8,128)(2,1)}, bf16[1024,512]{1,0:T(8,128)(2,1)S(1)}, u32[]{:S(2)}, u32[]{:S(2)}) %collective-permute-start.9) | collective-permute-done | bytes 1048608 | tf_op jit(solution)/shard_map/ppermute | solution.py:75
  246.1 1.5 collective-permute-start.14
  247.6 1.1 bitcast_dynamic-update-slice_fusion.5
  248.6 1.7 collective-permute-done.10
  250.3 1.1 bitcast_dynamic-update-slice_fusion.4
  251.4 70.4 %collective-permute-done.11 = bf16[1024,512]{1,0:T(8,128)(2,1)S(1)} collective-permute-done((bf16[1024,512]{1,0:T(8,128)(2,1)}, bf16[1024,512]{1,0:T(8,128)(2,1)S(1)}, u32[]{:S(2)}, u32[]{:S(2)}) %collective-permute-start.11) | collective-permute-done | bytes 1048608 | tf_op jit(solution)/shard_map/ppermute | solution.py:75
  321.8 1.1 bitcast_dynamic-update-slice_fusion.3
  322.9 1.0 bitcast_dynamic-update-slice_fusion.2
  323.9 16.1 %collective-permute-done.13 = bf16[1024,512]{1,0:T(8,128)(2,1)S(1)} collective-permute-done((bf16[1024,512]{1,0:T(8,128)(2,1)}, bf16[1024,512]{1,0:T(8,128)(2,1)S(1)}, u32[]{:S(2)}, u32[]{:S(2)}) %collective-permute-start.13) | collective-permute-done | bytes 1048608 | tf_op jit(solution)/shard_map/ppermute | solution.py:75
  340.0 1.0 bitcast_dynamic-update-slice_fusion.1
  341.1 1.0 bitcast_dynamic-update-slice_fusion.k_ref.v_ref
  342.1 88.5 %shard_map.113 = bf16[1024,256]{1,0:T(8,128)(2,1)} custom-call(s32[1]{0:T(128)} %bitcast.blk_ref, bf16[1024,256]{1,0:T(8,128)(2,1)} %q_ref.1, bf16[16,1024,512]{2,1,0:T(8,128)(2,1)} %bitcast_dynamic-update-slice_fusion.k_ref.v_ref, bf16[16,1024,512]{2,1,0:T(8,128)(2,1)} %bitcast_dynamic-update-slice_fusion.k_ref.v_ref), custom_call_target="tpu_custom_call" | custom-call | tf_op jit(solution)/shard_map/pallas_call | solution.py:89
  430.6 2.0 copy.47
  432.7 6.0 %all-to-all-start = ((bf16[8,128,256]{1,2,0:T(8,128)(2,1)}), bf16[8,128,256]{1,2,0:T(8,128)(2,1)S(1)}, u32[]{:S(2)}, u32[]{:S(2)}) async-start(bf16[8,128,256]{1,2,0:T(8,128)(2,1)} %copy.47), calls=%async_computation | async-start | bytes 1048576 | tf_op jit(solution)/shard_map/all_to_all | solution.py:175
  438.7 5.7 %convolution_convert_fusion.1 = bf16[64,2048]{1,0:T(8,128)(2,1)} fusion(bf16[64,2048]{1,0:T(8,128)(2,1)S(1)} %bitcast.96, bf16[2048,2048]{1,0:T(8,128)(2,1)} %param.19), kind=kOutput, calls=%fused_computation.14 | convolution fusion | flops 537001984 | bytes 8912896 | tf_op jit(solution)/shard_map/dot_general | solution.py:178
  444.4 1.4 all-to-all-done
  445.8 5.5 %convolution_convert_fusion = bf16[128,2048]{1,0:T(8,128)(2,1)} fusion(bf16[128,2048]{0,1:T(8,128)(2,1)S(1)} %bitcast.94, bf16[2048,2048]{1,0:T(8,128)(2,1)} %param.19), kind=kOutput, calls=%fused_computation.13 | convolution fusion | flops 1074003968 | bytes 9437184 | tf_op jit(solution)/shard_map/dot_general | solution.py:177
  (29 shorter events, 1.3 us)
Async XLA Ops:
  0.6 12.0 %copy-start = (bf16[64,2,16,256]{3,2,1,0:T(8,128)(2,1)S(1)}, bf16[64,2,16,256]{3,2,1,0:T(8,128)(2,1)}, u32[]{:S(2)}) copy-start(bf16[64,2,16,256]{3,2,1,0:T(8,128)(2,1)} %param.17) | copy-start | bytes 3145732
  4.6 141.4 %collective-permute-start = (bf16[1024,512]{1,0:T(8,128)(2,1)}, bf16[1024,512]{1,0:T(8,128)(2,1)}, u32[]{:S(2)}, u32[]{:S(2)}) collective-permute-start(bf16[1024,512]{1,0:T(8,128)(2,1)} %constant_dynamic-update-slice_fusion), channel_id=1, source_target_pairs={{0,8},{8,16},{16,24},{24,32},{32,40},{40,48},{48,56},{56,64},{64,7... | collective-permute-start | bytes 3145736 | tf_op jit(solution)/shard_map/ppermute | solution.py:75
  5.9 143.7 %collective-permute-start.1 = (bf16[1024,512]{1,0:T(8,128)(2,1)}, bf16[1024,512]{1,0:T(8,128)(2,1)}, u32[]{:S(2)}, u32[]{:S(2)}) collective-permute-start(bf16[1024,512]{1,0:T(8,128)(2,1)} %constant_dynamic-update-slice_fusion), channel_id=1, source_target_pairs={{0,16},{8,24},{16,32},{24,40},{32,48},{40,56},{48,64},{56,72},{64,... | collective-permute-start | bytes 3145736 | tf_op jit(solution)/shard_map/ppermute | solution.py:75
  7.2 146.0 %collective-permute-start.2 = (bf16[1024,512]{1,0:T(8,128)(2,1)}, bf16[1024,512]{1,0:T(8,128)(2,1)}, u32[]{:S(2)}, u32[]{:S(2)}) collective-permute-start(bf16[1024,512]{1,0:T(8,128)(2,1)} %constant_dynamic-update-slice_fusion), channel_id=1, source_target_pairs={{0,24},{8,32},{16,40},{24,48},{32,56},{40,64},{48,72},{56,80},{64,... | collective-permute-start | bytes 3145736 | tf_op jit(solution)/shard_map/ppermute | solution.py:75
  8.5 148.3 %collective-permute-start.3 = (bf16[1024,512]{1,0:T(8,128)(2,1)}, bf16[1024,512]{1,0:T(8,128)(2,1)}, u32[]{:S(2)}, u32[]{:S(2)}) collective-permute-start(bf16[1024,512]{1,0:T(8,128)(2,1)} %constant_dynamic-update-slice_fusion), channel_id=1, source_target_pairs={{0,32},{8,40},{16,48},{24,56},{32,64},{40,72},{48,80},{56,88},{64,... | collective-permute-start | bytes 3145736 | tf_op jit(solution)/shard_map/ppermute | solution.py:75
  9.8 150.5 %collective-permute-start.4 = (bf16[1024,512]{1,0:T(8,128)(2,1)}, bf16[1024,512]{1,0:T(8,128)(2,1)}, u32[]{:S(2)}, u32[]{:S(2)}) collective-permute-start(bf16[1024,512]{1,0:T(8,128)(2,1)} %constant_dynamic-update-slice_fusion), channel_id=1, source_target_pairs={{0,40},{8,48},{16,56},{24,64},{32,72},{40,80},{48,88},{56,96},{64,... | collective-permute-start | bytes 3145736 | tf_op jit(solution)/shard_map/ppermute | solution.py:75
  14.2 111.1 %all-to-all-start.1 = ((bf16[16,4,2,16,256]{4,3,2,1,0:T(8,128)(2,1)}), bf16[16,4,2,16,256]{4,3,2,1,0:T(8,128)(2,1)S(1)}, u32[]{:S(2)}, u32[]{:S(2)}) async-start(bf16[16,4,2,16,256]{4,3,2,1,0:T(8,128)(2,1)} %bitcast.23), calls=%async_computation.1 | async-start | bytes 2097152 | tf_op jit(solution)/shard_map/all_to_all | solution.py:130
  139.3 293.3 %all-to-all-start.2 = ((bf16[8,64,256]{2,1,0:T(8,128)(2,1)}), bf16[8,64,256]{2,1,0:T(8,128)(2,1)S(1)}, u32[]{:S(2)}, u32[]{:S(2)}) async-start(bf16[8,64,256]{2,1,0:T(8,128)(2,1)} %convert_element_type.31), calls=%async_computation.2 | async-start | bytes 524288 | tf_op jit(solution)/shard_map/all_to_all | solution.py:176
  146.0 29.5 %collective-permute-start.5 = (bf16[1024,512]{1,0:T(8,128)(2,1)}, bf16[1024,512]{1,0:T(8,128)(2,1)S(1)}, u32[]{:S(2)}, u32[]{:S(2)}) collective-permute-start(bf16[1024,512]{1,0:T(8,128)(2,1)} %constant_dynamic-update-slice_fusion), channel_id=1, source_target_pairs={{0,48},{8,56},{16,64},{24,72},{32,80},{40,88},{48,96},{56,104},{64... | collective-permute-start | bytes 3145736 | tf_op jit(solution)/shard_map/ppermute | solution.py:75
  149.6 37.4 %collective-permute-start.6 = (bf16[1024,512]{1,0:T(8,128)(2,1)}, bf16[1024,512]{1,0:T(8,128)(2,1)S(1)}, u32[]{:S(2)}, u32[]{:S(2)}) collective-permute-start(bf16[1024,512]{1,0:T(8,128)(2,1)} %constant_dynamic-update-slice_fusion), channel_id=1, source_target_pairs={{0,56},{8,64},{16,72},{24,80},{32,88},{40,96},{48,104},{56,112},{6... | collective-permute-start | bytes 3145736 | tf_op jit(solution)/shard_map/ppermute | solution.py:75
  153.2 63.9 %collective-permute-start.7 = (bf16[1024,512]{1,0:T(8,128)(2,1)}, bf16[1024,512]{1,0:T(8,128)(2,1)S(1)}, u32[]{:S(2)}, u32[]{:S(2)}) collective-permute-start(bf16[1024,512]{1,0:T(8,128)(2,1)} %constant_dynamic-update-slice_fusion), channel_id=1, source_target_pairs={{0,64},{8,72},{16,80},{24,88},{32,96},{40,104},{48,112},{56,120},{... | collective-permute-start | bytes 3145736 | tf_op jit(solution)/shard_map/ppermute | solution.py:75
  156.7 75.6 %collective-permute-start.8 = (bf16[1024,512]{1,0:T(8,128)(2,1)}, bf16[1024,512]{1,0:T(8,128)(2,1)S(1)}, u32[]{:S(2)}, u32[]{:S(2)}) collective-permute-start(bf16[1024,512]{1,0:T(8,128)(2,1)} %constant_dynamic-update-slice_fusion), channel_id=1, source_target_pairs={{0,72},{8,80},{16,88},{24,96},{32,104},{40,112},{48,120},{1,73},{9... | collective-permute-start | bytes 3145736 | tf_op jit(solution)/shard_map/ppermute | solution.py:75
  160.3 85.8 %collective-permute-start.9 = (bf16[1024,512]{1,0:T(8,128)(2,1)}, bf16[1024,512]{1,0:T(8,128)(2,1)S(1)}, u32[]{:S(2)}, u32[]{:S(2)}) collective-permute-start(bf16[1024,512]{1,0:T(8,128)(2,1)} %constant_dynamic-update-slice_fusion), channel_id=1, source_target_pairs={{0,80},{8,88},{16,96},{24,104},{32,112},{40,120},{1,81},{9,89},{17... | collective-permute-start | bytes 3145736 | tf_op jit(solution)/shard_map/ppermute | solution.py:75
  175.4 74.9 %collective-permute-start.10 = (bf16[1024,512]{1,0:T(8,128)(2,1)}, bf16[1024,512]{1,0:T(8,128)(2,1)S(1)}, u32[]{:S(2)}, u32[]{:S(2)}) collective-permute-start(bf16[1024,512]{1,0:T(8,128)(2,1)} %constant_dynamic-update-slice_fusion), channel_id=1, source_target_pairs={{0,88},{8,96},{16,104},{24,112},{32,120},{1,89},{9,97},{17,105},{2... | collective-permute-start | bytes 3145736 | tf_op jit(solution)/shard_map/ppermute | solution.py:75
  187.0 134.8 %collective-permute-start.11 = (bf16[1024,512]{1,0:T(8,128)(2,1)}, bf16[1024,512]{1,0:T(8,128)(2,1)S(1)}, u32[]{:S(2)}, u32[]{:S(2)}) collective-permute-start(bf16[1024,512]{1,0:T(8,128)(2,1)} %constant_dynamic-update-slice_fusion), channel_id=1, source_target_pairs={{0,96},{8,104},{16,112},{24,120},{1,97},{9,105},{17,113},{25,121},... | collective-permute-start | bytes 3145736 | tf_op jit(solution)/shard_map/ppermute | solution.py:75
  217.0 105.9 %collective-permute-start.12 = (bf16[1024,512]{1,0:T(8,128)(2,1)}, bf16[1024,512]{1,0:T(8,128)(2,1)S(1)}, u32[]{:S(2)}, u32[]{:S(2)}) collective-permute-start(bf16[1024,512]{1,0:T(8,128)(2,1)} %constant_dynamic-update-slice_fusion), channel_id=1, source_target_pairs={{0,104},{8,112},{16,120},{1,105},{9,113},{17,121},{2,106},{10,114}... | collective-permute-start | bytes 3145736 | tf_op jit(solution)/shard_map/ppermute | solution.py:75
  232.3 107.7 %collective-permute-start.13 = (bf16[1024,512]{1,0:T(8,128)(2,1)}, bf16[1024,512]{1,0:T(8,128)(2,1)S(1)}, u32[]{:S(2)}, u32[]{:S(2)}) collective-permute-start(bf16[1024,512]{1,0:T(8,128)(2,1)} %constant_dynamic-update-slice_fusion), channel_id=1, source_target_pairs={{0,112},{8,120},{1,113},{9,121},{2,114},{10,122},{3,115},{11,123},... | collective-permute-start | bytes 3145736 | tf_op jit(solution)/shard_map/ppermute | solution.py:75
  246.1 95.0 %collective-permute-start.14 = (bf16[1024,512]{1,0:T(8,128)(2,1)}, bf16[1024,512]{1,0:T(8,128)(2,1)S(1)}, u32[]{:S(2)}, u32[]{:S(2)}) collective-permute-start(bf16[1024,512]{1,0:T(8,128)(2,1)} %constant_dynamic-update-slice_fusion), channel_id=1, source_target_pairs={{0,120},{1,121},{2,122},{3,123},{4,124},{5,125},{6,126},{7,127}} | collective-permute-start | bytes 3145736 | tf_op jit(solution)/shard_map/ppermute | solution.py:75
  432.7 13.1 %all-to-all-start = ((bf16[8,128,256]{1,2,0:T(8,128)(2,1)}), bf16[8,128,256]{1,2,0:T(8,128)(2,1)S(1)}, u32[]{:S(2)}, u32[]{:S(2)}) async-start(bf16[8,128,256]{1,2,0:T(8,128)(2,1)} %copy.47), calls=%async_computation | async-start | bytes 1048576 | tf_op jit(solution)/shard_map/all_to_all | solution.py:175

commit v5 on v4

--- a/solution.py
+++ b/solution.py
@@ -64,24 +64,20 @@
             o_ref[:, h * HD:(h + 1) * HD] = (acc_sc[h] / l_sc[h]).astype(o_ref.dtype)
 
 
-def prompt_attention(queries, block_index, long_k, long_v):
+def prompt_attention(queries, block_index, long_k, long_v, early=None):
     row_count, width = queries.shape
     heads_dev = width // HD
-    block_count = lax.axis_size("blk")
-    own = jnp.concatenate([long_k, long_v], 1)
-    pieces = [own]
-    for shift in range(1, block_count):
-        pairs = [(src, src + shift) for src in range(block_count - shift)]
-        pieces.append(lax.ppermute(own, "blk", pairs))
-    stacked = jnp.stack(pieces)
-    piece_rows = block_count * row_count
+    kv_piece = lax.all_gather(jnp.concatenate([long_k, long_v], 1), "blk", axis=0, tiled=True)
+    if early is not None:
+        kv_piece, early = lax.optimization_barrier((kv_piece, early))
+    piece_rows = kv_piece.shape[0]
     tq = min(row_count, 512)
     tk = min(row_count, 1024)
 
     def kv_map(column):
         def index(q_tile, k_tile, blk_ref):
             last_tile = (blk_ref[0] * row_count + q_tile * tq + tq - 1) // tk
-            return (blk_ref[0] - jnp.minimum(k_tile, last_tile), 0, column)
+            return (jnp.minimum(k_tile, last_tile), column)
 
         return index
 
@@ -94,8 +90,8 @@
             grid=(row_count // tq, piece_rows // tk),
             in_specs=[
                 pl.BlockSpec((tq, width), lambda q_tile, k_tile, blk_ref: (q_tile, 0)),
-                pl.BlockSpec((None, tk, width), kv_map(0)),
-                pl.BlockSpec((None, tk, width), kv_map(1)),
+                pl.BlockSpec((tk, width), kv_map(0)),
+                pl.BlockSpec((tk, width), kv_map(1)),
             ],
             out_specs=pl.BlockSpec((tq, width), lambda q_tile, k_tile, blk_ref: (q_tile, 0)),
             scratch_shapes=[
@@ -105,7 +101,7 @@
             ],
         ),
         compiler_params=pltpu.CompilerParams(dimension_semantics=("arbitrary", "arbitrary")),
-    )(jnp.reshape(block_index, (1,)).astype(jnp.int32), queries, stacked, stacked)
+    )(jnp.reshape(block_index, (1,)).astype(jnp.int32), queries, kv_piece, kv_piece), early
 
 
 def pack_attention(
@@ -168,14 +164,14 @@
 ):
     block_count = lax.axis_size("blk")
     block_index = lax.axis_index("blk")
-    long_attn = prompt_attention(long_q, block_index, long_k, long_v)
     short_attn = pack_attention(
         short_q, short_k, short_v, short_seg, pool_kv, page_table, block_index, block_count
     )
+    short_rows = lax.all_to_all(short_attn, "req", 0, 1, tiled=True)
+    short_out = jnp.dot(short_rows, w_out, preferred_element_type=jnp.float32).astype(jnp.bfloat16)
+    long_attn, short_out = prompt_attention(long_q, block_index, long_k, long_v, short_out)
     long_rows = lax.all_to_all(long_attn, "req", 0, 1, tiled=True)
-    short_rows = lax.all_to_all(short_attn, "req", 0, 1, tiled=True)
     long_out = jnp.dot(long_rows, w_out, preferred_element_type=jnp.float32).astype(jnp.bfloat16)
-    short_out = jnp.dot(short_rows, w_out, preferred_element_type=jnp.float32).astype(jnp.bfloat16)
     return (long_out, short_out)
 
 

time: 453 us -> 243 us (0.54)
  waiting for transfers between devices: 246 us -> 70.9 us
  starting transfers between devices: 50.6 us -> 7.55 us
  local copies, waits for them, and re-layouts: 40.3 us -> 8.69 us
  blocking collectives: 0 us -> 26.2 us
  between operations: 0.92 us -> 14.3 us
    ppermute x15 -> x0, waiting for transfers between devices: 161 us -> none  [prompt_attention(): pieces.append(lax.ppermute(own, 'blk', pairs))]
    all_to_all x1, waiting for transfers between devices: 83.6 us -> 14.2 us  [pack_attention(): lax.all_to_all(outgoing, 'blk', split_axis=0, concat_axis=0, tiled=True)]
    all_gather x0 -> x1, waiting for transfers between devices: none -> 56.7 us  [prompt_attention(): lax.all_gather(jnp.concatenate([long_k, long_v], 1), 'blk', axis=0, tiled...]
    unnamed x21 -> x19, local copies, waits for them, and re-layouts: 28.3 us -> 0.41 us
    all_to_all x0 -> x2, blocking collectives: none -> 26.2 us  [the longest x1 13.4 us: per_device(): long_rows = lax.all_to_all(long_attn, 'req', 0, 1, tiled=True)]
    ppermute x15 -> x0, starting transfers between devices: 19.4 us -> none  [prompt_attention(): pieces.append(lax.ppermute(own, 'blk', pairs))]
    all_to_all x2 -> x0, starting transfers between devices: 12.7 us -> none  [the longest x1 6.65 us: per_device(): short_rows = lax.all_to_all(short_attn, 'req', 0, 1, tiled=True)]
    all_to_all x1, starting transfers between devices: 18.5 us -> 7.51 us  [pack_attention(): lax.all_to_all(outgoing, 'blk', split_axis=0, concat_axis=0, tiled=True)]
  transfers between devices with their start and end apart: 18 -> 2, of which waited for: 10 -> 2; matrix products, arithmetic and copies ran while one was open for 12% -> 11% of each run, Pallas kernels for 20% -> 0%
where the time goes in v5:
time: 243 us; the launch traced here: 242 us
  Pallas kernels  88.5 us (36%)
  waiting for transfers between devices  70.9 us (29%)
  blocking collectives  26.2 us (11%)
  matrix products  21.1 us (9%)
  between operations  14.3 us (6%)
  local copies, waits for them, and re-layouts  8.69 us (4%)
  starting transfers between devices  7.55 us (3%)
  other arithmetic  4.86 us (2%)
    pallas_call x1, Pallas kernels, prompt_attention(): pl.pallas_call(body, out_shape=jax.ShapeDtypeStruct((row_count, width), j...  88.5 us
    all_gather x1, waiting for transfers between devices, prompt_attention(): lax.all_gather(jnp.concatenate([long_k, long_v], 1), 'blk', axis=0, tiled...  56.7 us
    all_to_all x1, waiting for transfers between devices, pack_attention(): lax.all_to_all(outgoing, 'blk', split_axis=0, concat_axis=0, tiled=True)  14.2 us
    all_to_all x1, blocking collectives, per_device(): long_rows = lax.all_to_all(long_attn, 'req', 0, 1, tiled=True)  13.4 us
    all_to_all x1, blocking collectives, per_device(): short_rows = lax.all_to_all(short_attn, 'req', 0, 1, tiled=True)  12.8 us
    all_to_all x1, starting transfers between devices, pack_attention(): lax.all_to_all(outgoing, 'blk', split_axis=0, concat_axis=0, tiled=True)  7.51 us
    dot_general x1, matrix products, per_device(): jnp.dot(short_rows, w_out, preferred_element_type=jnp.float32)  6.22 us
    sub x1, matrix products, pack_attention(): weights = jnp.where(allowed, jnp.exp(scores - row_max[..., None]), 0.0)  6.1 us
  transfers between devices with their start and end apart: 2, of which 2 were waited for; matrix products, arithmetic and copies ran while one was open for 11% of the time, Pallas kernels for 0%

profile of v5, /device:TPU:23, one launch (start us, length us, event | category | flops | bytes accessed | tf_op | source)
XLA Modules:
  0.0 242.0 jit_solution(8457143018748562710)
XLA Ops:
  7.2 0.0 copy-start
  7.2 0.0 copy-start.5
  7.2 0.0 all-gather.2.cloned.1.call-start
  7.2 2.3 pad_maximum_fusion
  9.6 0.0 copy-start.2
  9.6 0.0 copy-start.3
  9.6 0.0 all-gather.2.cloned.1.call-update
  9.6 0.0 copy-done.5
  9.6 0.1 copy.47
  9.7 0.1 copy.48
  9.8 0.2 reduce_window_sum.11
  10.0 0.1 select_reduce_fusion
  10.2 0.1 copy.52
  10.2 0.1 reshape.238
  10.4 0.0 copy-done
  10.4 0.0 copy-start.7
  10.4 0.0 copy-start.6
  10.4 1.6 gather_fusion
  12.0 7.5 %all-to-all-start = ((bf16[16,4,2,16,256]{4,3,2,1,0:T(8,128)(2,1)}), bf16[16,4,2,16,256]{4,3,2,1,0:T(8,128)(2,1)S(1)}, u32[]{:S(2)}, u32[]{:S(2)}) async-start(bf16[16,4,2,16,256]{4,3,2,1,0:T(8,128)(2,1)} %bitcast.4), calls=%async_computation | async-start | bytes 2097152 | tf_op jit(solution)/shard_map/all_to_all | solution.py:126
  19.5 0.0 copy-done.2
  19.5 0.1 copy.53
  19.7 0.8 copy.55
  20.5 0.0 copy-done.3
  20.5 0.1 copy.57
  20.7 0.8 copy.59
  21.5 0.2 convert_reduce_fusion
  21.7 0.0 copy-done.7
  21.7 0.0 copy-done.6
  21.8 1.9 fusion.6
  23.7 14.2 %all-to-all-done = bf16[16,4,2,16,256]{4,3,2,1,0:T(8,128)(2,1)S(1)} async-done(((bf16[16,4,2,16,256]{4,3,2,1,0:T(8,128)(2,1)}), bf16[16,4,2,16,256]{4,3,2,1,0:T(8,128)(2,1)S(1)}, u32[]{:S(2)}, u32[]{:S(2)}) %all-to-all-start) | async-done | bytes 1048608 | tf_op jit(solution)/shard_map/all_to_all | solution.py:126
  37.9 0.6 gather_fusion.1
  38.5 0.9 fusion.46
  39.4 0.0 copy-start.1
  39.4 1.2 concatenate.25
  40.6 0.1 copy.54
  40.7 0.1 concatenate.28
  40.8 0.1 copy.58
  40.9 0.0 copy-done.1
  40.9 0.0 copy-start.4
  40.9 6.1 %fusion.47 = (f32[2,512]{1,0:T(2,128)S(1)}, bf16[2,512,1536]{1,2,0:T(8,128)(2,1)}) fusion(pred[512,1536]{0,1:T(8,128)(4,1)S(1)} %copy-done.1, bf16[512,2,128]{2,0,1:T(8,128)(2,1)} %copy.55, bf16[1024,2,128]{2,0,1:T(8,128)(2,1)S(1)} %copy.54, bf16[512,256]{1,0:T(8,128)(2,1)} %param.13), kind=kOutput, calls=%fused_computation.69 | convolution fusion | flops 413664768 | bytes 4984832 | tf_op jit(solution)/shard_map/sub | solution.py:150
  47.0 0.0 copy-done.4
  47.0 3.3 %fusion.14 = bf16[512,2,128]{2,0,1:T(8,128)(2,1)S(1)} fusion(bf16[2,512,1536]{1,2,0:T(8,128)(2,1)} %get-tuple-element.12, bf16[512,2,128]{2,0,1:T(8,128)(2,1)S(1)} %copy-done.4, bf16[1024,2,128]{2,0,1:T(8,128)(2,1)S(1)} %copy.58, f32[512,2]{0,1:T(2,128)S(1)} %bitcast.72), kind=kOutput, calls=%fused_computation.17 | convolution fusion | flops 404488192 | bytes 4198400 | tf_op jit(solution)/shard_map/hqk,khd->hqd/dot_general | solution.py:152
  50.3 0.3 copy.61
  50.6 0.2 convert_element_type.30
  50.8 12.8 %all_to_all.40 = bf16[8,64,256]{2,1,0:T(8,128)(2,1)S(1)} all-to-all(bf16[8,64,256]{2,1,0:T(8,128)(2,1)S(1)} %convert_element_type.30), channel_id=1, replica_groups=mesh['blk'=16,'req'=8] {'req'}, dimensions={0} | all-to-all | bytes 524288 | tf_op jit(solution)/shard_map/all_to_all | solution.py:170
  63.6 6.2 %convolution_convert_fusion.1 = bf16[64,2048]{1,0:T(8,128)(2,1)} fusion(bf16[64,2048]{1,0:T(8,128)(2,1)S(1)} %bitcast.64, bf16[2048,2048]{1,0:T(8,128)(2,1)} %param.19), kind=kOutput, calls=%fused_computation.14 | convolution fusion | flops 537001984 | bytes 8912896 | tf_op jit(solution)/shard_map/dot_general | solution.py:171
  69.8 56.7 %all-gather.2.cloned.1.call-done.k_ref.v_ref = bf16[16384,512]{1,0:T(8,128)(2,1)} async-done(((bf16[1024,512]{1,0:T(8,128)(2,1)}), bf16[16384,512]{1,0:T(8,128)(2,1)}) %all-gather.2.cloned.1.call-update) | async-done | bytes 16777232 | tf_op jit(solution)/shard_map/all_gather | solution.py:70
  126.5 88.5 %shard_map.113 = bf16[1024,256]{1,0:T(8,128)(2,1)} custom-call(s32[1]{0:T(128)} %bitcast.blk_ref, bf16[1024,256]{1,0:T(8,128)(2,1)} %q_ref.1, bf16[16384,512]{1,0:T(8,128)(2,1)} %all-gather.2.cloned.1.call-done.k_ref.v_ref, bf16[16384,512]{1,0:T(8,128)(2,1)} %all-gather.2.cloned.1.call-done.k_ref.v_ref), custom_call_target="tpu_custom_call" | custom-call | tf_op jit(solution)/shard_map/pallas_call | solution.py:85
  215.0 1.3 copy.63
  216.3 13.4 %all_to_all.41 = bf16[8,128,256]{1,2,0:T(8,128)(2,1)S(1)} all-to-all(bf16[8,128,256]{1,2,0:T(8,128)(2,1)S(1)} %copy.63), channel_id=1, replica_groups=mesh['blk'=16,'req'=8] {'req'}, dimensions={0} | all-to-all | bytes 1048576 | tf_op jit(solution)/shard_map/all_to_all | solution.py:173
  229.7 5.5 %convolution_convert_fusion = bf16[128,2048]{1,0:T(8,128)(2,1)} fusion(bf16[128,2048]{0,1:T(8,128)(2,1)S(1)} %bitcast.62, bf16[2048,2048]{1,0:T(8,128)(2,1)} %param.19), kind=kOutput, calls=%fused_computation.13 | convolution fusion | flops 1074003968 | bytes 9437184 | tf_op jit(solution)/shard_map/dot_general | solution.py:174
  (10 shorter events, 0.1 us)
Async XLA Ops:
  7.2 3.2 %copy-start = (bf16[64,2,16,256]{3,2,1,0:T(8,128)(2,1)S(1)}, bf16[64,2,16,256]{3,2,1,0:T(8,128)(2,1)}, u32[]{:S(2)}) copy-start(bf16[64,2,16,256]{3,2,1,0:T(8,128)(2,1)} %param.17) | copy-start | bytes 3145732
  7.2 2.4 copy-start.5
  7.2 119.3 %all-gather.2.cloned.1.call-start = ((), (), s32[]{:S(2)}) async-start(), calls=%async_computation.3 | async-start | bytes 17825792 | tf_op jit(solution)/shard_map/all_gather | solution.py:70
  9.6 10.0 %copy-start.2 = (bf16[512,256]{1,0:T(8,128)(2,1)S(1)}, bf16[512,256]{1,0:T(8,128)(2,1)}, u32[]{:S(2)}) copy-start(bf16[512,256]{1,0:T(8,128)(2,1)} %param.14) | copy-start | bytes 786436
  9.6 10.9 %copy-start.3 = (bf16[512,256]{1,0:T(8,128)(2,1)S(1)}, bf16[512,256]{1,0:T(8,128)(2,1)}, u32[]{:S(2)}) copy-start(bf16[512,256]{1,0:T(8,128)(2,1)} %param.15) | copy-start | bytes 786436
  10.4 11.3 %copy-start.7 = (s32[1,512]{1,0:T(1,128)S(1)}, s32[1,512]{1,0:T(1,128)}, u32[]{:S(2)}) copy-start(s32[1,512]{1,0:T(1,128)} %param.16) | copy-start | bytes 6148
  10.4 11.3 %copy-start.6 = (s32[1536]{0:T(1024)S(1)}, s32[1536]{0:T(1024)}, u32[]{:S(2)}) copy-start(s32[1536]{0:T(1024)} %constant.63.clone.1) | copy-start | bytes 18436
  12.0 25.9 %all-to-all-start = ((bf16[16,4,2,16,256]{4,3,2,1,0:T(8,128)(2,1)}), bf16[16,4,2,16,256]{4,3,2,1,0:T(8,128)(2,1)S(1)}, u32[]{:S(2)}, u32[]{:S(2)}) async-start(bf16[16,4,2,16,256]{4,3,2,1,0:T(8,128)(2,1)} %bitcast.4), calls=%async_computation | async-start | bytes 2097152 | tf_op jit(solution)/shard_map/all_to_all | solution.py:126
  39.4 1.5 copy-start.1
  40.9 6.1 %copy-start.4 = (bf16[512,2,128]{2,0,1:T(8,128)(2,1)S(1)}, bf16[512,2,128]{2,0,1:T(8,128)(2,1)}, u32[]{:S(2)}) copy-start(bf16[512,2,128]{2,0,1:T(8,128)(2,1)} %copy.59) | copy-start | bytes 786436
Sparse Core Ops, SparseCore 0:
  10.4 116.0 all-gather.1

commit v6 on v5

--- a/solution.py
+++ b/solution.py
@@ -18,7 +18,7 @@
 def flash_body(blk_ref, q_ref, k_ref, v_ref, o_ref, m_sc, l_sc, acc_sc, *, heads, tq, tk, q_rows):
     q_tile = pl.program_id(0)
     k_tile = pl.program_id(1)
-    first_query = blk_ref[0] * q_rows + q_tile * tq
+    first_query = blk_ref[q_tile] * q_rows + q_tile * tq
     last_tile = (first_query + tq - 1) // tk
 
     @pl.when(k_tile == 0)
@@ -71,18 +71,22 @@
     if early is not None:
         kv_piece, early = lax.optimization_barrier((kv_piece, early))
     piece_rows = kv_piece.shape[0]
-    tq = min(row_count, 512)
+    block_count = lax.axis_size("blk")
+    tq = row_count // 2
+    mirror = [(src, block_count - 1 - src) for src in range(block_count)]
+    partner_half = lax.ppermute(queries[tq:], "blk", mirror)
+    tile_blocks = jnp.stack([block_index, block_count - 1 - block_index]).astype(jnp.int32)
     tk = min(row_count, 1024)
 
     def kv_map(column):
         def index(q_tile, k_tile, blk_ref):
-            last_tile = (blk_ref[0] * row_count + q_tile * tq + tq - 1) // tk
+            last_tile = (blk_ref[q_tile] * row_count + q_tile * tq + tq - 1) // tk
             return (jnp.minimum(k_tile, last_tile), column)
 
         return index
 
     body = functools.partial(flash_body, heads=heads_dev, tq=tq, tk=tk, q_rows=row_count)
-    return pl.pallas_call(
+    result = pl.pallas_call(
         body,
         out_shape=jax.ShapeDtypeStruct((row_count, width), jnp.bfloat16),
         grid_spec=pltpu.PrefetchScalarGridSpec(
@@ -101,7 +105,9 @@
             ],
         ),
         compiler_params=pltpu.CompilerParams(dimension_semantics=("arbitrary", "arbitrary")),
-    )(jnp.reshape(block_index, (1,)).astype(jnp.int32), queries, kv_piece, kv_piece), early
+    )(tile_blocks, jnp.concatenate([queries[:tq], partner_half], 0), kv_piece, kv_piece)
+    merged = jnp.concatenate([result[:tq], lax.ppermute(result[tq:], "blk", mirror)], 0)
+    return merged, early
 
 
 def pack_attention(

time: 243 us -> 230 us (0.947)
  the two profiles are of different devices: /device:TPU:23 before, /device:TPU:0 now
where the time goes in v6:
time: 230 us; the launch traced here: 229 us
  waiting for transfers between devices  89.2 us (39%)
  Pallas kernels  52.4 us (23%)
  matrix products  22.3 us (10%)
  starting transfers between devices  17.6 us (8%)
  blocking collectives  14.8 us (6%)
  between operations  14.3 us (6%)
  local copies, waits for them, and re-layouts  11 us (5%)
  other arithmetic  7.33 us (3%)
    all_gather x1, waiting for transfers between devices, prompt_attention(): lax.all_gather(jnp.concatenate([long_k, long_v], 1), 'blk', axis=0, tiled...  61 us
    pallas_call x1, Pallas kernels, prompt_attention(): pl.pallas_call(body, out_shape=jax.ShapeDtypeStruct((row_count, width), j...  52.4 us
    all_to_all x1, blocking collectives, per_device(): long_rows = lax.all_to_all(long_attn, 'req', 0, 1, tiled=True)  14.8 us
    all_to_all x1, waiting for transfers between devices, pack_attention(): lax.all_to_all(outgoing, 'blk', split_axis=0, concat_axis=0, tiled=True)  11.9 us
    ppermute x1, waiting for transfers between devices, prompt_attention(): lax.ppermute(result[tq:], 'blk', mirror)  11.4 us
    dot_general x1, matrix products, per_device(): jnp.dot(short_rows, w_out, preferred_element_type=jnp.float32)  7.31 us
    all_to_all x1, starting transfers between devices, pack_attention(): lax.all_to_all(outgoing, 'blk', split_axis=0, concat_axis=0, tiled=True)  7.25 us
    sub x1, matrix products, pack_attention(): weights = jnp.where(allowed, jnp.exp(scores - row_max[..., None]), 0.0)  6.25 us
  transfers between devices with their start and end apart: 5, of which 4 were waited for; matrix products, arithmetic and copies ran while one was open for 14% of the time, Pallas kernels for 0%

profile of v6, /device:TPU:0, one launch (start us, length us, event | category | flops | bytes accessed | tf_op | source)
XLA Modules:
  0.0 228.9 jit_solution(2773690474511928262)
XLA Ops:
  7.2 0.0 copy-start
  7.2 0.0 copy-start.6
  7.2 0.0 all-gather.2.cloned.1.call-start
  7.2 2.3 %pad_maximum_fusion = bf16[1024,512]{1,0:T(8,128)(2,1)} fusion(bf16[1024,256]{1,0:T(8,128)(2,1)} %param.12, bf16[1024,256]{1,0:T(8,128)(2,1)} %param.11), kind=kLoop, calls=%fused_computation.18 | loop fusion | flops 2097152 | bytes 2097152 | tf_op jit(solution)/shard_map/concatenate | solution.py:70
  9.6 0.0 copy-start.2
  9.6 0.0 copy-start.3
  9.6 0.0 all-gather.2.cloned.1.call-update
  9.6 0.0 copy-done.6
  9.6 0.1 copy.47
  9.7 0.1 copy.48
  9.8 0.2 reduce_window_sum.11
  10.0 0.1 select_reduce_fusion
  10.2 0.1 copy.52
  10.3 0.1 reshape.234
  10.4 0.0 copy-done
  10.4 0.0 copy-start.4
  10.4 1.6 gather_fusion
  12.0 0.0 copy-start.8
  12.0 0.0 copy-start.7
  12.0 7.2 %all-to-all-start = ((bf16[16,4,2,16,256]{4,3,2,1,0:T(8,128)(2,1)}), bf16[16,4,2,16,256]{4,3,2,1,0:T(8,128)(2,1)S(1)}, u32[]{:S(2)}, u32[]{:S(2)}) async-start(bf16[16,4,2,16,256]{4,3,2,1,0:T(8,128)(2,1)} %bitcast.5), calls=%async_computation | async-start | bytes 2097152 | tf_op jit(solution)/shard_map/all_to_all | solution.py:132
  19.3 0.0 copy-done.2
  19.3 0.7 fusion.48
  20.0 5.3 %collective-permute-start = (bf16[512,256]{1,0:T(8,128)(2,1)}, bf16[512,256]{1,0:T(8,128)(2,1)}, u32[]{:S(2)}, u32[]{:S(2)}) collective-permute-start(bf16[512,256]{1,0:T(8,128)(2,1)} %get-tuple-element.14), channel_id=1, source_target_pairs={{0,120},{8,112},{16,104},{24,96},{32,88},{40,80},{48,72},{56,64},{... | collective-permute-start | bytes 786440 | tf_op jit(solution)/shard_map/ppermute | solution.py:77
  25.3 0.0 copy-done.3
  25.3 0.1 copy.53
  25.5 0.9 copy.55
  26.3 0.0 copy-done.4
  26.3 0.1 copy.57
  26.5 0.9 copy.59
  27.3 0.2 convert_reduce_fusion
  27.5 0.0 copy-done.8
  27.6 0.0 copy-done.7
  27.6 1.9 fusion.6
  29.5 11.9 %all-to-all-done = bf16[16,4,2,16,256]{4,3,2,1,0:T(8,128)(2,1)S(1)} async-done(((bf16[16,4,2,16,256]{4,3,2,1,0:T(8,128)(2,1)}), bf16[16,4,2,16,256]{4,3,2,1,0:T(8,128)(2,1)S(1)}, u32[]{:S(2)}, u32[]{:S(2)}) %all-to-all-start) | async-done | bytes 1048608 | tf_op jit(solution)/shard_map/all_to_all | solution.py:132
  41.4 0.6 gather_fusion.1
  42.0 0.9 fusion.46
  42.9 0.0 copy-start.1
  42.9 1.2 concatenate.32
  44.1 0.9 copy.54
  45.0 0.1 concatenate.35
  45.1 0.1 copy.58
  45.2 0.0 copy-done.1
  45.2 0.0 copy-start.5
  45.2 6.2 %fusion.49 = (f32[2,512]{1,0:T(2,128)S(1)}, bf16[2,512,1536]{1,2,0:T(8,128)(2,1)}) fusion(pred[512,1536]{0,1:T(8,128)(4,1)S(1)} %copy-done.1, bf16[512,2,128]{2,0,1:T(8,128)(2,1)} %copy.55, bf16[1024,2,128]{2,0,1:T(8,128)(2,1)} %copy.54, bf16[512,256]{1,0:T(8,128)(2,1)} %param.13), kind=kOutput, calls=%fused_computation.74 | convolution fusion | flops 413664768 | bytes 4984832 | tf_op jit(solution)/shard_map/sub | solution.py:156
  51.5 0.0 copy-done.5
  51.5 3.3 %fusion.14 = bf16[512,2,128]{2,0,1:T(8,128)(2,1)S(1)} fusion(bf16[2,512,1536]{1,2,0:T(8,128)(2,1)} %get-tuple-element.16, bf16[512,2,128]{2,0,1:T(8,128)(2,1)S(1)} %copy-done.5, bf16[1024,2,128]{2,0,1:T(8,128)(2,1)S(1)} %copy.58, f32[512,2]{0,1:T(2,128)S(1)} %bitcast.73), kind=kOutput, calls=%fused_computation.17 | convolution fusion | flops 404488192 | bytes 4198400 | tf_op jit(solution)/shard_map/hqk,khd->hqd/dot_general | solution.py:158
  54.8 0.3 copy.61
  55.0 0.9 convert_element_type.30
  55.9 4.9 %all-to-all-start.1 = ((bf16[8,64,256]{2,1,0:T(8,128)(2,1)}), bf16[8,64,256]{2,1,0:T(8,128)(2,1)S(1)}, u32[]{:S(2)}, u32[]{:S(2)}) async-start(bf16[8,64,256]{2,1,0:T(8,128)(2,1)} %convert_element_type.30), calls=%async_computation.1 | async-start | bytes 524288 | tf_op jit(solution)/shard_map/all_to_all | solution.py:176
  60.8 0.6 pad_add_fusion.1.blk_ref
  61.5 0.0 collective-permute-done
  61.5 1.8 pad_maximum_fusion.2.q_ref
  63.2 4.9 %all-to-all-done.1 = bf16[8,64,256]{2,1,0:T(8,128)(2,1)S(1)} async-done(((bf16[8,64,256]{2,1,0:T(8,128)(2,1)}), bf16[8,64,256]{2,1,0:T(8,128)(2,1)S(1)}, u32[]{:S(2)}, u32[]{:S(2)}) %all-to-all-start.1) | async-done | bytes 262176 | tf_op jit(solution)/shard_map/all_to_all | solution.py:176
  68.1 7.3 %convolution_convert_fusion.1 = bf16[64,2048]{1,0:T(8,128)(2,1)} fusion(bf16[64,2048]{1,0:T(8,128)(2,1)S(1)} %bitcast.65, bf16[2048,2048]{1,0:T(8,128)(2,1)} %param.19), kind=kOutput, calls=%fused_computation.14 | convolution fusion | flops 537001984 | bytes 8912896 | tf_op jit(solution)/shard_map/dot_general | solution.py:177
  75.4 61.0 %all-gather.2.cloned.1.call-done.k_ref.v_ref = bf16[16384,512]{1,0:T(8,128)(2,1)} async-done(((bf16[1024,512]{1,0:T(8,128)(2,1)}), bf16[16384,512]{1,0:T(8,128)(2,1)}) %all-gather.2.cloned.1.call-update) | async-done | bytes 16777232 | tf_op jit(solution)/shard_map/all_gather | solution.py:70
  136.5 52.4 %shard_map.113 = bf16[1024,256]{1,0:T(8,128)(2,1)} custom-call(s32[2]{0:T(128)} %pad_add_fusion.1.blk_ref, bf16[1024,256]{1,0:T(8,128)(2,1)} %pad_maximum_fusion.2.q_ref, bf16[16384,512]{1,0:T(8,128)(2,1)} %all-gather.2.cloned.1.call-done.k_ref.v_ref, bf16[16384,512]{1,0:T(8,128)(2,1)} %all-gather.2.cloned.1.call-done.k_ref.v_ref), custom_call_target="tpu_custom_call" | custom-call | tf_op jit(solution)/shard_map/pallas_call | solution.py:89
  188.9 1.1 fusion.47
  190.0 0.1 collective-permute-start.1
  190.1 11.4 %collective-permute-done.1 = bf16[512,256]{1,0:T(8,128)(2,1)S(1)} collective-permute-done((bf16[512,256]{1,0:T(8,128)(2,1)S(1)}, bf16[512,256]{1,0:T(8,128)(2,1)S(1)}, u32[]{:S(2)}, u32[]{:S(2)}) %collective-permute-start.1) | collective-permute-done | bytes 262176 | tf_op jit(solution)/shard_map/ppermute | solution.py:109
  201.5 0.3 copy.63
  201.8 14.8 %all_to_all.40 = bf16[8,128,256]{1,2,0:T(8,128)(2,1)S(1)} all-to-all(bf16[8,128,256]{1,2,0:T(8,128)(2,1)S(1)} %copy.63), channel_id=1, replica_groups=mesh['blk'=16,'req'=8] {'req'}, dimensions={0} | all-to-all | bytes 1048576 | tf_op jit(solution)/shard_map/all_to_all | solution.py:179
  216.6 5.5 %convolution_convert_fusion = bf16[128,2048]{1,0:T(8,128)(2,1)} fusion(bf16[128,2048]{0,1:T(8,128)(2,1)S(1)} %bitcast.63, bf16[2048,2048]{1,0:T(8,128)(2,1)} %param.19), kind=kOutput, calls=%fused_computation.13 | convolution fusion | flops 1074003968 | bytes 9437184 | tf_op jit(solution)/shard_map/dot_general | solution.py:180
  (11 shorter events, 0.1 us)
Async XLA Ops:
  7.2 3.2 %copy-start = (bf16[64,2,16,256]{3,2,1,0:T(8,128)(2,1)S(1)}, bf16[64,2,16,256]{3,2,1,0:T(8,128)(2,1)}, u32[]{:S(2)}) copy-start(bf16[64,2,16,256]{3,2,1,0:T(8,128)(2,1)} %param.17) | copy-start | bytes 3145732
  7.2 2.4 %copy-start.6 = (s32[16,16,4]{1,2,0:T(4,128)S(1)}, s32[16,16,4]{1,2,0:T(4,128)}, u32[]{:S(2)}) copy-start(s32[16,16,4]{1,2,0:T(4,128)} %param.18) | copy-start | bytes 12292
  7.2 129.3 %all-gather.2.cloned.1.call-start = ((), (), s32[]{:S(2)}) async-start(), calls=%async_computation.3 | async-start | bytes 17825792 | tf_op jit(solution)/shard_map/all_gather | solution.py:70
  9.6 9.7 %copy-start.2 = (bf16[1024,256]{1,0:T(8,128)(2,1)S(1)}, bf16[1024,256]{1,0:T(8,128)(2,1)}, u32[]{:S(2)}) copy-start(bf16[1024,256]{1,0:T(8,128)(2,1)} %param.10) | copy-start | bytes 1572868
  9.6 15.7 %copy-start.3 = (bf16[512,256]{1,0:T(8,128)(2,1)S(1)}, bf16[512,256]{1,0:T(8,128)(2,1)}, u32[]{:S(2)}) copy-start(bf16[512,256]{1,0:T(8,128)(2,1)} %param.14) | copy-start | bytes 786436
  10.4 15.9 %copy-start.4 = (bf16[512,256]{1,0:T(8,128)(2,1)S(1)}, bf16[512,256]{1,0:T(8,128)(2,1)}, u32[]{:S(2)}) copy-start(bf16[512,256]{1,0:T(8,128)(2,1)} %param.15) | copy-start | bytes 786436
  12.0 15.5 %copy-start.8 = (s32[1,512]{1,0:T(1,128)S(1)}, s32[1,512]{1,0:T(1,128)}, u32[]{:S(2)}) copy-start(s32[1,512]{1,0:T(1,128)} %param.16) | copy-start | bytes 6148
  12.0 15.6 %copy-start.7 = (s32[1536]{0:T(1024)S(1)}, s32[1536]{0:T(1024)}, u32[]{:S(2)}) copy-start(s32[1536]{0:T(1024)} %constant.65.clone.1) | copy-start | bytes 18436
  12.0 29.4 %all-to-all-start = ((bf16[16,4,2,16,256]{4,3,2,1,0:T(8,128)(2,1)}), bf16[16,4,2,16,256]{4,3,2,1,0:T(8,128)(2,1)S(1)}, u32[]{:S(2)}, u32[]{:S(2)}) async-start(bf16[16,4,2,16,256]{4,3,2,1,0:T(8,128)(2,1)} %bitcast.5), calls=%async_computation | async-start | bytes 2097152 | tf_op jit(solution)/shard_map/all_to_all | solution.py:132
  20.0 41.4 %collective-permute-start = (bf16[512,256]{1,0:T(8,128)(2,1)}, bf16[512,256]{1,0:T(8,128)(2,1)}, u32[]{:S(2)}, u32[]{:S(2)}) collective-permute-start(bf16[512,256]{1,0:T(8,128)(2,1)} %get-tuple-element.14), channel_id=1, source_target_pairs={{0,120},{8,112},{16,104},{24,96},{32,88},{40,80},{48,72},{56,64},{... | collective-permute-start | bytes 786440 | tf_op jit(solution)/shard_map/ppermute | solution.py:77
  42.9 2.3 %copy-start.1 = (pred[512,1536]{0,1:T(8,128)(4,1)S(1)}, pred[512,1536]{0,1:T(8,128)(4,1)}, u32[]{:S(2)}) copy-start(pred[512,1536]{0,1:T(8,128)(4,1)} %fusion.6) | copy-start | bytes 2359300
  45.2 6.3 %copy-start.5 = (bf16[512,2,128]{2,0,1:T(8,128)(2,1)S(1)}, bf16[512,2,128]{2,0,1:T(8,128)(2,1)}, u32[]{:S(2)}) copy-start(bf16[512,2,128]{2,0,1:T(8,128)(2,1)} %copy.59) | copy-start | bytes 786436
  55.9 12.2 %all-to-all-start.1 = ((bf16[8,64,256]{2,1,0:T(8,128)(2,1)}), bf16[8,64,256]{2,1,0:T(8,128)(2,1)S(1)}, u32[]{:S(2)}, u32[]{:S(2)}) async-start(bf16[8,64,256]{2,1,0:T(8,128)(2,1)} %convert_element_type.30), calls=%async_computation.1 | async-start | bytes 524288 | tf_op jit(solution)/shard_map/all_to_all | solution.py:176
  190.0 11.5 %collective-permute-start.1 = (bf16[512,256]{1,0:T(8,128)(2,1)S(1)}, bf16[512,256]{1,0:T(8,128)(2,1)S(1)}, u32[]{:S(2)}, u32[]{:S(2)}) collective-permute-start(bf16[512,256]{1,0:T(8,128)(2,1)S(1)} %get-tuple-element.12), channel_id=1, source_target_pairs={{0,120},{8,112},{16,104},{24,96},{32,88},{40,80},{48,72},{56,64},{... | collective-permute-start | bytes 786440 | tf_op jit(solution)/shard_map/ppermute | solution.py:109
Sparse Core Ops, SparseCore 0:
  10.4 126.0 all-gather.1

commit v7 on v3

--- a/solution.py
+++ b/solution.py
@@ -15,10 +15,10 @@
 very_negative = -1e30
 
 
-def flash_body(pos_ref, q_ref, a_ref, b_ref, o_ref, m_sc, l_sc, acc_sc, *, tq, tk, q_rows):
+def flash_body(pos_ref, q_ref, k_ref, v_ref, o_ref, m_sc, l_sc, acc_sc, *, tq, tk):
     q_tile = pl.program_id(0)
     k_tile = pl.program_id(1)
-    first_query = pos_ref[0] * q_rows + q_tile * tq
+    first_query = pos_ref[q_tile]
     last_tile = (first_query + tq - 1) // tk
 
     @pl.when(k_tile == 0)
@@ -27,7 +27,7 @@
         l_sc[...] = jnp.zeros(l_sc.shape, jnp.float32)
         acc_sc[...] = jnp.zeros(acc_sc.shape, jnp.float32)
 
-    def fold(masked, k_ref, v_ref):
+    def fold(masked):
         scores = lax.dot_general(
             q_ref[...], k_ref[...], (((1,), (1,)), ((), ())),
             preferred_element_type=jnp.float32,
@@ -47,45 +47,41 @@
         )
 
     needs_mask = (k_tile + 1) * tk - 1 > first_query
-    live = k_tile <= last_tile
-    keys_first = pos_ref[1] == 0
-    for masked in (False, True):
-        mask_case = needs_mask if masked else jnp.logical_not(needs_mask)
-
-        @pl.when(live & mask_case & keys_first)
-        def _():
-            fold(masked, a_ref, b_ref)
-
-        @pl.when(live & mask_case & jnp.logical_not(keys_first))
-        def _():
-            fold(masked, b_ref, a_ref)
+
+    @pl.when((k_tile <= last_tile) & jnp.logical_not(needs_mask))
+    def _():
+        fold(False)
+
+    @pl.when((k_tile <= last_tile) & needs_mask)
+    def _():
+        fold(True)
 
     @pl.when(k_tile == last_tile)
     def _():
         o_ref[...] = (acc_sc[...] / l_sc[...]).astype(o_ref.dtype)
 
 
-def flash_head(queries, head, block_index, core, first_piece, second_piece):
+def flash_call(tile_first, queries, kv_piece, tq, tk):
     row_count = queries.shape[0]
-    piece_rows = first_piece.shape[0]
-    tq = min(row_count, 512)
-    tk = min(row_count, 1024)
-
-    def kv_map(q_tile, k_tile, pos_ref):
-        last_tile = (pos_ref[0] * row_count + q_tile * tq + tq - 1) // tk
-        return (jnp.minimum(k_tile, last_tile), 0)
-
-    body = functools.partial(flash_body, tq=tq, tk=tk, q_rows=row_count)
+
+    def kv_map(column):
+        def index(q_tile, k_tile, pos_ref):
+            last_tile = (pos_ref[q_tile] + tq - 1) // tk
+            return (jnp.minimum(k_tile, last_tile), column)
+
+        return index
+
+    body = functools.partial(flash_body, tq=tq, tk=tk)
     return pl.pallas_call(
         body,
         out_shape=jax.ShapeDtypeStruct((row_count, HD), jnp.bfloat16),
         grid_spec=pltpu.PrefetchScalarGridSpec(
             num_scalar_prefetch=1,
-            grid=(row_count // tq, piece_rows // tk),
+            grid=(row_count // tq, kv_piece.shape[0] // tk),
             in_specs=[
-                pl.BlockSpec((tq, HD), lambda q_tile, k_tile, pos_ref: (q_tile, head)),
-                pl.BlockSpec((tk, HD), kv_map),
-                pl.BlockSpec((tk, HD), kv_map),
+                pl.BlockSpec((tq, HD), lambda q_tile, k_tile, pos_ref: (q_tile, 0)),
+                pl.BlockSpec((tk, HD), kv_map(0)),
+                pl.BlockSpec((tk, HD), kv_map(1)),
             ],
             out_specs=pl.BlockSpec((tq, HD), lambda q_tile, k_tile, pos_ref: (q_tile, 0)),
             scratch_shapes=[
@@ -95,28 +91,47 @@
             ],
         ),
         compiler_params=pltpu.CompilerParams(dimension_semantics=("arbitrary", "arbitrary")),
-    )(jnp.stack([block_index, core]).astype(jnp.int32), queries, first_piece, second_piece)
-
-
-def prompt_attention(queries, block_index, core, long_k, long_v):
-    heads_dev = queries.shape[1] // HD
+    )(tile_first, queries, kv_piece, kv_piece)
+
+
+def prompt_attention(long_q, long_k, long_v, chip, core, early):
+    row_count, width = long_q.shape
+    chip_count = lax.axis_size("chip")
     swap = [(0, 1), (1, 0)]
-    outs = []
-    for head in range(heads_dev):
-        cols = slice(head * HD, (head + 1) * HD)
-        key_head = long_k[:, cols]
-        value_head = long_v[:, cols]
-        first_core = core == 0
-        partner = lax.ppermute(jnp.where(first_core, value_head, key_head), "core", swap)
-        pair = jnp.where(
-            first_core,
-            jnp.concatenate([key_head, partner], 0),
-            jnp.concatenate([partner, value_head], 0),
-        )
-        first_piece = lax.all_gather(pair, "chip", axis=0, tiled=True)
-        second_piece = lax.ppermute(first_piece, "core", swap)
-        outs.append(flash_head(queries, head, block_index, core, first_piece, second_piece))
-    return jnp.concatenate(outs, 1)
+    first_core = core == 0
+    packed = jnp.concatenate([long_q, long_k, long_v], 1).reshape(row_count, 3, 2, HD)
+    mine = jnp.where(first_core, packed[:, :, 0], packed[:, :, 1]).reshape(row_count, 3 * HD)
+    given = jnp.where(first_core, packed[:, :, 1], packed[:, :, 0]).reshape(row_count, 3 * HD)
+    partner = lax.ppermute(given, "core", swap)
+    pair = jnp.where(
+        first_core,
+        jnp.concatenate([mine, partner], 0),
+        jnp.concatenate([partner, mine], 0),
+    )
+    kv_piece = lax.all_gather(pair[:, HD:], "chip", axis=0, tiled=True)
+    kv_piece, early = lax.optimization_barrier((kv_piece, early))
+    chip_rows = 2 * row_count
+    tq = chip_rows // 4
+    tk = min(row_count, 1024)
+    mirror = [(src, chip_count - 1 - src) for src in range(chip_count)]
+    queries = pair[:, :HD]
+    lent = lax.ppermute(queries[tq:3 * tq], "chip", mirror)
+    other = chip_count - 1 - chip
+    tile_first = jnp.stack(
+        [chip * chip_rows, chip * chip_rows + 3 * tq, other * chip_rows + tq, other * chip_rows + 2 * tq]
+    ).astype(jnp.int32)
+    result = flash_call(
+        tile_first, jnp.concatenate([queries[:tq], queries[3 * tq:], lent], 0), kv_piece, tq, tk
+    )
+    back = lax.ppermute(result[2 * tq:], "chip", mirror)
+    head_rows = jnp.concatenate([result[:tq], back, result[tq:2 * tq]], 0)
+    kept = jnp.where(first_core, head_rows[:row_count], head_rows[row_count:])
+    sent = jnp.where(first_core, head_rows[row_count:], head_rows[:row_count])
+    got = lax.ppermute(sent, "core", swap)
+    merged = jnp.where(
+        first_core, jnp.concatenate([kept, got], 1), jnp.concatenate([got, kept], 1)
+    )
+    return merged, early
 
 
 def pack_attention(
@@ -178,16 +193,17 @@
     long_q, long_k, long_v, short_q, short_k, short_v, short_seg, pool_kv, page_table, w_out
 ):
     block_count = lax.axis_size("chip") * lax.axis_size("core")
+    chip = lax.axis_index("chip")
     core = lax.axis_index("core")
-    block_index = lax.axis_index("chip") * lax.axis_size("core") + core
-    long_attn = prompt_attention(long_q, block_index, core, long_k, long_v)
+    block_index = chip * lax.axis_size("core") + core
     short_attn = pack_attention(
         short_q, short_k, short_v, short_seg, pool_kv, page_table, block_index, block_count
     )
+    short_rows = lax.all_to_all(short_attn, "req", 0, 1, tiled=True)
+    short_out = jnp.dot(short_rows, w_out, preferred_element_type=jnp.float32).astype(jnp.bfloat16)
+    long_attn, short_out = prompt_attention(long_q, long_k, long_v, chip, core, short_out)
     long_rows = lax.all_to_all(long_attn, "req", 0, 1, tiled=True)
-    short_rows = lax.all_to_all(short_attn, "req", 0, 1, tiled=True)
     long_out = jnp.dot(long_rows, w_out, preferred_element_type=jnp.float32).astype(jnp.bfloat16)
-    short_out = jnp.dot(short_rows, w_out, preferred_element_type=jnp.float32).astype(jnp.bfloat16)
     return (long_out, short_out)
 
 

time: 331 us -> 247 us (0.75)
  the two profiles are of different devices: /device:TPU:23 before, /device:TPU:0 now
where the time goes in v7:
time: 247 us
  waiting for transfers between devices  89.6 us (36%)
  Pallas kernels  62 us (25%)
  matrix products  21.6 us (9%)
  starting transfers between devices  18.9 us (8%)
  local copies, waits for them, and re-layouts  18.3 us (7%)
  blocking collectives  14.6 us (6%)
  between operations  14.4 us (6%)
  other arithmetic  7.2 us (3%)
    pallas_call x1, Pallas kernels, flash_call(): pl.pallas_call(body, out_shape=jax.ShapeDtypeStruct((row_count, HD), jnp....  62 us
    all_gather x1, waiting for transfers between devices, prompt_attention(): kv_piece = lax.all_gather(pair[:, HD:], 'chip', axis=0, tiled=True)  60.4 us
    all_to_all x1, blocking collectives, per_device(): long_rows = lax.all_to_all(long_attn, 'req', 0, 1, tiled=True)  14.6 us
    ppermute x1, waiting for transfers between devices, prompt_attention(): back = lax.ppermute(result[2 * tq:], 'chip', mirror)  10.2 us
    all_to_all x1, waiting for transfers between devices, pack_attention(): lax.all_to_all(outgoing, ('chip', 'core'), split_axis=0, concat_axis=0, t...  9.89 us
    all_to_all x1, starting transfers between devices, pack_attention(): lax.all_to_all(outgoing, ('chip', 'core'), split_axis=0, concat_axis=0, t...  7.17 us
    dot_general x1, matrix products, per_device(): jnp.dot(short_rows, w_out, preferred_element_type=jnp.float32)  6.47 us
    sub x1, matrix products, pack_attention(): weights = jnp.where(allowed, jnp.exp(scores - row_max[..., None]), 0.0)  6.32 us
  transfers between devices with their start and end apart: 7, of which 6 were waited for; matrix products, arithmetic and copies ran while one was open for 13% of the time, Pallas kernels for 0%

profile of v7, /device:TPU:0, one launch (start us, length us, event | category | flops | bytes accessed | tf_op | source)
XLA Modules:
  0.0 246.6 jit_solution(17713787439085374802)
XLA Ops:
  7.2 0.0 copy-start
  7.2 0.0 all-gather.2.cloned.1.call-start
  7.2 1.3 copy.64
  8.6 1.2 copy.65
  9.8 1.2 copy.66
  11.1 0.1 pad_maximum_fusion
  11.2 0.1 broadcast_select_fusion.1
  11.3 1.2 copy.67
  12.5 0.0 collective-permute-start
  12.5 0.4 copy.68
  12.8 0.0 copy-start.6
  12.9 2.3 collective-permute-done
  15.1 1.8 maximum_select_fusion
  16.9 1.1 slice.71
  17.9 0.0 all-gather.2.cloned.1.call-update
  18.0 0.1 copy.70
  18.1 0.1 copy.71
  18.1 0.2 reduce_window_sum.11
  18.4 0.1 select_reduce_fusion
  18.5 0.1 copy.75
  18.6 0.1 reshape.252
  18.7 0.0 copy-start.8
  18.8 0.0 copy-start.7
  18.8 1.6 gather_fusion
  20.4 7.2 %all-to-all-start = ((bf16[16,4,2,16,256]{4,3,2,1,0:T(8,128)(2,1)}), bf16[16,4,2,16,256]{4,3,2,1,0:T(8,128)(2,1)}, u32[]{:S(2)}, u32[]{:S(2)}) async-start(bf16[16,4,2,16,256]{4,3,2,1,0:T(8,128)(2,1)} %bitcast.71), calls=%async_computation | async-start | bytes 2097152 | tf_op jit(solution)/shard_map/all_to_all | solution.py:156
  27.6 0.2 convert_reduce_fusion
  27.8 0.7 pad_add_fusion.1.pos_ref
  28.4 0.1 copy.76
  28.6 0.8 copy.78
  29.4 0.1 copy.80
  29.6 0.9 copy.82
  30.5 1.9 fusion.6
  32.4 0.7 slice.70
  33.1 5.5 %collective-permute-start.1 = (bf16[1024,128]{1,0:T(8,128)(2,1)}, bf16[1024,128]{1,0:T(8,128)(2,1)}, u32[]{:S(2)}, u32[]{:S(2)}) collective-permute-start(bf16[1024,128]{1,0:T(8,128)(2,1)} %slice.70), channel_id=1, source_target_pairs={{0,112},{16,96},{32,80},{48,64},{64,48},{80,32},{96,16},{112,0},{1... | collective-permute-start | bytes 786440 | tf_op jit(solution)/shard_map/ppermute | solution.py:118
  38.6 0.7 fusion.46
  39.3 9.9 %all-to-all-done = bf16[16,4,2,16,256]{4,3,2,1,0:T(8,128)(2,1)} async-done(((bf16[16,4,2,16,256]{4,3,2,1,0:T(8,128)(2,1)}), bf16[16,4,2,16,256]{4,3,2,1,0:T(8,128)(2,1)}, u32[]{:S(2)}, u32[]{:S(2)}) %all-to-all-start) | async-done | bytes 1048608 | tf_op jit(solution)/shard_map/all_to_all | solution.py:156
  49.1 1.8 gather_fusion.1
  51.0 0.1 fusion.47
  51.1 0.1 concatenate.56
  51.2 0.9 copy.77
  52.1 0.1 concatenate.59
  52.2 0.1 copy.81
  52.3 6.3 %fusion.49 = (f32[2,512]{1,0:T(2,128)S(1)}, bf16[2,512,1536]{1,2,0:T(8,128)(2,1)}) fusion(pred[512,1536]{0,1:T(8,128)(4,1)S(1)} %copy-done.1, bf16[512,2,128]{2,0,1:T(8,128)(2,1)} %copy.78, bf16[1024,2,128]{2,0,1:T(8,128)(2,1)} %copy.77, bf16[512,256]{1,0:T(8,128)(2,1)} %param.13), kind=kOutput, calls=%fused_computation.81 | convolution fusion | flops 413664768 | bytes 4984832 | tf_op jit(solution)/shard_map/sub | solution.py:180
  58.6 3.3 %fusion.14 = bf16[512,2,128]{2,0,1:T(8,128)(2,1)S(1)} fusion(bf16[2,512,1536]{1,2,0:T(8,128)(2,1)} %get-tuple-element.20, bf16[512,2,128]{2,0,1:T(8,128)(2,1)S(1)} %copy-done.5, bf16[1024,2,128]{2,0,1:T(8,128)(2,1)S(1)} %copy.81, f32[512,2]{0,1:T(2,128)S(1)} %bitcast.83), kind=kOutput, calls=%fused_computation.19 | convolution fusion | flops 404488192 | bytes 4198400 | tf_op jit(solution)/shard_map/hqk,khd->hqd/dot_general | solution.py:182
  62.0 0.3 copy.84
  62.2 0.9 convert_element_type.30
  63.1 6.0 %all-to-all-start.1 = ((bf16[8,64,256]{2,1,0:T(8,128)(2,1)}), bf16[8,64,256]{2,1,0:T(8,128)(2,1)S(1)}, u32[]{:S(2)}, u32[]{:S(2)}) async-start(bf16[8,64,256]{2,1,0:T(8,128)(2,1)} %convert_element_type.30), calls=%async_computation.1 | async-start | bytes 524288 | tf_op jit(solution)/shard_map/all_to_all | solution.py:202
  69.2 1.8 pad_maximum_fusion.2.q_ref
  71.0 5.5 %all-to-all-done.1 = bf16[8,64,256]{2,1,0:T(8,128)(2,1)S(1)} async-done(((bf16[8,64,256]{2,1,0:T(8,128)(2,1)}), bf16[8,64,256]{2,1,0:T(8,128)(2,1)S(1)}, u32[]{:S(2)}, u32[]{:S(2)}) %all-to-all-start.1) | async-done | bytes 262176 | tf_op jit(solution)/shard_map/all_to_all | solution.py:202
  76.5 6.5 %convolution_convert_fusion.1 = bf16[64,2048]{1,0:T(8,128)(2,1)} fusion(bf16[64,2048]{1,0:T(8,128)(2,1)S(1)} %bitcast.74, bf16[2048,2048]{1,0:T(8,128)(2,1)} %param.19), kind=kOutput, calls=%fused_computation.14 | convolution fusion | flops 537001984 | bytes 8912896 | tf_op jit(solution)/shard_map/dot_general | solution.py:203
  82.9 60.4 %all-gather.2.cloned.1.call-done.k_ref.v_ref = bf16[16384,256]{1,0:T(8,128)(2,1)} async-done(((bf16[2048,256]{1,0:T(8,128)(2,1)}), bf16[16384,256]{1,0:T(8,128)(2,1)}) %all-gather.2.cloned.1.call-update) | async-done | bytes 8388624 | tf_op jit(solution)/shard_map/all_gather | solution.py:111
  143.4 62.0 %shard_map.113 = bf16[2048,128]{1,0:T(8,128)(2,1)} custom-call(s32[4]{0:T(128)} %pad_add_fusion.1.pos_ref, bf16[2048,128]{1,0:T(8,128)(2,1)} %pad_maximum_fusion.2.q_ref, bf16[16384,256]{1,0:T(8,128)(2,1)} %all-gather.2.cloned.1.call-done.k_ref.v_ref, bf16[16384,256]{1,0:T(8,128)(2,1)} %all-gather.2.cloned.1.call-done.k_ref.v_ref), custom_call_target="tpu_custom_call" | custom-call | tf_op jit(solution)/shard_map/pallas_call | solution.py:75
  205.4 1.0 slice.75
  206.4 0.1 collective-permute-start.2
  206.5 1.0 fusion.48
  207.4 10.2 %collective-permute-done.2 = bf16[1024,128]{1,0:T(8,128)(2,1)S(1)} collective-permute-done((bf16[1024,128]{1,0:T(8,128)(2,1)S(1)}, bf16[1024,128]{1,0:T(8,128)(2,1)S(1)}, u32[]{:S(2)}, u32[]{:S(2)}) %collective-permute-start.2) | collective-permute-done | bytes 262176 | tf_op jit(solution)/shard_map/ppermute | solution.py:126
  217.7 0.1 broadcast_select_fusion.3
  217.8 0.1 collective-permute-start.3
  217.9 0.2 copy.86
  218.1 1.3 collective-permute-done.3
  219.4 0.2 copy.87
  219.6 0.1 maximum_select_fusion.1
  219.7 14.6 %all_to_all.37 = bf16[8,128,256]{1,2,0:T(8,128)(2,1)S(1)} all-to-all(bf16[8,128,256]{1,2,0:T(8,128)(2,1)S(1)} %maximum_select_fusion.1), channel_id=1, replica_groups=mesh['chip'=8,'core'=2,'req'=8] {'req'}, dimensions={0} | all-to-all | bytes 1048576 | tf_op jit(solution)/shard_map/all_to_all | solution.py:205
  234.3 5.5 %convolution_convert_fusion = bf16[128,2048]{1,0:T(8,128)(2,1)} fusion(bf16[128,2048]{0,1:T(8,128)(2,1)S(1)} %bitcast.70, bf16[2048,2048]{1,0:T(8,128)(2,1)} %param.19), kind=kOutput, calls=%fused_computation.13 | convolution fusion | flops 1074003968 | bytes 9437184 | tf_op jit(solution)/shard_map/dot_general | solution.py:206
  (26 shorter events, 0.1 us)
Async XLA Ops:
  7.2 11.6 %copy-start = (bf16[64,2,16,256]{3,2,1,0:T(8,128)(2,1)S(1)}, bf16[64,2,16,256]{3,2,1,0:T(8,128)(2,1)}, u32[]{:S(2)}) copy-start(bf16[64,2,16,256]{3,2,1,0:T(8,128)(2,1)} %param.17) | copy-start | bytes 3145732
  7.2 136.2 %all-gather.2.cloned.1.call-start = ((), (), s32[]{:S(2)}) async-start(), calls=%async_computation.3 | async-start | bytes 9437184 | tf_op jit(solution)/shard_map/all_gather | solution.py:111
  12.5 2.6 %collective-permute-start = (bf16[1024,384]{1,0:T(8,128)(2,1)}, bf16[1024,384]{1,0:T(8,128)(2,1)}, u32[]{:S(2)}, u32[]{:S(2)}) collective-permute-start(bf16[1024,384]{1,0:T(8,128)(2,1)} %copy.67), channel_id=1, source_target_pairs={{0,8},{8,0},{1,9},{9,1},{2,10},{10,2},{3,11},{11,3},{4,12},{12,4},... | collective-permute-start | bytes 2359304 | tf_op jit(solution)/shard_map/ppermute | solution.py:105
  12.8 5.1 %copy-start.6 = (s32[16,16,4]{1,2,0:T(4,128)S(1)}, s32[16,16,4]{1,2,0:T(4,128)}, u32[]{:S(2)}) copy-start(s32[16,16,4]{1,2,0:T(4,128)} %param.18) | copy-start | bytes 12292
  17.9 10.5 %copy-start.3 = (bf16[512,256]{1,0:T(8,128)(2,1)S(1)}, bf16[512,256]{1,0:T(8,128)(2,1)}, u32[]{:S(2)}) copy-start(bf16[512,256]{1,0:T(8,128)(2,1)} %param.14) | copy-start | bytes 786436
  17.9 11.5 %copy-start.4 = (bf16[512,256]{1,0:T(8,128)(2,1)S(1)}, bf16[512,256]{1,0:T(8,128)(2,1)}, u32[]{:S(2)}) copy-start(bf16[512,256]{1,0:T(8,128)(2,1)} %param.15) | copy-start | bytes 786436
  18.7 11.7 %copy-start.8 = (s32[1,512]{1,0:T(1,128)S(1)}, s32[1,512]{1,0:T(1,128)}, u32[]{:S(2)}) copy-start(s32[1,512]{1,0:T(1,128)} %param.16) | copy-start | bytes 6148
  18.8 11.7 %copy-start.7 = (s32[1536]{0:T(1024)S(1)}, s32[1536]{0:T(1024)}, u32[]{:S(2)}) copy-start(s32[1536]{0:T(1024)} %constant.79.clone.1) | copy-start | bytes 18436
  20.4 28.8 %all-to-all-start = ((bf16[16,4,2,16,256]{4,3,2,1,0:T(8,128)(2,1)}), bf16[16,4,2,16,256]{4,3,2,1,0:T(8,128)(2,1)}, u32[]{:S(2)}, u32[]{:S(2)}) async-start(bf16[16,4,2,16,256]{4,3,2,1,0:T(8,128)(2,1)} %bitcast.71), calls=%async_computation | async-start | bytes 2097152 | tf_op jit(solution)/shard_map/all_to_all | solution.py:156
  33.1 36.1 %collective-permute-start.1 = (bf16[1024,128]{1,0:T(8,128)(2,1)}, bf16[1024,128]{1,0:T(8,128)(2,1)}, u32[]{:S(2)}, u32[]{:S(2)}) collective-permute-start(bf16[1024,128]{1,0:T(8,128)(2,1)} %slice.70), channel_id=1, source_target_pairs={{0,112},{16,96},{32,80},{48,64},{64,48},{80,32},{96,16},{112,0},{1... | collective-permute-start | bytes 786440 | tf_op jit(solution)/shard_map/ppermute | solution.py:118
  51.1 1.2 copy-start.1
  52.3 6.3 %copy-start.5 = (bf16[512,2,128]{2,0,1:T(8,128)(2,1)S(1)}, bf16[512,2,128]{2,0,1:T(8,128)(2,1)}, u32[]{:S(2)}) copy-start(bf16[512,2,128]{2,0,1:T(8,128)(2,1)} %copy.82) | copy-start | bytes 786436
  58.6 10.5 %copy-start.2 = (bf16[512,128]{1,0:T(8,128)(2,1)S(1)}, bf16[512,128]{1,0:T(8,128)(2,1)}, u32[]{:S(2)}) copy-start(bf16[512,128]{1,0:T(8,128)(2,1)} %get-tuple-element.10) | copy-start | bytes 393220
  63.1 13.3 %all-to-all-start.1 = ((bf16[8,64,256]{2,1,0:T(8,128)(2,1)}), bf16[8,64,256]{2,1,0:T(8,128)(2,1)S(1)}, u32[]{:S(2)}, u32[]{:S(2)}) async-start(bf16[8,64,256]{2,1,0:T(8,128)(2,1)} %convert_element_type.30), calls=%async_computation.1 | async-start | bytes 524288 | tf_op jit(solution)/shard_map/all_to_all | solution.py:202
  206.4 11.3 %collective-permute-start.2 = (bf16[1024,128]{1,0:T(8,128)(2,1)S(1)}, bf16[1024,128]{1,0:T(8,128)(2,1)S(1)}, u32[]{:S(2)}, u32[]{:S(2)}) collective-permute-start(bf16[1024,128]{1,0:T(8,128)(2,1)S(1)} %slice.75), channel_id=1, source_target_pairs={{0,112},{16,96},{32,80},{48,64},{64,48},{80,32},{96,16},{112,0},{1... | collective-permute-start | bytes 786440 | tf_op jit(solution)/shard_map/ppermute | solution.py:126
  217.8 1.6 collective-permute-start.3
Sparse Core Ops, SparseCore 0:
  18.1 125.2 all-gather.1

commit v8 on v6

--- a/solution.py
+++ b/solution.py
@@ -15,10 +15,14 @@
 very_negative = -1e30
 
 
-def flash_body(blk_ref, q_ref, k_ref, v_ref, o_ref, m_sc, l_sc, acc_sc, *, heads, tq, tk, q_rows):
-    q_tile = pl.program_id(0)
-    k_tile = pl.program_id(1)
-    first_query = blk_ref[q_tile] * q_rows + q_tile * tq
+def tile_of_step(step, pos_ref):
+    q_tile = (step >= pos_ref[2]).astype(jnp.int32)
+    return q_tile, step - q_tile * pos_ref[2]
+
+
+def flash_body(pos_ref, q_ref, k_ref, v_ref, o_ref, m_sc, l_sc, acc_sc, *, heads, tq, tk):
+    q_tile, k_tile = tile_of_step(pl.program_id(0), pos_ref)
+    first_query = pos_ref[q_tile]
     last_tile = (first_query + tq - 1) // tk
 
     @pl.when(k_tile == 0)
@@ -50,11 +54,11 @@
 
     needs_mask = (k_tile + 1) * tk - 1 > first_query
 
-    @pl.when((k_tile <= last_tile) & jnp.logical_not(needs_mask))
+    @pl.when(jnp.logical_not(needs_mask))
     def _():
         fold(False)
 
-    @pl.when((k_tile <= last_tile) & needs_mask)
+    @pl.when(needs_mask)
     def _():
         fold(True)
 
@@ -75,37 +79,43 @@
     tq = row_count // 2
     mirror = [(src, block_count - 1 - src) for src in range(block_count)]
     partner_half = lax.ppermute(queries[tq:], "blk", mirror)
-    tile_blocks = jnp.stack([block_index, block_count - 1 - block_index]).astype(jnp.int32)
     tk = min(row_count, 1024)
+    own_first = block_index * row_count
+    lent_first = (block_count - 1 - block_index) * row_count + tq
+    own_steps = (own_first + tq - 1) // tk + 1
+    tile_pos = jnp.stack([own_first, lent_first, own_steps]).astype(jnp.int32)
+    step_count = ((block_count - 1) * row_count + 2 * tq - 1) // tk + 2
 
     def kv_map(column):
-        def index(q_tile, k_tile, blk_ref):
-            last_tile = (blk_ref[q_tile] * row_count + q_tile * tq + tq - 1) // tk
-            return (jnp.minimum(k_tile, last_tile), column)
+        def index(step, pos_ref):
+            return (tile_of_step(step, pos_ref)[1], column)
 
         return index
 
-    body = functools.partial(flash_body, heads=heads_dev, tq=tq, tk=tk, q_rows=row_count)
+    def q_map(step, pos_ref):
+        return (tile_of_step(step, pos_ref)[0], 0)
+
+    body = functools.partial(flash_body, heads=heads_dev, tq=tq, tk=tk)
     result = pl.pallas_call(
         body,
         out_shape=jax.ShapeDtypeStruct((row_count, width), jnp.bfloat16),
         grid_spec=pltpu.PrefetchScalarGridSpec(
             num_scalar_prefetch=1,
-            grid=(row_count // tq, piece_rows // tk),
+            grid=(step_count,),
             in_specs=[
-                pl.BlockSpec((tq, width), lambda q_tile, k_tile, blk_ref: (q_tile, 0)),
+                pl.BlockSpec((tq, width), q_map),
                 pl.BlockSpec((tk, width), kv_map(0)),
                 pl.BlockSpec((tk, width), kv_map(1)),
             ],
-            out_specs=pl.BlockSpec((tq, width), lambda q_tile, k_tile, blk_ref: (q_tile, 0)),
+            out_specs=pl.BlockSpec((tq, width), q_map),
             scratch_shapes=[
                 pltpu.VMEM((heads_dev, tq, HD), jnp.float32),
                 pltpu.VMEM((heads_dev, tq, HD), jnp.float32),
                 pltpu.VMEM((heads_dev, tq, HD), jnp.float32),
             ],
         ),
-        compiler_params=pltpu.CompilerParams(dimension_semantics=("arbitrary", "arbitrary")),
-    )(tile_blocks, jnp.concatenate([queries[:tq], partner_half], 0), kv_piece, kv_piece)
+        compiler_params=pltpu.CompilerParams(dimension_semantics=("arbitrary",)),
+    )(tile_pos, jnp.concatenate([queries[:tq], partner_half], 0), kv_piece, kv_piece)
     merged = jnp.concatenate([result[:tq], lax.ppermute(result[tq:], "blk", mirror)], 0)
     return merged, early
 

time: 230 us -> 226 us (0.983)
  Pallas kernels: 52.4 us -> 48.6 us
    pallas_call x1, Pallas kernels: 52.4 us -> 48.6 us  [prompt_attention(): pl.pallas_call(body, out_shape=jax.ShapeDtypeStruct((row_count, width), j...]
where the time goes in v8:
time: 226 us; the launch traced here: 225 us
  waiting for transfers between devices  89 us (39%)
  Pallas kernels  48.6 us (22%)
  matrix products  22.3 us (10%)
  starting transfers between devices  18.2 us (8%)
  blocking collectives  14.6 us (6%)
  between operations  14.3 us (6%)
  local copies, waits for them, and re-layouts  11 us (5%)
  other arithmetic  7.33 us (3%)
    all_gather x1, waiting for transfers between devices, prompt_attention(): lax.all_gather(jnp.concatenate([long_k, long_v], 1), 'blk', axis=0, tiled...  61 us
    pallas_call x1, Pallas kernels, prompt_attention(): pl.pallas_call(body, out_shape=jax.ShapeDtypeStruct((row_count, width), j...  48.6 us
    all_to_all x1, blocking collectives, per_device(): long_rows = lax.all_to_all(long_attn, 'req', 0, 1, tiled=True)  14.6 us
    all_to_all x1, waiting for transfers between devices, pack_attention(): lax.all_to_all(outgoing, 'blk', split_axis=0, concat_axis=0, tiled=True)  11.9 us
    ppermute x1, waiting for transfers between devices, prompt_attention(): lax.ppermute(result[tq:], 'blk', mirror)  11.2 us
    dot_general x1, matrix products, per_device(): jnp.dot(short_rows, w_out, preferred_element_type=jnp.float32)  7.31 us
    all_to_all x1, starting transfers between devices, pack_attention(): lax.all_to_all(outgoing, 'blk', split_axis=0, concat_axis=0, tiled=True)  7.25 us
    sub x1, matrix products, pack_attention(): weights = jnp.where(allowed, jnp.exp(scores - row_max[..., None]), 0.0)  6.25 us
  transfers between devices with their start and end apart: 5, of which 4 were waited for; matrix products, arithmetic and copies ran while one was open for 14% of the time, Pallas kernels for 0%

profile of v8, /device:TPU:0, one launch (start us, length us, event | category | flops | bytes accessed | tf_op | source)
XLA Modules:
  0.0 225.3 jit_solution(4421666097717434388)
XLA Ops:
  7.2 0.0 copy-start
  7.2 0.0 copy-start.6
  7.2 0.0 all-gather.2.cloned.1.call-start
  7.2 2.3 %pad_maximum_fusion = bf16[1024,512]{1,0:T(8,128)(2,1)} fusion(bf16[1024,256]{1,0:T(8,128)(2,1)} %param.12, bf16[1024,256]{1,0:T(8,128)(2,1)} %param.11), kind=kLoop, calls=%fused_computation.18 | loop fusion | flops 2097152 | bytes 2097152 | tf_op jit(solution)/shard_map/concatenate | solution.py:74
  9.6 0.0 copy-start.2
  9.6 0.0 copy-start.3
  9.6 0.0 all-gather.2.cloned.1.call-update
  9.6 0.0 copy-done.6
  9.6 0.1 copy.47
  9.7 0.1 copy.48
  9.8 0.2 reduce_window_sum.11
  10.0 0.1 select_reduce_fusion
  10.2 0.1 copy.52
  10.3 0.1 reshape.234
  10.4 0.0 copy-done
  10.4 0.0 copy-start.4
  10.4 1.6 gather_fusion
  12.0 0.0 copy-start.8
  12.0 0.0 copy-start.7
  12.0 7.2 %all-to-all-start = ((bf16[16,4,2,16,256]{4,3,2,1,0:T(8,128)(2,1)}), bf16[16,4,2,16,256]{4,3,2,1,0:T(8,128)(2,1)S(1)}, u32[]{:S(2)}, u32[]{:S(2)}) async-start(bf16[16,4,2,16,256]{4,3,2,1,0:T(8,128)(2,1)} %bitcast.6), calls=%async_computation | async-start | bytes 2097152 | tf_op jit(solution)/shard_map/all_to_all | solution.py:142
  19.3 0.0 copy-done.2
  19.3 0.7 fusion.48
  20.0 5.3 %collective-permute-start = (bf16[512,256]{1,0:T(8,128)(2,1)}, bf16[512,256]{1,0:T(8,128)(2,1)}, u32[]{:S(2)}, u32[]{:S(2)}) collective-permute-start(bf16[512,256]{1,0:T(8,128)(2,1)} %get-tuple-element.14), channel_id=1, source_target_pairs={{0,120},{8,112},{16,104},{24,96},{32,88},{40,80},{48,72},{56,64},{... | collective-permute-start | bytes 786440 | tf_op jit(solution)/shard_map/ppermute | solution.py:81
  25.3 0.0 copy-done.3
  25.3 0.1 copy.53
  25.5 0.9 copy.55
  26.3 0.0 copy-done.4
  26.3 0.1 copy.57
  26.5 0.9 copy.59
  27.3 0.2 convert_reduce_fusion
  27.5 0.0 copy-done.8
  27.6 0.0 copy-done.7
  27.6 1.9 fusion.6
  29.5 11.9 %all-to-all-done = bf16[16,4,2,16,256]{4,3,2,1,0:T(8,128)(2,1)S(1)} async-done(((bf16[16,4,2,16,256]{4,3,2,1,0:T(8,128)(2,1)}), bf16[16,4,2,16,256]{4,3,2,1,0:T(8,128)(2,1)S(1)}, u32[]{:S(2)}, u32[]{:S(2)}) %all-to-all-start) | async-done | bytes 1048608 | tf_op jit(solution)/shard_map/all_to_all | solution.py:142
  41.4 0.6 gather_fusion.1
  42.0 0.9 fusion.46
  42.9 0.0 copy-start.1
  42.9 1.2 concatenate.32
  44.1 0.9 copy.54
  45.0 0.1 concatenate.35
  45.1 0.1 copy.58
  45.2 0.0 copy-done.1
  45.2 0.0 copy-start.5
  45.2 6.2 %fusion.49 = (f32[2,512]{1,0:T(2,128)S(1)}, bf16[2,512,1536]{1,2,0:T(8,128)(2,1)}) fusion(pred[512,1536]{0,1:T(8,128)(4,1)S(1)} %copy-done.1, bf16[512,2,128]{2,0,1:T(8,128)(2,1)} %copy.55, bf16[1024,2,128]{2,0,1:T(8,128)(2,1)} %copy.54, bf16[512,256]{1,0:T(8,128)(2,1)} %param.13), kind=kOutput, calls=%fused_computation.74 | convolution fusion | flops 413664768 | bytes 4984832 | tf_op jit(solution)/shard_map/sub | solution.py:166
  51.5 0.0 copy-done.5
  51.5 3.3 %fusion.14 = bf16[512,2,128]{2,0,1:T(8,128)(2,1)S(1)} fusion(bf16[2,512,1536]{1,2,0:T(8,128)(2,1)} %get-tuple-element.16, bf16[512,2,128]{2,0,1:T(8,128)(2,1)S(1)} %copy-done.5, bf16[1024,2,128]{2,0,1:T(8,128)(2,1)S(1)} %copy.58, f32[512,2]{0,1:T(2,128)S(1)} %bitcast.74), kind=kOutput, calls=%fused_computation.17 | convolution fusion | flops 404488192 | bytes 4198400 | tf_op jit(solution)/shard_map/hqk,khd->hqd/dot_general | solution.py:168
  54.8 0.3 copy.61
  55.0 0.9 convert_element_type.30
  55.9 4.9 %all-to-all-start.1 = ((bf16[8,64,256]{2,1,0:T(8,128)(2,1)}), bf16[8,64,256]{2,1,0:T(8,128)(2,1)S(1)}, u32[]{:S(2)}, u32[]{:S(2)}) async-start(bf16[8,64,256]{2,1,0:T(8,128)(2,1)} %convert_element_type.30), calls=%async_computation.1 | async-start | bytes 524288 | tf_op jit(solution)/shard_map/all_to_all | solution.py:186
  60.8 0.6 pad_add_fusion.1.pos_ref
  61.5 0.0 collective-permute-done
  61.5 1.8 pad_maximum_fusion.2.q_ref
  63.2 4.9 %all-to-all-done.1 = bf16[8,64,256]{2,1,0:T(8,128)(2,1)S(1)} async-done(((bf16[8,64,256]{2,1,0:T(8,128)(2,1)}), bf16[8,64,256]{2,1,0:T(8,128)(2,1)S(1)}, u32[]{:S(2)}, u32[]{:S(2)}) %all-to-all-start.1) | async-done | bytes 262176 | tf_op jit(solution)/shard_map/all_to_all | solution.py:186
  68.1 7.3 %convolution_convert_fusion.1 = bf16[64,2048]{1,0:T(8,128)(2,1)} fusion(bf16[64,2048]{1,0:T(8,128)(2,1)S(1)} %bitcast.66, bf16[2048,2048]{1,0:T(8,128)(2,1)} %param.19), kind=kOutput, calls=%fused_computation.14 | convolution fusion | flops 537001984 | bytes 8912896 | tf_op jit(solution)/shard_map/dot_general | solution.py:187
  75.4 61.0 %all-gather.2.cloned.1.call-done.k_ref.v_ref = bf16[16384,512]{1,0:T(8,128)(2,1)} async-done(((bf16[1024,512]{1,0:T(8,128)(2,1)}), bf16[16384,512]{1,0:T(8,128)(2,1)}) %all-gather.2.cloned.1.call-update) | async-done | bytes 16777232 | tf_op jit(solution)/shard_map/all_gather | solution.py:74
  136.5 48.6 %shard_map.113 = bf16[1024,256]{1,0:T(8,128)(2,1)} custom-call(s32[3]{0:T(128)} %pad_add_fusion.1.pos_ref, bf16[1024,256]{1,0:T(8,128)(2,1)} %pad_maximum_fusion.2.q_ref, bf16[16384,512]{1,0:T(8,128)(2,1)} %all-gather.2.cloned.1.call-done.k_ref.v_ref, bf16[16384,512]{1,0:T(8,128)(2,1)} %all-gather.2.cloned.1.call-done.k_ref.v_ref), custom_call_target="tpu_custom_call" | custom-call | tf_op jit(solution)/shard_map/pallas_call | solution.py:99
  185.1 1.1 fusion.47
  186.2 0.7 collective-permute-start.1
  186.9 11.2 %collective-permute-done.1 = bf16[512,256]{1,0:T(8,128)(2,1)S(1)} collective-permute-done((bf16[512,256]{1,0:T(8,128)(2,1)S(1)}, bf16[512,256]{1,0:T(8,128)(2,1)S(1)}, u32[]{:S(2)}, u32[]{:S(2)}) %collective-permute-start.1) | collective-permute-done | bytes 262176 | tf_op jit(solution)/shard_map/ppermute | solution.py:119
  198.1 0.3 copy.63
  198.4 14.6 %all_to_all.40 = bf16[8,128,256]{1,2,0:T(8,128)(2,1)S(1)} all-to-all(bf16[8,128,256]{1,2,0:T(8,128)(2,1)S(1)} %copy.63), channel_id=1, replica_groups=mesh['blk'=16,'req'=8] {'req'}, dimensions={0} | all-to-all | bytes 1048576 | tf_op jit(solution)/shard_map/all_to_all | solution.py:189
  213.0 5.5 %convolution_convert_fusion = bf16[128,2048]{1,0:T(8,128)(2,1)} fusion(bf16[128,2048]{0,1:T(8,128)(2,1)S(1)} %bitcast.64, bf16[2048,2048]{1,0:T(8,128)(2,1)} %param.19), kind=kOutput, calls=%fused_computation.13 | convolution fusion | flops 1074003968 | bytes 9437184 | tf_op jit(solution)/shard_map/dot_general | solution.py:190
  (11 shorter events, 0.1 us)
Async XLA Ops:
  7.2 3.2 %copy-start = (bf16[64,2,16,256]{3,2,1,0:T(8,128)(2,1)S(1)}, bf16[64,2,16,256]{3,2,1,0:T(8,128)(2,1)}, u32[]{:S(2)}) copy-start(bf16[64,2,16,256]{3,2,1,0:T(8,128)(2,1)} %param.17) | copy-start | bytes 3145732
  7.2 2.4 %copy-start.6 = (s32[16,16,4]{1,2,0:T(4,128)S(1)}, s32[16,16,4]{1,2,0:T(4,128)}, u32[]{:S(2)}) copy-start(s32[16,16,4]{1,2,0:T(4,128)} %param.18) | copy-start | bytes 12292
  7.2 129.3 %all-gather.2.cloned.1.call-start = ((), (), s32[]{:S(2)}) async-start(), calls=%async_computation.3 | async-start | bytes 17825792 | tf_op jit(solution)/shard_map/all_gather | solution.py:74
  9.6 9.7 %copy-start.2 = (bf16[1024,256]{1,0:T(8,128)(2,1)S(1)}, bf16[1024,256]{1,0:T(8,128)(2,1)}, u32[]{:S(2)}) copy-start(bf16[1024,256]{1,0:T(8,128)(2,1)} %param.10) | copy-start | bytes 1572868
  9.6 15.7 %copy-start.3 = (bf16[512,256]{1,0:T(8,128)(2,1)S(1)}, bf16[512,256]{1,0:T(8,128)(2,1)}, u32[]{:S(2)}) copy-start(bf16[512,256]{1,0:T(8,128)(2,1)} %param.14) | copy-start | bytes 786436
  10.4 15.9 %copy-start.4 = (bf16[512,256]{1,0:T(8,128)(2,1)S(1)}, bf16[512,256]{1,0:T(8,128)(2,1)}, u32[]{:S(2)}) copy-start(bf16[512,256]{1,0:T(8,128)(2,1)} %param.15) | copy-start | bytes 786436
  12.0 15.5 %copy-start.8 = (s32[1,512]{1,0:T(1,128)S(1)}, s32[1,512]{1,0:T(1,128)}, u32[]{:S(2)}) copy-start(s32[1,512]{1,0:T(1,128)} %param.16) | copy-start | bytes 6148
  12.0 15.6 %copy-start.7 = (s32[1536]{0:T(1024)S(1)}, s32[1536]{0:T(1024)}, u32[]{:S(2)}) copy-start(s32[1536]{0:T(1024)} %constant.85.clone.1) | copy-start | bytes 18436
  12.0 29.4 %all-to-all-start = ((bf16[16,4,2,16,256]{4,3,2,1,0:T(8,128)(2,1)}), bf16[16,4,2,16,256]{4,3,2,1,0:T(8,128)(2,1)S(1)}, u32[]{:S(2)}, u32[]{:S(2)}) async-start(bf16[16,4,2,16,256]{4,3,2,1,0:T(8,128)(2,1)} %bitcast.6), calls=%async_computation | async-start | bytes 2097152 | tf_op jit(solution)/shard_map/all_to_all | solution.py:142
  20.0 41.4 %collective-permute-start = (bf16[512,256]{1,0:T(8,128)(2,1)}, bf16[512,256]{1,0:T(8,128)(2,1)}, u32[]{:S(2)}, u32[]{:S(2)}) collective-permute-start(bf16[512,256]{1,0:T(8,128)(2,1)} %get-tuple-element.14), channel_id=1, source_target_pairs={{0,120},{8,112},{16,104},{24,96},{32,88},{40,80},{48,72},{56,64},{... | collective-permute-start | bytes 786440 | tf_op jit(solution)/shard_map/ppermute | solution.py:81
  42.9 2.3 %copy-start.1 = (pred[512,1536]{0,1:T(8,128)(4,1)S(1)}, pred[512,1536]{0,1:T(8,128)(4,1)}, u32[]{:S(2)}) copy-start(pred[512,1536]{0,1:T(8,128)(4,1)} %fusion.6) | copy-start | bytes 2359300
  45.2 6.3 %copy-start.5 = (bf16[512,2,128]{2,0,1:T(8,128)(2,1)S(1)}, bf16[512,2,128]{2,0,1:T(8,128)(2,1)}, u32[]{:S(2)}) copy-start(bf16[512,2,128]{2,0,1:T(8,128)(2,1)} %copy.59) | copy-start | bytes 786436
  55.9 12.2 %all-to-all-start.1 = ((bf16[8,64,256]{2,1,0:T(8,128)(2,1)}), bf16[8,64,256]{2,1,0:T(8,128)(2,1)S(1)}, u32[]{:S(2)}, u32[]{:S(2)}) async-start(bf16[8,64,256]{2,1,0:T(8,128)(2,1)} %convert_element_type.30), calls=%async_computation.1 | async-start | bytes 524288 | tf_op jit(solution)/shard_map/all_to_all | solution.py:186
  186.2 11.9 %collective-permute-start.1 = (bf16[512,256]{1,0:T(8,128)(2,1)S(1)}, bf16[512,256]{1,0:T(8,128)(2,1)S(1)}, u32[]{:S(2)}, u32[]{:S(2)}) collective-permute-start(bf16[512,256]{1,0:T(8,128)(2,1)S(1)} %get-tuple-element.12), channel_id=1, source_target_pairs={{0,120},{8,112},{16,104},{24,96},{32,88},{40,80},{48,72},{56,64},{... | collective-permute-start | bytes 786440 | tf_op jit(solution)/shard_map/ppermute | solution.py:119
Sparse Core Ops, SparseCore 0:
  10.4 126.0 all-gather.1

commit v9 on v8

--- a/solution.py
+++ b/solution.py
@@ -71,11 +71,12 @@
 def prompt_attention(queries, block_index, long_k, long_v, early=None):
     row_count, width = queries.shape
     heads_dev = width // HD
-    kv_piece = lax.all_gather(jnp.concatenate([long_k, long_v], 1), "blk", axis=0, tiled=True)
+    block_count = lax.axis_size("blk")
+    spread = jnp.broadcast_to(long_k[None], (block_count,) + long_k.shape)
+    key_piece = lax.all_to_all(spread, "blk", 0, 0, tiled=True).reshape(-1, width)
+    value_piece = lax.all_gather(long_v, "blk", axis=0, tiled=True)
     if early is not None:
-        kv_piece, early = lax.optimization_barrier((kv_piece, early))
-    piece_rows = kv_piece.shape[0]
-    block_count = lax.axis_size("blk")
+        key_piece, value_piece, early = lax.optimization_barrier((key_piece, value_piece, early))
     tq = row_count // 2
     mirror = [(src, block_count - 1 - src) for src in range(block_count)]
     partner_half = lax.ppermute(queries[tq:], "blk", mirror)
@@ -86,11 +87,8 @@
     tile_pos = jnp.stack([own_first, lent_first, own_steps]).astype(jnp.int32)
     step_count = ((block_count - 1) * row_count + 2 * tq - 1) // tk + 2
 
-    def kv_map(column):
-        def index(step, pos_ref):
-            return (tile_of_step(step, pos_ref)[1], column)
-
-        return index
+    def kv_map(step, pos_ref):
+        return (tile_of_step(step, pos_ref)[1], 0)
 
     def q_map(step, pos_ref):
         return (tile_of_step(step, pos_ref)[0], 0)
@@ -104,8 +102,8 @@
             grid=(step_count,),
             in_specs=[
                 pl.BlockSpec((tq, width), q_map),
-                pl.BlockSpec((tk, width), kv_map(0)),
-                pl.BlockSpec((tk, width), kv_map(1)),
+                pl.BlockSpec((tk, width), kv_map),
+                pl.BlockSpec((tk, width), kv_map),
             ],
             out_specs=pl.BlockSpec((tq, width), q_map),
             scratch_shapes=[
@@ -115,7 +113,7 @@
             ],
         ),
         compiler_params=pltpu.CompilerParams(dimension_semantics=("arbitrary",)),
-    )(tile_pos, jnp.concatenate([queries[:tq], partner_half], 0), kv_piece, kv_piece)
+    )(tile_pos, jnp.concatenate([queries[:tq], partner_half], 0), key_piece, value_piece)
     merged = jnp.concatenate([result[:tq], lax.ppermute(result[tq:], "blk", mirror)], 0)
     return merged, early
 

time: 226 us -> 303 us (1.34)
  waiting for transfers between devices: 89 us -> 145 us
  blocking collectives: 14.6 us -> 37.3 us
  local copies, waits for them, and re-layouts: 11 us -> 14.7 us
  other arithmetic: 7.33 us -> 3.99 us
    ppermute x1, waiting for transfers between devices: 0.01 us -> 103 us  [prompt_attention(): partner_half = lax.ppermute(queries[tq:], 'blk', mirror)]
    all_gather x1, waiting for transfers between devices: 61 us -> 0.01 us  [prompt_attention(): value_piece = lax.all_gather(long_v, 'blk', axis=0, tiled=True)]
    all_to_all x0 -> x1, blocking collectives: none -> 15 us  [per_device(): short_rows = lax.all_to_all(short_attn, 'req', 0, 1, tiled=True)]
    all_to_all x1, waiting for transfers between devices: 4.87 us -> 12.6 us  [prompt_attention(): lax.all_to_all(spread, 'blk', 0, 0, tiled=True).reshape(-1, width)]
    all_to_all x1, blocking collectives: 14.6 us -> 22.3 us  [per_device(): long_rows = lax.all_to_all(long_attn, 'req', 0, 1, tiled=True)]
    all_to_all x1, waiting for transfers between devices: 11.9 us -> 16.5 us  [pack_attention(): lax.all_to_all(outgoing, 'blk', split_axis=0, concat_axis=0, tiled=True)]
    broadcast_in_dim x0 -> x1, local copies, waits for them, and re-layouts: none -> 4.04 us  [prompt_attention(): spread = jnp.broadcast_to(long_k[None], (block_count,) + long_k.shape)]
  transfers between devices with their start and end apart: 5 -> 5, of which waited for: 4 -> 4; matrix products, arithmetic and copies ran while one was open for 14% -> 11% of each run, Pallas kernels for 0% -> 0%
where the time goes in v9:
time: 303 us; the launch traced here: 302 us
  waiting for transfers between devices  145 us (48%)
  Pallas kernels  48.5 us (16%)
  blocking collectives  37.3 us (12%)
  matrix products  21.1 us (7%)
  starting transfers between devices  17.6 us (6%)
  local copies, waits for them, and re-layouts  14.7 us (5%)
  between operations  14.3 us (5%)
  other arithmetic  3.99 us (1%)
    ppermute x1, waiting for transfers between devices, prompt_attention(): partner_half = lax.ppermute(queries[tq:], 'blk', mirror)  103 us
    pallas_call x1, Pallas kernels, prompt_attention(): pl.pallas_call(body, out_shape=jax.ShapeDtypeStruct((row_count, width), j...  48.5 us
    all_to_all x1, blocking collectives, per_device(): long_rows = lax.all_to_all(long_attn, 'req', 0, 1, tiled=True)  22.3 us
    all_to_all x1, waiting for transfers between devices, pack_attention(): lax.all_to_all(outgoing, 'blk', split_axis=0, concat_axis=0, tiled=True)  16.5 us
    all_to_all x1, blocking collectives, per_device(): short_rows = lax.all_to_all(short_attn, 'req', 0, 1, tiled=True)  15 us
    all_to_all x1, waiting for transfers between devices, prompt_attention(): lax.all_to_all(spread, 'blk', 0, 0, tiled=True).reshape(-1, width)  12.6 us
    ppermute x1, waiting for transfers between devices, prompt_attention(): lax.ppermute(result[tq:], 'blk', mirror)  12.1 us
    all_to_all x1, starting transfers between devices, pack_attention(): lax.all_to_all(outgoing, 'blk', split_axis=0, concat_axis=0, tiled=True)  7.12 us
  transfers between devices with their start and end apart: 5, of which 4 were waited for; matrix products, arithmetic and copies ran while one was open for 11% of the time, Pallas kernels for 0%

profile of v9, /device:TPU:0, one launch (start us, length us, event | category | flops | bytes accessed | tf_op | source)
XLA Modules:
  0.0 302.4 jit_solution(2501281267916961405)
XLA Ops:
  7.2 0.0 copy-start
  7.2 0.0 copy-start.3
  7.2 0.0 copy-start.4
  7.2 0.0 all-gather.2.cloned.1.call-start
  7.2 0.7 all-gather.2.cloned.1.call-update
  7.9 0.8 copy.47
  8.8 0.1 copy.48
  8.9 0.2 reduce_window_sum.11
  9.1 0.1 select_reduce_fusion
  9.2 0.1 copy.52
  9.3 0.1 reshape.239
  9.5 0.0 copy-done
  9.5 1.7 gather_fusion
  11.1 7.1 %all-to-all-start.1 = ((bf16[16,4,2,16,256]{4,3,2,1,0:T(8,128)(2,1)}), bf16[16,4,2,16,256]{4,3,2,1,0:T(8,128)(2,1)S(1)}, u32[]{:S(2)}, u32[]{:S(2)}) async-start(bf16[16,4,2,16,256]{4,3,2,1,0:T(8,128)(2,1)} %bitcast.7), calls=%async_computation.1 | async-start | bytes 2097152 | tf_op jit(solution)/shard_map/all_to_all | solution.py:140
  18.2 1.1 copy.53
  19.3 0.8 copy.55
  20.2 1.1 copy.57
  21.3 0.2 copy.59
  21.5 0.2 convert_reduce_fusion
  21.7 0.0 copy-done.4
  21.7 0.0 copy-done.3
  21.7 1.9 fusion.6
  23.6 16.5 %all-to-all-done.1 = bf16[16,4,2,16,256]{4,3,2,1,0:T(8,128)(2,1)S(1)} async-done(((bf16[16,4,2,16,256]{4,3,2,1,0:T(8,128)(2,1)}), bf16[16,4,2,16,256]{4,3,2,1,0:T(8,128)(2,1)S(1)}, u32[]{:S(2)}, u32[]{:S(2)}) %all-to-all-start.1) | async-done | bytes 1048608 | tf_op jit(solution)/shard_map/all_to_all | solution.py:140
  40.1 0.6 gather_fusion.1
  40.7 0.9 fusion.46
  41.6 1.2 concatenate.28
  42.8 0.1 copy.54
  42.8 0.1 concatenate.31
  43.0 0.1 copy.58
  43.0 6.7 %fusion.49 = (f32[2,512]{1,0:T(2,128)S(1)}, bf16[2,512,1536]{1,2,0:T(8,128)(2,1)}) fusion(pred[512,1536]{0,1:T(8,128)(4,1)} %fusion.6, bf16[512,2,128]{2,0,1:T(8,128)(2,1)} %copy.55, bf16[1024,2,128]{2,0,1:T(8,128)(2,1)S(1)} %copy.54, bf16[512,256]{1,0:T(8,128)(2,1)} %param.13), kind=kOutput, calls=%fused_computation.73 | convolution fusion | flops 413664768 | bytes 4984832 | tf_op jit(solution)/shard_map/sub | solution.py:164
  49.7 0.0 copy-start.1
  49.7 3.3 %fusion.14 = bf16[512,2,128]{2,0,1:T(8,128)(2,1)S(1)} fusion(bf16[2,512,1536]{1,2,0:T(8,128)(2,1)} %get-tuple-element.18, bf16[512,2,128]{2,0,1:T(8,128)(2,1)S(1)} %copy.59, bf16[1024,2,128]{2,0,1:T(8,128)(2,1)S(1)} %copy.58, f32[512,2]{0,1:T(2,128)S(1)} %bitcast.75), kind=kOutput, calls=%fused_computation.17 | convolution fusion | flops 404488192 | bytes 4198400 | tf_op jit(solution)/shard_map/hqk,khd->hqd/dot_general | solution.py:166
  53.0 0.3 copy.61
  53.3 0.2 convert_element_type.30
  53.5 15.0 %all_to_all.45 = bf16[8,64,256]{2,1,0:T(8,128)(2,1)S(1)} all-to-all(bf16[8,64,256]{2,1,0:T(8,128)(2,1)S(1)} %convert_element_type.30), channel_id=1, replica_groups=mesh['blk'=16,'req'=8] {'req'}, dimensions={0} | all-to-all | bytes 524288 | tf_op jit(solution)/shard_map/all_to_all | solution.py:184
  68.5 0.0 copy-done.1
  68.5 4.0 %broadcast_in_dim.32 = bf16[16,1024,256]{2,1,0:T(8,128)(2,1)} broadcast(bf16[1024,256]{1,0:T(8,128)(2,1)S(1)} %copy-done.1), dimensions={1,2} | broadcast | bytes 8912896 | tf_op jit(solution)/shard_map/broadcast_in_dim | solution.py:75
  72.5 0.0 copy-start.2
  72.5 4.9 %all-to-all-start = ((bf16[16,1024,256]{2,1,0:T(8,128)(2,1)}), bf16[16,1024,256]{2,1,0:T(8,128)(2,1)}, u32[]{:S(2)}, u32[]{:S(2)}) async-start(bf16[16,1024,256]{2,1,0:T(8,128)(2,1)} %broadcast_in_dim.32), calls=%async_computation | async-start | bytes 16777216 | tf_op jit(solution)/shard_map/all_to_all | solution.py:76
  77.5 0.0 copy-done.2
  77.5 5.5 %collective-permute-start = (bf16[512,256]{1,0:T(8,128)(2,1)S(1)}, bf16[512,256]{1,0:T(8,128)(2,1)S(1)}, u32[]{:S(2)}, u32[]{:S(2)}) collective-permute-start(bf16[512,256]{1,0:T(8,128)(2,1)S(1)} %get-tuple-element.16), channel_id=1, source_target_pairs={{0,120},{8,112},{16,104},{24,96},{32,88},{40,80},{48,72},{56,64},{... | collective-permute-start | bytes 786440 | tf_op jit(solution)/shard_map/ppermute | solution.py:82
  83.0 0.6 pad_add_fusion.1.pos_ref
  83.6 102.9 %collective-permute-done = bf16[512,256]{1,0:T(8,128)(2,1)S(1)} collective-permute-done((bf16[512,256]{1,0:T(8,128)(2,1)S(1)}, bf16[512,256]{1,0:T(8,128)(2,1)S(1)}, u32[]{:S(2)}, u32[]{:S(2)}) %collective-permute-start) | collective-permute-done | bytes 262176 | tf_op jit(solution)/shard_map/ppermute | solution.py:82
  186.5 0.8 pad_maximum_fusion.1.q_ref
  187.3 5.7 %convolution_convert_fusion.1 = bf16[64,2048]{1,0:T(8,128)(2,1)} fusion(bf16[64,2048]{1,0:T(8,128)(2,1)S(1)} %bitcast.67, bf16[2048,2048]{1,0:T(8,128)(2,1)} %param.19), kind=kOutput, calls=%fused_computation.14 | convolution fusion | flops 537001984 | bytes 8912896 | tf_op jit(solution)/shard_map/dot_general | solution.py:185
  193.0 12.6 %all-to-all-done = bf16[16,1024,256]{2,1,0:T(8,128)(2,1)} async-done(((bf16[16,1024,256]{2,1,0:T(8,128)(2,1)}), bf16[16,1024,256]{2,1,0:T(8,128)(2,1)}, u32[]{:S(2)}, u32[]{:S(2)}) %all-to-all-start) | async-done | bytes 8388640 | tf_op jit(solution)/shard_map/all_to_all | solution.py:76
  205.6 0.0 all-gather.2.cloned.1.call-done.v_ref
  205.6 48.5 %shard_map.113 = bf16[1024,256]{1,0:T(8,128)(2,1)} custom-call(s32[3]{0:T(128)} %pad_add_fusion.1.pos_ref, bf16[1024,256]{1,0:T(8,128)(2,1)} %pad_maximum_fusion.1.q_ref, bf16[16384,256]{1,0:T(8,128)(2,1)} %bitcast.3.k_ref, bf16[16384,256]{1,0:T(8,128)(2,1)} %all-gather.2.cloned.1.call-done.v_ref), custom_call_target="tpu_custom_call" | custom-call | tf_op jit(solution)/shard_map/pallas_call | solution.py:97
  254.2 1.1 fusion.47
  255.2 0.1 collective-permute-start.1
  255.3 12.1 %collective-permute-done.1 = bf16[512,256]{1,0:T(8,128)(2,1)S(1)} collective-permute-done((bf16[512,256]{1,0:T(8,128)(2,1)S(1)}, bf16[512,256]{1,0:T(8,128)(2,1)S(1)}, u32[]{:S(2)}, u32[]{:S(2)}) %collective-permute-start.1) | collective-permute-done | bytes 262176 | tf_op jit(solution)/shard_map/ppermute | solution.py:117
  267.5 0.3 copy.63
  267.8 22.3 %all_to_all.46 = bf16[8,128,256]{1,2,0:T(8,128)(2,1)S(1)} all-to-all(bf16[8,128,256]{1,2,0:T(8,128)(2,1)S(1)} %copy.63), channel_id=1, replica_groups=mesh['blk'=16,'req'=8] {'req'}, dimensions={0} | all-to-all | bytes 1048576 | tf_op jit(solution)/shard_map/all_to_all | solution.py:187
  290.1 5.5 %convolution_convert_fusion = bf16[128,2048]{1,0:T(8,128)(2,1)} fusion(bf16[128,2048]{0,1:T(8,128)(2,1)S(1)} %bitcast.65, bf16[2048,2048]{1,0:T(8,128)(2,1)} %param.19), kind=kOutput, calls=%fused_computation.13 | convolution fusion | flops 1074003968 | bytes 9437184 | tf_op jit(solution)/shard_map/dot_general | solution.py:188
  (12 shorter events, 0.2 us)
Async XLA Ops:
  7.2 2.3 copy-start
  7.2 14.5 %copy-start.3 = (s32[1536]{0:T(1024)S(1)}, s32[1536]{0:T(1024)}, u32[]{:S(2)}) copy-start(s32[1536]{0:T(1024)} %constant.85.clone.1) | copy-start | bytes 18436
  7.2 14.5 %copy-start.4 = (s32[1,512]{1,0:T(1,128)S(1)}, s32[1,512]{1,0:T(1,128)}, u32[]{:S(2)}) copy-start(s32[1,512]{1,0:T(1,128)} %param.16) | copy-start | bytes 6148
  7.2 198.4 %all-gather.2.cloned.1.call-start = ((), (), s32[]{:S(2)}) async-start(), calls=%async_computation.4 | async-start | bytes 8912896 | tf_op jit(solution)/shard_map/all_gather | solution.py:77
  11.1 29.0 %all-to-all-start.1 = ((bf16[16,4,2,16,256]{4,3,2,1,0:T(8,128)(2,1)}), bf16[16,4,2,16,256]{4,3,2,1,0:T(8,128)(2,1)S(1)}, u32[]{:S(2)}, u32[]{:S(2)}) async-start(bf16[16,4,2,16,256]{4,3,2,1,0:T(8,128)(2,1)} %bitcast.7), calls=%async_computation.1 | async-start | bytes 2097152 | tf_op jit(solution)/shard_map/all_to_all | solution.py:140
  49.7 18.8 %copy-start.1 = (bf16[1024,256]{1,0:T(8,128)(2,1)S(1)}, bf16[1024,256]{1,0:T(8,128)(2,1)}, u32[]{:S(2)}) copy-start(bf16[1024,256]{1,0:T(8,128)(2,1)} %param.11) | copy-start | bytes 1572868
  72.5 4.9 %copy-start.2 = (bf16[1024,256]{1,0:T(8,128)(2,1)S(1)}, bf16[1024,256]{1,0:T(8,128)(2,1)}, u32[]{:S(2)}) copy-start(bf16[1024,256]{1,0:T(8,128)(2,1)} %param.10) | copy-start | bytes 1572868
  72.5 133.1 %all-to-all-start = ((bf16[16,1024,256]{2,1,0:T(8,128)(2,1)}), bf16[16,1024,256]{2,1,0:T(8,128)(2,1)}, u32[]{:S(2)}, u32[]{:S(2)}) async-start(bf16[16,1024,256]{2,1,0:T(8,128)(2,1)} %broadcast_in_dim.32), calls=%async_computation | async-start | bytes 16777216 | tf_op jit(solution)/shard_map/all_to_all | solution.py:76
  77.5 109.0 %collective-permute-start = (bf16[512,256]{1,0:T(8,128)(2,1)S(1)}, bf16[512,256]{1,0:T(8,128)(2,1)S(1)}, u32[]{:S(2)}, u32[]{:S(2)}) collective-permute-start(bf16[512,256]{1,0:T(8,128)(2,1)S(1)} %get-tuple-element.16), channel_id=1, source_target_pairs={{0,120},{8,112},{16,104},{24,96},{32,88},{40,80},{48,72},{56,64},{... | collective-permute-start | bytes 786440 | tf_op jit(solution)/shard_map/ppermute | solution.py:82
  255.2 12.2 %collective-permute-start.1 = (bf16[512,256]{1,0:T(8,128)(2,1)S(1)}, bf16[512,256]{1,0:T(8,128)(2,1)S(1)}, u32[]{:S(2)}, u32[]{:S(2)}) collective-permute-start(bf16[512,256]{1,0:T(8,128)(2,1)S(1)} %get-tuple-element.14), channel_id=1, source_target_pairs={{0,120},{8,112},{16,104},{24,96},{32,88},{40,80},{48,72},{56,64},{... | collective-permute-start | bytes 786440 | tf_op jit(solution)/shard_map/ppermute | solution.py:117
Sparse Core Ops, SparseCore 0:
  10.4 106.9 all-gather.1

commit v10 on v8

--- a/solution.py
+++ b/solution.py
@@ -35,21 +35,22 @@
         for h in range(heads):
             cols = slice(h * HD, (h + 1) * HD)
             scores = lax.dot_general(
-                q_ref[:, cols], k_ref[:, cols], (((1,), (1,)), ((), ())),
+                k_ref[:, cols], q_ref[:, cols], (((1,), (1,)), ((), ())),
                 preferred_element_type=jnp.float32,
             ) * HD ** (-0.5)
             if masked:
-                query_pos = first_query + lax.broadcasted_iota(jnp.int32, (tq, tk), 0)
-                key_pos = k_tile * tk + lax.broadcasted_iota(jnp.int32, (tq, tk), 1)
+                key_pos = k_tile * tk + lax.broadcasted_iota(jnp.int32, (tk, tq), 0)
+                query_pos = first_query + lax.broadcasted_iota(jnp.int32, (tk, tq), 1)
                 scores = jnp.where(key_pos <= query_pos, scores, very_negative)
             run_max = m_sc[h]
-            new_max = jnp.maximum(run_max, jnp.max(scores, axis=1, keepdims=True))
-            weights = jnp.exp(scores - new_max[:, :1])
+            new_max = jnp.maximum(run_max, jnp.max(scores, axis=0, keepdims=True))
+            weights = jnp.exp(scores - new_max)
             factor = jnp.exp(run_max - new_max)
-            l_sc[h] = l_sc[h] * factor + jnp.sum(weights, axis=1, keepdims=True)
+            l_sc[h] = l_sc[h] * factor + jnp.sum(weights, axis=0, keepdims=True)
             m_sc[h] = new_max
-            acc_sc[h] = acc_sc[h] * factor + jnp.dot(
-                weights.astype(jnp.bfloat16), v_ref[:, cols], preferred_element_type=jnp.float32
+            acc_sc[h] = acc_sc[h] * factor + lax.dot_general(
+                v_ref[:, cols], weights.astype(jnp.bfloat16), (((0,), (0,)), ((), ())),
+                preferred_element_type=jnp.float32,
             )
 
     needs_mask = (k_tile + 1) * tk - 1 > first_query
@@ -65,7 +66,7 @@
     @pl.when(k_tile == last_tile)
     def _():
         for h in range(heads):
-            o_ref[:, h * HD:(h + 1) * HD] = (acc_sc[h] / l_sc[h]).astype(o_ref.dtype)
+            o_ref[:, h * HD:(h + 1) * HD] = (acc_sc[h] / l_sc[h]).T.astype(o_ref.dtype)
 
 
 def prompt_attention(queries, block_index, long_k, long_v, early=None):
@@ -109,9 +110,9 @@
             ],
             out_specs=pl.BlockSpec((tq, width), q_map),
             scratch_shapes=[
-                pltpu.VMEM((heads_dev, tq, HD), jnp.float32),
-                pltpu.VMEM((heads_dev, tq, HD), jnp.float32),
-                pltpu.VMEM((heads_dev, tq, HD), jnp.float32),
+                pltpu.VMEM((heads_dev, 1, tq), jnp.float32),
+                pltpu.VMEM((heads_dev, 1, tq), jnp.float32),
+                pltpu.VMEM((heads_dev, HD, tq), jnp.float32),
             ],
         ),
         compiler_params=pltpu.CompilerParams(dimension_semantics=("arbitrary",)),

time: 226 us -> 217 us (0.960)
  Pallas kernels: 48.6 us -> 39.6 us
    pallas_call x1, Pallas kernels: 48.6 us -> 39.6 us  [prompt_attention(): pl.pallas_call(body, out_shape=jax.ShapeDtypeStruct((row_count, width), j...]
  transfers between devices with their start and end apart: 5 -> 5, of which waited for: 4 -> 4; matrix products, arithmetic and copies ran while one was open for 14% -> 15% of each run, Pallas kernels for 0% -> 0%
where the time goes in v10:
time: 217 us; the launch traced here: 216 us
  waiting for transfers between devices  89 us (41%)
  Pallas kernels  39.6 us (18%)
  matrix products  22.3 us (10%)
  starting transfers between devices  18.3 us (8%)
  blocking collectives  14.6 us (7%)
  between operations  14.3 us (7%)
  local copies, waits for them, and re-layouts  11 us (5%)
  other arithmetic  7.33 us (3%)
    all_gather x1, waiting for transfers between devices, prompt_attention(): lax.all_gather(jnp.concatenate([long_k, long_v], 1), 'blk', axis=0, tiled...  61 us
    pallas_call x1, Pallas kernels, prompt_attention(): pl.pallas_call(body, out_shape=jax.ShapeDtypeStruct((row_count, width), j...  39.6 us
    all_to_all x1, blocking collectives, per_device(): long_rows = lax.all_to_all(long_attn, 'req', 0, 1, tiled=True)  14.6 us
    all_to_all x1, waiting for transfers between devices, pack_attention(): lax.all_to_all(outgoing, 'blk', split_axis=0, concat_axis=0, tiled=True)  11.9 us
    ppermute x1, waiting for transfers between devices, prompt_attention(): lax.ppermute(result[tq:], 'blk', mirror)  11.2 us
    dot_general x1, matrix products, per_device(): jnp.dot(short_rows, w_out, preferred_element_type=jnp.float32)  7.31 us
    all_to_all x1, starting transfers between devices, pack_attention(): lax.all_to_all(outgoing, 'blk', split_axis=0, concat_axis=0, tiled=True)  7.25 us
    sub x1, matrix products, pack_attention(): weights = jnp.where(allowed, jnp.exp(scores - row_max[..., None]), 0.0)  6.25 us
  transfers between devices with their start and end apart: 5, of which 4 were waited for; matrix products, arithmetic and copies ran while one was open for 15% of the time, Pallas kernels for 0%

profile of v10, /device:TPU:0, one launch (start us, length us, event | category | flops | bytes accessed | tf_op | source)
XLA Modules:
  0.0 216.4 jit_solution(18114203791608323841)
XLA Ops:
  7.2 0.0 copy-start
  7.2 0.0 copy-start.6
  7.2 0.0 all-gather.2.cloned.1.call-start
  7.2 2.3 %pad_maximum_fusion = bf16[1024,512]{1,0:T(8,128)(2,1)} fusion(bf16[1024,256]{1,0:T(8,128)(2,1)} %param.12, bf16[1024,256]{1,0:T(8,128)(2,1)} %param.11), kind=kLoop, calls=%fused_computation.18 | loop fusion | flops 2097152 | bytes 2097152 | tf_op jit(solution)/shard_map/concatenate | solution.py:75
  9.6 0.0 copy-start.2
  9.6 0.0 copy-start.3
  9.6 0.0 all-gather.2.cloned.1.call-update
  9.6 0.0 copy-done.6
  9.6 0.1 copy.47
  9.7 0.1 copy.48
  9.8 0.2 reduce_window_sum.11
  10.0 0.1 select_reduce_fusion
  10.2 0.1 copy.52
  10.3 0.1 reshape.234
  10.4 0.0 copy-done
  10.4 0.0 copy-start.4
  10.4 1.6 gather_fusion
  12.0 0.0 copy-start.8
  12.0 0.0 copy-start.7
  12.0 7.2 %all-to-all-start = ((bf16[16,4,2,16,256]{4,3,2,1,0:T(8,128)(2,1)}), bf16[16,4,2,16,256]{4,3,2,1,0:T(8,128)(2,1)S(1)}, u32[]{:S(2)}, u32[]{:S(2)}) async-start(bf16[16,4,2,16,256]{4,3,2,1,0:T(8,128)(2,1)} %bitcast.6), calls=%async_computation | async-start | bytes 2097152 | tf_op jit(solution)/shard_map/all_to_all | solution.py:143
  19.3 0.0 copy-done.2
  19.3 0.7 fusion.48
  20.0 5.3 %collective-permute-start = (bf16[512,256]{1,0:T(8,128)(2,1)}, bf16[512,256]{1,0:T(8,128)(2,1)}, u32[]{:S(2)}, u32[]{:S(2)}) collective-permute-start(bf16[512,256]{1,0:T(8,128)(2,1)} %get-tuple-element.14), channel_id=1, source_target_pairs={{0,120},{8,112},{16,104},{24,96},{32,88},{40,80},{48,72},{56,64},{... | collective-permute-start | bytes 786440 | tf_op jit(solution)/shard_map/ppermute | solution.py:82
  25.3 0.0 copy-done.3
  25.3 0.1 copy.53
  25.5 0.9 copy.55
  26.3 0.0 copy-done.4
  26.3 0.1 copy.57
  26.5 0.9 copy.59
  27.3 0.2 convert_reduce_fusion
  27.5 0.0 copy-done.8
  27.6 0.0 copy-done.7
  27.6 1.9 fusion.6
  29.5 11.9 %all-to-all-done = bf16[16,4,2,16,256]{4,3,2,1,0:T(8,128)(2,1)S(1)} async-done(((bf16[16,4,2,16,256]{4,3,2,1,0:T(8,128)(2,1)}), bf16[16,4,2,16,256]{4,3,2,1,0:T(8,128)(2,1)S(1)}, u32[]{:S(2)}, u32[]{:S(2)}) %all-to-all-start) | async-done | bytes 1048608 | tf_op jit(solution)/shard_map/all_to_all | solution.py:143
  41.4 0.6 gather_fusion.1
  42.0 0.9 fusion.46
  42.9 0.0 copy-start.1
  42.9 1.2 concatenate.32
  44.1 0.9 copy.54
  45.0 0.1 concatenate.35
  45.1 0.1 copy.58
  45.2 0.0 copy-done.1
  45.2 0.0 copy-start.5
  45.2 6.2 %fusion.49 = (f32[2,512]{1,0:T(2,128)S(1)}, bf16[2,512,1536]{1,2,0:T(8,128)(2,1)}) fusion(pred[512,1536]{0,1:T(8,128)(4,1)S(1)} %copy-done.1, bf16[512,2,128]{2,0,1:T(8,128)(2,1)} %copy.55, bf16[1024,2,128]{2,0,1:T(8,128)(2,1)} %copy.54, bf16[512,256]{1,0:T(8,128)(2,1)} %param.13), kind=kOutput, calls=%fused_computation.74 | convolution fusion | flops 413664768 | bytes 4984832 | tf_op jit(solution)/shard_map/sub | solution.py:167
  51.5 0.0 copy-done.5
  51.5 3.3 %fusion.14 = bf16[512,2,128]{2,0,1:T(8,128)(2,1)S(1)} fusion(bf16[2,512,1536]{1,2,0:T(8,128)(2,1)} %get-tuple-element.16, bf16[512,2,128]{2,0,1:T(8,128)(2,1)S(1)} %copy-done.5, bf16[1024,2,128]{2,0,1:T(8,128)(2,1)S(1)} %copy.58, f32[512,2]{0,1:T(2,128)S(1)} %bitcast.74), kind=kOutput, calls=%fused_computation.17 | convolution fusion | flops 404488192 | bytes 4198400 | tf_op jit(solution)/shard_map/hqk,khd->hqd/dot_general | solution.py:169
  54.8 0.3 copy.61
  55.0 0.9 convert_element_type.30
  55.9 4.9 %all-to-all-start.1 = ((bf16[8,64,256]{2,1,0:T(8,128)(2,1)}), bf16[8,64,256]{2,1,0:T(8,128)(2,1)S(1)}, u32[]{:S(2)}, u32[]{:S(2)}) async-start(bf16[8,64,256]{2,1,0:T(8,128)(2,1)} %convert_element_type.30), calls=%async_computation.1 | async-start | bytes 524288 | tf_op jit(solution)/shard_map/all_to_all | solution.py:187
  60.8 0.6 pad_add_fusion.1.pos_ref
  61.5 0.0 collective-permute-done
  61.5 1.8 pad_maximum_fusion.2.q_ref
  63.2 4.9 %all-to-all-done.1 = bf16[8,64,256]{2,1,0:T(8,128)(2,1)S(1)} async-done(((bf16[8,64,256]{2,1,0:T(8,128)(2,1)}), bf16[8,64,256]{2,1,0:T(8,128)(2,1)S(1)}, u32[]{:S(2)}, u32[]{:S(2)}) %all-to-all-start.1) | async-done | bytes 262176 | tf_op jit(solution)/shard_map/all_to_all | solution.py:187
  68.1 7.3 %convolution_convert_fusion.1 = bf16[64,2048]{1,0:T(8,128)(2,1)} fusion(bf16[64,2048]{1,0:T(8,128)(2,1)S(1)} %bitcast.66, bf16[2048,2048]{1,0:T(8,128)(2,1)} %param.19), kind=kOutput, calls=%fused_computation.14 | convolution fusion | flops 537001984 | bytes 8912896 | tf_op jit(solution)/shard_map/dot_general | solution.py:188
  75.4 61.0 %all-gather.2.cloned.1.call-done.k_ref.v_ref = bf16[16384,512]{1,0:T(8,128)(2,1)} async-done(((bf16[1024,512]{1,0:T(8,128)(2,1)}), bf16[16384,512]{1,0:T(8,128)(2,1)}) %all-gather.2.cloned.1.call-update) | async-done | bytes 16777232 | tf_op jit(solution)/shard_map/all_gather | solution.py:75
  136.5 39.6 %shard_map.113 = bf16[1024,256]{1,0:T(8,128)(2,1)} custom-call(s32[3]{0:T(128)} %pad_add_fusion.1.pos_ref, bf16[1024,256]{1,0:T(8,128)(2,1)} %pad_maximum_fusion.2.q_ref, bf16[16384,512]{1,0:T(8,128)(2,1)} %all-gather.2.cloned.1.call-done.k_ref.v_ref, bf16[16384,512]{1,0:T(8,128)(2,1)} %all-gather.2.cloned.1.call-done.k_ref.v_ref), custom_call_target="tpu_custom_call" | custom-call | tf_op jit(solution)/shard_map/pallas_call | solution.py:100
  176.1 1.1 fusion.47
  177.2 0.8 collective-permute-start.1
  177.9 11.2 %collective-permute-done.1 = bf16[512,256]{1,0:T(8,128)(2,1)S(1)} collective-permute-done((bf16[512,256]{1,0:T(8,128)(2,1)S(1)}, bf16[512,256]{1,0:T(8,128)(2,1)S(1)}, u32[]{:S(2)}, u32[]{:S(2)}) %collective-permute-start.1) | collective-permute-done | bytes 262176 | tf_op jit(solution)/shard_map/ppermute | solution.py:120
  189.2 0.3 copy.63
  189.4 14.6 %all_to_all.40 = bf16[8,128,256]{1,2,0:T(8,128)(2,1)S(1)} all-to-all(bf16[8,128,256]{1,2,0:T(8,128)(2,1)S(1)} %copy.63), channel_id=1, replica_groups=mesh['blk'=16,'req'=8] {'req'}, dimensions={0} | all-to-all | bytes 1048576 | tf_op jit(solution)/shard_map/all_to_all | solution.py:190
  204.1 5.5 %convolution_convert_fusion = bf16[128,2048]{1,0:T(8,128)(2,1)} fusion(bf16[128,2048]{0,1:T(8,128)(2,1)S(1)} %bitcast.64, bf16[2048,2048]{1,0:T(8,128)(2,1)} %param.19), kind=kOutput, calls=%fused_computation.13 | convolution fusion | flops 1074003968 | bytes 9437184 | tf_op jit(solution)/shard_map/dot_general | solution.py:191
  (11 shorter events, 0.1 us)
Async XLA Ops:
  7.2 3.2 %copy-start = (bf16[64,2,16,256]{3,2,1,0:T(8,128)(2,1)S(1)}, bf16[64,2,16,256]{3,2,1,0:T(8,128)(2,1)}, u32[]{:S(2)}) copy-start(bf16[64,2,16,256]{3,2,1,0:T(8,128)(2,1)} %param.17) | copy-start | bytes 3145732
  7.2 2.4 %copy-start.6 = (s32[16,16,4]{1,2,0:T(4,128)S(1)}, s32[16,16,4]{1,2,0:T(4,128)}, u32[]{:S(2)}) copy-start(s32[16,16,4]{1,2,0:T(4,128)} %param.18) | copy-start | bytes 12292
  7.2 129.3 %all-gather.2.cloned.1.call-start = ((), (), s32[]{:S(2)}) async-start(), calls=%async_computation.3 | async-start | bytes 17825792 | tf_op jit(solution)/shard_map/all_gather | solution.py:75
  9.6 9.7 %copy-start.2 = (bf16[1024,256]{1,0:T(8,128)(2,1)S(1)}, bf16[1024,256]{1,0:T(8,128)(2,1)}, u32[]{:S(2)}) copy-start(bf16[1024,256]{1,0:T(8,128)(2,1)} %param.10) | copy-start | bytes 1572868
  9.6 15.7 %copy-start.3 = (bf16[512,256]{1,0:T(8,128)(2,1)S(1)}, bf16[512,256]{1,0:T(8,128)(2,1)}, u32[]{:S(2)}) copy-start(bf16[512,256]{1,0:T(8,128)(2,1)} %param.14) | copy-start | bytes 786436
  10.4 15.9 %copy-start.4 = (bf16[512,256]{1,0:T(8,128)(2,1)S(1)}, bf16[512,256]{1,0:T(8,128)(2,1)}, u32[]{:S(2)}) copy-start(bf16[512,256]{1,0:T(8,128)(2,1)} %param.15) | copy-start | bytes 786436
  12.0 15.5 %copy-start.8 = (s32[1,512]{1,0:T(1,128)S(1)}, s32[1,512]{1,0:T(1,128)}, u32[]{:S(2)}) copy-start(s32[1,512]{1,0:T(1,128)} %param.16) | copy-start | bytes 6148
  12.0 15.6 %copy-start.7 = (s32[1536]{0:T(1024)S(1)}, s32[1536]{0:T(1024)}, u32[]{:S(2)}) copy-start(s32[1536]{0:T(1024)} %constant.85.clone.1) | copy-start | bytes 18436
  12.0 29.4 %all-to-all-start = ((bf16[16,4,2,16,256]{4,3,2,1,0:T(8,128)(2,1)}), bf16[16,4,2,16,256]{4,3,2,1,0:T(8,128)(2,1)S(1)}, u32[]{:S(2)}, u32[]{:S(2)}) async-start(bf16[16,4,2,16,256]{4,3,2,1,0:T(8,128)(2,1)} %bitcast.6), calls=%async_computation | async-start | bytes 2097152 | tf_op jit(solution)/shard_map/all_to_all | solution.py:143
  20.0 41.4 %collective-permute-start = (bf16[512,256]{1,0:T(8,128)(2,1)}, bf16[512,256]{1,0:T(8,128)(2,1)}, u32[]{:S(2)}, u32[]{:S(2)}) collective-permute-start(bf16[512,256]{1,0:T(8,128)(2,1)} %get-tuple-element.14), channel_id=1, source_target_pairs={{0,120},{8,112},{16,104},{24,96},{32,88},{40,80},{48,72},{56,64},{... | collective-permute-start | bytes 786440 | tf_op jit(solution)/shard_map/ppermute | solution.py:82
  42.9 2.3 %copy-start.1 = (pred[512,1536]{0,1:T(8,128)(4,1)S(1)}, pred[512,1536]{0,1:T(8,128)(4,1)}, u32[]{:S(2)}) copy-start(pred[512,1536]{0,1:T(8,128)(4,1)} %fusion.6) | copy-start | bytes 2359300
  45.2 6.3 %copy-start.5 = (bf16[512,2,128]{2,0,1:T(8,128)(2,1)S(1)}, bf16[512,2,128]{2,0,1:T(8,128)(2,1)}, u32[]{:S(2)}) copy-start(bf16[512,2,128]{2,0,1:T(8,128)(2,1)} %copy.59) | copy-start | bytes 786436
  55.9 12.2 %all-to-all-start.1 = ((bf16[8,64,256]{2,1,0:T(8,128)(2,1)}), bf16[8,64,256]{2,1,0:T(8,128)(2,1)S(1)}, u32[]{:S(2)}, u32[]{:S(2)}) async-start(bf16[8,64,256]{2,1,0:T(8,128)(2,1)} %convert_element_type.30), calls=%async_computation.1 | async-start | bytes 524288 | tf_op jit(solution)/shard_map/all_to_all | solution.py:187
  177.2 11.9 %collective-permute-start.1 = (bf16[512,256]{1,0:T(8,128)(2,1)S(1)}, bf16[512,256]{1,0:T(8,128)(2,1)S(1)}, u32[]{:S(2)}, u32[]{:S(2)}) collective-permute-start(bf16[512,256]{1,0:T(8,128)(2,1)S(1)} %get-tuple-element.12), channel_id=1, source_target_pairs={{0,120},{8,112},{16,104},{24,96},{32,88},{40,80},{48,72},{56,64},{... | collective-permute-start | bytes 786440 | tf_op jit(solution)/shard_map/ppermute | solution.py:120
Sparse Core Ops, SparseCore 0:
  10.4 126.0 all-gather.1

commit v11 on v10

--- a/solution.py
+++ b/solution.py
@@ -80,12 +80,17 @@
     tq = row_count // 2
     mirror = [(src, block_count - 1 - src) for src in range(block_count)]
     partner_half = lax.ppermute(queries[tq:], "blk", mirror)
-    tk = min(row_count, 1024)
+    tk = min(piece_rows, 2 * row_count)
     own_first = block_index * row_count
     lent_first = (block_count - 1 - block_index) * row_count + tq
     own_steps = (own_first + tq - 1) // tk + 1
     tile_pos = jnp.stack([own_first, lent_first, own_steps]).astype(jnp.int32)
-    step_count = ((block_count - 1) * row_count + 2 * tq - 1) // tk + 2
+    counts = {
+        (d * row_count + tq - 1) // tk + ((block_count - 1 - d) * row_count + 2 * tq - 1) // tk + 2
+        for d in range(block_count)
+    }
+    assert len(counts) == 1
+    step_count = counts.pop()
 
     def kv_map(column):
         def index(step, pos_ref):

time: 217 us -> 214 us (0.986)
  Pallas kernels: 39.6 us -> 37 us
    pallas_call x1, Pallas kernels: 39.6 us -> 37 us  [prompt_attention(): pl.pallas_call(body, out_shape=jax.ShapeDtypeStruct((row_count, width), j...]
where the time goes in v11:
time: 214 us
  waiting for transfers between devices  89.1 us (42%)
  Pallas kernels  37 us (17%)
  matrix products  22.3 us (10%)
  starting transfers between devices  18.2 us (9%)
  blocking collectives  14.6 us (7%)
  between operations  14.3 us (7%)
  local copies, waits for them, and re-layouts  11 us (5%)
  other arithmetic  7.33 us (3%)
    all_gather x1, waiting for transfers between devices, prompt_attention(): lax.all_gather(jnp.concatenate([long_k, long_v], 1), 'blk', axis=0, tiled...  61 us
    pallas_call x1, Pallas kernels, prompt_attention(): pl.pallas_call(body, out_shape=jax.ShapeDtypeStruct((row_count, width), j...  37 us
    all_to_all x1, blocking collectives, per_device(): long_rows = lax.all_to_all(long_attn, 'req', 0, 1, tiled=True)  14.6 us
    all_to_all x1, waiting for transfers between devices, pack_attention(): lax.all_to_all(outgoing, 'blk', split_axis=0, concat_axis=0, tiled=True)  11.9 us
    ppermute x1, waiting for transfers between devices, prompt_attention(): lax.ppermute(result[tq:], 'blk', mirror)  11.3 us
    dot_general x1, matrix products, per_device(): jnp.dot(short_rows, w_out, preferred_element_type=jnp.float32)  7.31 us
    all_to_all x1, starting transfers between devices, pack_attention(): lax.all_to_all(outgoing, 'blk', split_axis=0, concat_axis=0, tiled=True)  7.25 us
    sub x1, matrix products, pack_attention(): weights = jnp.where(allowed, jnp.exp(scores - row_max[..., None]), 0.0)  6.25 us
  transfers between devices with their start and end apart: 5, of which 4 were waited for; matrix products, arithmetic and copies ran while one was open for 15% of the time, Pallas kernels for 0%

profile of v11, /device:TPU:0, one launch (start us, length us, event | category | flops | bytes accessed | tf_op | source)
XLA Modules:
  0.0 213.8 jit_solution(1891762408446473984)
XLA Ops:
  7.2 0.0 copy-start
  7.2 0.0 copy-start.6
  7.2 0.0 all-gather.2.cloned.1.call-start
  7.2 2.3 %pad_maximum_fusion = bf16[1024,512]{1,0:T(8,128)(2,1)} fusion(bf16[1024,256]{1,0:T(8,128)(2,1)} %param.12, bf16[1024,256]{1,0:T(8,128)(2,1)} %param.11), kind=kLoop, calls=%fused_computation.18 | loop fusion | flops 2097152 | bytes 2097152 | tf_op jit(solution)/shard_map/concatenate | solution.py:75
  9.6 0.0 copy-start.2
  9.6 0.0 copy-start.3
  9.6 0.0 all-gather.2.cloned.1.call-update
  9.6 0.0 copy-done.6
  9.6 0.1 copy.47
  9.7 0.1 copy.48
  9.8 0.2 reduce_window_sum.11
  10.0 0.1 select_reduce_fusion
  10.2 0.1 copy.52
  10.3 0.1 reshape.234
  10.4 0.0 copy-done
  10.4 0.0 copy-start.4
  10.4 1.6 gather_fusion
  12.0 0.0 copy-start.8
  12.0 0.0 copy-start.7
  12.0 7.2 %all-to-all-start = ((bf16[16,4,2,16,256]{4,3,2,1,0:T(8,128)(2,1)}), bf16[16,4,2,16,256]{4,3,2,1,0:T(8,128)(2,1)S(1)}, u32[]{:S(2)}, u32[]{:S(2)}) async-start(bf16[16,4,2,16,256]{4,3,2,1,0:T(8,128)(2,1)} %bitcast.6), calls=%async_computation | async-start | bytes 2097152 | tf_op jit(solution)/shard_map/all_to_all | solution.py:148
  19.3 0.0 copy-done.2
  19.3 0.7 fusion.48
  20.0 5.3 %collective-permute-start = (bf16[512,256]{1,0:T(8,128)(2,1)}, bf16[512,256]{1,0:T(8,128)(2,1)}, u32[]{:S(2)}, u32[]{:S(2)}) collective-permute-start(bf16[512,256]{1,0:T(8,128)(2,1)} %get-tuple-element.14), channel_id=1, source_target_pairs={{0,120},{8,112},{16,104},{24,96},{32,88},{40,80},{48,72},{56,64},{... | collective-permute-start | bytes 786440 | tf_op jit(solution)/shard_map/ppermute | solution.py:82
  25.3 0.0 copy-done.3
  25.3 0.1 copy.53
  25.5 0.9 copy.55
  26.3 0.0 copy-done.4
  26.3 0.1 copy.57
  26.5 0.9 copy.59
  27.3 0.2 convert_reduce_fusion
  27.5 0.0 copy-done.8
  27.6 0.0 copy-done.7
  27.6 1.9 fusion.6
  29.5 11.9 %all-to-all-done = bf16[16,4,2,16,256]{4,3,2,1,0:T(8,128)(2,1)S(1)} async-done(((bf16[16,4,2,16,256]{4,3,2,1,0:T(8,128)(2,1)}), bf16[16,4,2,16,256]{4,3,2,1,0:T(8,128)(2,1)S(1)}, u32[]{:S(2)}, u32[]{:S(2)}) %all-to-all-start) | async-done | bytes 1048608 | tf_op jit(solution)/shard_map/all_to_all | solution.py:148
  41.4 0.6 gather_fusion.1
  42.0 0.9 fusion.46
  42.9 0.0 copy-start.1
  42.9 1.2 concatenate.32
  44.1 0.9 copy.54
  45.0 0.1 concatenate.35
  45.1 0.1 copy.58
  45.2 0.0 copy-done.1
  45.2 0.0 copy-start.5
  45.2 6.2 %fusion.49 = (f32[2,512]{1,0:T(2,128)S(1)}, bf16[2,512,1536]{1,2,0:T(8,128)(2,1)}) fusion(pred[512,1536]{0,1:T(8,128)(4,1)S(1)} %copy-done.1, bf16[512,2,128]{2,0,1:T(8,128)(2,1)} %copy.55, bf16[1024,2,128]{2,0,1:T(8,128)(2,1)} %copy.54, bf16[512,256]{1,0:T(8,128)(2,1)} %param.13), kind=kOutput, calls=%fused_computation.74 | convolution fusion | flops 413664768 | bytes 4984832 | tf_op jit(solution)/shard_map/sub | solution.py:172
  51.5 0.0 copy-done.5
  51.5 3.3 %fusion.14 = bf16[512,2,128]{2,0,1:T(8,128)(2,1)S(1)} fusion(bf16[2,512,1536]{1,2,0:T(8,128)(2,1)} %get-tuple-element.16, bf16[512,2,128]{2,0,1:T(8,128)(2,1)S(1)} %copy-done.5, bf16[1024,2,128]{2,0,1:T(8,128)(2,1)S(1)} %copy.58, f32[512,2]{0,1:T(2,128)S(1)} %bitcast.74), kind=kOutput, calls=%fused_computation.17 | convolution fusion | flops 404488192 | bytes 4198400 | tf_op jit(solution)/shard_map/hqk,khd->hqd/dot_general | solution.py:174
  54.8 0.3 copy.61
  55.0 0.9 convert_element_type.30
  55.9 4.9 %all-to-all-start.1 = ((bf16[8,64,256]{2,1,0:T(8,128)(2,1)}), bf16[8,64,256]{2,1,0:T(8,128)(2,1)S(1)}, u32[]{:S(2)}, u32[]{:S(2)}) async-start(bf16[8,64,256]{2,1,0:T(8,128)(2,1)} %convert_element_type.30), calls=%async_computation.1 | async-start | bytes 524288 | tf_op jit(solution)/shard_map/all_to_all | solution.py:192
  60.8 0.6 pad_add_fusion.1.pos_ref
  61.5 0.0 collective-permute-done
  61.5 1.8 pad_maximum_fusion.2.q_ref
  63.2 4.9 %all-to-all-done.1 = bf16[8,64,256]{2,1,0:T(8,128)(2,1)S(1)} async-done(((bf16[8,64,256]{2,1,0:T(8,128)(2,1)}), bf16[8,64,256]{2,1,0:T(8,128)(2,1)S(1)}, u32[]{:S(2)}, u32[]{:S(2)}) %all-to-all-start.1) | async-done | bytes 262176 | tf_op jit(solution)/shard_map/all_to_all | solution.py:192
  68.1 7.3 %convolution_convert_fusion.1 = bf16[64,2048]{1,0:T(8,128)(2,1)} fusion(bf16[64,2048]{1,0:T(8,128)(2,1)S(1)} %bitcast.66, bf16[2048,2048]{1,0:T(8,128)(2,1)} %param.19), kind=kOutput, calls=%fused_computation.14 | convolution fusion | flops 537001984 | bytes 8912896 | tf_op jit(solution)/shard_map/dot_general | solution.py:193
  75.4 61.0 %all-gather.2.cloned.1.call-done.k_ref.v_ref = bf16[16384,512]{1,0:T(8,128)(2,1)} async-done(((bf16[1024,512]{1,0:T(8,128)(2,1)}), bf16[16384,512]{1,0:T(8,128)(2,1)}) %all-gather.2.cloned.1.call-update) | async-done | bytes 16777232 | tf_op jit(solution)/shard_map/all_gather | solution.py:75
  136.5 37.0 %shard_map.113 = bf16[1024,256]{1,0:T(8,128)(2,1)} custom-call(s32[3]{0:T(128)} %pad_add_fusion.1.pos_ref, bf16[1024,256]{1,0:T(8,128)(2,1)} %pad_maximum_fusion.2.q_ref, bf16[16384,512]{1,0:T(8,128)(2,1)} %all-gather.2.cloned.1.call-done.k_ref.v_ref, bf16[16384,512]{1,0:T(8,128)(2,1)} %all-gather.2.cloned.1.call-done.k_ref.v_ref), custom_call_target="tpu_custom_call" | custom-call | tf_op jit(solution)/shard_map/pallas_call | solution.py:105
  173.5 1.1 fusion.47
  174.6 0.7 collective-permute-start.1
  175.3 11.3 %collective-permute-done.1 = bf16[512,256]{1,0:T(8,128)(2,1)S(1)} collective-permute-done((bf16[512,256]{1,0:T(8,128)(2,1)S(1)}, bf16[512,256]{1,0:T(8,128)(2,1)S(1)}, u32[]{:S(2)}, u32[]{:S(2)}) %collective-permute-start.1) | collective-permute-done | bytes 262176 | tf_op jit(solution)/shard_map/ppermute | solution.py:125
  186.6 0.3 copy.63
  186.9 14.6 %all_to_all.40 = bf16[8,128,256]{1,2,0:T(8,128)(2,1)S(1)} all-to-all(bf16[8,128,256]{1,2,0:T(8,128)(2,1)S(1)} %copy.63), channel_id=1, replica_groups=mesh['blk'=16,'req'=8] {'req'}, dimensions={0} | all-to-all | bytes 1048576 | tf_op jit(solution)/shard_map/all_to_all | solution.py:195
  201.4 5.5 %convolution_convert_fusion = bf16[128,2048]{1,0:T(8,128)(2,1)} fusion(bf16[128,2048]{0,1:T(8,128)(2,1)S(1)} %bitcast.64, bf16[2048,2048]{1,0:T(8,128)(2,1)} %param.19), kind=kOutput, calls=%fused_computation.13 | convolution fusion | flops 1074003968 | bytes 9437184 | tf_op jit(solution)/shard_map/dot_general | solution.py:196
  (11 shorter events, 0.1 us)
Async XLA Ops:
  7.2 3.2 %copy-start = (bf16[64,2,16,256]{3,2,1,0:T(8,128)(2,1)S(1)}, bf16[64,2,16,256]{3,2,1,0:T(8,128)(2,1)}, u32[]{:S(2)}) copy-start(bf16[64,2,16,256]{3,2,1,0:T(8,128)(2,1)} %param.17) | copy-start | bytes 3145732
  7.2 2.4 %copy-start.6 = (s32[16,16,4]{1,2,0:T(4,128)S(1)}, s32[16,16,4]{1,2,0:T(4,128)}, u32[]{:S(2)}) copy-start(s32[16,16,4]{1,2,0:T(4,128)} %param.18) | copy-start | bytes 12292
  7.2 129.3 %all-gather.2.cloned.1.call-start = ((), (), s32[]{:S(2)}) async-start(), calls=%async_computation.3 | async-start | bytes 17825792 | tf_op jit(solution)/shard_map/all_gather | solution.py:75
  9.6 9.7 %copy-start.2 = (bf16[1024,256]{1,0:T(8,128)(2,1)S(1)}, bf16[1024,256]{1,0:T(8,128)(2,1)}, u32[]{:S(2)}) copy-start(bf16[1024,256]{1,0:T(8,128)(2,1)} %param.10) | copy-start | bytes 1572868
  9.6 15.7 %copy-start.3 = (bf16[512,256]{1,0:T(8,128)(2,1)S(1)}, bf16[512,256]{1,0:T(8,128)(2,1)}, u32[]{:S(2)}) copy-start(bf16[512,256]{1,0:T(8,128)(2,1)} %param.14) | copy-start | bytes 786436
  10.4 15.9 %copy-start.4 = (bf16[512,256]{1,0:T(8,128)(2,1)S(1)}, bf16[512,256]{1,0:T(8,128)(2,1)}, u32[]{:S(2)}) copy-start(bf16[512,256]{1,0:T(8,128)(2,1)} %param.15) | copy-start | bytes 786436
  12.0 15.5 %copy-start.8 = (s32[1,512]{1,0:T(1,128)S(1)}, s32[1,512]{1,0:T(1,128)}, u32[]{:S(2)}) copy-start(s32[1,512]{1,0:T(1,128)} %param.16) | copy-start | bytes 6148
  12.0 15.6 %copy-start.7 = (s32[1536]{0:T(1024)S(1)}, s32[1536]{0:T(1024)}, u32[]{:S(2)}) copy-start(s32[1536]{0:T(1024)} %constant.86.clone.1) | copy-start | bytes 18436
  12.0 29.4 %all-to-all-start = ((bf16[16,4,2,16,256]{4,3,2,1,0:T(8,128)(2,1)}), bf16[16,4,2,16,256]{4,3,2,1,0:T(8,128)(2,1)S(1)}, u32[]{:S(2)}, u32[]{:S(2)}) async-start(bf16[16,4,2,16,256]{4,3,2,1,0:T(8,128)(2,1)} %bitcast.6), calls=%async_computation | async-start | bytes 2097152 | tf_op jit(solution)/shard_map/all_to_all | solution.py:148
  20.0 41.4 %collective-permute-start = (bf16[512,256]{1,0:T(8,128)(2,1)}, bf16[512,256]{1,0:T(8,128)(2,1)}, u32[]{:S(2)}, u32[]{:S(2)}) collective-permute-start(bf16[512,256]{1,0:T(8,128)(2,1)} %get-tuple-element.14), channel_id=1, source_target_pairs={{0,120},{8,112},{16,104},{24,96},{32,88},{40,80},{48,72},{56,64},{... | collective-permute-start | bytes 786440 | tf_op jit(solution)/shard_map/ppermute | solution.py:82
  42.9 2.3 %copy-start.1 = (pred[512,1536]{0,1:T(8,128)(4,1)S(1)}, pred[512,1536]{0,1:T(8,128)(4,1)}, u32[]{:S(2)}) copy-start(pred[512,1536]{0,1:T(8,128)(4,1)} %fusion.6) | copy-start | bytes 2359300
  45.2 6.3 %copy-start.5 = (bf16[512,2,128]{2,0,1:T(8,128)(2,1)S(1)}, bf16[512,2,128]{2,0,1:T(8,128)(2,1)}, u32[]{:S(2)}) copy-start(bf16[512,2,128]{2,0,1:T(8,128)(2,1)} %copy.59) | copy-start | bytes 786436
  55.9 12.2 %all-to-all-start.1 = ((bf16[8,64,256]{2,1,0:T(8,128)(2,1)}), bf16[8,64,256]{2,1,0:T(8,128)(2,1)S(1)}, u32[]{:S(2)}, u32[]{:S(2)}) async-start(bf16[8,64,256]{2,1,0:T(8,128)(2,1)} %convert_element_type.30), calls=%async_computation.1 | async-start | bytes 524288 | tf_op jit(solution)/shard_map/all_to_all | solution.py:192
  174.6 12.0 %collective-permute-start.1 = (bf16[512,256]{1,0:T(8,128)(2,1)S(1)}, bf16[512,256]{1,0:T(8,128)(2,1)S(1)}, u32[]{:S(2)}, u32[]{:S(2)}) collective-permute-start(bf16[512,256]{1,0:T(8,128)(2,1)S(1)} %get-tuple-element.12), channel_id=1, source_target_pairs={{0,120},{8,112},{16,104},{24,96},{32,88},{40,80},{48,72},{56,64},{... | collective-permute-start | bytes 786440 | tf_op jit(solution)/shard_map/ppermute | solution.py:125
Sparse Core Ops, SparseCore 0:
  10.4 126.0 all-gather.1

commit v12 on v11

--- a/solution.py
+++ b/solution.py
@@ -78,15 +78,17 @@
     piece_rows = kv_piece.shape[0]
     block_count = lax.axis_size("blk")
     tq = row_count // 2
-    mirror = [(src, block_count - 1 - src) for src in range(block_count)]
+    chip_count = block_count // 2
+    mirror = [(src, 2 * (chip_count - 1 - src // 2) + src % 2) for src in range(block_count)]
+    partner_block = 2 * (chip_count - 1 - block_index // 2) + block_index % 2
     partner_half = lax.ppermute(queries[tq:], "blk", mirror)
     tk = min(piece_rows, 2 * row_count)
     own_first = block_index * row_count
-    lent_first = (block_count - 1 - block_index) * row_count + tq
+    lent_first = partner_block * row_count + tq
     own_steps = (own_first + tq - 1) // tk + 1
     tile_pos = jnp.stack([own_first, lent_first, own_steps]).astype(jnp.int32)
     counts = {
-        (d * row_count + tq - 1) // tk + ((block_count - 1 - d) * row_count + 2 * tq - 1) // tk + 2
+        (d * row_count + tq - 1) // tk + (dict(mirror)[d] * row_count + 2 * tq - 1) // tk + 2
         for d in range(block_count)
     }
     assert len(counts) == 1

time: 214 us -> 214 us (level)
  no operation moved by 1% of the time
where the time goes in v12:
time: 214 us; the launch traced here: 213 us
  waiting for transfers between devices  88.8 us (41%)
  Pallas kernels  37 us (17%)
  matrix products  22.3 us (10%)
  starting transfers between devices  18.6 us (9%)
  between operations  14.3 us (7%)
  blocking collectives  13.9 us (6%)
  local copies, waits for them, and re-layouts  11 us (5%)
  other arithmetic  7.33 us (3%)
    all_gather x1, waiting for transfers between devices, prompt_attention(): lax.all_gather(jnp.concatenate([long_k, long_v], 1), 'blk', axis=0, tiled...  61 us
    pallas_call x1, Pallas kernels, prompt_attention(): pl.pallas_call(body, out_shape=jax.ShapeDtypeStruct((row_count, width), j...  37 us
    all_to_all x1, blocking collectives, per_device(): long_rows = lax.all_to_all(long_attn, 'req', 0, 1, tiled=True)  13.9 us
    all_to_all x1, waiting for transfers between devices, pack_attention(): lax.all_to_all(outgoing, 'blk', split_axis=0, concat_axis=0, tiled=True)  11.6 us
    ppermute x1, waiting for transfers between devices, prompt_attention(): lax.ppermute(result[tq:], 'blk', mirror)  11.3 us
    dot_general x1, matrix products, per_device(): jnp.dot(short_rows, w_out, preferred_element_type=jnp.float32)  7.31 us
    all_to_all x1, starting transfers between devices, pack_attention(): lax.all_to_all(outgoing, 'blk', split_axis=0, concat_axis=0, tiled=True)  7.25 us
    sub x1, matrix products, pack_attention(): weights = jnp.where(allowed, jnp.exp(scores - row_max[..., None]), 0.0)  6.24 us
  transfers between devices with their start and end apart: 5, of which 4 were waited for; matrix products, arithmetic and copies ran while one was open for 15% of the time, Pallas kernels for 0%

profile of v12, /device:TPU:0, one launch (start us, length us, event | category | flops | bytes accessed | tf_op | source)
XLA Modules:
  0.0 213.3 jit_solution(6884626717985647960)
XLA Ops:
  7.2 0.0 copy-start
  7.2 0.0 copy-start.6
  7.2 0.0 all-gather.2.cloned.1.call-start
  7.2 2.3 %pad_maximum_fusion = bf16[1024,512]{1,0:T(8,128)(2,1)} fusion(bf16[1024,256]{1,0:T(8,128)(2,1)} %param.12, bf16[1024,256]{1,0:T(8,128)(2,1)} %param.11), kind=kLoop, calls=%fused_computation.18 | loop fusion | flops 2097152 | bytes 2097152 | tf_op jit(solution)/shard_map/concatenate | solution.py:75
  9.6 0.0 copy-start.2
  9.6 0.0 copy-start.3
  9.6 0.0 all-gather.2.cloned.1.call-update
  9.6 0.0 copy-done.6
  9.6 0.1 copy.47
  9.7 0.1 copy.48
  9.8 0.2 reduce_window_sum.11
  10.0 0.1 select_reduce_fusion
  10.2 0.1 copy.52
  10.3 0.1 reshape.234
  10.4 0.0 copy-done
  10.4 0.0 copy-start.4
  10.4 1.6 gather_fusion
  12.0 0.0 copy-start.8
  12.0 0.0 copy-start.7
  12.0 7.2 %all-to-all-start = ((bf16[16,4,2,16,256]{4,3,2,1,0:T(8,128)(2,1)}), bf16[16,4,2,16,256]{4,3,2,1,0:T(8,128)(2,1)S(1)}, u32[]{:S(2)}, u32[]{:S(2)}) async-start(bf16[16,4,2,16,256]{4,3,2,1,0:T(8,128)(2,1)} %bitcast.6), calls=%async_computation | async-start | bytes 2097152 | tf_op jit(solution)/shard_map/all_to_all | solution.py:150
  19.3 0.0 copy-done.2
  19.3 0.7 fusion.48
  20.0 5.5 %collective-permute-start = (bf16[512,256]{1,0:T(8,128)(2,1)}, bf16[512,256]{1,0:T(8,128)(2,1)}, u32[]{:S(2)}, u32[]{:S(2)}) collective-permute-start(bf16[512,256]{1,0:T(8,128)(2,1)} %get-tuple-element.14), channel_id=1, source_target_pairs={{0,112},{8,120},{16,96},{24,104},{32,80},{40,88},{48,64},{56,72},{... | collective-permute-start | bytes 786440 | tf_op jit(solution)/shard_map/ppermute | solution.py:84
  25.6 0.0 copy-done.3
  25.6 0.1 copy.53
  25.7 0.9 copy.55
  26.6 0.0 copy-done.4
  26.6 0.1 copy.57
  26.7 0.9 copy.59
  27.6 0.2 convert_reduce_fusion
  27.8 0.0 copy-done.8
  27.8 0.0 copy-done.7
  27.8 1.9 fusion.6
  29.7 11.6 %all-to-all-done = bf16[16,4,2,16,256]{4,3,2,1,0:T(8,128)(2,1)S(1)} async-done(((bf16[16,4,2,16,256]{4,3,2,1,0:T(8,128)(2,1)}), bf16[16,4,2,16,256]{4,3,2,1,0:T(8,128)(2,1)S(1)}, u32[]{:S(2)}, u32[]{:S(2)}) %all-to-all-start) | async-done | bytes 1048608 | tf_op jit(solution)/shard_map/all_to_all | solution.py:150
  41.4 0.6 gather_fusion.1
  42.0 0.9 fusion.46
  42.9 0.0 copy-start.1
  42.9 1.2 concatenate.32
  44.1 0.9 copy.54
  45.0 0.1 concatenate.35
  45.1 0.1 copy.58
  45.2 0.0 copy-done.1
  45.2 0.0 copy-start.5
  45.2 6.2 %fusion.49 = (f32[2,512]{1,0:T(2,128)S(1)}, bf16[2,512,1536]{1,2,0:T(8,128)(2,1)}) fusion(pred[512,1536]{0,1:T(8,128)(4,1)S(1)} %copy-done.1, bf16[512,2,128]{2,0,1:T(8,128)(2,1)} %copy.55, bf16[1024,2,128]{2,0,1:T(8,128)(2,1)} %copy.54, bf16[512,256]{1,0:T(8,128)(2,1)} %param.13), kind=kOutput, calls=%fused_computation.74 | convolution fusion | flops 413664768 | bytes 4984832 | tf_op jit(solution)/shard_map/sub | solution.py:174
  51.5 0.0 copy-done.5
  51.5 3.3 %fusion.14 = bf16[512,2,128]{2,0,1:T(8,128)(2,1)S(1)} fusion(bf16[2,512,1536]{1,2,0:T(8,128)(2,1)} %get-tuple-element.16, bf16[512,2,128]{2,0,1:T(8,128)(2,1)S(1)} %copy-done.5, bf16[1024,2,128]{2,0,1:T(8,128)(2,1)S(1)} %copy.58, f32[512,2]{0,1:T(2,128)S(1)} %bitcast.74), kind=kOutput, calls=%fused_computation.17 | convolution fusion | flops 404488192 | bytes 4198400 | tf_op jit(solution)/shard_map/hqk,khd->hqd/dot_general | solution.py:176
  54.8 0.3 copy.61
  55.0 0.9 convert_element_type.30
  55.9 4.9 %all-to-all-start.1 = ((bf16[8,64,256]{2,1,0:T(8,128)(2,1)}), bf16[8,64,256]{2,1,0:T(8,128)(2,1)S(1)}, u32[]{:S(2)}, u32[]{:S(2)}) async-start(bf16[8,64,256]{2,1,0:T(8,128)(2,1)} %convert_element_type.30), calls=%async_computation.1 | async-start | bytes 524288 | tf_op jit(solution)/shard_map/all_to_all | solution.py:194
  60.8 0.6 pad_add_fusion.1.pos_ref
  61.5 0.0 collective-permute-done
  61.5 1.8 pad_maximum_fusion.2.q_ref
  63.2 4.9 %all-to-all-done.1 = bf16[8,64,256]{2,1,0:T(8,128)(2,1)S(1)} async-done(((bf16[8,64,256]{2,1,0:T(8,128)(2,1)}), bf16[8,64,256]{2,1,0:T(8,128)(2,1)S(1)}, u32[]{:S(2)}, u32[]{:S(2)}) %all-to-all-start.1) | async-done | bytes 262176 | tf_op jit(solution)/shard_map/all_to_all | solution.py:194
  68.1 7.3 %convolution_convert_fusion.1 = bf16[64,2048]{1,0:T(8,128)(2,1)} fusion(bf16[64,2048]{1,0:T(8,128)(2,1)S(1)} %bitcast.66, bf16[2048,2048]{1,0:T(8,128)(2,1)} %param.19), kind=kOutput, calls=%fused_computation.14 | convolution fusion | flops 537001984 | bytes 8912896 | tf_op jit(solution)/shard_map/dot_general | solution.py:195
  75.4 61.0 %all-gather.2.cloned.1.call-done.k_ref.v_ref = bf16[16384,512]{1,0:T(8,128)(2,1)} async-done(((bf16[1024,512]{1,0:T(8,128)(2,1)}), bf16[16384,512]{1,0:T(8,128)(2,1)}) %all-gather.2.cloned.1.call-update) | async-done | bytes 16777232 | tf_op jit(solution)/shard_map/all_gather | solution.py:75
  136.5 37.0 %shard_map.113 = bf16[1024,256]{1,0:T(8,128)(2,1)} custom-call(s32[3]{0:T(128)} %pad_add_fusion.1.pos_ref, bf16[1024,256]{1,0:T(8,128)(2,1)} %pad_maximum_fusion.2.q_ref, bf16[16384,512]{1,0:T(8,128)(2,1)} %all-gather.2.cloned.1.call-done.k_ref.v_ref, bf16[16384,512]{1,0:T(8,128)(2,1)} %all-gather.2.cloned.1.call-done.k_ref.v_ref), custom_call_target="tpu_custom_call" | custom-call | tf_op jit(solution)/shard_map/pallas_call | solution.py:107
  173.5 1.1 fusion.47
  174.6 0.9 collective-permute-start.1
  175.4 11.3 %collective-permute-done.1 = bf16[512,256]{1,0:T(8,128)(2,1)S(1)} collective-permute-done((bf16[512,256]{1,0:T(8,128)(2,1)S(1)}, bf16[512,256]{1,0:T(8,128)(2,1)S(1)}, u32[]{:S(2)}, u32[]{:S(2)}) %collective-permute-start.1) | collective-permute-done | bytes 262176 | tf_op jit(solution)/shard_map/ppermute | solution.py:127
  186.7 0.3 copy.63
  187.0 13.9 %all_to_all.40 = bf16[8,128,256]{1,2,0:T(8,128)(2,1)S(1)} all-to-all(bf16[8,128,256]{1,2,0:T(8,128)(2,1)S(1)} %copy.63), channel_id=1, replica_groups=mesh['blk'=16,'req'=8] {'req'}, dimensions={0} | all-to-all | bytes 1048576 | tf_op jit(solution)/shard_map/all_to_all | solution.py:197
  201.0 5.5 %convolution_convert_fusion = bf16[128,2048]{1,0:T(8,128)(2,1)} fusion(bf16[128,2048]{0,1:T(8,128)(2,1)S(1)} %bitcast.64, bf16[2048,2048]{1,0:T(8,128)(2,1)} %param.19), kind=kOutput, calls=%fused_computation.13 | convolution fusion | flops 1074003968 | bytes 9437184 | tf_op jit(solution)/shard_map/dot_general | solution.py:198
  (11 shorter events, 0.1 us)
Async XLA Ops:
  7.2 3.2 %copy-start = (bf16[64,2,16,256]{3,2,1,0:T(8,128)(2,1)S(1)}, bf16[64,2,16,256]{3,2,1,0:T(8,128)(2,1)}, u32[]{:S(2)}) copy-start(bf16[64,2,16,256]{3,2,1,0:T(8,128)(2,1)} %param.17) | copy-start | bytes 3145732
  7.2 2.4 %copy-start.6 = (s32[16,16,4]{1,2,0:T(4,128)S(1)}, s32[16,16,4]{1,2,0:T(4,128)}, u32[]{:S(2)}) copy-start(s32[16,16,4]{1,2,0:T(4,128)} %param.18) | copy-start | bytes 12292
  7.2 129.3 %all-gather.2.cloned.1.call-start = ((), (), s32[]{:S(2)}) async-start(), calls=%async_computation.3 | async-start | bytes 17825792 | tf_op jit(solution)/shard_map/all_gather | solution.py:75
  9.6 9.7 %copy-start.2 = (bf16[1024,256]{1,0:T(8,128)(2,1)S(1)}, bf16[1024,256]{1,0:T(8,128)(2,1)}, u32[]{:S(2)}) copy-start(bf16[1024,256]{1,0:T(8,128)(2,1)} %param.10) | copy-start | bytes 1572868
  9.6 16.0 %copy-start.3 = (bf16[512,256]{1,0:T(8,128)(2,1)S(1)}, bf16[512,256]{1,0:T(8,128)(2,1)}, u32[]{:S(2)}) copy-start(bf16[512,256]{1,0:T(8,128)(2,1)} %param.14) | copy-start | bytes 786436
  10.4 16.2 %copy-start.4 = (bf16[512,256]{1,0:T(8,128)(2,1)S(1)}, bf16[512,256]{1,0:T(8,128)(2,1)}, u32[]{:S(2)}) copy-start(bf16[512,256]{1,0:T(8,128)(2,1)} %param.15) | copy-start | bytes 786436
  12.0 15.8 %copy-start.8 = (s32[1,512]{1,0:T(1,128)S(1)}, s32[1,512]{1,0:T(1,128)}, u32[]{:S(2)}) copy-start(s32[1,512]{1,0:T(1,128)} %param.16) | copy-start | bytes 6148
  12.0 15.8 %copy-start.7 = (s32[1536]{0:T(1024)S(1)}, s32[1536]{0:T(1024)}, u32[]{:S(2)}) copy-start(s32[1536]{0:T(1024)} %constant.105.clone.1) | copy-start | bytes 18436
  12.0 29.4 %all-to-all-start = ((bf16[16,4,2,16,256]{4,3,2,1,0:T(8,128)(2,1)}), bf16[16,4,2,16,256]{4,3,2,1,0:T(8,128)(2,1)S(1)}, u32[]{:S(2)}, u32[]{:S(2)}) async-start(bf16[16,4,2,16,256]{4,3,2,1,0:T(8,128)(2,1)} %bitcast.6), calls=%async_computation | async-start | bytes 2097152 | tf_op jit(solution)/shard_map/all_to_all | solution.py:150
  20.0 41.4 %collective-permute-start = (bf16[512,256]{1,0:T(8,128)(2,1)}, bf16[512,256]{1,0:T(8,128)(2,1)}, u32[]{:S(2)}, u32[]{:S(2)}) collective-permute-start(bf16[512,256]{1,0:T(8,128)(2,1)} %get-tuple-element.14), channel_id=1, source_target_pairs={{0,112},{8,120},{16,96},{24,104},{32,80},{40,88},{48,64},{56,72},{... | collective-permute-start | bytes 786440 | tf_op jit(solution)/shard_map/ppermute | solution.py:84
  42.9 2.3 %copy-start.1 = (pred[512,1536]{0,1:T(8,128)(4,1)S(1)}, pred[512,1536]{0,1:T(8,128)(4,1)}, u32[]{:S(2)}) copy-start(pred[512,1536]{0,1:T(8,128)(4,1)} %fusion.6) | copy-start | bytes 2359300
  45.2 6.3 %copy-start.5 = (bf16[512,2,128]{2,0,1:T(8,128)(2,1)S(1)}, bf16[512,2,128]{2,0,1:T(8,128)(2,1)}, u32[]{:S(2)}) copy-start(bf16[512,2,128]{2,0,1:T(8,128)(2,1)} %copy.59) | copy-start | bytes 786436
  55.9 12.2 %all-to-all-start.1 = ((bf16[8,64,256]{2,1,0:T(8,128)(2,1)}), bf16[8,64,256]{2,1,0:T(8,128)(2,1)S(1)}, u32[]{:S(2)}, u32[]{:S(2)}) async-start(bf16[8,64,256]{2,1,0:T(8,128)(2,1)} %convert_element_type.30), calls=%async_computation.1 | async-start | bytes 524288 | tf_op jit(solution)/shard_map/all_to_all | solution.py:194
  174.6 12.1 %collective-permute-start.1 = (bf16[512,256]{1,0:T(8,128)(2,1)S(1)}, bf16[512,256]{1,0:T(8,128)(2,1)S(1)}, u32[]{:S(2)}, u32[]{:S(2)}) collective-permute-start(bf16[512,256]{1,0:T(8,128)(2,1)S(1)} %get-tuple-element.12), channel_id=1, source_target_pairs={{0,112},{8,120},{16,96},{24,104},{32,80},{40,88},{48,64},{56,72},{... | collective-permute-start | bytes 786440 | tf_op jit(solution)/shard_map/ppermute | solution.py:127
Sparse Core Ops, SparseCore 0:
  10.4 126.0 all-gather.1

commit v13 on v12

--- a/solution.py
+++ b/solution.py
@@ -69,10 +69,31 @@
             o_ref[:, h * HD:(h + 1) * HD] = (acc_sc[h] / l_sc[h]).T.astype(o_ref.dtype)
 
 
+def side_by_side_body(left_ref, right_ref, out_ref, sems):
+    width = left_ref.shape[1]
+    first = pltpu.make_async_copy(left_ref, out_ref.at[:, :width], sems.at[0])
+    second = pltpu.make_async_copy(right_ref, out_ref.at[:, width:], sems.at[1])
+    first.start()
+    second.start()
+    first.wait()
+    second.wait()
+
+
+def side_by_side(left, right):
+    rows, width = left.shape
+    return pl.pallas_call(
+        side_by_side_body,
+        out_shape=jax.ShapeDtypeStruct((rows, 2 * width), left.dtype),
+        in_specs=[pl.BlockSpec(memory_space=pl.ANY), pl.BlockSpec(memory_space=pl.ANY)],
+        out_specs=pl.BlockSpec(memory_space=pl.ANY),
+        scratch_shapes=[pltpu.SemaphoreType.DMA((2,))],
+    )(left, right)
+
+
 def prompt_attention(queries, block_index, long_k, long_v, early=None):
     row_count, width = queries.shape
     heads_dev = width // HD
-    kv_piece = lax.all_gather(jnp.concatenate([long_k, long_v], 1), "blk", axis=0, tiled=True)
+    kv_piece = lax.all_gather(side_by_side(long_k, long_v), "blk", axis=0, tiled=True)
     if early is not None:
         kv_piece, early = lax.optimization_barrier((kv_piece, early))
     piece_rows = kv_piece.shape[0]

time: 214 us -> 245 us (1.14)
  Pallas kernels: 37 us -> 69.9 us
    pallas_call x0 -> x1, Pallas kernels: none -> 32.9 us  [side_by_side(): pl.pallas_call(side_by_side_body, out_shape=jax.ShapeDtypeStruct((rows, 2...]
  transfers between devices with their start and end apart: 5 -> 5, of which waited for: 4 -> 4; matrix products, arithmetic and copies ran while one was open for 15% -> 12% of each run, Pallas kernels for 0% -> 0%
where the time goes in v13:
time: 245 us; the launch traced here: 244 us
  waiting for transfers between devices  88.8 us (36%)
  Pallas kernels  69.9 us (29%)
  matrix products  21.3 us (9%)
  starting transfers between devices  20.4 us (8%)
  between operations  14.3 us (6%)
  blocking collectives  13.9 us (6%)
  local copies, waits for them, and re-layouts  10.8 us (4%)
  other arithmetic  5.01 us (2%)
    all_gather x1, waiting for transfers between devices, prompt_attention(): lax.all_gather(side_by_side(long_k, long_v), 'blk', axis=0, tiled=True)  61 us
    pallas_call x1, Pallas kernels, prompt_attention(): pl.pallas_call(body, out_shape=jax.ShapeDtypeStruct((row_count, width), j...  37 us
    pallas_call x1, Pallas kernels, side_by_side(): pl.pallas_call(side_by_side_body, out_shape=jax.ShapeDtypeStruct((rows, 2...  32.9 us
    all_to_all x1, blocking collectives, per_device(): long_rows = lax.all_to_all(long_attn, 'req', 0, 1, tiled=True)  13.9 us
    ppermute x1, waiting for transfers between devices, prompt_attention(): lax.ppermute(result[tq:], 'blk', mirror)  11.3 us
    all_to_all x1, waiting for transfers between devices, pack_attention(): lax.all_to_all(outgoing, 'blk', split_axis=0, concat_axis=0, tiled=True)  11.2 us
    all_to_all x1, starting transfers between devices, pack_attention(): lax.all_to_all(outgoing, 'blk', split_axis=0, concat_axis=0, tiled=True)  7.12 us
    all_to_all x1, starting transfers between devices, per_device(): short_rows = lax.all_to_all(short_attn, 'req', 0, 1, tiled=True)  6.85 us
  transfers between devices with their start and end apart: 5, of which 4 were waited for; matrix products, arithmetic and copies ran while one was open for 12% of the time, Pallas kernels for 0%

profile of v13, /device:TPU:0, one launch (start us, length us, event | category | flops | bytes accessed | tf_op | source)
XLA Modules:
  0.0 244.4 jit_solution(8339077995572348796)
XLA Ops:
  7.2 0.0 copy-start
  7.2 0.0 copy-start.5
  7.2 0.0 copy-start.1
  7.2 0.0 copy-start.2
  7.2 0.0 copy-start.3
  7.2 0.0 copy-start.6
  7.2 0.0 all-gather.2.cloned.1.call-start
  7.3 32.9 %shard_map.113 = bf16[1024,512]{1,0:T(8,128)(2,1)} custom-call(bf16[1024,256]{1,0:T(8,128)(2,1)} %left_ref.1, bf16[1024,256]{1,0:T(8,128)(2,1)} %right_ref.1), custom_call_target="tpu_custom_call" | custom-call | tf_op jit(solution)/shard_map/pallas_call | solution.py:84
  40.2 0.0 all-gather.2.cloned.1.call-update
  40.2 0.8 copy.47
  41.0 0.1 copy.48
  41.1 0.2 reduce_window_sum.11
  41.4 0.1 select_reduce_fusion
  41.5 0.1 copy.52
  41.6 0.1 reshape.234
  41.7 0.0 copy-done
  41.7 1.6 gather_fusion
  43.3 7.1 %all-to-all-start = ((bf16[16,4,2,16,256]{4,3,2,1,0:T(8,128)(2,1)}), bf16[16,4,2,16,256]{4,3,2,1,0:T(8,128)(2,1)S(1)}, u32[]{:S(2)}, u32[]{:S(2)}) async-start(bf16[16,4,2,16,256]{4,3,2,1,0:T(8,128)(2,1)} %bitcast.6), calls=%async_computation | async-start | bytes 2097152 | tf_op jit(solution)/shard_map/all_to_all | solution.py:171
  50.4 0.0 copy-done.1
  50.4 0.7 fusion.48
  51.2 5.5 %collective-permute-start = (bf16[512,256]{1,0:T(8,128)(2,1)}, bf16[512,256]{1,0:T(8,128)(2,1)}, u32[]{:S(2)}, u32[]{:S(2)}) collective-permute-start(bf16[512,256]{1,0:T(8,128)(2,1)} %get-tuple-element.14), channel_id=1, source_target_pairs={{0,112},{8,120},{16,96},{24,104},{32,80},{40,88},{48,64},{56,72},{... | collective-permute-start | bytes 786440 | tf_op jit(solution)/shard_map/ppermute | solution.py:105
  56.7 0.0 copy-done.2
  56.7 0.1 copy.53
  56.9 0.8 copy.55
  57.7 0.0 copy-done.3
  57.7 0.1 copy.57
  57.9 0.8 copy.59
  58.7 0.2 convert_reduce_fusion
  58.9 0.0 copy-done.6
  59.0 0.0 copy-done.5
  59.0 1.9 fusion.6
  60.9 11.2 %all-to-all-done = bf16[16,4,2,16,256]{4,3,2,1,0:T(8,128)(2,1)S(1)} async-done(((bf16[16,4,2,16,256]{4,3,2,1,0:T(8,128)(2,1)}), bf16[16,4,2,16,256]{4,3,2,1,0:T(8,128)(2,1)S(1)}, u32[]{:S(2)}, u32[]{:S(2)}) %all-to-all-start) | async-done | bytes 1048608 | tf_op jit(solution)/shard_map/all_to_all | solution.py:171
  72.1 0.6 gather_fusion.1
  72.8 0.9 fusion.46
  73.6 1.2 concatenate.28
  74.8 0.1 copy.54
  74.9 0.1 concatenate.31
  75.0 0.1 copy.58
  75.1 0.0 copy-start.4
  75.1 6.6 %fusion.49 = (f32[2,512]{1,0:T(2,128)S(1)}, bf16[2,512,1536]{1,2,0:T(8,128)(2,1)}) fusion(pred[512,1536]{0,1:T(8,128)(4,1)} %fusion.6, bf16[512,2,128]{2,0,1:T(8,128)(2,1)} %copy.55, bf16[1024,2,128]{2,0,1:T(8,128)(2,1)S(1)} %copy.54, bf16[512,256]{1,0:T(8,128)(2,1)} %param.13), kind=kOutput, calls=%fused_computation.73 | convolution fusion | flops 413664768 | bytes 4984832 | tf_op jit(solution)/shard_map/sub | solution.py:195
  81.7 0.0 copy-done.4
  81.7 3.3 %fusion.14 = bf16[512,2,128]{2,0,1:T(8,128)(2,1)S(1)} fusion(bf16[2,512,1536]{1,2,0:T(8,128)(2,1)} %get-tuple-element.16, bf16[512,2,128]{2,0,1:T(8,128)(2,1)S(1)} %copy-done.4, bf16[1024,2,128]{2,0,1:T(8,128)(2,1)S(1)} %copy.58, f32[512,2]{0,1:T(2,128)S(1)} %bitcast.74), kind=kOutput, calls=%fused_computation.17 | convolution fusion | flops 404488192 | bytes 4198400 | tf_op jit(solution)/shard_map/hqk,khd->hqd/dot_general | solution.py:197
  85.0 0.3 copy.61
  85.3 0.9 convert_element_type.30
  86.2 6.9 %all-to-all-start.1 = ((bf16[8,64,256]{2,1,0:T(8,128)(2,1)}), bf16[8,64,256]{2,1,0:T(8,128)(2,1)S(1)}, u32[]{:S(2)}, u32[]{:S(2)}) async-start(bf16[8,64,256]{2,1,0:T(8,128)(2,1)} %convert_element_type.30), calls=%async_computation.1 | async-start | bytes 524288 | tf_op jit(solution)/shard_map/all_to_all | solution.py:215
  93.0 0.6 pad_add_fusion.1.pos_ref
  93.7 0.0 collective-permute-done
  93.7 1.8 pad_maximum_fusion.1.q_ref
  95.4 5.2 %all-to-all-done.1 = bf16[8,64,256]{2,1,0:T(8,128)(2,1)S(1)} async-done(((bf16[8,64,256]{2,1,0:T(8,128)(2,1)}), bf16[8,64,256]{2,1,0:T(8,128)(2,1)S(1)}, u32[]{:S(2)}, u32[]{:S(2)}) %all-to-all-start.1) | async-done | bytes 262176 | tf_op jit(solution)/shard_map/all_to_all | solution.py:215
  100.7 5.9 %convolution_convert_fusion.1 = bf16[64,2048]{1,0:T(8,128)(2,1)} fusion(bf16[64,2048]{1,0:T(8,128)(2,1)S(1)} %bitcast.66, bf16[2048,2048]{1,0:T(8,128)(2,1)} %param.19), kind=kOutput, calls=%fused_computation.14 | convolution fusion | flops 537001984 | bytes 8912896 | tf_op jit(solution)/shard_map/dot_general | solution.py:216
  106.6 61.0 %all-gather.2.cloned.1.call-done.k_ref.v_ref = bf16[16384,512]{1,0:T(8,128)(2,1)} async-done(((bf16[1024,512]{1,0:T(8,128)(2,1)}), bf16[16384,512]{1,0:T(8,128)(2,1)}) %all-gather.2.cloned.1.call-update) | async-done | bytes 16777232 | tf_op jit(solution)/shard_map/all_gather | solution.py:96
  167.7 37.0 %shard_map.114 = bf16[1024,256]{1,0:T(8,128)(2,1)} custom-call(s32[3]{0:T(128)} %pad_add_fusion.1.pos_ref, bf16[1024,256]{1,0:T(8,128)(2,1)} %pad_maximum_fusion.1.q_ref, bf16[16384,512]{1,0:T(8,128)(2,1)} %all-gather.2.cloned.1.call-done.k_ref.v_ref, bf16[16384,512]{1,0:T(8,128)(2,1)} %all-gather.2.cloned.1.call-done.k_ref.v_ref), custom_call_target="tpu_custom_call" | custom-call | tf_op jit(solution)/shard_map/pallas_call | solution.py:128
  204.6 1.1 fusion.47
  205.7 0.9 collective-permute-start.1
  206.6 11.3 %collective-permute-done.1 = bf16[512,256]{1,0:T(8,128)(2,1)S(1)} collective-permute-done((bf16[512,256]{1,0:T(8,128)(2,1)S(1)}, bf16[512,256]{1,0:T(8,128)(2,1)S(1)}, u32[]{:S(2)}, u32[]{:S(2)}) %collective-permute-start.1) | collective-permute-done | bytes 262176 | tf_op jit(solution)/shard_map/ppermute | solution.py:148
  217.9 0.3 copy.63
  218.2 13.9 %all_to_all.40 = bf16[8,128,256]{1,2,0:T(8,128)(2,1)S(1)} all-to-all(bf16[8,128,256]{1,2,0:T(8,128)(2,1)S(1)} %copy.63), channel_id=1, replica_groups=mesh['blk'=16,'req'=8] {'req'}, dimensions={0} | all-to-all | bytes 1048576 | tf_op jit(solution)/shard_map/all_to_all | solution.py:218
  232.1 5.5 %convolution_convert_fusion = bf16[128,2048]{1,0:T(8,128)(2,1)} fusion(bf16[128,2048]{0,1:T(8,128)(2,1)S(1)} %bitcast.64, bf16[2048,2048]{1,0:T(8,128)(2,1)} %param.19), kind=kOutput, calls=%fused_computation.13 | convolution fusion | flops 1074003968 | bytes 9437184 | tf_op jit(solution)/shard_map/dot_general | solution.py:219
  (11 shorter events, 0.1 us)
Async XLA Ops:
  7.2 34.6 %copy-start = (bf16[64,2,16,256]{3,2,1,0:T(8,128)(2,1)S(1)}, bf16[64,2,16,256]{3,2,1,0:T(8,128)(2,1)}, u32[]{:S(2)}) copy-start(bf16[64,2,16,256]{3,2,1,0:T(8,128)(2,1)} %param.17) | copy-start | bytes 3145732
  7.2 51.8 %copy-start.5 = (s32[1536]{0:T(1024)S(1)}, s32[1536]{0:T(1024)}, u32[]{:S(2)}) copy-start(s32[1536]{0:T(1024)} %constant.105.clone.1) | copy-start | bytes 18436
  7.2 43.2 %copy-start.1 = (bf16[1024,256]{1,0:T(8,128)(2,1)S(1)}, bf16[1024,256]{1,0:T(8,128)(2,1)}, u32[]{:S(2)}) copy-start(bf16[1024,256]{1,0:T(8,128)(2,1)} %param.10) | copy-start | bytes 1572868
  7.2 49.5 %copy-start.2 = (bf16[512,256]{1,0:T(8,128)(2,1)S(1)}, bf16[512,256]{1,0:T(8,128)(2,1)}, u32[]{:S(2)}) copy-start(bf16[512,256]{1,0:T(8,128)(2,1)} %param.14) | copy-start | bytes 786436
  7.2 50.5 %copy-start.3 = (bf16[512,256]{1,0:T(8,128)(2,1)S(1)}, bf16[512,256]{1,0:T(8,128)(2,1)}, u32[]{:S(2)}) copy-start(bf16[512,256]{1,0:T(8,128)(2,1)} %param.15) | copy-start | bytes 786436
  7.2 51.7 %copy-start.6 = (s32[1,512]{1,0:T(1,128)S(1)}, s32[1,512]{1,0:T(1,128)}, u32[]{:S(2)}) copy-start(s32[1,512]{1,0:T(1,128)} %param.16) | copy-start | bytes 6148
  7.2 160.4 %all-gather.2.cloned.1.call-start = ((), (), s32[]{:S(2)}) async-start(), calls=%async_computation.3 | async-start | bytes 17825792 | tf_op jit(solution)/shard_map/all_gather | solution.py:96
  43.3 28.8 %all-to-all-start = ((bf16[16,4,2,16,256]{4,3,2,1,0:T(8,128)(2,1)}), bf16[16,4,2,16,256]{4,3,2,1,0:T(8,128)(2,1)S(1)}, u32[]{:S(2)}, u32[]{:S(2)}) async-start(bf16[16,4,2,16,256]{4,3,2,1,0:T(8,128)(2,1)} %bitcast.6), calls=%async_computation | async-start | bytes 2097152 | tf_op jit(solution)/shard_map/all_to_all | solution.py:171
  51.2 42.5 %collective-permute-start = (bf16[512,256]{1,0:T(8,128)(2,1)}, bf16[512,256]{1,0:T(8,128)(2,1)}, u32[]{:S(2)}, u32[]{:S(2)}) collective-permute-start(bf16[512,256]{1,0:T(8,128)(2,1)} %get-tuple-element.14), channel_id=1, source_target_pairs={{0,112},{8,120},{16,96},{24,104},{32,80},{40,88},{48,64},{56,72},{... | collective-permute-start | bytes 786440 | tf_op jit(solution)/shard_map/ppermute | solution.py:105
  75.1 6.6 %copy-start.4 = (bf16[512,2,128]{2,0,1:T(8,128)(2,1)S(1)}, bf16[512,2,128]{2,0,1:T(8,128)(2,1)}, u32[]{:S(2)}) copy-start(bf16[512,2,128]{2,0,1:T(8,128)(2,1)} %copy.59) | copy-start | bytes 786436
  86.2 14.5 %all-to-all-start.1 = ((bf16[8,64,256]{2,1,0:T(8,128)(2,1)}), bf16[8,64,256]{2,1,0:T(8,128)(2,1)S(1)}, u32[]{:S(2)}, u32[]{:S(2)}) async-start(bf16[8,64,256]{2,1,0:T(8,128)(2,1)} %convert_element_type.30), calls=%async_computation.1 | async-start | bytes 524288 | tf_op jit(solution)/shard_map/all_to_all | solution.py:215
  205.7 12.2 %collective-permute-start.1 = (bf16[512,256]{1,0:T(8,128)(2,1)S(1)}, bf16[512,256]{1,0:T(8,128)(2,1)S(1)}, u32[]{:S(2)}, u32[]{:S(2)}) collective-permute-start(bf16[512,256]{1,0:T(8,128)(2,1)S(1)} %get-tuple-element.12), channel_id=1, source_target_pairs={{0,112},{8,120},{16,96},{24,104},{32,80},{40,88},{48,64},{56,72},{... | collective-permute-start | bytes 786440 | tf_op jit(solution)/shard_map/ppermute | solution.py:148
Sparse Core Ops, SparseCore 0:
  40.3 127.3 all-gather.1

commit v14 on v12

--- a/solution.py
+++ b/solution.py
@@ -35,7 +35,7 @@
         for h in range(heads):
             cols = slice(h * HD, (h + 1) * HD)
             scores = lax.dot_general(
-                k_ref[:, cols], q_ref[:, cols], (((1,), (1,)), ((), ())),
+                k_ref[:, :, cols].reshape(tk, HD), q_ref[:, cols], (((1,), (1,)), ((), ())),
                 preferred_element_type=jnp.float32,
             ) * HD ** (-0.5)
             if masked:
@@ -49,7 +49,7 @@
             l_sc[h] = l_sc[h] * factor + jnp.sum(weights, axis=0, keepdims=True)
             m_sc[h] = new_max
             acc_sc[h] = acc_sc[h] * factor + lax.dot_general(
-                v_ref[:, cols], weights.astype(jnp.bfloat16), (((0,), (0,)), ((), ())),
+                v_ref[:, :, cols].reshape(tk, HD), weights.astype(jnp.bfloat16), (((0,), (0,)), ((), ())),
                 preferred_element_type=jnp.float32,
             )
 
@@ -72,10 +72,11 @@
 def prompt_attention(queries, block_index, long_k, long_v, early=None):
     row_count, width = queries.shape
     heads_dev = width // HD
-    kv_piece = lax.all_gather(jnp.concatenate([long_k, long_v], 1), "blk", axis=0, tiled=True)
+    kv_piece = lax.all_gather(jnp.stack([long_k, long_v]), "blk", axis=0, tiled=True)
+    kv_piece = kv_piece.reshape(-1, 2, row_count, width)
     if early is not None:
         kv_piece, early = lax.optimization_barrier((kv_piece, early))
-    piece_rows = kv_piece.shape[0]
+    piece_rows = kv_piece.shape[0] * row_count
     block_count = lax.axis_size("blk")
     tq = row_count // 2
     chip_count = block_count // 2
@@ -96,7 +97,7 @@
 
     def kv_map(column):
         def index(step, pos_ref):
-            return (tile_of_step(step, pos_ref)[1], column)
+            return (tile_of_step(step, pos_ref)[1], column, 0, 0)
 
         return index
 
@@ -112,8 +113,8 @@
             grid=(step_count,),
             in_specs=[
                 pl.BlockSpec((tq, width), q_map),
-                pl.BlockSpec((tk, width), kv_map(0)),
-                pl.BlockSpec((tk, width), kv_map(1)),
+                pl.BlockSpec((tk // row_count, None, row_count, width), kv_map(0)),
+                pl.BlockSpec((tk // row_count, None, row_count, width), kv_map(1)),
             ],
             out_specs=pl.BlockSpec((tq, width), q_map),
             scratch_shapes=[

time: 214 us -> 215 us (level)
    another operation x0 -> x1, other arithmetic: none -> 2.41 us  [prompt_attention(): jnp.stack([long_k, long_v])]
    concatenate x1 -> x0, other arithmetic: 2.35 us -> none  [prompt_attention(): jnp.concatenate([long_k, long_v], 1)]
where the time goes in v14:
time: 215 us; the launch traced here: 214 us
  waiting for transfers between devices  88.2 us (41%)
  Pallas kernels  37.1 us (17%)
  matrix products  22.5 us (10%)
  starting transfers between devices  19.8 us (9%)
  between operations  14.3 us (7%)
  blocking collectives  13.9 us (6%)
  local copies, waits for them, and re-layouts  10.8 us (5%)
  other arithmetic  7.42 us (3%)
    all_gather x1, waiting for transfers between devices, prompt_attention(): lax.all_gather(jnp.stack([long_k, long_v]), 'blk', axis=0, tiled=True)  61 us
    pallas_call x1, Pallas kernels, prompt_attention(): pl.pallas_call(body, out_shape=jax.ShapeDtypeStruct((row_count, width), j...  37.1 us
    all_to_all x1, blocking collectives, per_device(): long_rows = lax.all_to_all(long_attn, 'req', 0, 1, tiled=True)  13.9 us
    ppermute x1, waiting for transfers between devices, prompt_attention(): lax.ppermute(result[tq:], 'blk', mirror)  11.3 us
    all_to_all x1, waiting for transfers between devices, pack_attention(): lax.all_to_all(outgoing, 'blk', split_axis=0, concat_axis=0, tiled=True)  11 us
    dot_general x1, matrix products, per_device(): jnp.dot(short_rows, w_out, preferred_element_type=jnp.float32)  7.16 us
    all_to_all x1, starting transfers between devices, pack_attention(): lax.all_to_all(outgoing, 'blk', split_axis=0, concat_axis=0, tiled=True)  7.12 us
    sub x1, matrix products, pack_attention(): weights = jnp.where(allowed, jnp.exp(scores - row_max[..., None]), 0.0)  6.6 us
  transfers between devices with their start and end apart: 5, of which 4 were waited for; matrix products, arithmetic and copies ran while one was open for 15% of the time, Pallas kernels for 0%

profile of v14, /device:TPU:0, one launch (start us, length us, event | category | flops | bytes accessed | tf_op | source)
XLA Modules:
  0.0 214.0 jit_solution(12061375456590155628)
XLA Ops:
  7.2 0.0 copy-start
  7.2 0.0 copy-start.5
  7.2 0.0 copy-start.1
  7.2 0.0 copy-start.2
  7.2 0.0 copy-start.3
  7.2 0.0 copy-start.6
  7.2 0.0 all-gather.2.cloned.1.call-start
  7.3 2.4 %pad_maximum_fusion = bf16[2,1024,256]{2,1,0:T(8,128)(2,1)} fusion(bf16[1,1024,256]{2,1,0:T(8,128)(2,1)} %bitcast.76, bf16[1,1024,256]{2,1,0:T(8,128)(2,1)} %bitcast.77), kind=kLoop, calls=%fused_computation.18 | loop fusion | flops 524288 | bytes 2097152 | tf_op jit(solution)/shard_map/stack | solution.py:75
  9.7 0.0 all-gather.2.cloned.1.call-update
  9.7 0.8 copy.63
  10.6 0.1 copy.64
  10.7 0.2 reduce_window_sum.11
  10.9 0.1 select_reduce_fusion
  11.0 0.1 copy.68
  11.1 0.1 reshape.238
  11.2 0.0 copy-done
  11.3 1.6 gather_fusion
  12.8 7.1 %all-to-all-start = ((bf16[16,4,2,16,256]{4,3,2,1,0:T(8,128)(2,1)}), bf16[16,4,2,16,256]{4,3,2,1,0:T(8,128)(2,1)S(1)}, u32[]{:S(2)}, u32[]{:S(2)}) async-start(bf16[16,4,2,16,256]{4,3,2,1,0:T(8,128)(2,1)} %bitcast.9), calls=%async_computation | async-start | bytes 2097152 | tf_op jit(solution)/shard_map/all_to_all | solution.py:151
  20.0 0.0 copy-done.1
  20.0 0.7 fusion.48
  20.7 5.5 %collective-permute-start = (bf16[512,256]{1,0:T(8,128)(2,1)}, bf16[512,256]{1,0:T(8,128)(2,1)}, u32[]{:S(2)}, u32[]{:S(2)}) collective-permute-start(bf16[512,256]{1,0:T(8,128)(2,1)} %get-tuple-element.14), channel_id=1, source_target_pairs={{0,112},{8,120},{16,96},{24,104},{32,80},{40,88},{48,64},{56,72},{... | collective-permute-start | bytes 786440 | tf_op jit(solution)/shard_map/ppermute | solution.py:85
  26.3 0.0 copy-done.2
  26.3 0.1 copy.69
  26.4 0.8 copy.71
  27.2 0.0 copy-done.3
  27.2 0.1 copy.73
  27.4 0.8 copy.75
  28.2 0.2 convert_reduce_fusion
  28.5 0.0 copy-done.6
  28.5 0.0 copy-done.5
  28.5 1.9 fusion.6
  30.4 11.0 %all-to-all-done = bf16[16,4,2,16,256]{4,3,2,1,0:T(8,128)(2,1)S(1)} async-done(((bf16[16,4,2,16,256]{4,3,2,1,0:T(8,128)(2,1)}), bf16[16,4,2,16,256]{4,3,2,1,0:T(8,128)(2,1)S(1)}, u32[]{:S(2)}, u32[]{:S(2)}) %all-to-all-start) | async-done | bytes 1048608 | tf_op jit(solution)/shard_map/all_to_all | solution.py:151
  41.4 0.6 gather_fusion.1
  42.1 0.9 fusion.46
  42.9 1.2 concatenate.28
  44.1 0.1 copy.70
  44.2 0.1 concatenate.31
  44.3 0.1 copy.74
  44.4 0.0 copy-start.4
  44.4 6.6 %fusion.49 = (f32[2,512]{1,0:T(2,128)S(1)}, bf16[2,512,1536]{1,2,0:T(8,128)(2,1)}) fusion(pred[512,1536]{0,1:T(8,128)(4,1)} %fusion.6, bf16[512,2,128]{2,0,1:T(8,128)(2,1)} %copy.71, bf16[1024,2,128]{2,0,1:T(8,128)(2,1)S(1)} %copy.70, bf16[512,256]{1,0:T(8,128)(2,1)} %param.13), kind=kOutput, calls=%fused_computation.74 | convolution fusion | flops 413664768 | bytes 4984832 | tf_op jit(solution)/shard_map/sub | solution.py:175
  51.0 0.0 copy-done.4
  51.0 3.3 %fusion.14 = bf16[512,2,128]{2,0,1:T(8,128)(2,1)S(1)} fusion(bf16[2,512,1536]{1,2,0:T(8,128)(2,1)} %get-tuple-element.16, bf16[512,2,128]{2,0,1:T(8,128)(2,1)S(1)} %copy-done.4, bf16[1024,2,128]{2,0,1:T(8,128)(2,1)S(1)} %copy.74, f32[512,2]{0,1:T(2,128)S(1)} %bitcast.81), kind=kOutput, calls=%fused_computation.17 | convolution fusion | flops 404488192 | bytes 4198400 | tf_op jit(solution)/shard_map/hqk,khd->hqd/dot_general | solution.py:177
  54.3 0.3 copy.77
  54.6 0.9 convert_element_type.30
  55.5 6.2 %all-to-all-start.1 = ((bf16[8,64,256]{2,1,0:T(8,128)(2,1)}), bf16[8,64,256]{2,1,0:T(8,128)(2,1)S(1)}, u32[]{:S(2)}, u32[]{:S(2)}) async-start(bf16[8,64,256]{2,1,0:T(8,128)(2,1)} %convert_element_type.30), calls=%async_computation.1 | async-start | bytes 524288 | tf_op jit(solution)/shard_map/all_to_all | solution.py:195
  61.7 0.6 pad_add_fusion.1.pos_ref
  62.3 0.0 collective-permute-done
  62.3 1.8 pad_maximum_fusion.2.q_ref
  64.1 4.8 %all-to-all-done.1 = bf16[8,64,256]{2,1,0:T(8,128)(2,1)S(1)} async-done(((bf16[8,64,256]{2,1,0:T(8,128)(2,1)}), bf16[8,64,256]{2,1,0:T(8,128)(2,1)S(1)}, u32[]{:S(2)}, u32[]{:S(2)}) %all-to-all-start.1) | async-done | bytes 262176 | tf_op jit(solution)/shard_map/all_to_all | solution.py:195
  69.0 7.2 %convolution_convert_fusion.1 = bf16[64,2048]{1,0:T(8,128)(2,1)} fusion(bf16[64,2048]{1,0:T(8,128)(2,1)S(1)} %bitcast.71, bf16[2048,2048]{1,0:T(8,128)(2,1)} %param.19), kind=kOutput, calls=%fused_computation.14 | convolution fusion | flops 537001984 | bytes 8912896 | tf_op jit(solution)/shard_map/dot_general | solution.py:196
  76.1 61.0 %all-gather.2.cloned.1.call-done = bf16[32,1024,256]{2,1,0:T(8,128)(2,1)} async-done(((bf16[2,1024,256]{2,1,0:T(8,128)(2,1)}), bf16[32,1024,256]{2,1,0:T(8,128)(2,1)}) %all-gather.2.cloned.1.call-update) | async-done | bytes 16777232 | tf_op jit(solution)/shard_map/all_gather | solution.py:75
  137.2 37.1 %shard_map.113 = bf16[1024,256]{1,0:T(8,128)(2,1)} custom-call(s32[3]{0:T(128)} %pad_add_fusion.1.pos_ref, bf16[1024,256]{1,0:T(8,128)(2,1)} %pad_maximum_fusion.2.q_ref, bf16[16,2,1024,256]{3,2,1,0:T(8,128)(2,1)} %bitcast.67, bf16[16,2,1024,256]{3,2,1,0:T(8,128)(2,1)} %bitcast.68), custom_call_target="tpu_custom_call" | custom-call | tf_op jit(solution)/shard_map/pallas_call | solution.py:108
  174.3 1.1 fusion.47
  175.4 0.9 collective-permute-start.1
  176.3 11.3 %collective-permute-done.1 = bf16[512,256]{1,0:T(8,128)(2,1)S(1)} collective-permute-done((bf16[512,256]{1,0:T(8,128)(2,1)S(1)}, bf16[512,256]{1,0:T(8,128)(2,1)S(1)}, u32[]{:S(2)}, u32[]{:S(2)}) %collective-permute-start.1) | collective-permute-done | bytes 262176 | tf_op jit(solution)/shard_map/ppermute | solution.py:128
  187.6 0.3 copy.79
  187.9 13.9 %all_to_all.40 = bf16[8,128,256]{1,2,0:T(8,128)(2,1)S(1)} all-to-all(bf16[8,128,256]{1,2,0:T(8,128)(2,1)S(1)} %copy.79), channel_id=1, replica_groups=mesh['blk'=16,'req'=8] {'req'}, dimensions={0} | all-to-all | bytes 1048576 | tf_op jit(solution)/shard_map/all_to_all | solution.py:198
  201.7 5.5 %convolution_convert_fusion = bf16[128,2048]{1,0:T(8,128)(2,1)} fusion(bf16[128,2048]{0,1:T(8,128)(2,1)S(1)} %bitcast.69, bf16[2048,2048]{1,0:T(8,128)(2,1)} %param.19), kind=kOutput, calls=%fused_computation.13 | convolution fusion | flops 1074003968 | bytes 9437184 | tf_op jit(solution)/shard_map/dot_general | solution.py:199
  (11 shorter events, 0.1 us)
Async XLA Ops:
  7.2 4.1 %copy-start = (bf16[64,2,16,256]{3,2,1,0:T(8,128)(2,1)S(1)}, bf16[64,2,16,256]{3,2,1,0:T(8,128)(2,1)}, u32[]{:S(2)}) copy-start(bf16[64,2,16,256]{3,2,1,0:T(8,128)(2,1)} %param.17) | copy-start | bytes 3145732
  7.2 21.3 %copy-start.5 = (s32[1536]{0:T(1024)S(1)}, s32[1536]{0:T(1024)}, u32[]{:S(2)}) copy-start(s32[1536]{0:T(1024)} %constant.105.clone.1) | copy-start | bytes 18436
  7.2 12.8 %copy-start.1 = (bf16[1024,256]{1,0:T(8,128)(2,1)S(1)}, bf16[1024,256]{1,0:T(8,128)(2,1)}, u32[]{:S(2)}) copy-start(bf16[1024,256]{1,0:T(8,128)(2,1)} %param.10) | copy-start | bytes 1572868
  7.2 19.0 %copy-start.2 = (bf16[512,256]{1,0:T(8,128)(2,1)S(1)}, bf16[512,256]{1,0:T(8,128)(2,1)}, u32[]{:S(2)}) copy-start(bf16[512,256]{1,0:T(8,128)(2,1)} %param.14) | copy-start | bytes 786436
  7.2 20.0 %copy-start.3 = (bf16[512,256]{1,0:T(8,128)(2,1)S(1)}, bf16[512,256]{1,0:T(8,128)(2,1)}, u32[]{:S(2)}) copy-start(bf16[512,256]{1,0:T(8,128)(2,1)} %param.15) | copy-start | bytes 786436
  7.2 21.2 %copy-start.6 = (s32[1,512]{1,0:T(1,128)S(1)}, s32[1,512]{1,0:T(1,128)}, u32[]{:S(2)}) copy-start(s32[1,512]{1,0:T(1,128)} %param.16) | copy-start | bytes 6148
  7.2 130.0 %all-gather.2.cloned.1.call-start = ((), (), s32[]{:S(2)}) async-start(), calls=%async_computation.3 | async-start | bytes 17825792 | tf_op jit(solution)/shard_map/all_gather | solution.py:75
  12.8 28.6 %all-to-all-start = ((bf16[16,4,2,16,256]{4,3,2,1,0:T(8,128)(2,1)}), bf16[16,4,2,16,256]{4,3,2,1,0:T(8,128)(2,1)S(1)}, u32[]{:S(2)}, u32[]{:S(2)}) async-start(bf16[16,4,2,16,256]{4,3,2,1,0:T(8,128)(2,1)} %bitcast.9), calls=%async_computation | async-start | bytes 2097152 | tf_op jit(solution)/shard_map/all_to_all | solution.py:151
  20.7 41.6 %collective-permute-start = (bf16[512,256]{1,0:T(8,128)(2,1)}, bf16[512,256]{1,0:T(8,128)(2,1)}, u32[]{:S(2)}, u32[]{:S(2)}) collective-permute-start(bf16[512,256]{1,0:T(8,128)(2,1)} %get-tuple-element.14), channel_id=1, source_target_pairs={{0,112},{8,120},{16,96},{24,104},{32,80},{40,88},{48,64},{56,72},{... | collective-permute-start | bytes 786440 | tf_op jit(solution)/shard_map/ppermute | solution.py:85
  44.4 6.6 %copy-start.4 = (bf16[512,2,128]{2,0,1:T(8,128)(2,1)S(1)}, bf16[512,2,128]{2,0,1:T(8,128)(2,1)}, u32[]{:S(2)}) copy-start(bf16[512,2,128]{2,0,1:T(8,128)(2,1)} %copy.75) | copy-start | bytes 786436
  55.5 13.5 %all-to-all-start.1 = ((bf16[8,64,256]{2,1,0:T(8,128)(2,1)}), bf16[8,64,256]{2,1,0:T(8,128)(2,1)S(1)}, u32[]{:S(2)}, u32[]{:S(2)}) async-start(bf16[8,64,256]{2,1,0:T(8,128)(2,1)} %convert_element_type.30), calls=%async_computation.1 | async-start | bytes 524288 | tf_op jit(solution)/shard_map/all_to_all | solution.py:195
  175.4 12.2 %collective-permute-start.1 = (bf16[512,256]{1,0:T(8,128)(2,1)S(1)}, bf16[512,256]{1,0:T(8,128)(2,1)S(1)}, u32[]{:S(2)}, u32[]{:S(2)}) collective-permute-start(bf16[512,256]{1,0:T(8,128)(2,1)S(1)} %get-tuple-element.12), channel_id=1, source_target_pairs={{0,112},{8,120},{16,96},{24,104},{32,80},{40,88},{48,64},{56,72},{... | collective-permute-start | bytes 786440 | tf_op jit(solution)/shard_map/ppermute | solution.py:128
Sparse Core Ops, SparseCore 0:
  10.5 126.6 all-gather.1

commit v15 on v12

--- a/solution.py
+++ b/solution.py
@@ -20,7 +20,7 @@
     return q_tile, step - q_tile * pos_ref[2]
 
 
-def flash_body(pos_ref, q_ref, k_ref, v_ref, o_ref, m_sc, l_sc, acc_sc, *, heads, tq, tk):
+def flash_body(pos_ref, q_ref, k_ref, v_ref, own_ref, lent_ref, m_sc, l_sc, acc_sc, *, heads, tq, tk):
     q_tile, k_tile = tile_of_step(pl.program_id(0), pos_ref)
     first_query = pos_ref[q_tile]
     last_tile = (first_query + tq - 1) // tk
@@ -63,10 +63,12 @@
     def _():
         fold(True)
 
-    @pl.when(k_tile == last_tile)
-    def _():
-        for h in range(heads):
-            o_ref[:, h * HD:(h + 1) * HD] = (acc_sc[h] / l_sc[h]).T.astype(o_ref.dtype)
+    for tile, o_ref in ((0, own_ref), (1, lent_ref)):
+
+        @pl.when((k_tile == last_tile) & (q_tile == tile))
+        def _():
+            for h in range(heads):
+                o_ref[:, h * HD:(h + 1) * HD] = (acc_sc[h] / l_sc[h]).T.astype(o_ref.dtype)
 
 
 def prompt_attention(queries, block_index, long_k, long_v, early=None):
@@ -106,7 +108,10 @@
     body = functools.partial(flash_body, heads=heads_dev, tq=tq, tk=tk)
     result = pl.pallas_call(
         body,
-        out_shape=jax.ShapeDtypeStruct((row_count, width), jnp.bfloat16),
+        out_shape=(
+            jax.ShapeDtypeStruct((tq, width), jnp.bfloat16),
+            jax.ShapeDtypeStruct((tq, width), jnp.bfloat16),
+        ),
         grid_spec=pltpu.PrefetchScalarGridSpec(
             num_scalar_prefetch=1,
             grid=(step_count,),
@@ -115,7 +120,10 @@
                 pl.BlockSpec((tk, width), kv_map(0)),
                 pl.BlockSpec((tk, width), kv_map(1)),
             ],
-            out_specs=pl.BlockSpec((tq, width), q_map),
+            out_specs=[
+                pl.BlockSpec((tq, width), lambda step, pos_ref: (0, 0)),
+                pl.BlockSpec((tq, width), lambda step, pos_ref: (0, 0)),
+            ],
             scratch_shapes=[
                 pltpu.VMEM((heads_dev, 1, tq), jnp.float32),
                 pltpu.VMEM((heads_dev, 1, tq), jnp.float32),
@@ -124,7 +132,8 @@
         ),
         compiler_params=pltpu.CompilerParams(dimension_semantics=("arbitrary",)),
     )(tile_pos, jnp.concatenate([queries[:tq], partner_half], 0), kv_piece, kv_piece)
-    merged = jnp.concatenate([result[:tq], lax.ppermute(result[tq:], "blk", mirror)], 0)
+    own_rows, lent_rows = result
+    merged = jnp.concatenate([own_rows, lax.ppermute(lent_rows, "blk", mirror)], 0)
     return merged, early
 
 

time: 214 us -> 214 us (level)
  no operation moved by 1% of the time
where the time goes in v15:
time: 214 us; the launch traced here: 213 us
  waiting for transfers between devices  89.1 us (42%)
  Pallas kernels  37 us (17%)
  matrix products  22.3 us (10%)
  starting transfers between devices  18.5 us (9%)
  between operations  14.3 us (7%)
  blocking collectives  13.9 us (6%)
  local copies, waits for them, and re-layouts  9.9 us (5%)
  other arithmetic  8.28 us (4%)
    all_gather x1, waiting for transfers between devices, prompt_attention(): lax.all_gather(jnp.concatenate([long_k, long_v], 1), 'blk', axis=0, tiled...  61 us
    pallas_call x1, Pallas kernels, prompt_attention(): pl.pallas_call(body, out_shape=(jax.ShapeDtypeStruct((tq, width), jnp.bfl...  37 us
    all_to_all x1, blocking collectives, per_device(): long_rows = lax.all_to_all(long_attn, 'req', 0, 1, tiled=True)  13.9 us
    all_to_all x1, waiting for transfers between devices, pack_attention(): lax.all_to_all(outgoing, 'blk', split_axis=0, concat_axis=0, tiled=True)  11.6 us
    ppermute x1, waiting for transfers between devices, prompt_attention(): lax.ppermute(lent_rows, 'blk', mirror)  11.5 us
    dot_general x1, matrix products, per_device(): jnp.dot(short_rows, w_out, preferred_element_type=jnp.float32)  7.31 us
    all_to_all x1, starting transfers between devices, pack_attention(): lax.all_to_all(outgoing, 'blk', split_axis=0, concat_axis=0, tiled=True)  7.25 us
    sub x1, matrix products, pack_attention(): weights = jnp.where(allowed, jnp.exp(scores - row_max[..., None]), 0.0)  6.24 us
  transfers between devices with their start and end apart: 5, of which 4 were waited for; matrix products, arithmetic and copies ran while one was open for 15% of the time, Pallas kernels for 0%

profile of v15, /device:TPU:0, one launch (start us, length us, event | category | flops | bytes accessed | tf_op | source)
XLA Modules:
  0.0 213.3 jit_solution(2507166854914353314)
XLA Ops:
  7.2 0.0 copy-start
  7.2 0.0 copy-start.6
  7.2 0.0 all-gather.2.cloned.1.call-start
  7.2 2.3 %pad_maximum_fusion = bf16[1024,512]{1,0:T(8,128)(2,1)} fusion(bf16[1024,256]{1,0:T(8,128)(2,1)} %param.12, bf16[1024,256]{1,0:T(8,128)(2,1)} %param.11), kind=kLoop, calls=%fused_computation.18 | loop fusion | flops 2097152 | bytes 2097152 | tf_op jit(solution)/shard_map/concatenate | solution.py:77
  9.6 0.0 copy-start.2
  9.6 0.0 copy-start.3
  9.6 0.0 all-gather.2.cloned.1.call-update
  9.6 0.0 copy-done.6
  9.6 0.1 copy.47
  9.7 0.1 copy.48
  9.8 0.2 reduce_window_sum.11
  10.0 0.1 select_reduce_fusion
  10.2 0.1 copy.52
  10.3 0.1 reshape.234
  10.4 0.0 copy-done
  10.4 0.0 copy-start.4
  10.4 1.6 gather_fusion
  12.0 0.0 copy-start.8
  12.0 0.0 copy-start.7
  12.0 7.2 %all-to-all-start = ((bf16[16,4,2,16,256]{4,3,2,1,0:T(8,128)(2,1)}), bf16[16,4,2,16,256]{4,3,2,1,0:T(8,128)(2,1)S(1)}, u32[]{:S(2)}, u32[]{:S(2)}) async-start(bf16[16,4,2,16,256]{4,3,2,1,0:T(8,128)(2,1)} %bitcast.6), calls=%async_computation | async-start | bytes 2097152 | tf_op jit(solution)/shard_map/all_to_all | solution.py:159
  19.3 0.0 copy-done.2
  19.3 0.7 fusion.47
  20.0 5.5 %collective-permute-start = (bf16[512,256]{1,0:T(8,128)(2,1)}, bf16[512,256]{1,0:T(8,128)(2,1)}, u32[]{:S(2)}, u32[]{:S(2)}) collective-permute-start(bf16[512,256]{1,0:T(8,128)(2,1)} %get-tuple-element.16), channel_id=1, source_target_pairs={{0,112},{8,120},{16,96},{24,104},{32,80},{40,88},{48,64},{56,72},{... | collective-permute-start | bytes 786440 | tf_op jit(solution)/shard_map/ppermute | solution.py:86
  25.6 0.0 copy-done.3
  25.6 0.1 copy.53
  25.7 0.9 copy.55
  26.6 0.0 copy-done.4
  26.6 0.1 copy.57
  26.7 0.9 copy.59
  27.6 0.2 convert_reduce_fusion
  27.8 0.0 copy-done.8
  27.8 0.0 copy-done.7
  27.8 1.9 fusion.6
  29.7 11.6 %all-to-all-done = bf16[16,4,2,16,256]{4,3,2,1,0:T(8,128)(2,1)S(1)} async-done(((bf16[16,4,2,16,256]{4,3,2,1,0:T(8,128)(2,1)}), bf16[16,4,2,16,256]{4,3,2,1,0:T(8,128)(2,1)S(1)}, u32[]{:S(2)}, u32[]{:S(2)}) %all-to-all-start) | async-done | bytes 1048608 | tf_op jit(solution)/shard_map/all_to_all | solution.py:159
  41.4 0.6 gather_fusion.1
  42.0 0.9 fusion.46
  42.9 0.0 copy-start.1
  42.9 1.2 concatenate.32
  44.1 0.9 copy.54
  45.0 0.1 concatenate.35
  45.1 0.1 copy.58
  45.2 0.0 copy-done.1
  45.2 0.0 copy-start.5
  45.2 6.2 %fusion.48 = (f32[2,512]{1,0:T(2,128)S(1)}, bf16[2,512,1536]{1,2,0:T(8,128)(2,1)}) fusion(pred[512,1536]{0,1:T(8,128)(4,1)S(1)} %copy-done.1, bf16[512,2,128]{2,0,1:T(8,128)(2,1)} %copy.55, bf16[1024,2,128]{2,0,1:T(8,128)(2,1)} %copy.54, bf16[512,256]{1,0:T(8,128)(2,1)} %param.13), kind=kOutput, calls=%fused_computation.73 | convolution fusion | flops 413664768 | bytes 4984832 | tf_op jit(solution)/shard_map/sub | solution.py:183
  51.5 0.0 copy-done.5
  51.5 3.3 %fusion.14 = bf16[512,2,128]{2,0,1:T(8,128)(2,1)S(1)} fusion(bf16[2,512,1536]{1,2,0:T(8,128)(2,1)} %get-tuple-element.18, bf16[512,2,128]{2,0,1:T(8,128)(2,1)S(1)} %copy-done.5, bf16[1024,2,128]{2,0,1:T(8,128)(2,1)S(1)} %copy.58, f32[512,2]{0,1:T(2,128)S(1)} %bitcast.74), kind=kOutput, calls=%fused_computation.17 | convolution fusion | flops 404488192 | bytes 4198400 | tf_op jit(solution)/shard_map/hqk,khd->hqd/dot_general | solution.py:185
  54.8 0.3 copy.61
  55.0 0.9 convert_element_type.30
  55.9 4.9 %all-to-all-start.1 = ((bf16[8,64,256]{2,1,0:T(8,128)(2,1)}), bf16[8,64,256]{2,1,0:T(8,128)(2,1)S(1)}, u32[]{:S(2)}, u32[]{:S(2)}) async-start(bf16[8,64,256]{2,1,0:T(8,128)(2,1)} %convert_element_type.30), calls=%async_computation.1 | async-start | bytes 524288 | tf_op jit(solution)/shard_map/all_to_all | solution.py:203
  60.8 0.6 pad_add_fusion.1.pos_ref
  61.5 0.0 collective-permute-done
  61.5 1.8 pad_maximum_fusion.2.q_ref
  63.2 4.9 %all-to-all-done.1 = bf16[8,64,256]{2,1,0:T(8,128)(2,1)S(1)} async-done(((bf16[8,64,256]{2,1,0:T(8,128)(2,1)}), bf16[8,64,256]{2,1,0:T(8,128)(2,1)S(1)}, u32[]{:S(2)}, u32[]{:S(2)}) %all-to-all-start.1) | async-done | bytes 262176 | tf_op jit(solution)/shard_map/all_to_all | solution.py:203
  68.1 7.3 %convolution_convert_fusion.1 = bf16[64,2048]{1,0:T(8,128)(2,1)} fusion(bf16[64,2048]{1,0:T(8,128)(2,1)S(1)} %bitcast.66, bf16[2048,2048]{1,0:T(8,128)(2,1)} %param.19), kind=kOutput, calls=%fused_computation.14 | convolution fusion | flops 537001984 | bytes 8912896 | tf_op jit(solution)/shard_map/dot_general | solution.py:204
  75.4 61.0 %all-gather.2.cloned.1.call-done.k_ref.v_ref = bf16[16384,512]{1,0:T(8,128)(2,1)} async-done(((bf16[1024,512]{1,0:T(8,128)(2,1)}), bf16[16384,512]{1,0:T(8,128)(2,1)}) %all-gather.2.cloned.1.call-update) | async-done | bytes 16777232 | tf_op jit(solution)/shard_map/all_gather | solution.py:77
  136.5 37.0 %shard_map.113 = (bf16[512,256]{1,0:T(8,128)(2,1)}, bf16[512,256]{1,0:T(8,128)(2,1)}) custom-call(s32[3]{0:T(128)} %pad_add_fusion.1.pos_ref, bf16[1024,256]{1,0:T(8,128)(2,1)} %pad_maximum_fusion.2.q_ref, bf16[16384,512]{1,0:T(8,128)(2,1)} %all-gather.2.cloned.1.call-done.k_ref.v_ref, bf16[16384,512]{1,0:T(8,128)(2,1)} %all-gather.2.cloned.1.call-done.k_ref.v_ref), custom_call_target="tpu_custom_call" | custom-call | tf_op jit(solution)/shard_map/pallas_call | solution.py:109
  173.5 0.8 collective-permute-start.1
  174.3 11.5 %collective-permute-done.1 = bf16[512,256]{1,0:T(8,128)(2,1)S(1)} collective-permute-done((bf16[512,256]{1,0:T(8,128)(2,1)}, bf16[512,256]{1,0:T(8,128)(2,1)S(1)}, u32[]{:S(2)}, u32[]{:S(2)}) %collective-permute-start.1) | collective-permute-done | bytes 262176 | tf_op jit(solution)/shard_map/ppermute | solution.py:136
  185.8 1.0 pad_maximum_fusion.3
  186.8 0.3 copy.63
  187.1 13.9 %all_to_all.40 = bf16[8,128,256]{1,2,0:T(8,128)(2,1)S(1)} all-to-all(bf16[8,128,256]{1,2,0:T(8,128)(2,1)S(1)} %copy.63), channel_id=1, replica_groups=mesh['blk'=16,'req'=8] {'req'}, dimensions={0} | all-to-all | bytes 1048576 | tf_op jit(solution)/shard_map/all_to_all | solution.py:206
  200.9 5.5 %convolution_convert_fusion = bf16[128,2048]{1,0:T(8,128)(2,1)} fusion(bf16[128,2048]{0,1:T(8,128)(2,1)S(1)} %bitcast.64, bf16[2048,2048]{1,0:T(8,128)(2,1)} %param.19), kind=kOutput, calls=%fused_computation.13 | convolution fusion | flops 1074003968 | bytes 9437184 | tf_op jit(solution)/shard_map/dot_general | solution.py:207
  (10 shorter events, 0.1 us)
Async XLA Ops:
  7.2 3.2 %copy-start = (bf16[64,2,16,256]{3,2,1,0:T(8,128)(2,1)S(1)}, bf16[64,2,16,256]{3,2,1,0:T(8,128)(2,1)}, u32[]{:S(2)}) copy-start(bf16[64,2,16,256]{3,2,1,0:T(8,128)(2,1)} %param.17) | copy-start | bytes 3145732
  7.2 2.4 %copy-start.6 = (s32[16,16,4]{1,2,0:T(4,128)S(1)}, s32[16,16,4]{1,2,0:T(4,128)}, u32[]{:S(2)}) copy-start(s32[16,16,4]{1,2,0:T(4,128)} %param.18) | copy-start | bytes 12292
  7.2 129.3 %all-gather.2.cloned.1.call-start = ((), (), s32[]{:S(2)}) async-start(), calls=%async_computation.3 | async-start | bytes 17825792 | tf_op jit(solution)/shard_map/all_gather | solution.py:77
  9.6 9.7 %copy-start.2 = (bf16[1024,256]{1,0:T(8,128)(2,1)S(1)}, bf16[1024,256]{1,0:T(8,128)(2,1)}, u32[]{:S(2)}) copy-start(bf16[1024,256]{1,0:T(8,128)(2,1)} %param.10) | copy-start | bytes 1572868
  9.6 16.0 %copy-start.3 = (bf16[512,256]{1,0:T(8,128)(2,1)S(1)}, bf16[512,256]{1,0:T(8,128)(2,1)}, u32[]{:S(2)}) copy-start(bf16[512,256]{1,0:T(8,128)(2,1)} %param.14) | copy-start | bytes 786436
  10.4 16.2 %copy-start.4 = (bf16[512,256]{1,0:T(8,128)(2,1)S(1)}, bf16[512,256]{1,0:T(8,128)(2,1)}, u32[]{:S(2)}) copy-start(bf16[512,256]{1,0:T(8,128)(2,1)} %param.15) | copy-start | bytes 786436
  12.0 15.8 %copy-start.8 = (s32[1,512]{1,0:T(1,128)S(1)}, s32[1,512]{1,0:T(1,128)}, u32[]{:S(2)}) copy-start(s32[1,512]{1,0:T(1,128)} %param.16) | copy-start | bytes 6148
  12.0 15.8 %copy-start.7 = (s32[1536]{0:T(1024)S(1)}, s32[1536]{0:T(1024)}, u32[]{:S(2)}) copy-start(s32[1536]{0:T(1024)} %constant.105.clone.1) | copy-start | bytes 18436
  12.0 29.4 %all-to-all-start = ((bf16[16,4,2,16,256]{4,3,2,1,0:T(8,128)(2,1)}), bf16[16,4,2,16,256]{4,3,2,1,0:T(8,128)(2,1)S(1)}, u32[]{:S(2)}, u32[]{:S(2)}) async-start(bf16[16,4,2,16,256]{4,3,2,1,0:T(8,128)(2,1)} %bitcast.6), calls=%async_computation | async-start | bytes 2097152 | tf_op jit(solution)/shard_map/all_to_all | solution.py:159
  20.0 41.4 %collective-permute-start = (bf16[512,256]{1,0:T(8,128)(2,1)}, bf16[512,256]{1,0:T(8,128)(2,1)}, u32[]{:S(2)}, u32[]{:S(2)}) collective-permute-start(bf16[512,256]{1,0:T(8,128)(2,1)} %get-tuple-element.16), channel_id=1, source_target_pairs={{0,112},{8,120},{16,96},{24,104},{32,80},{40,88},{48,64},{56,72},{... | collective-permute-start | bytes 786440 | tf_op jit(solution)/shard_map/ppermute | solution.py:86
  42.9 2.3 %copy-start.1 = (pred[512,1536]{0,1:T(8,128)(4,1)S(1)}, pred[512,1536]{0,1:T(8,128)(4,1)}, u32[]{:S(2)}) copy-start(pred[512,1536]{0,1:T(8,128)(4,1)} %fusion.6) | copy-start | bytes 2359300
  45.2 6.3 %copy-start.5 = (bf16[512,2,128]{2,0,1:T(8,128)(2,1)S(1)}, bf16[512,2,128]{2,0,1:T(8,128)(2,1)}, u32[]{:S(2)}) copy-start(bf16[512,2,128]{2,0,1:T(8,128)(2,1)} %copy.59) | copy-start | bytes 786436
  55.9 12.2 %all-to-all-start.1 = ((bf16[8,64,256]{2,1,0:T(8,128)(2,1)}), bf16[8,64,256]{2,1,0:T(8,128)(2,1)S(1)}, u32[]{:S(2)}, u32[]{:S(2)}) async-start(bf16[8,64,256]{2,1,0:T(8,128)(2,1)} %convert_element_type.30), calls=%async_computation.1 | async-start | bytes 524288 | tf_op jit(solution)/shard_map/all_to_all | solution.py:203
  173.5 12.3 %collective-permute-start.1 = (bf16[512,256]{1,0:T(8,128)(2,1)}, bf16[512,256]{1,0:T(8,128)(2,1)S(1)}, u32[]{:S(2)}, u32[]{:S(2)}) collective-permute-start(bf16[512,256]{1,0:T(8,128)(2,1)} %get-tuple-element.8), channel_id=1, source_target_pairs={{0,112},{8,120},{16,96},{24,104},{32,80},{40,88},{48,64},{56,72},{... | collective-permute-start | bytes 786440 | tf_op jit(solution)/shard_map/ppermute | solution.py:136
Sparse Core Ops, SparseCore 0:
  10.4 126.0 all-gather.1

commit v16 on v12

--- a/solution.py
+++ b/solution.py
@@ -72,16 +72,19 @@
 def prompt_attention(queries, block_index, long_k, long_v, early=None):
     row_count, width = queries.shape
     heads_dev = width // HD
-    kv_piece = lax.all_gather(jnp.concatenate([long_k, long_v], 1), "blk", axis=0, tiled=True)
-    if early is not None:
-        kv_piece, early = lax.optimization_barrier((kv_piece, early))
-    piece_rows = kv_piece.shape[0]
     block_count = lax.axis_size("blk")
     tq = row_count // 2
     chip_count = block_count // 2
     mirror = [(src, 2 * (chip_count - 1 - src // 2) + src % 2) for src in range(block_count)]
     partner_block = 2 * (chip_count - 1 - block_index // 2) + block_index % 2
     partner_half = lax.ppermute(queries[tq:], "blk", mirror)
+    own_kv, partner_half = lax.optimization_barrier(
+        (jnp.concatenate([long_k, long_v], 1), partner_half)
+    )
+    kv_piece = lax.all_gather(own_kv, "blk", axis=0, tiled=True)
+    if early is not None:
+        kv_piece, early = lax.optimization_barrier((kv_piece, early))
+    piece_rows = kv_piece.shape[0]
     tk = min(piece_rows, 2 * row_count)
     own_first = block_index * row_count
     lent_first = partner_block * row_count + tq

time: 214 us -> 220 us (1.028)
  waiting for transfers between devices: 88.8 us -> 94.6 us
  starting transfers between devices: 18.6 us -> 21.1 us
    all_gather x1, waiting for transfers between devices: 61 us -> 55.4 us  [prompt_attention(): kv_piece = lax.all_gather(own_kv, 'blk', axis=0, tiled=True)]
    all_to_all x1, waiting for transfers between devices: 11.6 us -> 16.8 us  [pack_attention(): lax.all_to_all(outgoing, 'blk', split_axis=0, concat_axis=0, tiled=True)]
    ppermute x1, waiting for transfers between devices: 0.01 us -> 4.04 us  [prompt_attention(): partner_half = lax.ppermute(queries[tq:], 'blk', mirror)]
    all_to_all x1, waiting for transfers between devices: 4.87 us -> 8.38 us  [per_device(): short_rows = lax.all_to_all(short_attn, 'req', 0, 1, tiled=True)]
  transfers between devices with their start and end apart: 5 -> 5, of which waited for: 4 -> 5; matrix products, arithmetic and copies ran while one was open for 15% -> 14% of each run, Pallas kernels for 0% -> 0%
where the time goes in v16:
time: 220 us; the launch traced here: 219 us
  waiting for transfers between devices  94.6 us (43%)
  Pallas kernels  37 us (17%)
  starting transfers between devices  21.1 us (10%)
  matrix products  20.7 us (9%)
  between operations  14.3 us (6%)
  blocking collectives  13.9 us (6%)
  local copies, waits for them, and re-layouts  11.4 us (5%)
  other arithmetic  6.23 us (3%)
    all_gather x1, waiting for transfers between devices, prompt_attention(): kv_piece = lax.all_gather(own_kv, 'blk', axis=0, tiled=True)  55.4 us
    pallas_call x1, Pallas kernels, prompt_attention(): pl.pallas_call(body, out_shape=jax.ShapeDtypeStruct((row_count, width), j...  37 us
    all_to_all x1, waiting for transfers between devices, pack_attention(): lax.all_to_all(outgoing, 'blk', split_axis=0, concat_axis=0, tiled=True)  16.8 us
    all_to_all x1, blocking collectives, per_device(): long_rows = lax.all_to_all(long_attn, 'req', 0, 1, tiled=True)  13.9 us
    ppermute x1, waiting for transfers between devices, prompt_attention(): lax.ppermute(result[tq:], 'blk', mirror)  10 us
    all_to_all x1, waiting for transfers between devices, per_device(): short_rows = lax.all_to_all(short_attn, 'req', 0, 1, tiled=True)  8.38 us
    all_to_all x1, starting transfers between devices, pack_attention(): lax.all_to_all(outgoing, 'blk', split_axis=0, concat_axis=0, tiled=True)  6.73 us
    all_to_all x1, starting transfers between devices, per_device(): short_rows = lax.all_to_all(short_attn, 'req', 0, 1, tiled=True)  6.6 us
  transfers between devices with their start and end apart: 5, of which 5 were waited for; matrix products, arithmetic and copies ran while one was open for 14% of the time, Pallas kernels for 0%

profile of v16, /device:TPU:0, one launch (start us, length us, event | category | flops | bytes accessed | tf_op | source)
XLA Modules:
  0.0 219.2 jit_solution(4101985307012998480)
XLA Ops:
  7.2 0.0 copy-start
  7.2 0.0 copy-start.7
  7.2 0.0 all-gather.2.cloned.1.call-start
  7.2 1.1 fusion.48
  8.4 5.6 %collective-permute-start = (bf16[512,256]{1,0:T(8,128)(2,1)S(1)}, bf16[512,256]{1,0:T(8,128)(2,1)S(1)}, u32[]{:S(2)}, u32[]{:S(2)}) collective-permute-start(bf16[512,256]{1,0:T(8,128)(2,1)S(1)} %get-tuple-element.18), channel_id=1, source_target_pairs={{0,112},{8,120},{16,96},{24,104},{32,80},{40,88},{48,64},{56,72},{... | collective-permute-start | bytes 786440 | tf_op jit(solution)/shard_map/ppermute | solution.py:80
  13.9 2.3 %pad_maximum_fusion = bf16[1024,512]{1,0:T(8,128)(2,1)} fusion(bf16[1024,256]{1,0:T(8,128)(2,1)} %param.12, bf16[1024,256]{1,0:T(8,128)(2,1)} %param.11), kind=kLoop, calls=%fused_computation.18 | loop fusion | flops 2097152 | bytes 2097152 | tf_op jit(solution)/shard_map/concatenate | solution.py:82
  16.2 0.0 copy-start.2
  16.2 0.0 copy-start.3
  16.2 4.0 %collective-permute-done = bf16[512,256]{1,0:T(8,128)(2,1)S(1)} collective-permute-done((bf16[512,256]{1,0:T(8,128)(2,1)S(1)}, bf16[512,256]{1,0:T(8,128)(2,1)S(1)}, u32[]{:S(2)}, u32[]{:S(2)}) %collective-permute-start) | collective-permute-done | bytes 262176 | tf_op jit(solution)/shard_map/ppermute | solution.py:80
  20.2 0.0 copy-start.5
  20.2 0.0 all-gather.2.cloned.1.call-update
  20.3 0.0 copy-done.7
  20.3 0.1 copy.47
  20.4 0.1 copy.48
  20.5 0.2 reduce_window_sum.11
  20.7 0.1 select_reduce_fusion
  20.8 0.1 copy.52
  20.9 0.1 reshape.234
  21.0 0.0 copy-done
  21.1 0.0 copy-start.9
  21.1 0.0 copy-start.8
  21.1 1.6 gather_fusion
  22.7 6.7 %all-to-all-start = ((bf16[16,4,2,16,256]{4,3,2,1,0:T(8,128)(2,1)}), bf16[16,4,2,16,256]{4,3,2,1,0:T(8,128)(2,1)S(1)}, u32[]{:S(2)}, u32[]{:S(2)}) async-start(bf16[16,4,2,16,256]{4,3,2,1,0:T(8,128)(2,1)} %bitcast.6), calls=%async_computation | async-start | bytes 2097152 | tf_op jit(solution)/shard_map/all_to_all | solution.py:153
  29.4 0.0 copy-done.2
  29.4 0.1 copy.53
  29.6 0.8 copy.55
  30.4 0.0 copy-done.5
  30.4 0.0 copy-done.3
  30.4 0.1 copy.57
  30.6 0.9 copy.59
  31.4 0.2 convert_reduce_fusion
  31.7 0.0 copy-done.9
  31.7 0.0 copy-done.8
  31.7 1.9 fusion.6
  33.6 16.8 %all-to-all-done = bf16[16,4,2,16,256]{4,3,2,1,0:T(8,128)(2,1)S(1)} async-done(((bf16[16,4,2,16,256]{4,3,2,1,0:T(8,128)(2,1)}), bf16[16,4,2,16,256]{4,3,2,1,0:T(8,128)(2,1)S(1)}, u32[]{:S(2)}, u32[]{:S(2)}) %all-to-all-start) | async-done | bytes 1048608 | tf_op jit(solution)/shard_map/all_to_all | solution.py:153
  50.4 0.6 gather_fusion.1
  51.0 0.9 fusion.46
  51.9 0.0 copy-start.1
  51.9 1.2 concatenate.32
  53.2 0.9 copy.54
  54.0 0.1 concatenate.35
  54.1 0.1 copy.58
  54.2 0.0 copy-done.1
  54.2 0.0 copy-start.4
  54.2 6.2 %fusion.49 = (f32[2,512]{1,0:T(2,128)S(1)}, bf16[2,512,1536]{1,2,0:T(8,128)(2,1)}) fusion(pred[512,1536]{0,1:T(8,128)(4,1)S(1)} %copy-done.1, bf16[512,2,128]{2,0,1:T(8,128)(2,1)} %copy.55, bf16[1024,2,128]{2,0,1:T(8,128)(2,1)} %copy.54, bf16[512,256]{1,0:T(8,128)(2,1)} %param.13), kind=kOutput, calls=%fused_computation.74 | convolution fusion | flops 413664768 | bytes 4984832 | tf_op jit(solution)/shard_map/sub | solution.py:177
  60.5 0.0 copy-done.4
  60.5 0.0 copy-start.6
  60.5 3.3 %fusion.14 = bf16[512,2,128]{2,0,1:T(8,128)(2,1)S(1)} fusion(bf16[2,512,1536]{1,2,0:T(8,128)(2,1)} %get-tuple-element.20, bf16[512,2,128]{2,0,1:T(8,128)(2,1)S(1)} %copy-done.4, bf16[1024,2,128]{2,0,1:T(8,128)(2,1)S(1)} %copy.58, f32[512,2]{0,1:T(2,128)S(1)} %bitcast.74), kind=kOutput, calls=%fused_computation.17 | convolution fusion | flops 404488192 | bytes 4198400 | tf_op jit(solution)/shard_map/hqk,khd->hqd/dot_general | solution.py:179
  63.8 0.3 copy.61
  64.1 0.9 convert_element_type.30
  65.0 6.6 %all-to-all-start.1 = ((bf16[8,64,256]{2,1,0:T(8,128)(2,1)}), bf16[8,64,256]{2,1,0:T(8,128)(2,1)S(1)}, u32[]{:S(2)}, u32[]{:S(2)}) async-start(bf16[8,64,256]{2,1,0:T(8,128)(2,1)} %convert_element_type.30), calls=%async_computation.1 | async-start | bytes 524288 | tf_op jit(solution)/shard_map/all_to_all | solution.py:197
  71.6 0.6 pad_add_fusion.1.pos_ref
  72.2 0.0 copy-done.6
  72.2 0.8 pad_maximum_fusion.2.q_ref
  73.0 8.4 %all-to-all-done.1 = bf16[8,64,256]{2,1,0:T(8,128)(2,1)S(1)} async-done(((bf16[8,64,256]{2,1,0:T(8,128)(2,1)}), bf16[8,64,256]{2,1,0:T(8,128)(2,1)S(1)}, u32[]{:S(2)}, u32[]{:S(2)}) %all-to-all-start.1) | async-done | bytes 262176 | tf_op jit(solution)/shard_map/all_to_all | solution.py:197
  81.4 5.7 %convolution_convert_fusion.1 = bf16[64,2048]{1,0:T(8,128)(2,1)} fusion(bf16[64,2048]{1,0:T(8,128)(2,1)S(1)} %bitcast.66, bf16[2048,2048]{1,0:T(8,128)(2,1)} %param.19), kind=kOutput, calls=%fused_computation.14 | convolution fusion | flops 537001984 | bytes 8912896 | tf_op jit(solution)/shard_map/dot_general | solution.py:198
  87.0 55.4 %all-gather.2.cloned.1.call-done.k_ref.v_ref = bf16[16384,512]{1,0:T(8,128)(2,1)} async-done(((bf16[1024,512]{1,0:T(8,128)(2,1)}), bf16[16384,512]{1,0:T(8,128)(2,1)}) %all-gather.2.cloned.1.call-update) | async-done | bytes 16777232 | tf_op jit(solution)/shard_map/all_gather | solution.py:84
  142.4 37.0 %shard_map.113 = bf16[1024,256]{1,0:T(8,128)(2,1)} custom-call(s32[3]{0:T(128)} %pad_add_fusion.1.pos_ref, bf16[1024,256]{1,0:T(8,128)(2,1)} %pad_maximum_fusion.2.q_ref, bf16[16384,512]{1,0:T(8,128)(2,1)} %all-gather.2.cloned.1.call-done.k_ref.v_ref, bf16[16384,512]{1,0:T(8,128)(2,1)} %all-gather.2.cloned.1.call-done.k_ref.v_ref), custom_call_target="tpu_custom_call" | custom-call | tf_op jit(solution)/shard_map/pallas_call | solution.py:110
  179.4 1.1 fusion.47
  180.5 2.2 collective-permute-start.1
  182.6 10.0 %collective-permute-done.1 = bf16[512,256]{1,0:T(8,128)(2,1)S(1)} collective-permute-done((bf16[512,256]{1,0:T(8,128)(2,1)S(1)}, bf16[512,256]{1,0:T(8,128)(2,1)S(1)}, u32[]{:S(2)}, u32[]{:S(2)}) %collective-permute-start.1) | collective-permute-done | bytes 262176 | tf_op jit(solution)/shard_map/ppermute | solution.py:130
  192.7 0.3 copy.63
  192.9 13.9 %all_to_all.40 = bf16[8,128,256]{1,2,0:T(8,128)(2,1)S(1)} all-to-all(bf16[8,128,256]{1,2,0:T(8,128)(2,1)S(1)} %copy.63), channel_id=1, replica_groups=mesh['blk'=16,'req'=8] {'req'}, dimensions={0} | all-to-all | bytes 1048576 | tf_op jit(solution)/shard_map/all_to_all | solution.py:200
  206.9 5.5 %convolution_convert_fusion = bf16[128,2048]{1,0:T(8,128)(2,1)} fusion(bf16[128,2048]{0,1:T(8,128)(2,1)S(1)} %bitcast.64, bf16[2048,2048]{1,0:T(8,128)(2,1)} %param.19), kind=kOutput, calls=%fused_computation.13 | convolution fusion | flops 1074003968 | bytes 9437184 | tf_op jit(solution)/shard_map/dot_general | solution.py:201
  (11 shorter events, 0.1 us)
Async XLA Ops:
  7.2 13.9 %copy-start = (bf16[64,2,16,256]{3,2,1,0:T(8,128)(2,1)S(1)}, bf16[64,2,16,256]{3,2,1,0:T(8,128)(2,1)}, u32[]{:S(2)}) copy-start(bf16[64,2,16,256]{3,2,1,0:T(8,128)(2,1)} %param.17) | copy-start | bytes 3145732
  7.2 13.1 %copy-start.7 = (s32[16,16,4]{1,2,0:T(4,128)S(1)}, s32[16,16,4]{1,2,0:T(4,128)}, u32[]{:S(2)}) copy-start(s32[16,16,4]{1,2,0:T(4,128)} %param.18) | copy-start | bytes 12292
  7.2 135.2 %all-gather.2.cloned.1.call-start = ((), (), s32[]{:S(2)}) async-start(), calls=%async_computation.3 | async-start | bytes 17825792 | tf_op jit(solution)/shard_map/all_gather | solution.py:84
  8.4 11.9 %collective-permute-start = (bf16[512,256]{1,0:T(8,128)(2,1)S(1)}, bf16[512,256]{1,0:T(8,128)(2,1)S(1)}, u32[]{:S(2)}, u32[]{:S(2)}) collective-permute-start(bf16[512,256]{1,0:T(8,128)(2,1)S(1)} %get-tuple-element.18), channel_id=1, source_target_pairs={{0,112},{8,120},{16,96},{24,104},{32,80},{40,88},{48,64},{56,72},{... | collective-permute-start | bytes 786440 | tf_op jit(solution)/shard_map/ppermute | solution.py:80
  16.2 13.2 %copy-start.2 = (bf16[512,256]{1,0:T(8,128)(2,1)S(1)}, bf16[512,256]{1,0:T(8,128)(2,1)}, u32[]{:S(2)}) copy-start(bf16[512,256]{1,0:T(8,128)(2,1)} %param.14) | copy-start | bytes 786436
  16.2 14.2 %copy-start.3 = (bf16[512,256]{1,0:T(8,128)(2,1)S(1)}, bf16[512,256]{1,0:T(8,128)(2,1)}, u32[]{:S(2)}) copy-start(bf16[512,256]{1,0:T(8,128)(2,1)} %param.15) | copy-start | bytes 786436
  20.2 10.2 %copy-start.5 = (bf16[512,256]{1,0:T(8,128)(2,1)}, bf16[512,256]{1,0:T(8,128)(2,1)S(1)}, u32[]{:S(2)}) copy-start(bf16[512,256]{1,0:T(8,128)(2,1)S(1)} %collective-permute-done) | copy-start | bytes 786436
  21.1 10.6 %copy-start.9 = (s32[1,512]{1,0:T(1,128)S(1)}, s32[1,512]{1,0:T(1,128)}, u32[]{:S(2)}) copy-start(s32[1,512]{1,0:T(1,128)} %param.16) | copy-start | bytes 6148
  21.1 10.6 %copy-start.8 = (s32[1536]{0:T(1024)S(1)}, s32[1536]{0:T(1024)}, u32[]{:S(2)}) copy-start(s32[1536]{0:T(1024)} %constant.105.clone.1) | copy-start | bytes 18436
  22.7 27.7 %all-to-all-start = ((bf16[16,4,2,16,256]{4,3,2,1,0:T(8,128)(2,1)}), bf16[16,4,2,16,256]{4,3,2,1,0:T(8,128)(2,1)S(1)}, u32[]{:S(2)}, u32[]{:S(2)}) async-start(bf16[16,4,2,16,256]{4,3,2,1,0:T(8,128)(2,1)} %bitcast.6), calls=%async_computation | async-start | bytes 2097152 | tf_op jit(solution)/shard_map/all_to_all | solution.py:153
  51.9 2.3 %copy-start.1 = (pred[512,1536]{0,1:T(8,128)(4,1)S(1)}, pred[512,1536]{0,1:T(8,128)(4,1)}, u32[]{:S(2)}) copy-start(pred[512,1536]{0,1:T(8,128)(4,1)} %fusion.6) | copy-start | bytes 2359300
  54.2 6.3 %copy-start.4 = (bf16[512,2,128]{2,0,1:T(8,128)(2,1)S(1)}, bf16[512,2,128]{2,0,1:T(8,128)(2,1)}, u32[]{:S(2)}) copy-start(bf16[512,2,128]{2,0,1:T(8,128)(2,1)} %copy.59) | copy-start | bytes 786436
  60.5 11.7 %copy-start.6 = (bf16[512,256]{1,0:T(8,128)(2,1)S(1)}, bf16[512,256]{1,0:T(8,128)(2,1)}, u32[]{:S(2)}) copy-start(bf16[512,256]{1,0:T(8,128)(2,1)} %copy-done.5) | copy-start | bytes 786436
  65.0 16.4 %all-to-all-start.1 = ((bf16[8,64,256]{2,1,0:T(8,128)(2,1)}), bf16[8,64,256]{2,1,0:T(8,128)(2,1)S(1)}, u32[]{:S(2)}, u32[]{:S(2)}) async-start(bf16[8,64,256]{2,1,0:T(8,128)(2,1)} %convert_element_type.30), calls=%async_computation.1 | async-start | bytes 524288 | tf_op jit(solution)/shard_map/all_to_all | solution.py:197
  180.5 12.2 %collective-permute-start.1 = (bf16[512,256]{1,0:T(8,128)(2,1)S(1)}, bf16[512,256]{1,0:T(8,128)(2,1)S(1)}, u32[]{:S(2)}, u32[]{:S(2)}) collective-permute-start(bf16[512,256]{1,0:T(8,128)(2,1)S(1)} %get-tuple-element.16), channel_id=1, source_target_pairs={{0,112},{8,120},{16,96},{24,104},{32,80},{40,88},{48,64},{56,72},{... | collective-permute-start | bytes 786440 | tf_op jit(solution)/shard_map/ppermute | solution.py:130
Sparse Core Ops, SparseCore 0:
  20.4 122.0 all-gather.1

commit v17 on v11

--- a/solution.py
+++ b/solution.py
@@ -31,16 +31,16 @@
         l_sc[...] = jnp.zeros(l_sc.shape, jnp.float32)
         acc_sc[...] = jnp.zeros(acc_sc.shape, jnp.float32)
 
-    def fold(masked):
+    def fold(masked, keys=tk):
         for h in range(heads):
             cols = slice(h * HD, (h + 1) * HD)
             scores = lax.dot_general(
-                k_ref[:, cols], q_ref[:, cols], (((1,), (1,)), ((), ())),
+                k_ref[:keys, cols], q_ref[:, cols], (((1,), (1,)), ((), ())),
                 preferred_element_type=jnp.float32,
             ) * HD ** (-0.5)
             if masked:
-                key_pos = k_tile * tk + lax.broadcasted_iota(jnp.int32, (tk, tq), 0)
-                query_pos = first_query + lax.broadcasted_iota(jnp.int32, (tk, tq), 1)
+                key_pos = k_tile * tk + lax.broadcasted_iota(jnp.int32, (keys, tq), 0)
+                query_pos = first_query + lax.broadcasted_iota(jnp.int32, (keys, tq), 1)
                 scores = jnp.where(key_pos <= query_pos, scores, very_negative)
             run_max = m_sc[h]
             new_max = jnp.maximum(run_max, jnp.max(scores, axis=0, keepdims=True))
@@ -49,7 +49,7 @@
             l_sc[h] = l_sc[h] * factor + jnp.sum(weights, axis=0, keepdims=True)
             m_sc[h] = new_max
             acc_sc[h] = acc_sc[h] * factor + lax.dot_general(
-                v_ref[:, cols], weights.astype(jnp.bfloat16), (((0,), (0,)), ((), ())),
+                v_ref[:keys, cols], weights.astype(jnp.bfloat16), (((0,), (0,)), ((), ())),
                 preferred_element_type=jnp.float32,
             )
 
@@ -59,7 +59,13 @@
     def _():
         fold(False)
 
-    @pl.when(needs_mask)
+    half_only = k_tile * tk + tk // 2 > first_query + tq - 1
+
+    @pl.when(needs_mask & half_only)
+    def _():
+        fold(True, tk // 2)
+
+    @pl.when(needs_mask & jnp.logical_not(half_only))
     def _():
         fold(True)
 

time: 214 us -> 213 us (level)
  no operation moved by 1% of the time
where the time goes in v17:
time: 213 us; the launch traced here: 212 us
  waiting for transfers between devices  89 us (42%)
  Pallas kernels  35.5 us (17%)
  matrix products  22.3 us (10%)
  starting transfers between devices  18.2 us (9%)
  blocking collectives  14.6 us (7%)
  between operations  14.3 us (7%)
  local copies, waits for them, and re-layouts  11 us (5%)
  other arithmetic  7.33 us (3%)
    all_gather x1, waiting for transfers between devices, prompt_attention(): lax.all_gather(jnp.concatenate([long_k, long_v], 1), 'blk', axis=0, tiled...  61 us
    pallas_call x1, Pallas kernels, prompt_attention(): pl.pallas_call(body, out_shape=jax.ShapeDtypeStruct((row_count, width), j...  35.5 us
    all_to_all x1, blocking collectives, per_device(): long_rows = lax.all_to_all(long_attn, 'req', 0, 1, tiled=True)  14.6 us
    all_to_all x1, waiting for transfers between devices, pack_attention(): lax.all_to_all(outgoing, 'blk', split_axis=0, concat_axis=0, tiled=True)  11.9 us
    ppermute x1, waiting for transfers between devices, prompt_attention(): lax.ppermute(result[tq:], 'blk', mirror)  11.2 us
    dot_general x1, matrix products, per_device(): jnp.dot(short_rows, w_out, preferred_element_type=jnp.float32)  7.31 us
    all_to_all x1, starting transfers between devices, pack_attention(): lax.all_to_all(outgoing, 'blk', split_axis=0, concat_axis=0, tiled=True)  7.25 us
    sub x1, matrix products, pack_attention(): weights = jnp.where(allowed, jnp.exp(scores - row_max[..., None]), 0.0)  6.25 us
  transfers between devices with their start and end apart: 5, of which 4 were waited for; matrix products, arithmetic and copies ran while one was open for 15% of the time, Pallas kernels for 0%

profile of v17, /device:TPU:0, one launch (start us, length us, event | category | flops | bytes accessed | tf_op | source)
XLA Modules:
  0.0 212.3 jit_solution(8743146890376143229)
XLA Ops:
  7.2 0.0 copy-start
  7.2 0.0 copy-start.6
  7.2 0.0 all-gather.2.cloned.1.call-start
  7.2 2.3 %pad_maximum_fusion = bf16[1024,512]{1,0:T(8,128)(2,1)} fusion(bf16[1024,256]{1,0:T(8,128)(2,1)} %param.12, bf16[1024,256]{1,0:T(8,128)(2,1)} %param.11), kind=kLoop, calls=%fused_computation.18 | loop fusion | flops 2097152 | bytes 2097152 | tf_op jit(solution)/shard_map/concatenate | solution.py:81
  9.6 0.0 copy-start.2
  9.6 0.0 copy-start.3
  9.6 0.0 all-gather.2.cloned.1.call-update
  9.6 0.0 copy-done.6
  9.6 0.1 copy.47
  9.7 0.1 copy.48
  9.8 0.2 reduce_window_sum.11
  10.0 0.1 select_reduce_fusion
  10.2 0.1 copy.52
  10.3 0.1 reshape.234
  10.4 0.0 copy-done
  10.4 0.0 copy-start.4
  10.4 1.6 gather_fusion
  12.0 0.0 copy-start.8
  12.0 0.0 copy-start.7
  12.0 7.2 %all-to-all-start = ((bf16[16,4,2,16,256]{4,3,2,1,0:T(8,128)(2,1)}), bf16[16,4,2,16,256]{4,3,2,1,0:T(8,128)(2,1)S(1)}, u32[]{:S(2)}, u32[]{:S(2)}) async-start(bf16[16,4,2,16,256]{4,3,2,1,0:T(8,128)(2,1)} %bitcast.6), calls=%async_computation | async-start | bytes 2097152 | tf_op jit(solution)/shard_map/all_to_all | solution.py:154
  19.3 0.0 copy-done.2
  19.3 0.7 fusion.48
  20.0 5.3 %collective-permute-start = (bf16[512,256]{1,0:T(8,128)(2,1)}, bf16[512,256]{1,0:T(8,128)(2,1)}, u32[]{:S(2)}, u32[]{:S(2)}) collective-permute-start(bf16[512,256]{1,0:T(8,128)(2,1)} %get-tuple-element.14), channel_id=1, source_target_pairs={{0,120},{8,112},{16,104},{24,96},{32,88},{40,80},{48,72},{56,64},{... | collective-permute-start | bytes 786440 | tf_op jit(solution)/shard_map/ppermute | solution.py:88
  25.3 0.0 copy-done.3
  25.3 0.1 copy.53
  25.5 0.9 copy.55
  26.3 0.0 copy-done.4
  26.3 0.1 copy.57
  26.5 0.9 copy.59
  27.3 0.2 convert_reduce_fusion
  27.5 0.0 copy-done.8
  27.6 0.0 copy-done.7
  27.6 1.9 fusion.6
  29.5 11.9 %all-to-all-done = bf16[16,4,2,16,256]{4,3,2,1,0:T(8,128)(2,1)S(1)} async-done(((bf16[16,4,2,16,256]{4,3,2,1,0:T(8,128)(2,1)}), bf16[16,4,2,16,256]{4,3,2,1,0:T(8,128)(2,1)S(1)}, u32[]{:S(2)}, u32[]{:S(2)}) %all-to-all-start) | async-done | bytes 1048608 | tf_op jit(solution)/shard_map/all_to_all | solution.py:154
  41.4 0.6 gather_fusion.1
  42.0 0.9 fusion.46
  42.9 0.0 copy-start.1
  42.9 1.2 concatenate.32
  44.1 0.9 copy.54
  45.0 0.1 concatenate.35
  45.1 0.1 copy.58
  45.2 0.0 copy-done.1
  45.2 0.0 copy-start.5
  45.2 6.2 %fusion.49 = (f32[2,512]{1,0:T(2,128)S(1)}, bf16[2,512,1536]{1,2,0:T(8,128)(2,1)}) fusion(pred[512,1536]{0,1:T(8,128)(4,1)S(1)} %copy-done.1, bf16[512,2,128]{2,0,1:T(8,128)(2,1)} %copy.55, bf16[1024,2,128]{2,0,1:T(8,128)(2,1)} %copy.54, bf16[512,256]{1,0:T(8,128)(2,1)} %param.13), kind=kOutput, calls=%fused_computation.74 | convolution fusion | flops 413664768 | bytes 4984832 | tf_op jit(solution)/shard_map/sub | solution.py:178
  51.5 0.0 copy-done.5
  51.5 3.3 %fusion.14 = bf16[512,2,128]{2,0,1:T(8,128)(2,1)S(1)} fusion(bf16[2,512,1536]{1,2,0:T(8,128)(2,1)} %get-tuple-element.16, bf16[512,2,128]{2,0,1:T(8,128)(2,1)S(1)} %copy-done.5, bf16[1024,2,128]{2,0,1:T(8,128)(2,1)S(1)} %copy.58, f32[512,2]{0,1:T(2,128)S(1)} %bitcast.74), kind=kOutput, calls=%fused_computation.17 | convolution fusion | flops 404488192 | bytes 4198400 | tf_op jit(solution)/shard_map/hqk,khd->hqd/dot_general | solution.py:180
  54.8 0.3 copy.61
  55.0 0.9 convert_element_type.30
  55.9 4.9 %all-to-all-start.1 = ((bf16[8,64,256]{2,1,0:T(8,128)(2,1)}), bf16[8,64,256]{2,1,0:T(8,128)(2,1)S(1)}, u32[]{:S(2)}, u32[]{:S(2)}) async-start(bf16[8,64,256]{2,1,0:T(8,128)(2,1)} %convert_element_type.30), calls=%async_computation.1 | async-start | bytes 524288 | tf_op jit(solution)/shard_map/all_to_all | solution.py:198
  60.8 0.6 pad_add_fusion.1.pos_ref
  61.5 0.0 collective-permute-done
  61.5 1.8 pad_maximum_fusion.2.q_ref
  63.2 4.9 %all-to-all-done.1 = bf16[8,64,256]{2,1,0:T(8,128)(2,1)S(1)} async-done(((bf16[8,64,256]{2,1,0:T(8,128)(2,1)}), bf16[8,64,256]{2,1,0:T(8,128)(2,1)S(1)}, u32[]{:S(2)}, u32[]{:S(2)}) %all-to-all-start.1) | async-done | bytes 262176 | tf_op jit(solution)/shard_map/all_to_all | solution.py:198
  68.1 7.3 %convolution_convert_fusion.1 = bf16[64,2048]{1,0:T(8,128)(2,1)} fusion(bf16[64,2048]{1,0:T(8,128)(2,1)S(1)} %bitcast.66, bf16[2048,2048]{1,0:T(8,128)(2,1)} %param.19), kind=kOutput, calls=%fused_computation.14 | convolution fusion | flops 537001984 | bytes 8912896 | tf_op jit(solution)/shard_map/dot_general | solution.py:199
  75.4 61.0 %all-gather.2.cloned.1.call-done.k_ref.v_ref = bf16[16384,512]{1,0:T(8,128)(2,1)} async-done(((bf16[1024,512]{1,0:T(8,128)(2,1)}), bf16[16384,512]{1,0:T(8,128)(2,1)}) %all-gather.2.cloned.1.call-update) | async-done | bytes 16777232 | tf_op jit(solution)/shard_map/all_gather | solution.py:81
  136.5 35.5 %shard_map.113 = bf16[1024,256]{1,0:T(8,128)(2,1)} custom-call(s32[3]{0:T(128)} %pad_add_fusion.1.pos_ref, bf16[1024,256]{1,0:T(8,128)(2,1)} %pad_maximum_fusion.2.q_ref, bf16[16384,512]{1,0:T(8,128)(2,1)} %all-gather.2.cloned.1.call-done.k_ref.v_ref, bf16[16384,512]{1,0:T(8,128)(2,1)} %all-gather.2.cloned.1.call-done.k_ref.v_ref), custom_call_target="tpu_custom_call" | custom-call | tf_op jit(solution)/shard_map/pallas_call | solution.py:111
  172.0 1.1 fusion.47
  173.1 0.8 collective-permute-start.1
  173.8 11.2 %collective-permute-done.1 = bf16[512,256]{1,0:T(8,128)(2,1)S(1)} collective-permute-done((bf16[512,256]{1,0:T(8,128)(2,1)S(1)}, bf16[512,256]{1,0:T(8,128)(2,1)S(1)}, u32[]{:S(2)}, u32[]{:S(2)}) %collective-permute-start.1) | collective-permute-done | bytes 262176 | tf_op jit(solution)/shard_map/ppermute | solution.py:131
  185.0 0.3 copy.63
  185.3 14.6 %all_to_all.40 = bf16[8,128,256]{1,2,0:T(8,128)(2,1)S(1)} all-to-all(bf16[8,128,256]{1,2,0:T(8,128)(2,1)S(1)} %copy.63), channel_id=1, replica_groups=mesh['blk'=16,'req'=8] {'req'}, dimensions={0} | all-to-all | bytes 1048576 | tf_op jit(solution)/shard_map/all_to_all | solution.py:201
  199.9 5.5 %convolution_convert_fusion = bf16[128,2048]{1,0:T(8,128)(2,1)} fusion(bf16[128,2048]{0,1:T(8,128)(2,1)S(1)} %bitcast.64, bf16[2048,2048]{1,0:T(8,128)(2,1)} %param.19), kind=kOutput, calls=%fused_computation.13 | convolution fusion | flops 1074003968 | bytes 9437184 | tf_op jit(solution)/shard_map/dot_general | solution.py:202
  (11 shorter events, 0.1 us)
Async XLA Ops:
  7.2 3.2 %copy-start = (bf16[64,2,16,256]{3,2,1,0:T(8,128)(2,1)S(1)}, bf16[64,2,16,256]{3,2,1,0:T(8,128)(2,1)}, u32[]{:S(2)}) copy-start(bf16[64,2,16,256]{3,2,1,0:T(8,128)(2,1)} %param.17) | copy-start | bytes 3145732
  7.2 2.4 %copy-start.6 = (s32[16,16,4]{1,2,0:T(4,128)S(1)}, s32[16,16,4]{1,2,0:T(4,128)}, u32[]{:S(2)}) copy-start(s32[16,16,4]{1,2,0:T(4,128)} %param.18) | copy-start | bytes 12292
  7.2 129.3 %all-gather.2.cloned.1.call-start = ((), (), s32[]{:S(2)}) async-start(), calls=%async_computation.3 | async-start | bytes 17825792 | tf_op jit(solution)/shard_map/all_gather | solution.py:81
  9.6 9.7 %copy-start.2 = (bf16[1024,256]{1,0:T(8,128)(2,1)S(1)}, bf16[1024,256]{1,0:T(8,128)(2,1)}, u32[]{:S(2)}) copy-start(bf16[1024,256]{1,0:T(8,128)(2,1)} %param.10) | copy-start | bytes 1572868
  9.6 15.7 %copy-start.3 = (bf16[512,256]{1,0:T(8,128)(2,1)S(1)}, bf16[512,256]{1,0:T(8,128)(2,1)}, u32[]{:S(2)}) copy-start(bf16[512,256]{1,0:T(8,128)(2,1)} %param.14) | copy-start | bytes 786436
  10.4 15.9 %copy-start.4 = (bf16[512,256]{1,0:T(8,128)(2,1)S(1)}, bf16[512,256]{1,0:T(8,128)(2,1)}, u32[]{:S(2)}) copy-start(bf16[512,256]{1,0:T(8,128)(2,1)} %param.15) | copy-start | bytes 786436
  12.0 15.5 %copy-start.8 = (s32[1,512]{1,0:T(1,128)S(1)}, s32[1,512]{1,0:T(1,128)}, u32[]{:S(2)}) copy-start(s32[1,512]{1,0:T(1,128)} %param.16) | copy-start | bytes 6148
  12.0 15.6 %copy-start.7 = (s32[1536]{0:T(1024)S(1)}, s32[1536]{0:T(1024)}, u32[]{:S(2)}) copy-start(s32[1536]{0:T(1024)} %constant.86.clone.1) | copy-start | bytes 18436
  12.0 29.4 %all-to-all-start = ((bf16[16,4,2,16,256]{4,3,2,1,0:T(8,128)(2,1)}), bf16[16,4,2,16,256]{4,3,2,1,0:T(8,128)(2,1)S(1)}, u32[]{:S(2)}, u32[]{:S(2)}) async-start(bf16[16,4,2,16,256]{4,3,2,1,0:T(8,128)(2,1)} %bitcast.6), calls=%async_computation | async-start | bytes 2097152 | tf_op jit(solution)/shard_map/all_to_all | solution.py:154
  20.0 41.4 %collective-permute-start = (bf16[512,256]{1,0:T(8,128)(2,1)}, bf16[512,256]{1,0:T(8,128)(2,1)}, u32[]{:S(2)}, u32[]{:S(2)}) collective-permute-start(bf16[512,256]{1,0:T(8,128)(2,1)} %get-tuple-element.14), channel_id=1, source_target_pairs={{0,120},{8,112},{16,104},{24,96},{32,88},{40,80},{48,72},{56,64},{... | collective-permute-start | bytes 786440 | tf_op jit(solution)/shard_map/ppermute | solution.py:88
  42.9 2.3 %copy-start.1 = (pred[512,1536]{0,1:T(8,128)(4,1)S(1)}, pred[512,1536]{0,1:T(8,128)(4,1)}, u32[]{:S(2)}) copy-start(pred[512,1536]{0,1:T(8,128)(4,1)} %fusion.6) | copy-start | bytes 2359300
  45.2 6.3 %copy-start.5 = (bf16[512,2,128]{2,0,1:T(8,128)(2,1)S(1)}, bf16[512,2,128]{2,0,1:T(8,128)(2,1)}, u32[]{:S(2)}) copy-start(bf16[512,2,128]{2,0,1:T(8,128)(2,1)} %copy.59) | copy-start | bytes 786436
  55.9 12.2 %all-to-all-start.1 = ((bf16[8,64,256]{2,1,0:T(8,128)(2,1)}), bf16[8,64,256]{2,1,0:T(8,128)(2,1)S(1)}, u32[]{:S(2)}, u32[]{:S(2)}) async-start(bf16[8,64,256]{2,1,0:T(8,128)(2,1)} %convert_element_type.30), calls=%async_computation.1 | async-start | bytes 524288 | tf_op jit(solution)/shard_map/all_to_all | solution.py:198
  173.1 11.9 %collective-permute-start.1 = (bf16[512,256]{1,0:T(8,128)(2,1)S(1)}, bf16[512,256]{1,0:T(8,128)(2,1)S(1)}, u32[]{:S(2)}, u32[]{:S(2)}) collective-permute-start(bf16[512,256]{1,0:T(8,128)(2,1)S(1)} %get-tuple-element.12), channel_id=1, source_target_pairs={{0,120},{8,112},{16,104},{24,96},{32,88},{40,80},{48,72},{56,64},{... | collective-permute-start | bytes 786440 | tf_op jit(solution)/shard_map/ppermute | solution.py:131
Sparse Core Ops, SparseCore 0:
  10.4 126.0 all-gather.1

commit v18 on v17

--- a/solution.py
+++ b/solution.py
@@ -20,7 +20,7 @@
     return q_tile, step - q_tile * pos_ref[2]
 
 
-def flash_body(pos_ref, q_ref, k_ref, v_ref, o_ref, m_sc, l_sc, acc_sc, *, heads, tq, tk):
+def flash_body(pos_ref, q_ref, k_ref, v_ref, own_ref, lent_ref, m_sc, l_sc, acc_sc, *, heads, tq, tk):
     q_tile, k_tile = tile_of_step(pl.program_id(0), pos_ref)
     first_query = pos_ref[q_tile]
     last_tile = (first_query + tq - 1) // tk
@@ -69,10 +69,12 @@
     def _():
         fold(True)
 
-    @pl.when(k_tile == last_tile)
-    def _():
-        for h in range(heads):
-            o_ref[:, h * HD:(h + 1) * HD] = (acc_sc[h] / l_sc[h]).T.astype(o_ref.dtype)
+    for tile, o_ref in ((0, own_ref), (1, lent_ref)):
+
+        @pl.when((k_tile == last_tile) & (q_tile == tile))
+        def _():
+            for h in range(heads):
+                o_ref[:, h * HD:(h + 1) * HD] = (acc_sc[h] / l_sc[h]).T.astype(o_ref.dtype)
 
 
 def prompt_attention(queries, block_index, long_k, long_v, early=None):
@@ -110,7 +112,10 @@
     body = functools.partial(flash_body, heads=heads_dev, tq=tq, tk=tk)
     result = pl.pallas_call(
         body,
-        out_shape=jax.ShapeDtypeStruct((row_count, width), jnp.bfloat16),
+        out_shape=(
+            jax.ShapeDtypeStruct((tq, width), jnp.bfloat16),
+            jax.ShapeDtypeStruct((tq, width), jnp.bfloat16),
+        ),
         grid_spec=pltpu.PrefetchScalarGridSpec(
             num_scalar_prefetch=1,
             grid=(step_count,),
@@ -119,7 +124,10 @@
                 pl.BlockSpec((tk, width), kv_map(0)),
                 pl.BlockSpec((tk, width), kv_map(1)),
             ],
-            out_specs=pl.BlockSpec((tq, width), q_map),
+            out_specs=[
+                pl.BlockSpec((tq, width), lambda step, pos_ref: (0, 0)),
+                pl.BlockSpec((tq, width), lambda step, pos_ref: (0, 0)),
+            ],
             scratch_shapes=[
                 pltpu.VMEM((heads_dev, 1, tq), jnp.float32),
                 pltpu.VMEM((heads_dev, 1, tq), jnp.float32),
@@ -128,7 +136,8 @@
         ),
         compiler_params=pltpu.CompilerParams(dimension_semantics=("arbitrary",)),
     )(tile_pos, jnp.concatenate([queries[:tq], partner_half], 0), kv_piece, kv_piece)
-    merged = jnp.concatenate([result[:tq], lax.ppermute(result[tq:], "blk", mirror)], 0)
+    own_rows, lent_rows = result
+    merged = jnp.concatenate([own_rows, lax.ppermute(lent_rows, "blk", mirror)], 0)
     return merged, early
 
 

time: 213 us -> 213 us (level)
  no operation moved by 1% of the time
where the time goes in v18:
time: 213 us; the launch traced here: 212 us
  waiting for transfers between devices  89.2 us (42%)
  Pallas kernels  35.5 us (17%)
  matrix products  22.3 us (10%)
  starting transfers between devices  18.2 us (9%)
  blocking collectives  14.6 us (7%)
  between operations  14.3 us (7%)
  local copies, waits for them, and re-layouts  9.9 us (5%)
  other arithmetic  8.28 us (4%)
    all_gather x1, waiting for transfers between devices, prompt_attention(): lax.all_gather(jnp.concatenate([long_k, long_v], 1), 'blk', axis=0, tiled...  61 us
    pallas_call x1, Pallas kernels, prompt_attention(): pl.pallas_call(body, out_shape=(jax.ShapeDtypeStruct((tq, width), jnp.bfl...  35.5 us
    all_to_all x1, blocking collectives, per_device(): long_rows = lax.all_to_all(long_attn, 'req', 0, 1, tiled=True)  14.6 us
    all_to_all x1, waiting for transfers between devices, pack_attention(): lax.all_to_all(outgoing, 'blk', split_axis=0, concat_axis=0, tiled=True)  11.9 us
    ppermute x1, waiting for transfers between devices, prompt_attention(): lax.ppermute(lent_rows, 'blk', mirror)  11.4 us
    dot_general x1, matrix products, per_device(): jnp.dot(short_rows, w_out, preferred_element_type=jnp.float32)  7.31 us
    all_to_all x1, starting transfers between devices, pack_attention(): lax.all_to_all(outgoing, 'blk', split_axis=0, concat_axis=0, tiled=True)  7.25 us
    sub x1, matrix products, pack_attention(): weights = jnp.where(allowed, jnp.exp(scores - row_max[..., None]), 0.0)  6.25 us
  transfers between devices with their start and end apart: 5, of which 4 were waited for; matrix products, arithmetic and copies ran while one was open for 15% of the time, Pallas kernels for 0%

profile of v18, /device:TPU:0, one launch (start us, length us, event | category | flops | bytes accessed | tf_op | source)
XLA Modules:
  0.0 212.3 jit_solution(6921206475635719070)
XLA Ops:
  7.2 0.0 copy-start
  7.2 0.0 copy-start.6
  7.2 0.0 all-gather.2.cloned.1.call-start
  7.2 2.3 %pad_maximum_fusion = bf16[1024,512]{1,0:T(8,128)(2,1)} fusion(bf16[1024,256]{1,0:T(8,128)(2,1)} %param.12, bf16[1024,256]{1,0:T(8,128)(2,1)} %param.11), kind=kLoop, calls=%fused_computation.18 | loop fusion | flops 2097152 | bytes 2097152 | tf_op jit(solution)/shard_map/concatenate | solution.py:83
  9.6 0.0 copy-start.2
  9.6 0.0 copy-start.3
  9.6 0.0 all-gather.2.cloned.1.call-update
  9.6 0.0 copy-done.6
  9.6 0.1 copy.47
  9.7 0.1 copy.48
  9.8 0.2 reduce_window_sum.11
  10.0 0.1 select_reduce_fusion
  10.2 0.1 copy.52
  10.3 0.1 reshape.234
  10.4 0.0 copy-done
  10.4 0.0 copy-start.4
  10.4 1.6 gather_fusion
  12.0 0.0 copy-start.8
  12.0 0.0 copy-start.7
  12.0 7.2 %all-to-all-start = ((bf16[16,4,2,16,256]{4,3,2,1,0:T(8,128)(2,1)}), bf16[16,4,2,16,256]{4,3,2,1,0:T(8,128)(2,1)S(1)}, u32[]{:S(2)}, u32[]{:S(2)}) async-start(bf16[16,4,2,16,256]{4,3,2,1,0:T(8,128)(2,1)} %bitcast.6), calls=%async_computation | async-start | bytes 2097152 | tf_op jit(solution)/shard_map/all_to_all | solution.py:163
  19.3 0.0 copy-done.2
  19.3 0.7 fusion.47
  20.0 5.3 %collective-permute-start = (bf16[512,256]{1,0:T(8,128)(2,1)}, bf16[512,256]{1,0:T(8,128)(2,1)}, u32[]{:S(2)}, u32[]{:S(2)}) collective-permute-start(bf16[512,256]{1,0:T(8,128)(2,1)} %get-tuple-element.16), channel_id=1, source_target_pairs={{0,120},{8,112},{16,104},{24,96},{32,88},{40,80},{48,72},{56,64},{... | collective-permute-start | bytes 786440 | tf_op jit(solution)/shard_map/ppermute | solution.py:90
  25.3 0.0 copy-done.3
  25.3 0.1 copy.53
  25.5 0.9 copy.55
  26.3 0.0 copy-done.4
  26.3 0.1 copy.57
  26.5 0.9 copy.59
  27.3 0.2 convert_reduce_fusion
  27.5 0.0 copy-done.8
  27.6 0.0 copy-done.7
  27.6 1.9 fusion.6
  29.5 11.9 %all-to-all-done = bf16[16,4,2,16,256]{4,3,2,1,0:T(8,128)(2,1)S(1)} async-done(((bf16[16,4,2,16,256]{4,3,2,1,0:T(8,128)(2,1)}), bf16[16,4,2,16,256]{4,3,2,1,0:T(8,128)(2,1)S(1)}, u32[]{:S(2)}, u32[]{:S(2)}) %all-to-all-start) | async-done | bytes 1048608 | tf_op jit(solution)/shard_map/all_to_all | solution.py:163
  41.4 0.6 gather_fusion.1
  42.0 0.9 fusion.46
  42.9 0.0 copy-start.1
  42.9 1.2 concatenate.32
  44.1 0.9 copy.54
  45.0 0.1 concatenate.35
  45.1 0.1 copy.58
  45.2 0.0 copy-done.1
  45.2 0.0 copy-start.5
  45.2 6.2 %fusion.48 = (f32[2,512]{1,0:T(2,128)S(1)}, bf16[2,512,1536]{1,2,0:T(8,128)(2,1)}) fusion(pred[512,1536]{0,1:T(8,128)(4,1)S(1)} %copy-done.1, bf16[512,2,128]{2,0,1:T(8,128)(2,1)} %copy.55, bf16[1024,2,128]{2,0,1:T(8,128)(2,1)} %copy.54, bf16[512,256]{1,0:T(8,128)(2,1)} %param.13), kind=kOutput, calls=%fused_computation.73 | convolution fusion | flops 413664768 | bytes 4984832 | tf_op jit(solution)/shard_map/sub | solution.py:187
  51.5 0.0 copy-done.5
  51.5 3.3 %fusion.14 = bf16[512,2,128]{2,0,1:T(8,128)(2,1)S(1)} fusion(bf16[2,512,1536]{1,2,0:T(8,128)(2,1)} %get-tuple-element.18, bf16[512,2,128]{2,0,1:T(8,128)(2,1)S(1)} %copy-done.5, bf16[1024,2,128]{2,0,1:T(8,128)(2,1)S(1)} %copy.58, f32[512,2]{0,1:T(2,128)S(1)} %bitcast.74), kind=kOutput, calls=%fused_computation.17 | convolution fusion | flops 404488192 | bytes 4198400 | tf_op jit(solution)/shard_map/hqk,khd->hqd/dot_general | solution.py:189
  54.8 0.3 copy.61
  55.0 0.9 convert_element_type.30
  55.9 4.9 %all-to-all-start.1 = ((bf16[8,64,256]{2,1,0:T(8,128)(2,1)}), bf16[8,64,256]{2,1,0:T(8,128)(2,1)S(1)}, u32[]{:S(2)}, u32[]{:S(2)}) async-start(bf16[8,64,256]{2,1,0:T(8,128)(2,1)} %convert_element_type.30), calls=%async_computation.1 | async-start | bytes 524288 | tf_op jit(solution)/shard_map/all_to_all | solution.py:207
  60.8 0.6 pad_add_fusion.1.pos_ref
  61.5 0.0 collective-permute-done
  61.5 1.8 pad_maximum_fusion.2.q_ref
  63.2 4.9 %all-to-all-done.1 = bf16[8,64,256]{2,1,0:T(8,128)(2,1)S(1)} async-done(((bf16[8,64,256]{2,1,0:T(8,128)(2,1)}), bf16[8,64,256]{2,1,0:T(8,128)(2,1)S(1)}, u32[]{:S(2)}, u32[]{:S(2)}) %all-to-all-start.1) | async-done | bytes 262176 | tf_op jit(solution)/shard_map/all_to_all | solution.py:207
  68.1 7.3 %convolution_convert_fusion.1 = bf16[64,2048]{1,0:T(8,128)(2,1)} fusion(bf16[64,2048]{1,0:T(8,128)(2,1)S(1)} %bitcast.66, bf16[2048,2048]{1,0:T(8,128)(2,1)} %param.19), kind=kOutput, calls=%fused_computation.14 | convolution fusion | flops 537001984 | bytes 8912896 | tf_op jit(solution)/shard_map/dot_general | solution.py:208
  75.4 61.0 %all-gather.2.cloned.1.call-done.k_ref.v_ref = bf16[16384,512]{1,0:T(8,128)(2,1)} async-done(((bf16[1024,512]{1,0:T(8,128)(2,1)}), bf16[16384,512]{1,0:T(8,128)(2,1)}) %all-gather.2.cloned.1.call-update) | async-done | bytes 16777232 | tf_op jit(solution)/shard_map/all_gather | solution.py:83
  136.5 35.5 %shard_map.113 = (bf16[512,256]{1,0:T(8,128)(2,1)}, bf16[512,256]{1,0:T(8,128)(2,1)}) custom-call(s32[3]{0:T(128)} %pad_add_fusion.1.pos_ref, bf16[1024,256]{1,0:T(8,128)(2,1)} %pad_maximum_fusion.2.q_ref, bf16[16384,512]{1,0:T(8,128)(2,1)} %all-gather.2.cloned.1.call-done.k_ref.v_ref, bf16[16384,512]{1,0:T(8,128)(2,1)} %all-gather.2.cloned.1.call-done.k_ref.v_ref), custom_call_target="tpu_custom_call" | custom-call | tf_op jit(solution)/shard_map/pallas_call | solution.py:113
  172.0 0.7 collective-permute-start.1
  172.7 11.4 %collective-permute-done.1 = bf16[512,256]{1,0:T(8,128)(2,1)S(1)} collective-permute-done((bf16[512,256]{1,0:T(8,128)(2,1)}, bf16[512,256]{1,0:T(8,128)(2,1)S(1)}, u32[]{:S(2)}, u32[]{:S(2)}) %collective-permute-start.1) | collective-permute-done | bytes 262176 | tf_op jit(solution)/shard_map/ppermute | solution.py:140
  184.1 1.0 pad_maximum_fusion.3
  185.1 0.3 copy.63
  185.4 14.6 %all_to_all.40 = bf16[8,128,256]{1,2,0:T(8,128)(2,1)S(1)} all-to-all(bf16[8,128,256]{1,2,0:T(8,128)(2,1)S(1)} %copy.63), channel_id=1, replica_groups=mesh['blk'=16,'req'=8] {'req'}, dimensions={0} | all-to-all | bytes 1048576 | tf_op jit(solution)/shard_map/all_to_all | solution.py:210
  200.0 5.5 %convolution_convert_fusion = bf16[128,2048]{1,0:T(8,128)(2,1)} fusion(bf16[128,2048]{0,1:T(8,128)(2,1)S(1)} %bitcast.64, bf16[2048,2048]{1,0:T(8,128)(2,1)} %param.19), kind=kOutput, calls=%fused_computation.13 | convolution fusion | flops 1074003968 | bytes 9437184 | tf_op jit(solution)/shard_map/dot_general | solution.py:211
  (10 shorter events, 0.1 us)
Async XLA Ops:
  7.2 3.2 %copy-start = (bf16[64,2,16,256]{3,2,1,0:T(8,128)(2,1)S(1)}, bf16[64,2,16,256]{3,2,1,0:T(8,128)(2,1)}, u32[]{:S(2)}) copy-start(bf16[64,2,16,256]{3,2,1,0:T(8,128)(2,1)} %param.17) | copy-start | bytes 3145732
  7.2 2.4 %copy-start.6 = (s32[16,16,4]{1,2,0:T(4,128)S(1)}, s32[16,16,4]{1,2,0:T(4,128)}, u32[]{:S(2)}) copy-start(s32[16,16,4]{1,2,0:T(4,128)} %param.18) | copy-start | bytes 12292
  7.2 129.3 %all-gather.2.cloned.1.call-start = ((), (), s32[]{:S(2)}) async-start(), calls=%async_computation.3 | async-start | bytes 17825792 | tf_op jit(solution)/shard_map/all_gather | solution.py:83
  9.6 9.7 %copy-start.2 = (bf16[1024,256]{1,0:T(8,128)(2,1)S(1)}, bf16[1024,256]{1,0:T(8,128)(2,1)}, u32[]{:S(2)}) copy-start(bf16[1024,256]{1,0:T(8,128)(2,1)} %param.10) | copy-start | bytes 1572868
  9.6 15.7 %copy-start.3 = (bf16[512,256]{1,0:T(8,128)(2,1)S(1)}, bf16[512,256]{1,0:T(8,128)(2,1)}, u32[]{:S(2)}) copy-start(bf16[512,256]{1,0:T(8,128)(2,1)} %param.14) | copy-start | bytes 786436
  10.4 15.9 %copy-start.4 = (bf16[512,256]{1,0:T(8,128)(2,1)S(1)}, bf16[512,256]{1,0:T(8,128)(2,1)}, u32[]{:S(2)}) copy-start(bf16[512,256]{1,0:T(8,128)(2,1)} %param.15) | copy-start | bytes 786436
  12.0 15.5 %copy-start.8 = (s32[1,512]{1,0:T(1,128)S(1)}, s32[1,512]{1,0:T(1,128)}, u32[]{:S(2)}) copy-start(s32[1,512]{1,0:T(1,128)} %param.16) | copy-start | bytes 6148
  12.0 15.6 %copy-start.7 = (s32[1536]{0:T(1024)S(1)}, s32[1536]{0:T(1024)}, u32[]{:S(2)}) copy-start(s32[1536]{0:T(1024)} %constant.86.clone.1) | copy-start | bytes 18436
  12.0 29.4 %all-to-all-start = ((bf16[16,4,2,16,256]{4,3,2,1,0:T(8,128)(2,1)}), bf16[16,4,2,16,256]{4,3,2,1,0:T(8,128)(2,1)S(1)}, u32[]{:S(2)}, u32[]{:S(2)}) async-start(bf16[16,4,2,16,256]{4,3,2,1,0:T(8,128)(2,1)} %bitcast.6), calls=%async_computation | async-start | bytes 2097152 | tf_op jit(solution)/shard_map/all_to_all | solution.py:163
  20.0 41.4 %collective-permute-start = (bf16[512,256]{1,0:T(8,128)(2,1)}, bf16[512,256]{1,0:T(8,128)(2,1)}, u32[]{:S(2)}, u32[]{:S(2)}) collective-permute-start(bf16[512,256]{1,0:T(8,128)(2,1)} %get-tuple-element.16), channel_id=1, source_target_pairs={{0,120},{8,112},{16,104},{24,96},{32,88},{40,80},{48,72},{56,64},{... | collective-permute-start | bytes 786440 | tf_op jit(solution)/shard_map/ppermute | solution.py:90
  42.9 2.3 %copy-start.1 = (pred[512,1536]{0,1:T(8,128)(4,1)S(1)}, pred[512,1536]{0,1:T(8,128)(4,1)}, u32[]{:S(2)}) copy-start(pred[512,1536]{0,1:T(8,128)(4,1)} %fusion.6) | copy-start | bytes 2359300
  45.2 6.3 %copy-start.5 = (bf16[512,2,128]{2,0,1:T(8,128)(2,1)S(1)}, bf16[512,2,128]{2,0,1:T(8,128)(2,1)}, u32[]{:S(2)}) copy-start(bf16[512,2,128]{2,0,1:T(8,128)(2,1)} %copy.59) | copy-start | bytes 786436
  55.9 12.2 %all-to-all-start.1 = ((bf16[8,64,256]{2,1,0:T(8,128)(2,1)}), bf16[8,64,256]{2,1,0:T(8,128)(2,1)S(1)}, u32[]{:S(2)}, u32[]{:S(2)}) async-start(bf16[8,64,256]{2,1,0:T(8,128)(2,1)} %convert_element_type.30), calls=%async_computation.1 | async-start | bytes 524288 | tf_op jit(solution)/shard_map/all_to_all | solution.py:207
  172.0 12.1 %collective-permute-start.1 = (bf16[512,256]{1,0:T(8,128)(2,1)}, bf16[512,256]{1,0:T(8,128)(2,1)S(1)}, u32[]{:S(2)}, u32[]{:S(2)}) collective-permute-start(bf16[512,256]{1,0:T(8,128)(2,1)} %get-tuple-element.8), channel_id=1, source_target_pairs={{0,120},{8,112},{16,104},{24,96},{32,88},{40,80},{48,72},{56,64},{... | collective-permute-start | bytes 786440 | tf_op jit(solution)/shard_map/ppermute | solution.py:140
Sparse Core Ops, SparseCore 0:
  10.4 126.0 all-gather.1
